TPU v7x, 128 devices: a whole 4x4x4 slice. The times are simulated.
128 devices in a mesh: segment: 4 (over x), fsdp: 16 (over y, z_hi, core), rep: 2 (over z_lo).
Axes of the slice: x: 4, y: 4, z: 4 (z_hi: 2, z_lo: 2; z = z_hi * 2 + z_lo), core: 2. Of those that a mesh axis runs over, the one named last changes fastest.
Arguments:
- token_ids: int32 [128, 128], P('fsdp'), may hold values from 0 to 127
- seq_lengths: int32 [128], P('fsdp'), may hold values from 32 to 128, as said below
- quant_scores: int32 [128], P('fsdp'), may hold values from 0 to 64
- embed_table: bfloat16 [128, 4096], replicated, may hold values from -6 to 6
- prior_weight: bfloat16 [4, 4096, 4096], P('segment', None, 'rep'), may hold values from -0.09375 to 0.09375
- prior_gain: float32 [4, 4096], P('segment'), may hold values from 0.25 to 1.75
- final_gain: float32 [4096], replicated, may hold values from 0.25 to 1.75
- head_weight: bfloat16 [4096, 128], replicated, may hold values from -0.25 to 0.25
- agent_down: bfloat16 [4096, 256], P('fsdp'), may hold values from -0.09375 to 0.09375
- agent_up: bfloat16 [4096, 256], P('fsdp'), may hold values from -0.375 to 0.375
Outputs:
- down_gradient: float32 [4096, 256], P(('segment', 'fsdp', 'rep'))
- up_gradient: float32 [4096, 256], P(('segment', 'fsdp', 'rep'))
Inputs may be any that keep to these rules, and one draw needn't show every extreme that they name: `seq_lengths`: every sequence keeps at least 32 tokens, and some sequence in every draw has all 128.
All inputs are finite; a program needn't handle non-finite values.
Results may differ from a plain program's by a relative error of at most 0.0081.
Values may be sent and summed in bfloat16 or wider, within the bound.
No kernel may reach another device: no remote copies, remote signals or barrier semaphores. Data moves between devices by JAX's collectives and lax.ppermute only.
A program may use at most 128 MiB of HBM per device.

v0:
```python
import jax
import jax.numpy as jnp
from jax import lax
from jax.sharding import PartitionSpec as P

LEVELS = 64


epsilon = 1e-05
sigma_weight = 2.0


def passed_along(x, axis, by):
    size = lax.axis_size(axis)
    pairs = [(i, i + by) for i in range(size) if 0 <= i + by < size]
    return lax.ppermute(x, axis, pairs)


def spread(x, axis, root):
    mine = lax.axis_index(axis) == root
    return lax.psum(jnp.where(mine, x, jnp.zeros_like(x)), axis)


def rms_scale(values):
    squares = jnp.mean(values * values, axis=-1, keepdims=True)
    return lax.rsqrt(squares + epsilon)


def lookup_rows(row_ids, embed_table):
    vocab_size = embed_table.shape[0]
    column = jnp.arange(vocab_size, dtype=jnp.int32)
    onehot = (row_ids[:, None] == column[None, :]).astype(jnp.bfloat16)
    return jnp.dot(onehot, embed_table, preferred_element_type=jnp.float32).astype(jnp.bfloat16)


def picked_logprob(logprob, targets):
    vocab_size = logprob.shape[-1]
    column = jnp.arange(vocab_size, dtype=jnp.int32)
    return jnp.sum(jnp.where(column[None, :] == targets[:, None], logprob, 0.0), axis=-1)


def on_device(
    token_ids,
    seq_lengths,
    quant_scores,
    embed_table,
    prior_weight,
    prior_gain,
    final_gain,
    head_weight,
    agent_down,
    agent_up,
):
    segments = lax.axis_size("segment")
    replicas = lax.axis_size("rep")
    segment_pos = lax.axis_index("segment")
    rep_pos = lax.axis_index("rep")
    group_seqs, seq_len = token_ids.shape
    model_width = embed_table.shape[1]
    vocab_size = embed_table.shape[0]
    half_width = prior_weight.shape[2]
    per_device = group_seqs // (segments * replicas)
    micro_count = 4
    total_rows = group_seqs * seq_len
    block_rows = total_rows // micro_count
    tick_count = micro_count + segments - 1
    flat_ids = token_ids.reshape(-1)
    weight_local = prior_weight[0]
    gain_local = prior_gain[0]
    is_first = segment_pos == 0
    is_last = segment_pos == segments - 1

    def apply_segment(current):
        wide_rows = current.astype(jnp.float32)
        normed = (wide_rows * rms_scale(wide_rows) * gain_local).astype(jnp.bfloat16)
        update = jnp.dot(normed, weight_local, preferred_element_type=jnp.float32)
        own_half = lax.dynamic_slice_in_dim(wide_rows, rep_pos * half_width, half_width, 1)
        return (own_half + update).astype(jnp.bfloat16)

    def skip_segment(current):
        return jnp.zeros((block_rows, half_width), jnp.bfloat16)

    def segment_step(tick_pos, received_full):
        micro_pos = tick_pos - segment_pos
        active = (micro_pos >= 0) & (micro_pos < micro_count)
        fresh_pos = jnp.clip(tick_pos, 0, micro_count - 1)
        embedded = lookup_rows(
            lax.dynamic_slice_in_dim(flat_ids, fresh_pos * block_rows, block_rows, 0), embed_table
        )
        current = jnp.where(is_first, embedded, received_full)
        result = lax.cond(active, apply_segment, skip_segment, current)
        return (active, jnp.clip(micro_pos, 0, micro_count - 1), result)

    def store_block(stored, active, slot_pos, block):
        previous = lax.dynamic_slice_in_dim(stored, slot_pos * block_rows, block_rows, 0)
        chosen = jnp.where(active & is_last, block, previous)
        return lax.dynamic_update_slice_in_dim(stored, chosen, slot_pos * block_rows, 0)

    def tick_whole(tick_pos, state_pair):
        incoming, stored = state_pair
        active, slot_pos, result = segment_step(tick_pos, incoming)
        joined = lax.all_gather(result, "rep", axis=1, tiled=True)
        stored = store_block(stored, active, slot_pos, joined)
        incoming = passed_along(joined, "segment", 1)
        return (incoming, stored)

    initial = (
        jnp.zeros((block_rows, model_width), jnp.bfloat16),
        jnp.zeros((total_rows, model_width), jnp.bfloat16),
    )
    final_rows = lax.fori_loop(0, tick_count, tick_whole, initial)[1]
    positions = jnp.arange(seq_len, dtype=jnp.int32)
    next_ids = jnp.concatenate([token_ids[:, 1:], token_ids[:, :1]], axis=1)
    live_mask = (positions[None, :] < seq_lengths[:, None] - 1).astype(jnp.float32)
    counts = (seq_lengths - 1).astype(jnp.float32)

    def prior_scores(rows_bf):
        wide_rows = rows_bf.astype(jnp.float32)
        prior_final = (wide_rows * rms_scale(wide_rows) * final_gain).astype(jnp.bfloat16)
        logprob = jax.nn.log_softmax(
            jnp.dot(prior_final, head_weight, preferred_element_type=jnp.float32), axis=-1
        )
        token_terms = picked_logprob(logprob, next_ids.reshape(-1)).reshape(group_seqs, seq_len)
        return jnp.sum(token_terms * live_mask, axis=1) / counts

    def no_scores(rows_bf):
        return jnp.zeros((group_seqs,), jnp.float32)

    prior_group = lax.cond(is_last, prior_scores, no_scores, final_rows)
    prior_group = spread(prior_group, "segment", segments - 1)
    own_seq = (segment_pos * replicas + rep_pos) * per_device
    prior_mine = lax.dynamic_slice_in_dim(prior_group, own_seq, per_device, 0)
    mine_ids = lax.dynamic_slice_in_dim(token_ids, own_seq, per_device, 0).reshape(-1)
    mine_next = lax.dynamic_slice_in_dim(next_ids, own_seq, per_device, 0).reshape(-1)
    mine_live = lax.dynamic_slice_in_dim(live_mask, own_seq, per_device, 0)
    mine_counts = lax.dynamic_slice_in_dim(counts, own_seq, per_device, 0)
    mine_scores = lax.dynamic_slice_in_dim(quant_scores, own_seq, per_device, 0)
    down_full, up_full = (
        lax.all_gather(agent_down, "fsdp", axis=0, tiled=True),
        lax.all_gather(agent_up, "fsdp", axis=0, tiled=True),
    )
    start_wide = lookup_rows(mine_ids, embed_table).astype(jnp.float32)
    unit_rows = (start_wide * rms_scale(start_wide)).astype(jnp.bfloat16)
    latent = jnp.dot(unit_rows, down_full, preferred_element_type=jnp.float32).astype(jnp.bfloat16)
    hidden = start_wide + lax.dot_general(
        latent, up_full, (((1,), (1,)), ((), ())), preferred_element_type=jnp.float32
    )
    inverse = rms_scale(hidden)
    agent_final = (hidden * inverse * final_gain).astype(jnp.bfloat16)
    logprob = jax.nn.log_softmax(
        jnp.dot(agent_final, head_weight, preferred_element_type=jnp.float32), axis=-1
    )
    agent_ll = (
        jnp.sum(picked_logprob(logprob, mine_next).reshape(per_device, seq_len) * mine_live, axis=1)
        / mine_counts
    )
    margin = prior_mine + sigma_weight * mine_scores.astype(jnp.float32) / LEVELS - agent_ll
    row_factor = ((2.0 * margin / mine_counts)[:, None] * mine_live).reshape(-1)
    column = jnp.arange(vocab_size, dtype=jnp.int32)
    onehot_next = (mine_next[:, None] == column[None, :]).astype(jnp.float32)
    logit_grad = (row_factor[:, None] * (jnp.exp(logprob) - onehot_next)).astype(jnp.bfloat16)
    scaled_grad = (
        lax.dot_general(
            logit_grad, head_weight, (((1,), (1,)), ((), ())), preferred_element_type=jnp.float32
        )
        * final_gain
    )
    hidden_grad = (
        inverse * scaled_grad
        - hidden
        * inverse
        * inverse
        * inverse
        * jnp.mean(hidden * scaled_grad, axis=-1, keepdims=True)
    ).astype(jnp.bfloat16)
    up_grad = lax.dot_general(
        hidden_grad, latent, (((0,), (0,)), ((), ())), preferred_element_type=jnp.float32
    )
    latent_grad = jnp.dot(hidden_grad, up_full, preferred_element_type=jnp.float32).astype(
        jnp.bfloat16
    )
    down_grad = lax.dot_general(
        unit_rows, latent_grad, (((0,), (0,)), ((), ())), preferred_element_type=jnp.float32
    )
    down_share, up_share = (
        lax.psum_scatter(down_grad, ("segment", "fsdp", "rep"), scatter_dimension=0, tiled=True),
        lax.psum_scatter(up_grad, ("segment", "fsdp", "rep"), scatter_dimension=0, tiled=True),
    )
    return (down_share, up_share)


def solution(mesh):
    placed = (
        P("fsdp", None),
        P("fsdp"),
        P("fsdp"),
        P(),
        P("segment", None, "rep"),
        P("segment", None),
        P(),
        P(),
        P("fsdp", None),
        P("fsdp", None),
    )
    return jax.shard_map(
        on_device,
        mesh=mesh,
        in_specs=placed,
        out_specs=(P(("segment", "fsdp", "rep"), None), P(("segment", "fsdp", "rep"), None)),
        check_vma=False,
    )
```

profile of v0, /device:TPU:0, one launch (start us, length us, event | category | flops | bytes accessed | tf_op | source)
XLA Modules:
  0.0 2145.9 jit_solution(12127194747232947936)
XLA Ops:
  8.3 4.3 broadcast_in_dim.30
  12.6 715.6 %while.15 = (s32[]{:T(128)}, bf16[256,4096]{1,0:T(8,128)(2,1)S(1)}, bf16[1024,4096]{1,0:T(8,128)(2,1)}, s32[]{:T(128)}, s32[1024]{0:T(1024)S(1)}, /*index=5*/bf1...) while((s32[]{:T(128)}, bf16[256,4096]{1,0:T(8,128)(2,1)S(1)}, ...), condition=%wide.region_6.7_spmd, body=%wide.region_2.6_spmd.sunk | while | flops 4573921792 | bytes 63987248 | solution.py:111
  13.5 14.8 conditional.4
  16.2 12.1 fusion
  29.3 35.9 %all-gather.8.cloned.1.call-done = bf16[256,4096]{1,0:T(8,128)(2,1)} async-done(((bf16[256,2048]{1,0:T(8,128)(2,1)}), bf16[256,4096]{1,0:T(8,128)(2,1)}) %all-gather.8.cloned.1.call-update) | async-done | bytes 2097168 | tf_op jit(solution)/shard_map/while/body/eval_jaxpr/all_gather | solution.py:102
  68.7 3.8 select_dynamic-update-slice_fusion.2
  72.4 41.1 %collective-permute-done = bf16[256,4096]{1,0:T(8,128)(2,1)S(1)} collective-permute-done((bf16[256,4096]{1,0:T(8,128)(2,1)}, bf16[256,4096]{1,0:T(8,128)(2,1)S(1)}, u32[]{:S(2)}, u32[]{:S(2)}) %collective-permute-start) | collective-permute-done | bytes 2097184 | tf_op jit(solution)/shard_map/while/body/eval_jaxpr/ppermute | solution.py:16
  114.4 14.8 conditional.4
  117.0 12.1 fusion
  130.2 36.2 %all-gather.8.cloned.1.call-done = bf16[256,4096]{1,0:T(8,128)(2,1)} async-done(((bf16[256,2048]{1,0:T(8,128)(2,1)}), bf16[256,4096]{1,0:T(8,128)(2,1)}) %all-gather.8.cloned.1.call-update) | async-done | bytes 2097168 | tf_op jit(solution)/shard_map/while/body/eval_jaxpr/all_gather | solution.py:102
  173.6 41.2 %collective-permute-done = bf16[256,4096]{1,0:T(8,128)(2,1)S(1)} collective-permute-done((bf16[256,4096]{1,0:T(8,128)(2,1)}, bf16[256,4096]{1,0:T(8,128)(2,1)S(1)}, u32[]{:S(2)}, u32[]{:S(2)}) %collective-permute-start) | collective-permute-done | bytes 2097184 | tf_op jit(solution)/shard_map/while/body/eval_jaxpr/ppermute | solution.py:16
  215.6 14.8 conditional.4
  218.3 12.1 fusion
  231.4 37.7 %all-gather.8.cloned.1.call-done = bf16[256,4096]{1,0:T(8,128)(2,1)} async-done(((bf16[256,2048]{1,0:T(8,128)(2,1)}), bf16[256,4096]{1,0:T(8,128)(2,1)}) %all-gather.8.cloned.1.call-update) | async-done | bytes 2097168 | tf_op jit(solution)/shard_map/while/body/eval_jaxpr/all_gather | solution.py:102
  276.4 41.1 %collective-permute-done = bf16[256,4096]{1,0:T(8,128)(2,1)S(1)} collective-permute-done((bf16[256,4096]{1,0:T(8,128)(2,1)}, bf16[256,4096]{1,0:T(8,128)(2,1)S(1)}, u32[]{:S(2)}, u32[]{:S(2)}) %collective-permute-start) | collective-permute-done | bytes 2097184 | tf_op jit(solution)/shard_map/while/body/eval_jaxpr/ppermute | solution.py:16
  318.3 14.8 conditional.4
  321.0 12.1 fusion
  334.1 37.7 %all-gather.8.cloned.1.call-done = bf16[256,4096]{1,0:T(8,128)(2,1)} async-done(((bf16[256,2048]{1,0:T(8,128)(2,1)}), bf16[256,4096]{1,0:T(8,128)(2,1)}) %all-gather.8.cloned.1.call-update) | async-done | bytes 2097168 | tf_op jit(solution)/shard_map/while/body/eval_jaxpr/all_gather | solution.py:102
  375.4 3.7 select_dynamic-update-slice_fusion.2
  379.1 41.1 %collective-permute-done = bf16[256,4096]{1,0:T(8,128)(2,1)S(1)} collective-permute-done((bf16[256,4096]{1,0:T(8,128)(2,1)}, bf16[256,4096]{1,0:T(8,128)(2,1)S(1)}, u32[]{:S(2)}, u32[]{:S(2)}) %collective-permute-start) | collective-permute-done | bytes 2097184 | tf_op jit(solution)/shard_map/while/body/eval_jaxpr/ppermute | solution.py:16
  422.2 52.4 %all-gather.8.cloned.1.call-done = bf16[256,4096]{1,0:T(8,128)(2,1)} async-done(((bf16[256,2048]{1,0:T(8,128)(2,1)}), bf16[256,4096]{1,0:T(8,128)(2,1)}) %all-gather.8.cloned.1.call-update) | async-done | bytes 2097168 | tf_op jit(solution)/shard_map/while/body/eval_jaxpr/all_gather | solution.py:102
  481.8 41.1 %collective-permute-done = bf16[256,4096]{1,0:T(8,128)(2,1)S(1)} collective-permute-done((bf16[256,4096]{1,0:T(8,128)(2,1)}, bf16[256,4096]{1,0:T(8,128)(2,1)S(1)}, u32[]{:S(2)}, u32[]{:S(2)}) %collective-permute-start) | collective-permute-done | bytes 2097184 | tf_op jit(solution)/shard_map/while/body/eval_jaxpr/ppermute | solution.py:16
  524.9 52.4 %all-gather.8.cloned.1.call-done = bf16[256,4096]{1,0:T(8,128)(2,1)} async-done(((bf16[256,2048]{1,0:T(8,128)(2,1)}), bf16[256,4096]{1,0:T(8,128)(2,1)}) %all-gather.8.cloned.1.call-update) | async-done | bytes 2097168 | tf_op jit(solution)/shard_map/while/body/eval_jaxpr/all_gather | solution.py:102
  584.6 41.1 %collective-permute-done = bf16[256,4096]{1,0:T(8,128)(2,1)S(1)} collective-permute-done((bf16[256,4096]{1,0:T(8,128)(2,1)}, bf16[256,4096]{1,0:T(8,128)(2,1)S(1)}, u32[]{:S(2)}, u32[]{:S(2)}) %collective-permute-start) | collective-permute-done | bytes 2097184 | tf_op jit(solution)/shard_map/while/body/eval_jaxpr/ppermute | solution.py:16
  627.7 52.1 %all-gather.8.cloned.1.call-done = bf16[256,4096]{1,0:T(8,128)(2,1)} async-done(((bf16[256,2048]{1,0:T(8,128)(2,1)}), bf16[256,4096]{1,0:T(8,128)(2,1)}) %all-gather.8.cloned.1.call-update) | async-done | bytes 2097168 | tf_op jit(solution)/shard_map/while/body/eval_jaxpr/all_gather | solution.py:102
  687.0 41.1 %collective-permute-done = bf16[256,4096]{1,0:T(8,128)(2,1)S(1)} collective-permute-done((bf16[256,4096]{1,0:T(8,128)(2,1)}, bf16[256,4096]{1,0:T(8,128)(2,1)S(1)}, u32[]{:S(2)}, u32[]{:S(2)}) %collective-permute-start) | collective-permute-done | bytes 2097184 | tf_op jit(solution)/shard_map/while/body/eval_jaxpr/ppermute | solution.py:16
  729.6 21.7 %psum.7 = f32[8]{0:T(128)S(1)} all-reduce(f32[8]{0:T(128)S(1)} %broadcast_select_fusion), channel_id=1, replica_groups=mesh['segment'=4,'fsdp'=16,'rep'=2] {'segment'}, use_global_device_ids=true, to_apply=%region_14.15 | all-reduce | flops 8 | bytes 64 | tf_op jit(solution)/shard_map/psum | solution.py:21
  755.1 26.0 %all-gather.4.cloned.1.call-done = bf16[4096,256]{1,0:T(8,128)(2,1)} async-done(((bf16[256,256]{1,0:T(8,128)(2,1)}), bf16[4096,256]{1,0:T(8,128)(2,1)}) %all-gather.4.cloned.1.call-update) | async-done | bytes 2097168 | tf_op jit(solution)/shard_map/all_gather | solution.py:139
  783.2 47.1 %all-gather.6.cloned.1.call-done = bf16[4096,256]{1,0:T(8,128)(2,1)} async-done(((bf16[256,256]{1,0:T(8,128)(2,1)}), bf16[4096,256]{1,0:T(8,128)(2,1)}) %all-gather.6.cloned.1.call-update) | async-done | bytes 2097168 | tf_op jit(solution)/shard_map/all_gather | solution.py:140
  837.4 5.2 fusion.13
  845.4 646.0 %reduce-scatter.3.cloned.1.call-done = f32[32,256]{1,0:T(8,128)} async-done(((f32[4096,256]{1,0:T(8,128)}), f32[32,256]{1,0:T(8,128)}) %reduce-scatter.3.cloned.1.call-update) | async-done | bytes 32784 | tf_op jit(solution)/shard_map/reduce_scatter | solution.py:186
  1491.3 647.0 %reduce-scatter.5.cloned.1.call-done = f32[32,256]{1,0:T(8,128)} async-done(((f32[4096,256]{1,0:T(8,128)}), f32[32,256]{1,0:T(8,128)}) %reduce-scatter.5.cloned.1.call-update) | async-done | bytes 32784 | tf_op jit(solution)/shard_map/reduce_scatter | solution.py:187
  (117 shorter events, 81.1 us)
Async XLA Ops:
  8.2 4.3 copy-start.2
  8.3 4.3 copy-start.5
  8.3 4.3 copy-start.6
  12.6 716.9 %copy-start.7 = (s32[8]{0:T(128)S(1)}, s32[8]{0:T(128)}, u32[]{:S(2)}) copy-start(s32[8]{0:T(128)} %param.17) | copy-start | bytes 100
  12.6 717.0 %copy-start.4 = (f32[4096]{0:T(1024)S(1)}, f32[4096]{0:T(1024)}, u32[]{:S(2)}) copy-start(f32[4096]{0:T(1024)} %param.22) | copy-start | bytes 49156
  12.6 52.6 %all-gather.8.cloned.1.call-start = ((), (), s32[]{:S(2)}) async-start(), calls=%async_computation.6 | async-start | bytes 3145728 | tf_op jit(solution)/shard_map/while/body/eval_jaxpr/all_gather | solution.py:102
  28.3 1.0 copy-start
  65.2 48.4 %collective-permute-start = (bf16[256,4096]{1,0:T(8,128)(2,1)}, bf16[256,4096]{1,0:T(8,128)(2,1)S(1)}, u32[]{:S(2)}, u32[]{:S(2)}) collective-permute-start(bf16[256,4096]{1,0:T(8,128)(2,1)} %all-gather.8.cloned.1.call-done), channel_id=1, source_target_pairs={{0,32},{32,64},{64,96},{1,33},{33,65},{65,97},{2,34},{34,66},{66,9... | collective-permute-start | bytes 6291464 | tf_op jit(solution)/shard_map/while/body/eval_jaxpr/ppermute | solution.py:16
  113.5 52.8 %all-gather.8.cloned.1.call-start = ((), (), s32[]{:S(2)}) async-start(), calls=%async_computation.6 | async-start | bytes 3145728 | tf_op jit(solution)/shard_map/while/body/eval_jaxpr/all_gather | solution.py:102
  129.2 1.0 copy-start
  166.4 48.4 %collective-permute-start = (bf16[256,4096]{1,0:T(8,128)(2,1)}, bf16[256,4096]{1,0:T(8,128)(2,1)S(1)}, u32[]{:S(2)}, u32[]{:S(2)}) collective-permute-start(bf16[256,4096]{1,0:T(8,128)(2,1)} %all-gather.8.cloned.1.call-done), channel_id=1, source_target_pairs={{0,32},{32,64},{64,96},{1,33},{33,65},{65,97},{2,34},{34,66},{66,9... | collective-permute-start | bytes 6291464 | tf_op jit(solution)/shard_map/while/body/eval_jaxpr/ppermute | solution.py:16
  214.8 54.3 %all-gather.8.cloned.1.call-start = ((), (), s32[]{:S(2)}) async-start(), calls=%async_computation.6 | async-start | bytes 3145728 | tf_op jit(solution)/shard_map/while/body/eval_jaxpr/all_gather | solution.py:102
  230.4 1.0 copy-start
  269.1 48.4 %collective-permute-start = (bf16[256,4096]{1,0:T(8,128)(2,1)}, bf16[256,4096]{1,0:T(8,128)(2,1)S(1)}, u32[]{:S(2)}, u32[]{:S(2)}) collective-permute-start(bf16[256,4096]{1,0:T(8,128)(2,1)} %all-gather.8.cloned.1.call-done), channel_id=1, source_target_pairs={{0,32},{32,64},{64,96},{1,33},{33,65},{65,97},{2,34},{34,66},{66,9... | collective-permute-start | bytes 6291464 | tf_op jit(solution)/shard_map/while/body/eval_jaxpr/ppermute | solution.py:16
  317.5 54.3 %all-gather.8.cloned.1.call-start = ((), (), s32[]{:S(2)}) async-start(), calls=%async_computation.6 | async-start | bytes 3145728 | tf_op jit(solution)/shard_map/while/body/eval_jaxpr/all_gather | solution.py:102
  333.1 1.0 copy-start
  371.8 48.4 %collective-permute-start = (bf16[256,4096]{1,0:T(8,128)(2,1)}, bf16[256,4096]{1,0:T(8,128)(2,1)S(1)}, u32[]{:S(2)}, u32[]{:S(2)}) collective-permute-start(bf16[256,4096]{1,0:T(8,128)(2,1)} %all-gather.8.cloned.1.call-done), channel_id=1, source_target_pairs={{0,32},{32,64},{64,96},{1,33},{33,65},{65,97},{2,34},{34,66},{66,9... | collective-permute-start | bytes 6291464 | tf_op jit(solution)/shard_map/while/body/eval_jaxpr/ppermute | solution.py:16
  420.2 54.3 %all-gather.8.cloned.1.call-start = ((), (), s32[]{:S(2)}) async-start(), calls=%async_computation.6 | async-start | bytes 3145728 | tf_op jit(solution)/shard_map/while/body/eval_jaxpr/all_gather | solution.py:102
  421.2 1.0 copy-start
  474.6 48.4 %collective-permute-start = (bf16[256,4096]{1,0:T(8,128)(2,1)}, bf16[256,4096]{1,0:T(8,128)(2,1)S(1)}, u32[]{:S(2)}, u32[]{:S(2)}) collective-permute-start(bf16[256,4096]{1,0:T(8,128)(2,1)} %all-gather.8.cloned.1.call-done), channel_id=1, source_target_pairs={{0,32},{32,64},{64,96},{1,33},{33,65},{65,97},{2,34},{34,66},{66,9... | collective-permute-start | bytes 6291464 | tf_op jit(solution)/shard_map/while/body/eval_jaxpr/ppermute | solution.py:16
  523.0 54.3 %all-gather.8.cloned.1.call-start = ((), (), s32[]{:S(2)}) async-start(), calls=%async_computation.6 | async-start | bytes 3145728 | tf_op jit(solution)/shard_map/while/body/eval_jaxpr/all_gather | solution.py:102
  523.9 1.0 copy-start
  577.3 48.4 %collective-permute-start = (bf16[256,4096]{1,0:T(8,128)(2,1)}, bf16[256,4096]{1,0:T(8,128)(2,1)S(1)}, u32[]{:S(2)}, u32[]{:S(2)}) collective-permute-start(bf16[256,4096]{1,0:T(8,128)(2,1)} %all-gather.8.cloned.1.call-done), channel_id=1, source_target_pairs={{0,32},{32,64},{64,96},{1,33},{33,65},{65,97},{2,34},{34,66},{66,9... | collective-permute-start | bytes 6291464 | tf_op jit(solution)/shard_map/while/body/eval_jaxpr/ppermute | solution.py:16
  625.7 54.1 %all-gather.8.cloned.1.call-start = ((), (), s32[]{:S(2)}) async-start(), calls=%async_computation.6 | async-start | bytes 3145728 | tf_op jit(solution)/shard_map/while/body/eval_jaxpr/all_gather | solution.py:102
  626.7 1.0 copy-start
  679.7 48.4 %collective-permute-start = (bf16[256,4096]{1,0:T(8,128)(2,1)}, bf16[256,4096]{1,0:T(8,128)(2,1)S(1)}, u32[]{:S(2)}, u32[]{:S(2)}) collective-permute-start(bf16[256,4096]{1,0:T(8,128)(2,1)} %all-gather.8.cloned.1.call-done), channel_id=1, source_target_pairs={{0,32},{32,64},{64,96},{1,33},{33,65},{65,97},{2,34},{34,66},{66,9... | collective-permute-start | bytes 6291464 | tf_op jit(solution)/shard_map/while/body/eval_jaxpr/ppermute | solution.py:16
  728.1 52.9 %all-gather.4.cloned.1.call-start = ((), (), s32[]{:S(2)}) async-start(), calls=%async_computation.2 | async-start | bytes 2228224 | tf_op jit(solution)/shard_map/all_gather | solution.py:139
  728.7 101.5 %all-gather.6.cloned.1.call-start = ((), (), s32[]{:S(2)}) async-start(), calls=%async_computation.3 | async-start | bytes 2228224 | tf_op jit(solution)/shard_map/all_gather | solution.py:140
  729.3 762.0 %reduce-scatter.3.cloned.1.call-start = ((), (), s32[]{:S(2)}) async-start(), calls=%async_computation.4 | async-start | bytes 4227072 | tf_op jit(solution)/shard_map/reduce_scatter | solution.py:186
  729.6 23.0 %copy-start.8 = (s32[8]{0:T(128)S(1)}, s32[8]{0:T(128)}, u32[]{:S(2)}) copy-start(s32[8]{0:T(128)} %param.18) | copy-start | bytes 100
  783.1 49.6 %copy-start.3 = (bf16[4096,128]{1,0:T(8,128)(2,1)S(1)}, bf16[4096,128]{1,0:T(8,128)(2,1)}, u32[]{:S(2)}) copy-start(bf16[4096,128]{1,0:T(8,128)(2,1)} %param.23) | copy-start | bytes 3145732
  842.6 1295.7 %reduce-scatter.5.cloned.1.call-start = ((), (), s32[]{:S(2)}) async-start(), calls=%async_computation.5 | async-start | bytes 4227072 | tf_op jit(solution)/shard_map/reduce_scatter | solution.py:187
Sparse Core Ops, SparseCore 0:
  29.4 35.7 all-gather.7
  130.3 36.0 all-gather.7
  231.5 37.5 all-gather.7
  334.2 37.5 all-gather.7
  422.4 52.1 all-gather.7
  525.1 52.1 all-gather.7
  628.1 51.5 all-gather.7
Sparse Core Ops, SparseCore 1:
  731.0 50.0 all-gather.3
  783.3 46.8 all-gather.5
  842.7 648.6 reduce-scatter.2
  1494.3 644.0 reduce-scatter.4
where the time goes:
time: 2150 us
  waiting for transfers between devices  1960 us (91%)
  matrix products  67.8 us (3%)
  other arithmetic  38.2 us (2%)
  starting transfers between devices  24.6 us (1%)
  blocking collectives  21.7 us (1%)
    reduce_scatter x1, waiting for transfers between devices, on_device(): lax.psum_scatter(up_grad, ('segment', 'fsdp', 'rep'), scatter_dimension=0...  647 us
    reduce_scatter x1, waiting for transfers between devices, on_device(): lax.psum_scatter(down_grad, ('segment', 'fsdp', 'rep'), scatter_dimension...  646 us
    all_gather x7, waiting for transfers between devices, tick_whole(): joined = lax.all_gather(result, 'rep', axis=1, tiled=True)  304 us
    ppermute x7, waiting for transfers between devices, passed_along(): return lax.ppermute(x, axis, pairs)  288 us
    dot_general x4, matrix products, apply_segment(): update = jnp.dot(normed, weight_local, preferred_element_type=jnp.float32)  48.4 us
    all_gather x1, waiting for transfers between devices, on_device(): lax.all_gather(agent_up, 'fsdp', axis=0, tiled=True)  47.1 us
  transfers between devices with their start and end apart: 18, of which 18 were waited for; matrix products, arithmetic and copies ran while one was open for 2% of the time, Pallas kernels for 0%

commit v1 on v0

--- a/solution.py
+++ b/solution.py
@@ -8,17 +8,6 @@
 
 epsilon = 1e-05
 sigma_weight = 2.0
-
-
-def passed_along(x, axis, by):
-    size = lax.axis_size(axis)
-    pairs = [(i, i + by) for i in range(size) if 0 <= i + by < size]
-    return lax.ppermute(x, axis, pairs)
-
-
-def spread(x, axis, root):
-    mine = lax.axis_index(axis) == root
-    return lax.psum(jnp.where(mine, x, jnp.zeros_like(x)), axis)
 
 
 def rms_scale(values):
@@ -37,6 +26,53 @@
     vocab_size = logprob.shape[-1]
     column = jnp.arange(vocab_size, dtype=jnp.int32)
     return jnp.sum(jnp.where(column[None, :] == targets[:, None], logprob, 0.0), axis=-1)
+
+
+def shifted(x, axis, size, by):
+    return lax.ppermute(x, axis, [(i, (i + by) % size) for i in range(size)])
+
+
+def fsdp_moved(x, mapping):
+    return lax.ppermute(x, "fsdp", [(f, mapping(f)) for f in range(16)])
+
+
+def ring_scatter(blocks, me, size, move):
+    half = blocks.shape[-1] // 2
+    ahead = blocks[..., :half]
+    behind = blocks[..., half:]
+    cur_a = lax.dynamic_index_in_dim(ahead, (me - 1) % size, 0, keepdims=False)
+    cur_b = lax.dynamic_index_in_dim(behind, (me + 1) % size, 0, keepdims=False)
+    for step in range(size - 1):
+        got_a = move(cur_a, 1)
+        got_b = move(cur_b, -1)
+        cur_a = got_a + lax.dynamic_index_in_dim(ahead, (me - step - 2) % size, 0, keepdims=False)
+        cur_b = got_b + lax.dynamic_index_in_dim(behind, (me + step + 2) % size, 0, keepdims=False)
+    return jnp.concatenate([cur_a, cur_b], axis=-1)
+
+
+def pair_scatter(blocks, axis_pos, me, move):
+    keep = lax.dynamic_index_in_dim(blocks, me, axis_pos, keepdims=False)
+    send = lax.dynamic_index_in_dim(blocks, 1 - me, axis_pos, keepdims=False)
+    return keep + move(send)
+
+
+def gradient_scatter(joined):
+    rows, cols = joined.shape
+    seg = lax.axis_index("segment")
+    f = lax.axis_index("fsdp")
+    rep = lax.axis_index("rep")
+    y_pos = f // 4
+    zh_pos = (f // 2) % 2
+    core_pos = f % 2
+    blocks = joined.reshape(4, 4, 2, 2, 2, rows // 128, cols)
+    blocks = pair_scatter(blocks, 3, core_pos, lambda v: fsdp_moved(v, lambda g: g ^ 1))
+    blocks = ring_scatter(blocks, seg, 4, lambda v, by: shifted(v, "segment", 4, by))
+    blocks = ring_scatter(
+        blocks, y_pos, 4, lambda v, by: fsdp_moved(v, lambda g: ((g // 4 + by) % 4) * 4 + g % 4)
+    )
+    blocks = pair_scatter(blocks, 1, rep, lambda v: shifted(v, "rep", 2, 1))
+    blocks = pair_scatter(blocks, 0, zh_pos, lambda v: fsdp_moved(v, lambda g: g ^ 2))
+    return blocks
 
 
 def on_device(
@@ -60,15 +96,21 @@
     vocab_size = embed_table.shape[0]
     half_width = prior_weight.shape[2]
     per_device = group_seqs // (segments * replicas)
-    micro_count = 4
+    micro_count = 8
     total_rows = group_seqs * seq_len
     block_rows = total_rows // micro_count
-    tick_count = micro_count + segments - 1
+    tick_count = micro_count + 2 * (segments - 1)
     flat_ids = token_ids.reshape(-1)
     weight_local = prior_weight[0]
     gain_local = prior_gain[0]
     is_first = segment_pos == 0
     is_last = segment_pos == segments - 1
+    own_first = rep_pos == 0
+
+    down_full, up_full = (
+        lax.all_gather(agent_down, "fsdp", axis=0, tiled=True),
+        lax.all_gather(agent_up, "fsdp", axis=0, tiled=True),
+    )
 
     def apply_segment(current):
         wide_rows = current.astype(jnp.float32)
@@ -80,54 +122,56 @@
     def skip_segment(current):
         return jnp.zeros((block_rows, half_width), jnp.bfloat16)
 
-    def segment_step(tick_pos, received_full):
-        micro_pos = tick_pos - segment_pos
+    def tick_whole(tick_pos, state):
+        arrived, computed, stored = state
+        partner = shifted(arrived, "rep", replicas, 1)
+        passed = lax.ppermute(computed, "segment", [(i, i + 1) for i in range(segments - 1)])
+        micro_pos = tick_pos - 2 * segment_pos
         active = (micro_pos >= 0) & (micro_pos < micro_count)
-        fresh_pos = jnp.clip(tick_pos, 0, micro_count - 1)
+        slot_pos = jnp.clip(micro_pos, 0, micro_count - 1)
         embedded = lookup_rows(
-            lax.dynamic_slice_in_dim(flat_ids, fresh_pos * block_rows, block_rows, 0), embed_table
+            lax.dynamic_slice_in_dim(flat_ids, slot_pos * block_rows, block_rows, 0), embed_table
         )
-        current = jnp.where(is_first, embedded, received_full)
+        low = jnp.where(own_first, arrived, partner)
+        high = jnp.where(own_first, partner, arrived)
+        joined = jnp.concatenate([low, high], axis=1)
+        current = jnp.where(is_first, embedded, joined)
         result = lax.cond(active, apply_segment, skip_segment, current)
-        return (active, jnp.clip(micro_pos, 0, micro_count - 1), result)
-
-    def store_block(stored, active, slot_pos, block):
         previous = lax.dynamic_slice_in_dim(stored, slot_pos * block_rows, block_rows, 0)
-        chosen = jnp.where(active & is_last, block, previous)
-        return lax.dynamic_update_slice_in_dim(stored, chosen, slot_pos * block_rows, 0)
-
-    def tick_whole(tick_pos, state_pair):
-        incoming, stored = state_pair
-        active, slot_pos, result = segment_step(tick_pos, incoming)
-        joined = lax.all_gather(result, "rep", axis=1, tiled=True)
-        stored = store_block(stored, active, slot_pos, joined)
-        incoming = passed_along(joined, "segment", 1)
-        return (incoming, stored)
+        chosen = jnp.where(active & is_last, result, previous)
+        stored = lax.dynamic_update_slice_in_dim(stored, chosen, slot_pos * block_rows, 0)
+        return (passed, result, stored)
 
     initial = (
-        jnp.zeros((block_rows, model_width), jnp.bfloat16),
-        jnp.zeros((total_rows, model_width), jnp.bfloat16),
-    )
-    final_rows = lax.fori_loop(0, tick_count, tick_whole, initial)[1]
+        jnp.zeros((block_rows, half_width), jnp.bfloat16),
+        jnp.zeros((block_rows, half_width), jnp.bfloat16),
+        jnp.zeros((total_rows, half_width), jnp.bfloat16),
+    )
+    final_half = lax.fori_loop(0, tick_count, tick_whole, initial)[2]
+
     positions = jnp.arange(seq_len, dtype=jnp.int32)
     next_ids = jnp.concatenate([token_ids[:, 1:], token_ids[:, :1]], axis=1)
     live_mask = (positions[None, :] < seq_lengths[:, None] - 1).astype(jnp.float32)
     counts = (seq_lengths - 1).astype(jnp.float32)
 
-    def prior_scores(rows_bf):
-        wide_rows = rows_bf.astype(jnp.float32)
-        prior_final = (wide_rows * rms_scale(wide_rows) * final_gain).astype(jnp.bfloat16)
-        logprob = jax.nn.log_softmax(
-            jnp.dot(prior_final, head_weight, preferred_element_type=jnp.float32), axis=-1
-        )
-        token_terms = picked_logprob(logprob, next_ids.reshape(-1)).reshape(group_seqs, seq_len)
-        return jnp.sum(token_terms * live_mask, axis=1) / counts
-
-    def no_scores(rows_bf):
-        return jnp.zeros((group_seqs,), jnp.float32)
-
-    prior_group = lax.cond(is_last, prior_scores, no_scores, final_rows)
-    prior_group = spread(prior_group, "segment", segments - 1)
+    wide_half = final_half.astype(jnp.float32)
+    own_squares = jnp.sum(wide_half * wide_half, axis=-1, keepdims=True)
+    squares = own_squares + shifted(own_squares, "rep", replicas, 1)
+    final_scale = lax.rsqrt(squares / model_width + epsilon)
+    gain_half = lax.dynamic_slice_in_dim(final_gain, rep_pos * half_width, half_width, 0)
+    head_half = lax.dynamic_slice_in_dim(head_weight, rep_pos * half_width, half_width, 0)
+    prior_half = (wide_half * final_scale * gain_half).astype(jnp.bfloat16)
+    own_logits = jnp.dot(prior_half, head_half, preferred_element_type=jnp.float32)
+    prior_logits = own_logits + shifted(own_logits, "rep", replicas, 1)
+    prior_logp = jax.nn.log_softmax(prior_logits, axis=-1)
+    token_terms = picked_logprob(prior_logp, next_ids.reshape(-1)).reshape(group_seqs, seq_len)
+    prior_group = jnp.sum(token_terms * live_mask, axis=1) / counts
+    from_last = prior_group
+    for by in range(1, segments):
+        moved = shifted(prior_group, "segment", segments, by)
+        from_last = jnp.where((segment_pos - by) % segments == segments - 1, moved, from_last)
+    prior_group = from_last
+
     own_seq = (segment_pos * replicas + rep_pos) * per_device
     prior_mine = lax.dynamic_slice_in_dim(prior_group, own_seq, per_device, 0)
     mine_ids = lax.dynamic_slice_in_dim(token_ids, own_seq, per_device, 0).reshape(-1)
@@ -135,10 +179,6 @@
     mine_live = lax.dynamic_slice_in_dim(live_mask, own_seq, per_device, 0)
     mine_counts = lax.dynamic_slice_in_dim(counts, own_seq, per_device, 0)
     mine_scores = lax.dynamic_slice_in_dim(quant_scores, own_seq, per_device, 0)
-    down_full, up_full = (
-        lax.all_gather(agent_down, "fsdp", axis=0, tiled=True),
-        lax.all_gather(agent_up, "fsdp", axis=0, tiled=True),
-    )
     start_wide = lookup_rows(mine_ids, embed_table).astype(jnp.float32)
     unit_rows = (start_wide * rms_scale(start_wide)).astype(jnp.bfloat16)
     latent = jnp.dot(unit_rows, down_full, preferred_element_type=jnp.float32).astype(jnp.bfloat16)
@@ -182,11 +222,9 @@
     down_grad = lax.dot_general(
         unit_rows, latent_grad, (((0,), (0,)), ((), ())), preferred_element_type=jnp.float32
     )
-    down_share, up_share = (
-        lax.psum_scatter(down_grad, ("segment", "fsdp", "rep"), scatter_dimension=0, tiled=True),
-        lax.psum_scatter(up_grad, ("segment", "fsdp", "rep"), scatter_dimension=0, tiled=True),
-    )
-    return (down_share, up_share)
+    rank = down_grad.shape[1]
+    shares = gradient_scatter(jnp.concatenate([down_grad, up_grad], axis=1))
+    return (shares[:, :rank], shares[:, rank:])
 
 
 def solution(mesh):

time: 2150 us -> 533 us (0.25)
  waiting for transfers between devices: 1960 us -> 119 us
  starting transfers between devices: 24.6 us -> 120 us
  local copies, waits for them, and re-layouts: 14.1 us -> 71.9 us
  other arithmetic: 38.2 us -> 86.4 us
  matrix products: 67.8 us -> 113 us
  blocking collectives: 21.7 us -> 0 us
    reduce_scatter x2 -> x0, waiting for transfers between devices: 1290 us -> none  [the longest x1 647 us: on_device(): lax.psum_scatter(up_grad, ('segment', 'fsdp', 'rep'), scatter_dimension=0...]
    all_gather x7 -> x0, waiting for transfers between devices: 304 us -> none  [tick_whole(): joined = lax.all_gather(result, 'rep', axis=1, tiled=True)]
    ppermute x7 -> x48, waiting for transfers between devices: 288 us -> 118 us  [the longest x26 95.4 us: shifted(): return lax.ppermute(x, axis, [(i, (i + by) % size) for i in range(size)])]
    ppermute x7 -> x48, starting transfers between devices: 24.5 us -> 120 us  [the longest x14 56.1 us: tick_whole(): lax.ppermute(computed, 'segment', [(i, i + 1) for i in range(segments - 1)])]
    all_gather x1, waiting for transfers between devices: 47.1 us -> 0.02 us  [on_device(): lax.all_gather(agent_up, 'fsdp', axis=0, tiled=True)]
    another operation x4 -> x22, local copies, waits for them, and re-layouts: 0.33 us -> 32.6 us
    all_gather x1, waiting for transfers between devices: 26 us -> 0.02 us  [on_device(): lax.all_gather(agent_down, 'fsdp', axis=0, tiled=True)]
    dot_general x4 -> x8, matrix products: 48.4 us -> 72.2 us  [apply_segment(): update = jnp.dot(normed, weight_local, preferred_element_type=jnp.float32)]
  transfers between devices with their start and end apart: 18 -> 50, of which waited for: 18 -> 29; matrix products, arithmetic and copies ran while one was open for 2% -> 43% of each run, Pallas kernels for 0% -> 0%
where the time goes in v1:
time: 533 us; the launch traced here: 528 us
  starting transfers between devices  120 us (23%)
  waiting for transfers between devices  119 us (22%)
  matrix products  113 us (21%)
  other arithmetic  86.4 us (16%)
  local copies, waits for them, and re-layouts  71.9 us (13%)
  between operations  17.5 us (3%)
    ppermute x26, waiting for transfers between devices, shifted(): return lax.ppermute(x, axis, [(i, (i + by) % size) for i in range(size)])  95.4 us
    dot_general x8, matrix products, apply_segment(): update = jnp.dot(normed, weight_local, preferred_element_type=jnp.float32)  72.2 us
    ppermute x14, starting transfers between devices, tick_whole(): lax.ppermute(computed, 'segment', [(i, i + 1) for i in range(segments - 1)])  56.1 us
    ppermute x26, starting transfers between devices, shifted(): return lax.ppermute(x, axis, [(i, (i + by) % size) for i in range(size)])  48 us
    another operation x22, local copies, waits for them, and re-layouts  32.6 us
    dynamic_update_slice x14, other arithmetic, tick_whole(): lax.dynamic_update_slice_in_dim(stored, chosen, slot_pos * block_rows, 0)  28.8 us
    dot_general x15, matrix products, lookup_rows(): jnp.dot(onehot, embed_table, preferred_element_type=jnp.float32)  22.6 us
    ppermute x8, waiting for transfers between devices, fsdp_moved(): return lax.ppermute(x, 'fsdp', [(f, mapping(f)) for f in range(16)])  18.1 us
  transfers between devices with their start and end apart: 50, of which 29 were waited for; matrix products, arithmetic and copies ran while one was open for 43% of the time, Pallas kernels for 0%

profile of v1, /device:TPU:0, one launch (start us, length us, event | category | flops | bytes accessed | tf_op | source)
XLA Modules:
  0.0 528.0 jit_solution(11127590580645713045)
XLA Ops:
  12.1 330.8 %while.19 = (s32[]{:T(128)}, bf16[128,2048]{1,0:T(8,128)(2,1)S(1)}, bf16[128,2048]{1,0:T(8,128)(2,1)}, bf16[1024,2048]{1,0:T(8,128)(2,1)}, s32[]{:T(128)}, /*ind...) while((s32[]{:T(128)}, bf16[128,2048]{1,0:T(8,128)(2,1)S(1)}, ...), condition=%wide.region_6.7_spmd, body=%wide.region_2.0_spmd.sunk | while | flops 2289320192 | bytes 43012100 | solution.py:150
  21.8 5.2 collective-permute-done.1
  28.2 10.7 %conditional.2 = (bf16[128,2048]{1,0:T(8,128)(2,1)}) conditional(s32[]{:T(128)} %convert_element_type.134, () %tuple.59, (pred[]{:T(512)}, bf16[128,4096]{1,0:T(8,128)(2,1)}, bf16[128,4096]{1,0:T(8,128)(2,1)}, s32[]{:T(128)}, f32[1,4096]{1,0:T(1,128)S(1)}, /*index=5*/bf16[4096,2048]{1,0:T(8,128)(2,1)}) %tuple.60), branch_computations={%region_3.3_spmd, %region_4.5_spmd} | conditional | flops 2151678208 | bytes 24660028 | solution.py:139
  29.9 9.0 %fusion = bf16[128,2048]{1,0:T(8,128)(2,1)} fusion(bf16[4096,2048]{1,0:T(8,128)(2,1)} %get-tuple-element.309, f32[128,4096]{1,0:T(8,128)S(1)} %get-tuple-element.355, f32[4096]{0:T(1024)S(1)} %bitcast.88, f32[128]{0:T(128)S(1)} %add_rsqrt_fusion, s32[]{:T(128)S(6)} %select_n.222), kind=kOutput, calls=%fused_computation.1 | convolution fusion | flops 2149580800 | bytes 20464132 | tf_op jit(solution)/shard_map/while/body/eval_jaxpr/cond/branch_1_fun/dot_general | solution.py:118
  49.8 10.5 %collective-permute-done.1 = bf16[128,2048]{1,0:T(8,128)(2,1)S(1)} collective-permute-done((bf16[128,2048]{1,0:T(8,128)(2,1)S(1)}, bf16[128,2048]{1,0:T(8,128)(2,1)S(1)}, u32[]{:S(2)}, u32[]{:S(2)}) %collective-permute-start.1) | collective-permute-done | bytes 524320 | tf_op jit(solution)/shard_map/while/body/eval_jaxpr/ppermute | solution.py:32
  61.5 10.7 %conditional.2 = (bf16[128,2048]{1,0:T(8,128)(2,1)}) conditional(s32[]{:T(128)} %convert_element_type.134, () %tuple.59, (pred[]{:T(512)}, bf16[128,4096]{1,0:T(8,128)(2,1)}, bf16[128,4096]{1,0:T(8,128)(2,1)}, s32[]{:T(128)}, f32[1,4096]{1,0:T(1,128)S(1)}, /*index=5*/bf16[4096,2048]{1,0:T(8,128)(2,1)}) %tuple.60), branch_computations={%region_3.3_spmd, %region_4.5_spmd} | conditional | flops 2151678208 | bytes 24660028 | solution.py:139
  63.2 9.0 %fusion = bf16[128,2048]{1,0:T(8,128)(2,1)} fusion(bf16[4096,2048]{1,0:T(8,128)(2,1)} %get-tuple-element.309, f32[128,4096]{1,0:T(8,128)S(1)} %get-tuple-element.355, f32[4096]{0:T(1024)S(1)} %bitcast.88, f32[128]{0:T(128)S(1)} %add_rsqrt_fusion, s32[]{:T(128)S(6)} %select_n.222), kind=kOutput, calls=%fused_computation.1 | convolution fusion | flops 2149580800 | bytes 20464132 | tf_op jit(solution)/shard_map/while/body/eval_jaxpr/cond/branch_1_fun/dot_general | solution.py:118
  82.5 6.8 %collective-permute-done.1 = bf16[128,2048]{1,0:T(8,128)(2,1)S(1)} collective-permute-done((bf16[128,2048]{1,0:T(8,128)(2,1)S(1)}, bf16[128,2048]{1,0:T(8,128)(2,1)S(1)}, u32[]{:S(2)}, u32[]{:S(2)}) %collective-permute-start.1) | collective-permute-done | bytes 524320 | tf_op jit(solution)/shard_map/while/body/eval_jaxpr/ppermute | solution.py:32
  90.5 10.9 %conditional.2 = (bf16[128,2048]{1,0:T(8,128)(2,1)}) conditional(s32[]{:T(128)} %convert_element_type.134, () %tuple.59, (pred[]{:T(512)}, bf16[128,4096]{1,0:T(8,128)(2,1)}, bf16[128,4096]{1,0:T(8,128)(2,1)}, s32[]{:T(128)}, f32[1,4096]{1,0:T(1,128)S(1)}, /*index=5*/bf16[4096,2048]{1,0:T(8,128)(2,1)}) %tuple.60), branch_computations={%region_3.3_spmd, %region_4.5_spmd} | conditional | flops 2151678208 | bytes 24660028 | solution.py:139
  92.2 9.2 %fusion = bf16[128,2048]{1,0:T(8,128)(2,1)} fusion(bf16[4096,2048]{1,0:T(8,128)(2,1)} %get-tuple-element.309, f32[128,4096]{1,0:T(8,128)S(1)} %get-tuple-element.355, f32[4096]{0:T(1024)S(1)} %bitcast.88, f32[128]{0:T(128)S(1)} %add_rsqrt_fusion, s32[]{:T(128)S(6)} %select_n.222), kind=kOutput, calls=%fused_computation.1 | convolution fusion | flops 2149580800 | bytes 20464132 | tf_op jit(solution)/shard_map/while/body/eval_jaxpr/cond/branch_1_fun/dot_general | solution.py:118
  111.9 5.5 %collective-permute-done.1 = bf16[128,2048]{1,0:T(8,128)(2,1)S(1)} collective-permute-done((bf16[128,2048]{1,0:T(8,128)(2,1)S(1)}, bf16[128,2048]{1,0:T(8,128)(2,1)S(1)}, u32[]{:S(2)}, u32[]{:S(2)}) %collective-permute-start.1) | collective-permute-done | bytes 524320 | tf_op jit(solution)/shard_map/while/body/eval_jaxpr/ppermute | solution.py:32
  118.5 10.7 %conditional.2 = (bf16[128,2048]{1,0:T(8,128)(2,1)}) conditional(s32[]{:T(128)} %convert_element_type.134, () %tuple.59, (pred[]{:T(512)}, bf16[128,4096]{1,0:T(8,128)(2,1)}, bf16[128,4096]{1,0:T(8,128)(2,1)}, s32[]{:T(128)}, f32[1,4096]{1,0:T(1,128)S(1)}, /*index=5*/bf16[4096,2048]{1,0:T(8,128)(2,1)}) %tuple.60), branch_computations={%region_3.3_spmd, %region_4.5_spmd} | conditional | flops 2151678208 | bytes 24660028 | solution.py:139
  120.2 9.0 %fusion = bf16[128,2048]{1,0:T(8,128)(2,1)} fusion(bf16[4096,2048]{1,0:T(8,128)(2,1)} %get-tuple-element.309, f32[128,4096]{1,0:T(8,128)S(1)} %get-tuple-element.355, f32[4096]{0:T(1024)S(1)} %bitcast.88, f32[128]{0:T(128)S(1)} %add_rsqrt_fusion, s32[]{:T(128)S(6)} %select_n.222), kind=kOutput, calls=%fused_computation.1 | convolution fusion | flops 2149580800 | bytes 20464132 | tf_op jit(solution)/shard_map/while/body/eval_jaxpr/cond/branch_1_fun/dot_general | solution.py:118
  145.4 10.7 %conditional.2 = (bf16[128,2048]{1,0:T(8,128)(2,1)}) conditional(s32[]{:T(128)} %convert_element_type.134, () %tuple.59, (pred[]{:T(512)}, bf16[128,4096]{1,0:T(8,128)(2,1)}, bf16[128,4096]{1,0:T(8,128)(2,1)}, s32[]{:T(128)}, f32[1,4096]{1,0:T(1,128)S(1)}, /*index=5*/bf16[4096,2048]{1,0:T(8,128)(2,1)}) %tuple.60), branch_computations={%region_3.3_spmd, %region_4.5_spmd} | conditional | flops 2151678208 | bytes 24660028 | solution.py:139
  147.1 9.0 %fusion = bf16[128,2048]{1,0:T(8,128)(2,1)} fusion(bf16[4096,2048]{1,0:T(8,128)(2,1)} %get-tuple-element.309, f32[128,4096]{1,0:T(8,128)S(1)} %get-tuple-element.355, f32[4096]{0:T(1024)S(1)} %bitcast.88, f32[128]{0:T(128)S(1)} %add_rsqrt_fusion, s32[]{:T(128)S(6)} %select_n.222), kind=kOutput, calls=%fused_computation.1 | convolution fusion | flops 2149580800 | bytes 20464132 | tf_op jit(solution)/shard_map/while/body/eval_jaxpr/cond/branch_1_fun/dot_general | solution.py:118
  171.4 10.7 %conditional.2 = (bf16[128,2048]{1,0:T(8,128)(2,1)}) conditional(s32[]{:T(128)} %convert_element_type.134, () %tuple.59, (pred[]{:T(512)}, bf16[128,4096]{1,0:T(8,128)(2,1)}, bf16[128,4096]{1,0:T(8,128)(2,1)}, s32[]{:T(128)}, f32[1,4096]{1,0:T(1,128)S(1)}, /*index=5*/bf16[4096,2048]{1,0:T(8,128)(2,1)}) %tuple.60), branch_computations={%region_3.3_spmd, %region_4.5_spmd} | conditional | flops 2151678208 | bytes 24660028 | solution.py:139
  173.1 9.0 %fusion = bf16[128,2048]{1,0:T(8,128)(2,1)} fusion(bf16[4096,2048]{1,0:T(8,128)(2,1)} %get-tuple-element.309, f32[128,4096]{1,0:T(8,128)S(1)} %get-tuple-element.355, f32[4096]{0:T(1024)S(1)} %bitcast.88, f32[128]{0:T(128)S(1)} %add_rsqrt_fusion, s32[]{:T(128)S(6)} %select_n.222), kind=kOutput, calls=%fused_computation.1 | convolution fusion | flops 2149580800 | bytes 20464132 | tf_op jit(solution)/shard_map/while/body/eval_jaxpr/cond/branch_1_fun/dot_general | solution.py:118
  196.5 10.7 %conditional.2 = (bf16[128,2048]{1,0:T(8,128)(2,1)}) conditional(s32[]{:T(128)} %convert_element_type.134, () %tuple.59, (pred[]{:T(512)}, bf16[128,4096]{1,0:T(8,128)(2,1)}, bf16[128,4096]{1,0:T(8,128)(2,1)}, s32[]{:T(128)}, f32[1,4096]{1,0:T(1,128)S(1)}, /*index=5*/bf16[4096,2048]{1,0:T(8,128)(2,1)}) %tuple.60), branch_computations={%region_3.3_spmd, %region_4.5_spmd} | conditional | flops 2151678208 | bytes 24660028 | solution.py:139
  198.2 9.0 %fusion = bf16[128,2048]{1,0:T(8,128)(2,1)} fusion(bf16[4096,2048]{1,0:T(8,128)(2,1)} %get-tuple-element.309, f32[128,4096]{1,0:T(8,128)S(1)} %get-tuple-element.355, f32[4096]{0:T(1024)S(1)} %bitcast.88, f32[128]{0:T(128)S(1)} %add_rsqrt_fusion, s32[]{:T(128)S(6)} %select_n.222), kind=kOutput, calls=%fused_computation.1 | convolution fusion | flops 2149580800 | bytes 20464132 | tf_op jit(solution)/shard_map/while/body/eval_jaxpr/cond/branch_1_fun/dot_general | solution.py:118
  220.8 10.7 %conditional.2 = (bf16[128,2048]{1,0:T(8,128)(2,1)}) conditional(s32[]{:T(128)} %convert_element_type.134, () %tuple.59, (pred[]{:T(512)}, bf16[128,4096]{1,0:T(8,128)(2,1)}, bf16[128,4096]{1,0:T(8,128)(2,1)}, s32[]{:T(128)}, f32[1,4096]{1,0:T(1,128)S(1)}, /*index=5*/bf16[4096,2048]{1,0:T(8,128)(2,1)}) %tuple.60), branch_computations={%region_3.3_spmd, %region_4.5_spmd} | conditional | flops 2151678208 | bytes 24660028 | solution.py:139
  222.5 9.0 %fusion = bf16[128,2048]{1,0:T(8,128)(2,1)} fusion(bf16[4096,2048]{1,0:T(8,128)(2,1)} %get-tuple-element.309, f32[128,4096]{1,0:T(8,128)S(1)} %get-tuple-element.355, f32[4096]{0:T(1024)S(1)} %bitcast.88, f32[128]{0:T(128)S(1)} %add_rsqrt_fusion, s32[]{:T(128)S(6)} %select_n.222), kind=kOutput, calls=%fused_computation.1 | convolution fusion | flops 2149580800 | bytes 20464132 | tf_op jit(solution)/shard_map/while/body/eval_jaxpr/cond/branch_1_fun/dot_general | solution.py:118
  266.8 12.3 %collective-permute-start = (bf16[128,2048]{1,0:T(8,128)(2,1)}, bf16[128,2048]{1,0:T(8,128)(2,1)}, u32[]{:S(2)}, u32[]{:S(2)}) collective-permute-start(bf16[128,2048]{1,0:T(8,128)(2,1)} %copy.24), channel_id=1, source_target_pairs={{0,32},{32,64},{64,96},{1,33},{33,65},{65,97},{2,34},{34,66},{66,9... | collective-permute-start | bytes 1572872 | tf_op jit(solution)/shard_map/while/body/eval_jaxpr/ppermute | solution.py:128
  325.5 10.2 %collective-permute-start = (bf16[128,2048]{1,0:T(8,128)(2,1)}, bf16[128,2048]{1,0:T(8,128)(2,1)}, u32[]{:S(2)}, u32[]{:S(2)}) collective-permute-start(bf16[128,2048]{1,0:T(8,128)(2,1)} %copy.24), channel_id=1, source_target_pairs={{0,32},{32,64},{64,96},{1,33},{33,65},{65,97},{2,34},{34,66},{66,9... | collective-permute-start | bytes 1572872 | tf_op jit(solution)/shard_map/while/body/eval_jaxpr/ppermute | solution.py:128
  356.0 9.1 %collective-permute-done.3 = f32[1024,128]{0,1:T(8,128)S(1)} collective-permute-done((f32[1024,128]{0,1:T(8,128)S(1)}, f32[1024,128]{0,1:T(8,128)S(1)}, u32[]{:S(2)}, u32[]{:S(2)}) %collective-permute-start.3) | collective-permute-done | bytes 524320 | tf_op jit(solution)/shard_map/ppermute | solution.py:32
  365.6 10.6 %collective-permute-start.4 = (f32[8]{0:T(128)S(1)}, f32[8]{0:T(128)S(1)}, u32[]{:S(2)}, u32[]{:S(2)}) collective-permute-start(f32[8]{0:T(128)S(1)} %convert_divide_fusion), channel_id=1, source_target_pairs={{0,96},{32,0},{64,32},{96,64},{1,97},{33,1},{65,33},{97,65},{2,98}... | collective-permute-start | bytes 104 | tf_op jit(solution)/shard_map/ppermute | solution.py:32
  395.2 5.6 %fusion.12 = f32[4096,256]{0,1:T(8,128)} fusion(bf16[128,4096]{1,0:T(8,128)(2,1)} %copy-done.4, bf16[4096,256]{1,0:T(8,128)(2,1)} %all-gather.5.cloned.1.call-done, f32[128,4096]{1,0:T(8,128)S(1)} %copy-done.3, f32[128]{0:T(128)S(1)} %add_rsqrt_fusion.3), kind=kOutput, calls=%fused_computation.38 | convolution fusion | flops 537952256 | bytes 9437696 | tf_op jit(solution)/shard_map/dot_general | solution.py:222
  400.8 7.7 %pad_maximum_fusion.1 = f32[4096,512]{0,1:T(8,128)} fusion(f32[4096,256]{0,1:T(8,128)} %fusion.38, f32[4096,256]{0,1:T(8,128)} %fusion.12), kind=kLoop, calls=%fused_computation.20 | loop fusion | flops 2097152 | bytes 16777216 | tf_op jit(solution)/shard_map/concatenate | solution.py:226
  408.5 9.0 %copy.14 = f32[4096,512]{1,0:T(8,128)} copy(f32[4096,512]{0,1:T(8,128)} %pad_maximum_fusion.1) | data formatting | bytes 16777216 | tf_op jit(solution)/shard_map/concatenate | solution.py:226
  422.4 7.5 %collective-permute-done.7 = f32[4,4,2,2,32,512]{5,4,3,2,1,0:T(8,128)} collective-permute-done((f32[4,4,2,2,32,512]{5,4,3,2,1,0:T(8,128)}, f32[4,4,2,2,32,512]{5,4,3,2,1,0:T(8,128)}, u32[]{:S(2)}, u32[]{:S(2)}) %collective-permute-start.7) | collective-permute-done | bytes 4194336 | tf_op jit(solution)/shard_map/ppermute | solution.py:36
  441.3 11.4 %collective-permute-done.8 = f32[4,2,2,32,256]{4,3,2,1,0:T(8,128)} collective-permute-done((f32[4,2,2,32,256]{4,3,2,1,0:T(8,128)}, f32[4,2,2,32,256]{4,3,2,1,0:T(8,128)}, u32[]{:S(2)}, u32[]{:S(2)}) %collective-permute-start.8) | collective-permute-done | bytes 524320 | tf_op jit(solution)/shard_map/ppermute | solution.py:32
  460.0 9.5 %collective-permute-done.9 = f32[4,2,2,32,256]{4,3,2,1,0:T(8,128)} collective-permute-done((f32[4,2,2,32,256]{4,3,2,1,0:T(8,128)}, f32[4,2,2,32,256]{4,3,2,1,0:T(8,128)}, u32[]{:S(2)}, u32[]{:S(2)}) %collective-permute-start.9) | collective-permute-done | bytes 524320 | tf_op jit(solution)/shard_map/ppermute | solution.py:32
  476.7 8.6 %collective-permute-done.10 = f32[4,2,2,32,256]{4,3,2,1,0:T(8,128)} collective-permute-done((f32[4,2,2,32,256]{4,3,2,1,0:T(8,128)}, f32[4,2,2,32,256]{4,3,2,1,0:T(8,128)}, u32[]{:S(2)}, u32[]{:S(2)}) %collective-permute-start.10) | collective-permute-done | bytes 524320 | tf_op jit(solution)/shard_map/ppermute | solution.py:32
  (327 shorter events, 313.7 us)
Async XLA Ops:
  7.2 375.3 %all-gather.3.cloned.1.call-start = ((), (), s32[]{:S(2)}) async-start(), calls=%async_computation | async-start | bytes 2228224 | tf_op jit(solution)/shard_map/all_gather | solution.py:111
  7.9 376.7 %all-gather.5.cloned.1.call-start = ((), (), s32[]{:S(2)}) async-start(), calls=%async_computation.1 | async-start | bytes 2228224 | tf_op jit(solution)/shard_map/all_gather | solution.py:112
  12.1 15.0 %collective-permute-start.1 = (bf16[128,2048]{1,0:T(8,128)(2,1)S(1)}, bf16[128,2048]{1,0:T(8,128)(2,1)S(1)}, u32[]{:S(2)}, u32[]{:S(2)}) collective-permute-start(bf16[128,2048]{1,0:T(8,128)(2,1)S(1)} %get-tuple-element.477), channel_id=1, source_target_pairs={{0,1},{1,0},{2,3},{3,2},{4,5},{5,4},{6,7},{7,6},{8,9},{9,8},{10,11... | collective-permute-start | bytes 1572872 | tf_op jit(solution)/shard_map/while/body/eval_jaxpr/ppermute | solution.py:32
  16.1 24.9 %collective-permute-start = (bf16[128,2048]{1,0:T(8,128)(2,1)}, bf16[128,2048]{1,0:T(8,128)(2,1)}, u32[]{:S(2)}, u32[]{:S(2)}) collective-permute-start(bf16[128,2048]{1,0:T(8,128)(2,1)} %copy.24), channel_id=1, source_target_pairs={{0,32},{32,64},{64,96},{1,33},{33,65},{65,97},{2,34},{34,66},{66,9... | collective-permute-start | bytes 1572872 | tf_op jit(solution)/shard_map/while/body/eval_jaxpr/ppermute | solution.py:128
  42.0 18.2 %collective-permute-start.1 = (bf16[128,2048]{1,0:T(8,128)(2,1)S(1)}, bf16[128,2048]{1,0:T(8,128)(2,1)S(1)}, u32[]{:S(2)}, u32[]{:S(2)}) collective-permute-start(bf16[128,2048]{1,0:T(8,128)(2,1)S(1)} %get-tuple-element.477), channel_id=1, source_target_pairs={{0,1},{1,0},{2,3},{3,2},{4,5},{5,4},{6,7},{7,6},{8,9},{9,8},{10,11... | collective-permute-start | bytes 1572872 | tf_op jit(solution)/shard_map/while/body/eval_jaxpr/ppermute | solution.py:32
  46.1 28.1 %collective-permute-start = (bf16[128,2048]{1,0:T(8,128)(2,1)}, bf16[128,2048]{1,0:T(8,128)(2,1)}, u32[]{:S(2)}, u32[]{:S(2)}) collective-permute-start(bf16[128,2048]{1,0:T(8,128)(2,1)} %copy.24), channel_id=1, source_target_pairs={{0,32},{32,64},{64,96},{1,33},{33,65},{65,97},{2,34},{34,66},{66,9... | collective-permute-start | bytes 1572872 | tf_op jit(solution)/shard_map/while/body/eval_jaxpr/ppermute | solution.py:128
  75.3 14.1 %collective-permute-start.1 = (bf16[128,2048]{1,0:T(8,128)(2,1)S(1)}, bf16[128,2048]{1,0:T(8,128)(2,1)S(1)}, u32[]{:S(2)}, u32[]{:S(2)}) collective-permute-start(bf16[128,2048]{1,0:T(8,128)(2,1)S(1)} %get-tuple-element.477), channel_id=1, source_target_pairs={{0,1},{1,0},{2,3},{3,2},{4,5},{5,4},{6,7},{7,6},{8,9},{9,8},{10,11... | collective-permute-start | bytes 1572872 | tf_op jit(solution)/shard_map/while/body/eval_jaxpr/ppermute | solution.py:32
  78.9 24.7 %collective-permute-start = (bf16[128,2048]{1,0:T(8,128)(2,1)}, bf16[128,2048]{1,0:T(8,128)(2,1)}, u32[]{:S(2)}, u32[]{:S(2)}) collective-permute-start(bf16[128,2048]{1,0:T(8,128)(2,1)} %copy.24), channel_id=1, source_target_pairs={{0,32},{32,64},{64,96},{1,33},{33,65},{65,97},{2,34},{34,66},{66,9... | collective-permute-start | bytes 1572872 | tf_op jit(solution)/shard_map/while/body/eval_jaxpr/ppermute | solution.py:128
  104.6 12.7 %collective-permute-start.1 = (bf16[128,2048]{1,0:T(8,128)(2,1)S(1)}, bf16[128,2048]{1,0:T(8,128)(2,1)S(1)}, u32[]{:S(2)}, u32[]{:S(2)}) collective-permute-start(bf16[128,2048]{1,0:T(8,128)(2,1)S(1)} %get-tuple-element.477), channel_id=1, source_target_pairs={{0,1},{1,0},{2,3},{3,2},{4,5},{5,4},{6,7},{7,6},{8,9},{9,8},{10,11... | collective-permute-start | bytes 1572872 | tf_op jit(solution)/shard_map/while/body/eval_jaxpr/ppermute | solution.py:32
  108.3 23.0 %collective-permute-start = (bf16[128,2048]{1,0:T(8,128)(2,1)}, bf16[128,2048]{1,0:T(8,128)(2,1)}, u32[]{:S(2)}, u32[]{:S(2)}) collective-permute-start(bf16[128,2048]{1,0:T(8,128)(2,1)} %copy.24), channel_id=1, source_target_pairs={{0,32},{32,64},{64,96},{1,33},{33,65},{65,97},{2,34},{34,66},{66,9... | collective-permute-start | bytes 1572872 | tf_op jit(solution)/shard_map/while/body/eval_jaxpr/ppermute | solution.py:128
  132.3 11.9 %collective-permute-start.1 = (bf16[128,2048]{1,0:T(8,128)(2,1)S(1)}, bf16[128,2048]{1,0:T(8,128)(2,1)S(1)}, u32[]{:S(2)}, u32[]{:S(2)}) collective-permute-start(bf16[128,2048]{1,0:T(8,128)(2,1)S(1)} %get-tuple-element.477), channel_id=1, source_target_pairs={{0,1},{1,0},{2,3},{3,2},{4,5},{5,4},{6,7},{7,6},{8,9},{9,8},{10,11... | collective-permute-start | bytes 1572872 | tf_op jit(solution)/shard_map/while/body/eval_jaxpr/ppermute | solution.py:32
  135.9 22.2 %collective-permute-start = (bf16[128,2048]{1,0:T(8,128)(2,1)}, bf16[128,2048]{1,0:T(8,128)(2,1)}, u32[]{:S(2)}, u32[]{:S(2)}) collective-permute-start(bf16[128,2048]{1,0:T(8,128)(2,1)} %copy.24), channel_id=1, source_target_pairs={{0,32},{32,64},{64,96},{1,33},{33,65},{65,97},{2,34},{34,66},{66,9... | collective-permute-start | bytes 1572872 | tf_op jit(solution)/shard_map/while/body/eval_jaxpr/ppermute | solution.py:128
  159.1 11.0 %collective-permute-start.1 = (bf16[128,2048]{1,0:T(8,128)(2,1)S(1)}, bf16[128,2048]{1,0:T(8,128)(2,1)S(1)}, u32[]{:S(2)}, u32[]{:S(2)}) collective-permute-start(bf16[128,2048]{1,0:T(8,128)(2,1)S(1)} %get-tuple-element.477), channel_id=1, source_target_pairs={{0,1},{1,0},{2,3},{3,2},{4,5},{5,4},{6,7},{7,6},{8,9},{9,8},{10,11... | collective-permute-start | bytes 1572872 | tf_op jit(solution)/shard_map/while/body/eval_jaxpr/ppermute | solution.py:32
  162.8 21.3 %collective-permute-start = (bf16[128,2048]{1,0:T(8,128)(2,1)}, bf16[128,2048]{1,0:T(8,128)(2,1)}, u32[]{:S(2)}, u32[]{:S(2)}) collective-permute-start(bf16[128,2048]{1,0:T(8,128)(2,1)} %copy.24), channel_id=1, source_target_pairs={{0,32},{32,64},{64,96},{1,33},{33,65},{65,97},{2,34},{34,66},{66,9... | collective-permute-start | bytes 1572872 | tf_op jit(solution)/shard_map/while/body/eval_jaxpr/ppermute | solution.py:128
  185.1 10.2 %collective-permute-start.1 = (bf16[128,2048]{1,0:T(8,128)(2,1)S(1)}, bf16[128,2048]{1,0:T(8,128)(2,1)S(1)}, u32[]{:S(2)}, u32[]{:S(2)}) collective-permute-start(bf16[128,2048]{1,0:T(8,128)(2,1)S(1)} %get-tuple-element.477), channel_id=1, source_target_pairs={{0,1},{1,0},{2,3},{3,2},{4,5},{5,4},{6,7},{7,6},{8,9},{9,8},{10,11... | collective-permute-start | bytes 1572872 | tf_op jit(solution)/shard_map/while/body/eval_jaxpr/ppermute | solution.py:32
  188.8 20.5 %collective-permute-start = (bf16[128,2048]{1,0:T(8,128)(2,1)}, bf16[128,2048]{1,0:T(8,128)(2,1)}, u32[]{:S(2)}, u32[]{:S(2)}) collective-permute-start(bf16[128,2048]{1,0:T(8,128)(2,1)} %copy.24), channel_id=1, source_target_pairs={{0,32},{32,64},{64,96},{1,33},{33,65},{65,97},{2,34},{34,66},{66,9... | collective-permute-start | bytes 1572872 | tf_op jit(solution)/shard_map/while/body/eval_jaxpr/ppermute | solution.py:128
  213.9 19.6 %collective-permute-start = (bf16[128,2048]{1,0:T(8,128)(2,1)}, bf16[128,2048]{1,0:T(8,128)(2,1)}, u32[]{:S(2)}, u32[]{:S(2)}) collective-permute-start(bf16[128,2048]{1,0:T(8,128)(2,1)} %copy.24), channel_id=1, source_target_pairs={{0,32},{32,64},{64,96},{1,33},{33,65},{65,97},{2,34},{34,66},{66,9... | collective-permute-start | bytes 1572872 | tf_op jit(solution)/shard_map/while/body/eval_jaxpr/ppermute | solution.py:128
  263.2 17.4 %collective-permute-start.1 = (bf16[128,2048]{1,0:T(8,128)(2,1)S(1)}, bf16[128,2048]{1,0:T(8,128)(2,1)S(1)}, u32[]{:S(2)}, u32[]{:S(2)}) collective-permute-start(bf16[128,2048]{1,0:T(8,128)(2,1)S(1)} %get-tuple-element.477), channel_id=1, source_target_pairs={{0,1},{1,0},{2,3},{3,2},{4,5},{5,4},{6,7},{7,6},{8,9},{9,8},{10,11... | collective-permute-start | bytes 1572872 | tf_op jit(solution)/shard_map/while/body/eval_jaxpr/ppermute | solution.py:32
  266.8 18.5 %collective-permute-start = (bf16[128,2048]{1,0:T(8,128)(2,1)}, bf16[128,2048]{1,0:T(8,128)(2,1)}, u32[]{:S(2)}, u32[]{:S(2)}) collective-permute-start(bf16[128,2048]{1,0:T(8,128)(2,1)} %copy.24), channel_id=1, source_target_pairs={{0,32},{32,64},{64,96},{1,33},{33,65},{65,97},{2,34},{34,66},{66,9... | collective-permute-start | bytes 1572872 | tf_op jit(solution)/shard_map/while/body/eval_jaxpr/ppermute | solution.py:128
  286.3 11.4 %collective-permute-start.1 = (bf16[128,2048]{1,0:T(8,128)(2,1)S(1)}, bf16[128,2048]{1,0:T(8,128)(2,1)S(1)}, u32[]{:S(2)}, u32[]{:S(2)}) collective-permute-start(bf16[128,2048]{1,0:T(8,128)(2,1)S(1)} %get-tuple-element.477), channel_id=1, source_target_pairs={{0,1},{1,0},{2,3},{3,2},{4,5},{5,4},{6,7},{7,6},{8,9},{9,8},{10,11... | collective-permute-start | bytes 1572872 | tf_op jit(solution)/shard_map/while/body/eval_jaxpr/ppermute | solution.py:32
  290.9 13.9 %collective-permute-start = (bf16[128,2048]{1,0:T(8,128)(2,1)}, bf16[128,2048]{1,0:T(8,128)(2,1)}, u32[]{:S(2)}, u32[]{:S(2)}) collective-permute-start(bf16[128,2048]{1,0:T(8,128)(2,1)} %copy.24), channel_id=1, source_target_pairs={{0,32},{32,64},{64,96},{1,33},{33,65},{65,97},{2,34},{34,66},{66,9... | collective-permute-start | bytes 1572872 | tf_op jit(solution)/shard_map/while/body/eval_jaxpr/ppermute | solution.py:128
  305.9 12.5 %collective-permute-start.1 = (bf16[128,2048]{1,0:T(8,128)(2,1)S(1)}, bf16[128,2048]{1,0:T(8,128)(2,1)S(1)}, u32[]{:S(2)}, u32[]{:S(2)}) collective-permute-start(bf16[128,2048]{1,0:T(8,128)(2,1)S(1)} %get-tuple-element.477), channel_id=1, source_target_pairs={{0,1},{1,0},{2,3},{3,2},{4,5},{5,4},{6,7},{7,6},{8,9},{9,8},{10,11... | collective-permute-start | bytes 1572872 | tf_op jit(solution)/shard_map/while/body/eval_jaxpr/ppermute | solution.py:32
  307.8 14.7 %collective-permute-start = (bf16[128,2048]{1,0:T(8,128)(2,1)}, bf16[128,2048]{1,0:T(8,128)(2,1)}, u32[]{:S(2)}, u32[]{:S(2)}) collective-permute-start(bf16[128,2048]{1,0:T(8,128)(2,1)} %copy.24), channel_id=1, source_target_pairs={{0,32},{32,64},{64,96},{1,33},{33,65},{65,97},{2,34},{34,66},{66,9... | collective-permute-start | bytes 1572872 | tf_op jit(solution)/shard_map/while/body/eval_jaxpr/ppermute | solution.py:128
  323.6 13.7 %collective-permute-start.1 = (bf16[128,2048]{1,0:T(8,128)(2,1)S(1)}, bf16[128,2048]{1,0:T(8,128)(2,1)S(1)}, u32[]{:S(2)}, u32[]{:S(2)}) collective-permute-start(bf16[128,2048]{1,0:T(8,128)(2,1)S(1)} %get-tuple-element.477), channel_id=1, source_target_pairs={{0,1},{1,0},{2,3},{3,2},{4,5},{5,4},{6,7},{7,6},{8,9},{9,8},{10,11... | collective-permute-start | bytes 1572872 | tf_op jit(solution)/shard_map/while/body/eval_jaxpr/ppermute | solution.py:32
  325.5 16.4 %collective-permute-start = (bf16[128,2048]{1,0:T(8,128)(2,1)}, bf16[128,2048]{1,0:T(8,128)(2,1)}, u32[]{:S(2)}, u32[]{:S(2)}) collective-permute-start(bf16[128,2048]{1,0:T(8,128)(2,1)} %copy.24), channel_id=1, source_target_pairs={{0,32},{32,64},{64,96},{1,33},{33,65},{65,97},{2,34},{34,66},{66,9... | collective-permute-start | bytes 1572872 | tf_op jit(solution)/shard_map/while/body/eval_jaxpr/ppermute | solution.py:128
  365.6 11.9 %collective-permute-start.4 = (f32[8]{0:T(128)S(1)}, f32[8]{0:T(128)S(1)}, u32[]{:S(2)}, u32[]{:S(2)}) collective-permute-start(f32[8]{0:T(128)S(1)} %convert_divide_fusion), channel_id=1, source_target_pairs={{0,96},{32,0},{64,32},{96,64},{1,97},{33,1},{65,33},{97,65},{2,98}... | collective-permute-start | bytes 104 | tf_op jit(solution)/shard_map/ppermute | solution.py:32
  437.3 15.5 %collective-permute-start.8 = (f32[4,2,2,32,256]{4,3,2,1,0:T(8,128)}, f32[4,2,2,32,256]{4,3,2,1,0:T(8,128)}, u32[]{:S(2)}, u32[]{:S(2)}) collective-permute-start(f32[4,2,2,32,256]{4,3,2,1,0:T(8,128)} %dynamic-slice_bitcast_fusion.2), channel_id=1, source_target_pairs={{0,32},{32,64},{64,96},{96,0},{1,33},{33,65},{65,97},{97,1},{2,34}... | collective-permute-start | bytes 1572872 | tf_op jit(solution)/shard_map/ppermute | solution.py:32
  438.1 16.7 %collective-permute-start.14 = (f32[4,2,2,32,256]{4,3,2,1,0:T(8,128)}, f32[4,2,2,32,256]{4,3,2,1,0:T(8,128)}, u32[]{:S(2)}, u32[]{:S(2)}) collective-permute-start(f32[4,2,2,32,256]{4,3,2,1,0:T(8,128)} %dynamic-slice_bitcast_fusion.1), channel_id=1, source_target_pairs={{0,96},{32,0},{64,32},{96,64},{1,97},{33,1},{65,33},{97,65},{2,98}... | collective-permute-start | bytes 1572872 | tf_op jit(solution)/shard_map/ppermute | solution.py:32
  454.8 14.6 %collective-permute-start.9 = (f32[4,2,2,32,256]{4,3,2,1,0:T(8,128)}, f32[4,2,2,32,256]{4,3,2,1,0:T(8,128)}, u32[]{:S(2)}, u32[]{:S(2)}) collective-permute-start(f32[4,2,2,32,256]{4,3,2,1,0:T(8,128)} %bitcast_add_fusion.6), channel_id=1, source_target_pairs={{0,32},{32,64},{64,96},{96,0},{1,33},{33,65},{65,97},{97,1},{2,34}... | collective-permute-start | bytes 1572872 | tf_op jit(solution)/shard_map/ppermute | solution.py:32
  456.7 14.8 %collective-permute-start.15 = (f32[4,2,2,32,256]{4,3,2,1,0:T(8,128)}, f32[4,2,2,32,256]{4,3,2,1,0:T(8,128)}, u32[]{:S(2)}, u32[]{:S(2)}) collective-permute-start(f32[4,2,2,32,256]{4,3,2,1,0:T(8,128)} %bitcast_add_fusion.3), channel_id=1, source_target_pairs={{0,96},{32,0},{64,32},{96,64},{1,97},{33,1},{65,33},{97,65},{2,98}... | collective-permute-start | bytes 1572872 | tf_op jit(solution)/shard_map/ppermute | solution.py:32
  471.5 13.8 %collective-permute-start.10 = (f32[4,2,2,32,256]{4,3,2,1,0:T(8,128)}, f32[4,2,2,32,256]{4,3,2,1,0:T(8,128)}, u32[]{:S(2)}, u32[]{:S(2)}) collective-permute-start(f32[4,2,2,32,256]{4,3,2,1,0:T(8,128)} %bitcast_add_fusion.5), channel_id=1, source_target_pairs={{0,32},{32,64},{64,96},{96,0},{1,33},{33,65},{65,97},{97,1},{2,34}... | collective-permute-start | bytes 1572872 | tf_op jit(solution)/shard_map/ppermute | solution.py:32
  473.5 15.2 %collective-permute-start.16 = (f32[4,2,2,32,256]{4,3,2,1,0:T(8,128)}, f32[4,2,2,32,256]{4,3,2,1,0:T(8,128)}, u32[]{:S(2)}, u32[]{:S(2)}) collective-permute-start(f32[4,2,2,32,256]{4,3,2,1,0:T(8,128)} %bitcast_add_fusion.2), channel_id=1, source_target_pairs={{0,96},{32,0},{64,32},{96,64},{1,97},{33,1},{65,33},{97,65},{2,98}... | collective-permute-start | bytes 1572872 | tf_op jit(solution)/shard_map/ppermute | solution.py:32
  (42 other events, 576.4 us)
Sparse Core Ops, SparseCore 0:
  10.4 56.1 all-gather.2
  69.0 46.2 all-gather.4

commit v2 on v1

--- a/solution.py
+++ b/solution.py
@@ -56,23 +56,34 @@
     return keep + move(send)
 
 
-def gradient_scatter(joined):
-    rows, cols = joined.shape
+def gradient_scatter(first, second):
+    rows, cols = first.shape
     seg = lax.axis_index("segment")
     f = lax.axis_index("fsdp")
     rep = lax.axis_index("rep")
     y_pos = f // 4
     zh_pos = (f // 2) % 2
     core_pos = f % 2
-    blocks = joined.reshape(4, 4, 2, 2, 2, rows // 128, cols)
-    blocks = pair_scatter(blocks, 3, core_pos, lambda v: fsdp_moved(v, lambda g: g ^ 1))
-    blocks = ring_scatter(blocks, seg, 4, lambda v, by: shifted(v, "segment", 4, by))
-    blocks = ring_scatter(
-        blocks, y_pos, 4, lambda v, by: fsdp_moved(v, lambda g: ((g // 4 + by) % 4) * 4 + g % 4)
-    )
-    blocks = pair_scatter(blocks, 1, rep, lambda v: shifted(v, "rep", 2, 1))
-    blocks = pair_scatter(blocks, 0, zh_pos, lambda v: fsdp_moved(v, lambda g: g ^ 2))
-    return blocks
+    along_x = lambda v, by: shifted(v, "segment", 4, by)
+    along_y = lambda v, by: fsdp_moved(v, lambda g: ((g // 4 + by) % 4) * 4 + g % 4)
+    along_core = lambda v: fsdp_moved(v, lambda g: g ^ 1)
+    along_zh = lambda v: fsdp_moved(v, lambda g: g ^ 2)
+    along_zl = lambda v: shifted(v, "rep", 2, 1)
+    outs = []
+    for grad, order in ((first, 0), (second, 1)):
+        blocks = grad.reshape(4, 4, 2, 2, 2, rows // 128, cols)
+        blocks = pair_scatter(blocks, 3, core_pos, along_core)
+        if order == 0:
+            blocks = ring_scatter(blocks, seg, 4, along_x)
+            blocks = ring_scatter(blocks, y_pos, 4, along_y)
+        else:
+            blocks = jnp.swapaxes(blocks, 0, 1)
+            blocks = ring_scatter(blocks, y_pos, 4, along_y)
+            blocks = ring_scatter(blocks, seg, 4, along_x)
+        outs.append(blocks)
+    outs = [pair_scatter(b, 1, rep, along_zl) for b in outs]
+    outs = [pair_scatter(b, 0, zh_pos, along_zh) for b in outs]
+    return outs
 
 
 def on_device(
@@ -119,8 +130,7 @@
         own_half = lax.dynamic_slice_in_dim(wide_rows, rep_pos * half_width, half_width, 1)
         return (own_half + update).astype(jnp.bfloat16)
 
-    def skip_segment(current):
-        return jnp.zeros((block_rows, half_width), jnp.bfloat16)
+    embedded_all = lookup_rows(flat_ids, embed_table)
 
     def tick_whole(tick_pos, state):
         arrived, computed, stored = state
@@ -129,14 +139,12 @@
         micro_pos = tick_pos - 2 * segment_pos
         active = (micro_pos >= 0) & (micro_pos < micro_count)
         slot_pos = jnp.clip(micro_pos, 0, micro_count - 1)
-        embedded = lookup_rows(
-            lax.dynamic_slice_in_dim(flat_ids, slot_pos * block_rows, block_rows, 0), embed_table
-        )
+        embedded = lax.dynamic_slice_in_dim(embedded_all, slot_pos * block_rows, block_rows, 0)
         low = jnp.where(own_first, arrived, partner)
         high = jnp.where(own_first, partner, arrived)
         joined = jnp.concatenate([low, high], axis=1)
         current = jnp.where(is_first, embedded, joined)
-        result = lax.cond(active, apply_segment, skip_segment, current)
+        result = apply_segment(current)
         previous = lax.dynamic_slice_in_dim(stored, slot_pos * block_rows, block_rows, 0)
         chosen = jnp.where(active & is_last, result, previous)
         stored = lax.dynamic_update_slice_in_dim(stored, chosen, slot_pos * block_rows, 0)
@@ -222,9 +230,8 @@
     down_grad = lax.dot_general(
         unit_rows, latent_grad, (((0,), (0,)), ((), ())), preferred_element_type=jnp.float32
     )
-    rank = down_grad.shape[1]
-    shares = gradient_scatter(jnp.concatenate([down_grad, up_grad], axis=1))
-    return (shares[:, :rank], shares[:, rank:])
+    down_share, up_share = gradient_scatter(down_grad, up_grad)
+    return (down_share, up_share)
 
 
 def solution(mesh):

time: 533 us -> 471 us (0.88)
  local copies, waits for them, and re-layouts: 71.9 us -> 12.6 us
  matrix products: 113 us -> 155 us
  other arithmetic: 86.4 us -> 49.5 us
  starting transfers between devices: 120 us -> 111 us
    dot_general x8 -> x14, matrix products: 72.2 us -> 132 us  [apply_segment(): update = jnp.dot(normed, weight_local, preferred_element_type=jnp.float32)]
    another operation x22 -> x1, local copies, waits for them, and re-layouts: 32.6 us -> 0.05 us
    dynamic_update_slice x14 -> x0, other arithmetic: 28.8 us -> none  [tick_whole(): lax.dynamic_update_slice_in_dim(stored, chosen, slot_pos * block_rows, 0)]
    concatenate x15 -> x0, other arithmetic: 23.1 us -> none  [the longest x14 15.4 us: tick_whole(): joined = jnp.concatenate([low, high], axis=1)]
    dot_general x15 -> x2, matrix products: 22.6 us -> 6.91 us  [lookup_rows(): jnp.dot(onehot, embed_table, preferred_element_type=jnp.float32)]
    ppermute x26 -> x33, waiting for transfers between devices: 95.4 us -> 111 us  [shifted(): return lax.ppermute(x, axis, [(i, (i + by) % size) for i in range(size)])]
    ppermute x26 -> x33, starting transfers between devices: 48 us -> 33.6 us  [shifted(): return lax.ppermute(x, axis, [(i, (i + by) % size) for i in range(size)])]
    while x42 -> x14, local copies, waits for them, and re-layouts: 14.7 us -> 0.57 us
  transfers between devices with their start and end apart: 50 -> 65, of which waited for: 29 -> 28; matrix products, arithmetic and copies ran while one was open for 43% -> 44% of each run, Pallas kernels for 0% -> 0%
where the time goes in v2:
time: 471 us; the launch traced here: 469 us
  matrix products  155 us (33%)
  waiting for transfers between devices  122 us (26%)
  starting transfers between devices  111 us (24%)
  other arithmetic  49.5 us (11%)
  between operations  18 us (4%)
  local copies, waits for them, and re-layouts  12.6 us (3%)
    dot_general x14, matrix products, apply_segment(): update = jnp.dot(normed, weight_local, preferred_element_type=jnp.float32)  132 us
    ppermute x33, waiting for transfers between devices, shifted(): return lax.ppermute(x, axis, [(i, (i + by) % size) for i in range(size)])  111 us
    ppermute x14, starting transfers between devices, tick_whole(): lax.ppermute(computed, 'segment', [(i, i + 1) for i in range(segments - 1)])  49.6 us
    ppermute x33, starting transfers between devices, shifted(): return lax.ppermute(x, axis, [(i, (i + by) % size) for i in range(size)])  33.6 us
    ppermute x16, starting transfers between devices, fsdp_moved(): return lax.ppermute(x, 'fsdp', [(f, mapping(f)) for f in range(16)])  27.5 us
    reduce_sum x14, other arithmetic, rms_scale(): squares = jnp.mean(values * values, axis=-1, keepdims=True)  23.3 us
    while x14, other arithmetic  14.1 us
    ppermute x16, waiting for transfers between devices, fsdp_moved(): return lax.ppermute(x, 'fsdp', [(f, mapping(f)) for f in range(16)])  9.86 us
  transfers between devices with their start and end apart: 65, of which 28 were waited for; matrix products, arithmetic and copies ran while one was open for 44% of the time, Pallas kernels for 0%

profile of v2, /device:TPU:0, one launch (start us, length us, event | category | flops | bytes accessed | tf_op | source)
XLA Modules:
  0.0 468.7 jit_solution(2315400758755468762)
XLA Ops:
  8.7 6.3 %convolution_convert_fusion = bf16[1024,4096]{1,0:T(8,128)(2,1)} fusion(bf16[128,4096]{1,0:T(8,128)(2,1)S(1)} %copy-done, s32[1024]{0:T(1024)} %bitcast.144), kind=kOutput, calls=%fused_computation.18 | convolution fusion | flops 1078067200 | bytes 9441280 | tf_op jit(solution)/shard_map/dot_general | solution.py:22
  17.6 327.9 %while.20 = (s32[]{:T(128)}, bf16[128,2048]{1,0:T(8,128)(2,1)S(1)}, bf16[128,2048]{1,0:T(8,128)(2,1)}, bf16[1024,2048]{1,0:T(8,128)(2,1)}, pred[]{:T(512)}, /*in...) while((s32[]{:T(128)}, bf16[128,2048]{1,0:T(8,128)(2,1)S(1)}, ...), condition=%wide.region_4.5_spmd.clone, body=%wide.region_2.4_spmd.clone.sunk | while | flops 2154823936 | bytes 34098032 | solution.py:158
  23.2 9.8 %collective-permute-done.1 = bf16[128,2048]{1,0:T(8,128)(2,1)S(1)} collective-permute-done((bf16[128,2048]{1,0:T(8,128)(2,1)S(1)}, bf16[128,2048]{1,0:T(8,128)(2,1)S(1)}, u32[]{:S(2)}, u32[]{:S(2)}) %collective-permute-start.1) | collective-permute-done | bytes 524320 | tf_op jit(solution)/shard_map/while/body/eval_jaxpr/ppermute | solution.py:32
  34.8 9.5 %select_dynamic-update-slice_fusion.2 = (bf16[1024,2048]{1,0:T(8,128)(2,1)}, bf16[128,2048]{1,0:T(8,128)(2,1)}) fusion(bf16[1024,2048]{1,0:T(8,128)(2,1)} %get-tuple-element.476, s32[]{:T(128)S(6)} %select_n.436, pred[]{:T(512)S(6)} %and.148, bf16[4096,2048]{1,0:T(8,128)(2,1)} %get-tuple-element.501, f32[128,4096]{1,0:T(8,128)S(1)} %get-tuple-element.451, ...), kind=kOutput, calls=%fused_computation.8.clone.1 | convolution fusion | flops 2149842944 | bytes 21513220 | tf_op jit(solution)/shard_map/while/body/eval_jaxpr/dot_general | solution.py:129
  50.7 12.0 %collective-permute-done.1 = bf16[128,2048]{1,0:T(8,128)(2,1)S(1)} collective-permute-done((bf16[128,2048]{1,0:T(8,128)(2,1)S(1)}, bf16[128,2048]{1,0:T(8,128)(2,1)S(1)}, u32[]{:S(2)}, u32[]{:S(2)}) %collective-permute-start.1) | collective-permute-done | bytes 524320 | tf_op jit(solution)/shard_map/while/body/eval_jaxpr/ppermute | solution.py:32
  64.4 9.4 %select_dynamic-update-slice_fusion.2 = (bf16[1024,2048]{1,0:T(8,128)(2,1)}, bf16[128,2048]{1,0:T(8,128)(2,1)}) fusion(bf16[1024,2048]{1,0:T(8,128)(2,1)} %get-tuple-element.476, s32[]{:T(128)S(6)} %select_n.436, pred[]{:T(512)S(6)} %and.148, bf16[4096,2048]{1,0:T(8,128)(2,1)} %get-tuple-element.501, f32[128,4096]{1,0:T(8,128)S(1)} %get-tuple-element.451, ...), kind=kOutput, calls=%fused_computation.8.clone.1 | convolution fusion | flops 2149842944 | bytes 21513220 | tf_op jit(solution)/shard_map/while/body/eval_jaxpr/dot_general | solution.py:129
  79.1 9.6 %collective-permute-done.1 = bf16[128,2048]{1,0:T(8,128)(2,1)S(1)} collective-permute-done((bf16[128,2048]{1,0:T(8,128)(2,1)S(1)}, bf16[128,2048]{1,0:T(8,128)(2,1)S(1)}, u32[]{:S(2)}, u32[]{:S(2)}) %collective-permute-start.1) | collective-permute-done | bytes 524320 | tf_op jit(solution)/shard_map/while/body/eval_jaxpr/ppermute | solution.py:32
  90.5 9.4 %select_dynamic-update-slice_fusion.2 = (bf16[1024,2048]{1,0:T(8,128)(2,1)}, bf16[128,2048]{1,0:T(8,128)(2,1)}) fusion(bf16[1024,2048]{1,0:T(8,128)(2,1)} %get-tuple-element.476, s32[]{:T(128)S(6)} %select_n.436, pred[]{:T(512)S(6)} %and.148, bf16[4096,2048]{1,0:T(8,128)(2,1)} %get-tuple-element.501, f32[128,4096]{1,0:T(8,128)S(1)} %get-tuple-element.451, ...), kind=kOutput, calls=%fused_computation.8.clone.1 | convolution fusion | flops 2149842944 | bytes 21513220 | tf_op jit(solution)/shard_map/while/body/eval_jaxpr/dot_general | solution.py:129
  105.2 12.5 %collective-permute-done.1 = bf16[128,2048]{1,0:T(8,128)(2,1)S(1)} collective-permute-done((bf16[128,2048]{1,0:T(8,128)(2,1)S(1)}, bf16[128,2048]{1,0:T(8,128)(2,1)S(1)}, u32[]{:S(2)}, u32[]{:S(2)}) %collective-permute-start.1) | collective-permute-done | bytes 524320 | tf_op jit(solution)/shard_map/while/body/eval_jaxpr/ppermute | solution.py:32
  119.5 9.4 %select_dynamic-update-slice_fusion.2 = (bf16[1024,2048]{1,0:T(8,128)(2,1)}, bf16[128,2048]{1,0:T(8,128)(2,1)}) fusion(bf16[1024,2048]{1,0:T(8,128)(2,1)} %get-tuple-element.476, s32[]{:T(128)S(6)} %select_n.436, pred[]{:T(512)S(6)} %and.148, bf16[4096,2048]{1,0:T(8,128)(2,1)} %get-tuple-element.501, f32[128,4096]{1,0:T(8,128)S(1)} %get-tuple-element.451, ...), kind=kOutput, calls=%fused_computation.8.clone.1 | convolution fusion | flops 2149842944 | bytes 21513220 | tf_op jit(solution)/shard_map/while/body/eval_jaxpr/dot_general | solution.py:129
  134.0 8.2 %collective-permute-done.1 = bf16[128,2048]{1,0:T(8,128)(2,1)S(1)} collective-permute-done((bf16[128,2048]{1,0:T(8,128)(2,1)S(1)}, bf16[128,2048]{1,0:T(8,128)(2,1)S(1)}, u32[]{:S(2)}, u32[]{:S(2)}) %collective-permute-start.1) | collective-permute-done | bytes 524320 | tf_op jit(solution)/shard_map/while/body/eval_jaxpr/ppermute | solution.py:32
  144.0 9.4 %select_dynamic-update-slice_fusion.2 = (bf16[1024,2048]{1,0:T(8,128)(2,1)}, bf16[128,2048]{1,0:T(8,128)(2,1)}) fusion(bf16[1024,2048]{1,0:T(8,128)(2,1)} %get-tuple-element.476, s32[]{:T(128)S(6)} %select_n.436, pred[]{:T(512)S(6)} %and.148, bf16[4096,2048]{1,0:T(8,128)(2,1)} %get-tuple-element.501, f32[128,4096]{1,0:T(8,128)S(1)} %get-tuple-element.451, ...), kind=kOutput, calls=%fused_computation.8.clone.1 | convolution fusion | flops 2149842944 | bytes 21513220 | tf_op jit(solution)/shard_map/while/body/eval_jaxpr/dot_general | solution.py:129
  158.6 7.3 %collective-permute-done.1 = bf16[128,2048]{1,0:T(8,128)(2,1)S(1)} collective-permute-done((bf16[128,2048]{1,0:T(8,128)(2,1)S(1)}, bf16[128,2048]{1,0:T(8,128)(2,1)S(1)}, u32[]{:S(2)}, u32[]{:S(2)}) %collective-permute-start.1) | collective-permute-done | bytes 524320 | tf_op jit(solution)/shard_map/while/body/eval_jaxpr/ppermute | solution.py:32
  167.6 9.4 %select_dynamic-update-slice_fusion.2 = (bf16[1024,2048]{1,0:T(8,128)(2,1)}, bf16[128,2048]{1,0:T(8,128)(2,1)}) fusion(bf16[1024,2048]{1,0:T(8,128)(2,1)} %get-tuple-element.476, s32[]{:T(128)S(6)} %select_n.436, pred[]{:T(512)S(6)} %and.148, bf16[4096,2048]{1,0:T(8,128)(2,1)} %get-tuple-element.501, f32[128,4096]{1,0:T(8,128)S(1)} %get-tuple-element.451, ...), kind=kOutput, calls=%fused_computation.8.clone.1 | convolution fusion | flops 2149842944 | bytes 21513220 | tf_op jit(solution)/shard_map/while/body/eval_jaxpr/dot_general | solution.py:129
  182.3 6.3 %collective-permute-done.1 = bf16[128,2048]{1,0:T(8,128)(2,1)S(1)} collective-permute-done((bf16[128,2048]{1,0:T(8,128)(2,1)S(1)}, bf16[128,2048]{1,0:T(8,128)(2,1)S(1)}, u32[]{:S(2)}, u32[]{:S(2)}) %collective-permute-start.1) | collective-permute-done | bytes 524320 | tf_op jit(solution)/shard_map/while/body/eval_jaxpr/ppermute | solution.py:32
  190.4 9.4 %select_dynamic-update-slice_fusion.2 = (bf16[1024,2048]{1,0:T(8,128)(2,1)}, bf16[128,2048]{1,0:T(8,128)(2,1)}) fusion(bf16[1024,2048]{1,0:T(8,128)(2,1)} %get-tuple-element.476, s32[]{:T(128)S(6)} %select_n.436, pred[]{:T(512)S(6)} %and.148, bf16[4096,2048]{1,0:T(8,128)(2,1)} %get-tuple-element.501, f32[128,4096]{1,0:T(8,128)S(1)} %get-tuple-element.451, ...), kind=kOutput, calls=%fused_computation.8.clone.1 | convolution fusion | flops 2149842944 | bytes 21513220 | tf_op jit(solution)/shard_map/while/body/eval_jaxpr/dot_general | solution.py:129
  205.2 5.4 %collective-permute-done.1 = bf16[128,2048]{1,0:T(8,128)(2,1)S(1)} collective-permute-done((bf16[128,2048]{1,0:T(8,128)(2,1)S(1)}, bf16[128,2048]{1,0:T(8,128)(2,1)S(1)}, u32[]{:S(2)}, u32[]{:S(2)}) %collective-permute-start.1) | collective-permute-done | bytes 524320 | tf_op jit(solution)/shard_map/while/body/eval_jaxpr/ppermute | solution.py:32
  212.4 9.4 %select_dynamic-update-slice_fusion.2 = (bf16[1024,2048]{1,0:T(8,128)(2,1)}, bf16[128,2048]{1,0:T(8,128)(2,1)}) fusion(bf16[1024,2048]{1,0:T(8,128)(2,1)} %get-tuple-element.476, s32[]{:T(128)S(6)} %select_n.436, pred[]{:T(512)S(6)} %and.148, bf16[4096,2048]{1,0:T(8,128)(2,1)} %get-tuple-element.501, f32[128,4096]{1,0:T(8,128)S(1)} %get-tuple-element.451, ...), kind=kOutput, calls=%fused_computation.8.clone.1 | convolution fusion | flops 2149842944 | bytes 21513220 | tf_op jit(solution)/shard_map/while/body/eval_jaxpr/dot_general | solution.py:129
  227.2 4.5 collective-permute-done.1
  233.4 9.4 %select_dynamic-update-slice_fusion.2 = (bf16[1024,2048]{1,0:T(8,128)(2,1)}, bf16[128,2048]{1,0:T(8,128)(2,1)}) fusion(bf16[1024,2048]{1,0:T(8,128)(2,1)} %get-tuple-element.476, s32[]{:T(128)S(6)} %select_n.436, pred[]{:T(512)S(6)} %and.148, bf16[4096,2048]{1,0:T(8,128)(2,1)} %get-tuple-element.501, f32[128,4096]{1,0:T(8,128)S(1)} %get-tuple-element.451, ...), kind=kOutput, calls=%fused_computation.8.clone.1 | convolution fusion | flops 2149842944 | bytes 21513220 | tf_op jit(solution)/shard_map/while/body/eval_jaxpr/dot_general | solution.py:129
  248.3 3.9 collective-permute-done.1
  254.0 9.4 %select_dynamic-update-slice_fusion.2 = (bf16[1024,2048]{1,0:T(8,128)(2,1)}, bf16[128,2048]{1,0:T(8,128)(2,1)}) fusion(bf16[1024,2048]{1,0:T(8,128)(2,1)} %get-tuple-element.476, s32[]{:T(128)S(6)} %select_n.436, pred[]{:T(512)S(6)} %and.148, bf16[4096,2048]{1,0:T(8,128)(2,1)} %get-tuple-element.501, f32[128,4096]{1,0:T(8,128)S(1)} %get-tuple-element.451, ...), kind=kOutput, calls=%fused_computation.8.clone.1 | convolution fusion | flops 2149842944 | bytes 21513220 | tf_op jit(solution)/shard_map/while/body/eval_jaxpr/dot_general | solution.py:129
  268.9 3.9 collective-permute-done.1
  274.5 9.4 %select_dynamic-update-slice_fusion.2 = (bf16[1024,2048]{1,0:T(8,128)(2,1)}, bf16[128,2048]{1,0:T(8,128)(2,1)}) fusion(bf16[1024,2048]{1,0:T(8,128)(2,1)} %get-tuple-element.476, s32[]{:T(128)S(6)} %select_n.436, pred[]{:T(512)S(6)} %and.148, bf16[4096,2048]{1,0:T(8,128)(2,1)} %get-tuple-element.501, f32[128,4096]{1,0:T(8,128)S(1)} %get-tuple-element.451, ...), kind=kOutput, calls=%fused_computation.8.clone.1 | convolution fusion | flops 2149842944 | bytes 21513220 | tf_op jit(solution)/shard_map/while/body/eval_jaxpr/dot_general | solution.py:129
  289.4 3.9 collective-permute-done.1
  295.0 9.4 %select_dynamic-update-slice_fusion.2 = (bf16[1024,2048]{1,0:T(8,128)(2,1)}, bf16[128,2048]{1,0:T(8,128)(2,1)}) fusion(bf16[1024,2048]{1,0:T(8,128)(2,1)} %get-tuple-element.476, s32[]{:T(128)S(6)} %select_n.436, pred[]{:T(512)S(6)} %and.148, bf16[4096,2048]{1,0:T(8,128)(2,1)} %get-tuple-element.501, f32[128,4096]{1,0:T(8,128)S(1)} %get-tuple-element.451, ...), kind=kOutput, calls=%fused_computation.8.clone.1 | convolution fusion | flops 2149842944 | bytes 21513220 | tf_op jit(solution)/shard_map/while/body/eval_jaxpr/dot_general | solution.py:129
  309.9 3.9 collective-permute-done.1
  315.5 9.4 %select_dynamic-update-slice_fusion.2 = (bf16[1024,2048]{1,0:T(8,128)(2,1)}, bf16[128,2048]{1,0:T(8,128)(2,1)}) fusion(bf16[1024,2048]{1,0:T(8,128)(2,1)} %get-tuple-element.476, s32[]{:T(128)S(6)} %select_n.436, pred[]{:T(512)S(6)} %and.148, bf16[4096,2048]{1,0:T(8,128)(2,1)} %get-tuple-element.501, f32[128,4096]{1,0:T(8,128)S(1)} %get-tuple-element.451, ...), kind=kOutput, calls=%fused_computation.8.clone.1 | convolution fusion | flops 2149842944 | bytes 21513220 | tf_op jit(solution)/shard_map/while/body/eval_jaxpr/dot_general | solution.py:129
  330.4 3.9 collective-permute-done.1
  336.0 9.4 %select_dynamic-update-slice_fusion.2 = (bf16[1024,2048]{1,0:T(8,128)(2,1)}, bf16[128,2048]{1,0:T(8,128)(2,1)}) fusion(bf16[1024,2048]{1,0:T(8,128)(2,1)} %get-tuple-element.476, s32[]{:T(128)S(6)} %select_n.436, pred[]{:T(512)S(6)} %and.148, bf16[4096,2048]{1,0:T(8,128)(2,1)} %get-tuple-element.501, f32[128,4096]{1,0:T(8,128)S(1)} %get-tuple-element.451, ...), kind=kOutput, calls=%fused_computation.8.clone.1 | convolution fusion | flops 2149842944 | bytes 21513220 | tf_op jit(solution)/shard_map/while/body/eval_jaxpr/dot_general | solution.py:129
  357.5 8.1 %collective-permute-done.3 = f32[1024,128]{0,1:T(8,128)S(1)} collective-permute-done((f32[1024,128]{0,1:T(8,128)S(1)}, f32[1024,128]{0,1:T(8,128)S(1)}, u32[]{:S(2)}, u32[]{:S(2)}) %collective-permute-start.3) | collective-permute-done | bytes 524320 | tf_op jit(solution)/shard_map/ppermute | solution.py:32
  389.1 5.5 %fusion.13 = f32[4096,256]{1,0:T(8,128)} fusion(bf16[128,4096]{1,0:T(8,128)(2,1)} %copy-done.2, bf16[4096,256]{1,0:T(8,128)(2,1)} %all-gather.5.cloned.1.call-done, f32[128,4096]{1,0:T(8,128)S(1)} %get-tuple-element.363, f32[128]{0:T(128)S(1)} %add_rsqrt_fusion.3), kind=kOutput, calls=%fused_computation.39 | convolution fusion | flops 537952256 | bytes 9437696 | tf_op jit(solution)/shard_map/dot_general | solution.py:230
  (294 shorter events, 202.6 us)
Async XLA Ops:
  7.2 368.3 %all-gather.3.cloned.1.call-start = ((), (), s32[]{:S(2)}) async-start(), calls=%async_computation | async-start | bytes 2228224 | tf_op jit(solution)/shard_map/all_gather | solution.py:122
  7.9 369.7 %all-gather.5.cloned.1.call-start = ((), (), s32[]{:S(2)}) async-start(), calls=%async_computation.1 | async-start | bytes 2228224 | tf_op jit(solution)/shard_map/all_gather | solution.py:123
  17.6 15.4 %collective-permute-start.1 = (bf16[128,2048]{1,0:T(8,128)(2,1)S(1)}, bf16[128,2048]{1,0:T(8,128)(2,1)S(1)}, u32[]{:S(2)}, u32[]{:S(2)}) collective-permute-start(bf16[128,2048]{1,0:T(8,128)(2,1)S(1)} %get-tuple-element.474), channel_id=1, source_target_pairs={{0,1},{1,0},{2,3},{3,2},{4,5},{5,4},{6,7},{7,6},{8,9},{9,8},{10,11... | collective-permute-start | bytes 1572872 | tf_op jit(solution)/shard_map/while/body/eval_jaxpr/ppermute | solution.py:32
  19.8 24.5 %collective-permute-start = (bf16[128,2048]{1,0:T(8,128)(2,1)S(1)}, bf16[128,2048]{1,0:T(8,128)(2,1)S(1)}, u32[]{:S(2)}, u32[]{:S(2)}) collective-permute-start(bf16[128,2048]{1,0:T(8,128)(2,1)S(1)} %broadcast_select_fusion.8), channel_id=1, source_target_pairs={{0,32},{32,64},{64,96},{1,33},{33,65},{65,97},{2,34},{34,66},{66,9... | collective-permute-start | bytes 1572872 | tf_op jit(solution)/shard_map/while/body/eval_jaxpr/ppermute | solution.py:138
  44.4 18.3 %collective-permute-start.1 = (bf16[128,2048]{1,0:T(8,128)(2,1)S(1)}, bf16[128,2048]{1,0:T(8,128)(2,1)S(1)}, u32[]{:S(2)}, u32[]{:S(2)}) collective-permute-start(bf16[128,2048]{1,0:T(8,128)(2,1)S(1)} %get-tuple-element.474), channel_id=1, source_target_pairs={{0,1},{1,0},{2,3},{3,2},{4,5},{5,4},{6,7},{7,6},{8,9},{9,8},{10,11... | collective-permute-start | bytes 1572872 | tf_op jit(solution)/shard_map/while/body/eval_jaxpr/ppermute | solution.py:32
  47.3 26.6 %collective-permute-start = (bf16[128,2048]{1,0:T(8,128)(2,1)S(1)}, bf16[128,2048]{1,0:T(8,128)(2,1)S(1)}, u32[]{:S(2)}, u32[]{:S(2)}) collective-permute-start(bf16[128,2048]{1,0:T(8,128)(2,1)S(1)} %broadcast_select_fusion.8), channel_id=1, source_target_pairs={{0,32},{32,64},{64,96},{1,33},{33,65},{65,97},{2,34},{34,66},{66,9... | collective-permute-start | bytes 1572872 | tf_op jit(solution)/shard_map/while/body/eval_jaxpr/ppermute | solution.py:138
  73.9 14.8 %collective-permute-start.1 = (bf16[128,2048]{1,0:T(8,128)(2,1)S(1)}, bf16[128,2048]{1,0:T(8,128)(2,1)S(1)}, u32[]{:S(2)}, u32[]{:S(2)}) collective-permute-start(bf16[128,2048]{1,0:T(8,128)(2,1)S(1)} %get-tuple-element.474), channel_id=1, source_target_pairs={{0,1},{1,0},{2,3},{3,2},{4,5},{5,4},{6,7},{7,6},{8,9},{9,8},{10,11... | collective-permute-start | bytes 1572872 | tf_op jit(solution)/shard_map/while/body/eval_jaxpr/ppermute | solution.py:32
  75.4 24.5 %collective-permute-start = (bf16[128,2048]{1,0:T(8,128)(2,1)S(1)}, bf16[128,2048]{1,0:T(8,128)(2,1)S(1)}, u32[]{:S(2)}, u32[]{:S(2)}) collective-permute-start(bf16[128,2048]{1,0:T(8,128)(2,1)S(1)} %broadcast_select_fusion.8), channel_id=1, source_target_pairs={{0,32},{32,64},{64,96},{1,33},{33,65},{65,97},{2,34},{34,66},{66,9... | collective-permute-start | bytes 1572872 | tf_op jit(solution)/shard_map/while/body/eval_jaxpr/ppermute | solution.py:138
  100.0 17.8 %collective-permute-start.1 = (bf16[128,2048]{1,0:T(8,128)(2,1)S(1)}, bf16[128,2048]{1,0:T(8,128)(2,1)S(1)}, u32[]{:S(2)}, u32[]{:S(2)}) collective-permute-start(bf16[128,2048]{1,0:T(8,128)(2,1)S(1)} %get-tuple-element.474), channel_id=1, source_target_pairs={{0,1},{1,0},{2,3},{3,2},{4,5},{5,4},{6,7},{7,6},{8,9},{9,8},{10,11... | collective-permute-start | bytes 1572872 | tf_op jit(solution)/shard_map/while/body/eval_jaxpr/ppermute | solution.py:32
  101.5 27.5 %collective-permute-start = (bf16[128,2048]{1,0:T(8,128)(2,1)S(1)}, bf16[128,2048]{1,0:T(8,128)(2,1)S(1)}, u32[]{:S(2)}, u32[]{:S(2)}) collective-permute-start(bf16[128,2048]{1,0:T(8,128)(2,1)S(1)} %broadcast_select_fusion.8), channel_id=1, source_target_pairs={{0,32},{32,64},{64,96},{1,33},{33,65},{65,97},{2,34},{34,66},{66,9... | collective-permute-start | bytes 1572872 | tf_op jit(solution)/shard_map/while/body/eval_jaxpr/ppermute | solution.py:138
  129.0 13.2 %collective-permute-start.1 = (bf16[128,2048]{1,0:T(8,128)(2,1)S(1)}, bf16[128,2048]{1,0:T(8,128)(2,1)S(1)}, u32[]{:S(2)}, u32[]{:S(2)}) collective-permute-start(bf16[128,2048]{1,0:T(8,128)(2,1)S(1)} %get-tuple-element.474), channel_id=1, source_target_pairs={{0,1},{1,0},{2,3},{3,2},{4,5},{5,4},{6,7},{7,6},{8,9},{9,8},{10,11... | collective-permute-start | bytes 1572872 | tf_op jit(solution)/shard_map/while/body/eval_jaxpr/ppermute | solution.py:32
  130.4 23.0 %collective-permute-start = (bf16[128,2048]{1,0:T(8,128)(2,1)S(1)}, bf16[128,2048]{1,0:T(8,128)(2,1)S(1)}, u32[]{:S(2)}, u32[]{:S(2)}) collective-permute-start(bf16[128,2048]{1,0:T(8,128)(2,1)S(1)} %broadcast_select_fusion.8), channel_id=1, source_target_pairs={{0,32},{32,64},{64,96},{1,33},{33,65},{65,97},{2,34},{34,66},{66,9... | collective-permute-start | bytes 1572872 | tf_op jit(solution)/shard_map/while/body/eval_jaxpr/ppermute | solution.py:138
  153.5 12.4 %collective-permute-start.1 = (bf16[128,2048]{1,0:T(8,128)(2,1)S(1)}, bf16[128,2048]{1,0:T(8,128)(2,1)S(1)}, u32[]{:S(2)}, u32[]{:S(2)}) collective-permute-start(bf16[128,2048]{1,0:T(8,128)(2,1)S(1)} %get-tuple-element.474), channel_id=1, source_target_pairs={{0,1},{1,0},{2,3},{3,2},{4,5},{5,4},{6,7},{7,6},{8,9},{9,8},{10,11... | collective-permute-start | bytes 1572872 | tf_op jit(solution)/shard_map/while/body/eval_jaxpr/ppermute | solution.py:32
  155.0 22.1 %collective-permute-start = (bf16[128,2048]{1,0:T(8,128)(2,1)S(1)}, bf16[128,2048]{1,0:T(8,128)(2,1)S(1)}, u32[]{:S(2)}, u32[]{:S(2)}) collective-permute-start(bf16[128,2048]{1,0:T(8,128)(2,1)S(1)} %broadcast_select_fusion.8), channel_id=1, source_target_pairs={{0,32},{32,64},{64,96},{1,33},{33,65},{65,97},{2,34},{34,66},{66,9... | collective-permute-start | bytes 1572872 | tf_op jit(solution)/shard_map/while/body/eval_jaxpr/ppermute | solution.py:138
  177.1 11.5 %collective-permute-start.1 = (bf16[128,2048]{1,0:T(8,128)(2,1)S(1)}, bf16[128,2048]{1,0:T(8,128)(2,1)S(1)}, u32[]{:S(2)}, u32[]{:S(2)}) collective-permute-start(bf16[128,2048]{1,0:T(8,128)(2,1)S(1)} %get-tuple-element.474), channel_id=1, source_target_pairs={{0,1},{1,0},{2,3},{3,2},{4,5},{5,4},{6,7},{7,6},{8,9},{9,8},{10,11... | collective-permute-start | bytes 1572872 | tf_op jit(solution)/shard_map/while/body/eval_jaxpr/ppermute | solution.py:32
  178.7 21.2 %collective-permute-start = (bf16[128,2048]{1,0:T(8,128)(2,1)S(1)}, bf16[128,2048]{1,0:T(8,128)(2,1)S(1)}, u32[]{:S(2)}, u32[]{:S(2)}) collective-permute-start(bf16[128,2048]{1,0:T(8,128)(2,1)S(1)} %broadcast_select_fusion.8), channel_id=1, source_target_pairs={{0,32},{32,64},{64,96},{1,33},{33,65},{65,97},{2,34},{34,66},{66,9... | collective-permute-start | bytes 1572872 | tf_op jit(solution)/shard_map/while/body/eval_jaxpr/ppermute | solution.py:138
  199.9 10.7 %collective-permute-start.1 = (bf16[128,2048]{1,0:T(8,128)(2,1)S(1)}, bf16[128,2048]{1,0:T(8,128)(2,1)S(1)}, u32[]{:S(2)}, u32[]{:S(2)}) collective-permute-start(bf16[128,2048]{1,0:T(8,128)(2,1)S(1)} %get-tuple-element.474), channel_id=1, source_target_pairs={{0,1},{1,0},{2,3},{3,2},{4,5},{5,4},{6,7},{7,6},{8,9},{9,8},{10,11... | collective-permute-start | bytes 1572872 | tf_op jit(solution)/shard_map/while/body/eval_jaxpr/ppermute | solution.py:32
  201.6 20.2 %collective-permute-start = (bf16[128,2048]{1,0:T(8,128)(2,1)S(1)}, bf16[128,2048]{1,0:T(8,128)(2,1)S(1)}, u32[]{:S(2)}, u32[]{:S(2)}) collective-permute-start(bf16[128,2048]{1,0:T(8,128)(2,1)S(1)} %broadcast_select_fusion.8), channel_id=1, source_target_pairs={{0,32},{32,64},{64,96},{1,33},{33,65},{65,97},{2,34},{34,66},{66,9... | collective-permute-start | bytes 1572872 | tf_op jit(solution)/shard_map/while/body/eval_jaxpr/ppermute | solution.py:138
  221.9 9.8 %collective-permute-start.1 = (bf16[128,2048]{1,0:T(8,128)(2,1)S(1)}, bf16[128,2048]{1,0:T(8,128)(2,1)S(1)}, u32[]{:S(2)}, u32[]{:S(2)}) collective-permute-start(bf16[128,2048]{1,0:T(8,128)(2,1)S(1)} %get-tuple-element.474), channel_id=1, source_target_pairs={{0,1},{1,0},{2,3},{3,2},{4,5},{5,4},{6,7},{7,6},{8,9},{9,8},{10,11... | collective-permute-start | bytes 1572872 | tf_op jit(solution)/shard_map/while/body/eval_jaxpr/ppermute | solution.py:32
  223.6 19.3 %collective-permute-start = (bf16[128,2048]{1,0:T(8,128)(2,1)S(1)}, bf16[128,2048]{1,0:T(8,128)(2,1)S(1)}, u32[]{:S(2)}, u32[]{:S(2)}) collective-permute-start(bf16[128,2048]{1,0:T(8,128)(2,1)S(1)} %broadcast_select_fusion.8), channel_id=1, source_target_pairs={{0,32},{32,64},{64,96},{1,33},{33,65},{65,97},{2,34},{34,66},{66,9... | collective-permute-start | bytes 1572872 | tf_op jit(solution)/shard_map/while/body/eval_jaxpr/ppermute | solution.py:138
  242.9 9.3 %collective-permute-start.1 = (bf16[128,2048]{1,0:T(8,128)(2,1)S(1)}, bf16[128,2048]{1,0:T(8,128)(2,1)S(1)}, u32[]{:S(2)}, u32[]{:S(2)}) collective-permute-start(bf16[128,2048]{1,0:T(8,128)(2,1)S(1)} %get-tuple-element.474), channel_id=1, source_target_pairs={{0,1},{1,0},{2,3},{3,2},{4,5},{5,4},{6,7},{7,6},{8,9},{9,8},{10,11... | collective-permute-start | bytes 1572872 | tf_op jit(solution)/shard_map/while/body/eval_jaxpr/ppermute | solution.py:32
  244.8 18.6 %collective-permute-start = (bf16[128,2048]{1,0:T(8,128)(2,1)S(1)}, bf16[128,2048]{1,0:T(8,128)(2,1)S(1)}, u32[]{:S(2)}, u32[]{:S(2)}) collective-permute-start(bf16[128,2048]{1,0:T(8,128)(2,1)S(1)} %broadcast_select_fusion.8), channel_id=1, source_target_pairs={{0,32},{32,64},{64,96},{1,33},{33,65},{65,97},{2,34},{34,66},{66,9... | collective-permute-start | bytes 1572872 | tf_op jit(solution)/shard_map/while/body/eval_jaxpr/ppermute | solution.py:138
  263.5 9.3 %collective-permute-start.1 = (bf16[128,2048]{1,0:T(8,128)(2,1)S(1)}, bf16[128,2048]{1,0:T(8,128)(2,1)S(1)}, u32[]{:S(2)}, u32[]{:S(2)}) collective-permute-start(bf16[128,2048]{1,0:T(8,128)(2,1)S(1)} %get-tuple-element.474), channel_id=1, source_target_pairs={{0,1},{1,0},{2,3},{3,2},{4,5},{5,4},{6,7},{7,6},{8,9},{9,8},{10,11... | collective-permute-start | bytes 1572872 | tf_op jit(solution)/shard_map/while/body/eval_jaxpr/ppermute | solution.py:32
  265.3 18.6 %collective-permute-start = (bf16[128,2048]{1,0:T(8,128)(2,1)S(1)}, bf16[128,2048]{1,0:T(8,128)(2,1)S(1)}, u32[]{:S(2)}, u32[]{:S(2)}) collective-permute-start(bf16[128,2048]{1,0:T(8,128)(2,1)S(1)} %broadcast_select_fusion.8), channel_id=1, source_target_pairs={{0,32},{32,64},{64,96},{1,33},{33,65},{65,97},{2,34},{34,66},{66,9... | collective-permute-start | bytes 1572872 | tf_op jit(solution)/shard_map/while/body/eval_jaxpr/ppermute | solution.py:138
  284.0 9.3 %collective-permute-start.1 = (bf16[128,2048]{1,0:T(8,128)(2,1)S(1)}, bf16[128,2048]{1,0:T(8,128)(2,1)S(1)}, u32[]{:S(2)}, u32[]{:S(2)}) collective-permute-start(bf16[128,2048]{1,0:T(8,128)(2,1)S(1)} %get-tuple-element.474), channel_id=1, source_target_pairs={{0,1},{1,0},{2,3},{3,2},{4,5},{5,4},{6,7},{7,6},{8,9},{9,8},{10,11... | collective-permute-start | bytes 1572872 | tf_op jit(solution)/shard_map/while/body/eval_jaxpr/ppermute | solution.py:32
  285.8 18.6 %collective-permute-start = (bf16[128,2048]{1,0:T(8,128)(2,1)S(1)}, bf16[128,2048]{1,0:T(8,128)(2,1)S(1)}, u32[]{:S(2)}, u32[]{:S(2)}) collective-permute-start(bf16[128,2048]{1,0:T(8,128)(2,1)S(1)} %broadcast_select_fusion.8), channel_id=1, source_target_pairs={{0,32},{32,64},{64,96},{1,33},{33,65},{65,97},{2,34},{34,66},{66,9... | collective-permute-start | bytes 1572872 | tf_op jit(solution)/shard_map/while/body/eval_jaxpr/ppermute | solution.py:138
  304.5 9.3 %collective-permute-start.1 = (bf16[128,2048]{1,0:T(8,128)(2,1)S(1)}, bf16[128,2048]{1,0:T(8,128)(2,1)S(1)}, u32[]{:S(2)}, u32[]{:S(2)}) collective-permute-start(bf16[128,2048]{1,0:T(8,128)(2,1)S(1)} %get-tuple-element.474), channel_id=1, source_target_pairs={{0,1},{1,0},{2,3},{3,2},{4,5},{5,4},{6,7},{7,6},{8,9},{9,8},{10,11... | collective-permute-start | bytes 1572872 | tf_op jit(solution)/shard_map/while/body/eval_jaxpr/ppermute | solution.py:32
  306.4 18.6 %collective-permute-start = (bf16[128,2048]{1,0:T(8,128)(2,1)S(1)}, bf16[128,2048]{1,0:T(8,128)(2,1)S(1)}, u32[]{:S(2)}, u32[]{:S(2)}) collective-permute-start(bf16[128,2048]{1,0:T(8,128)(2,1)S(1)} %broadcast_select_fusion.8), channel_id=1, source_target_pairs={{0,32},{32,64},{64,96},{1,33},{33,65},{65,97},{2,34},{34,66},{66,9... | collective-permute-start | bytes 1572872 | tf_op jit(solution)/shard_map/while/body/eval_jaxpr/ppermute | solution.py:138
  325.0 9.3 %collective-permute-start.1 = (bf16[128,2048]{1,0:T(8,128)(2,1)S(1)}, bf16[128,2048]{1,0:T(8,128)(2,1)S(1)}, u32[]{:S(2)}, u32[]{:S(2)}) collective-permute-start(bf16[128,2048]{1,0:T(8,128)(2,1)S(1)} %get-tuple-element.474), channel_id=1, source_target_pairs={{0,1},{1,0},{2,3},{3,2},{4,5},{5,4},{6,7},{7,6},{8,9},{9,8},{10,11... | collective-permute-start | bytes 1572872 | tf_op jit(solution)/shard_map/while/body/eval_jaxpr/ppermute | solution.py:32
  326.9 18.6 %collective-permute-start = (bf16[128,2048]{1,0:T(8,128)(2,1)S(1)}, bf16[128,2048]{1,0:T(8,128)(2,1)S(1)}, u32[]{:S(2)}, u32[]{:S(2)}) collective-permute-start(bf16[128,2048]{1,0:T(8,128)(2,1)S(1)} %broadcast_select_fusion.8), channel_id=1, source_target_pairs={{0,32},{32,64},{64,96},{1,33},{33,65},{65,97},{2,34},{34,66},{66,9... | collective-permute-start | bytes 1572872 | tf_op jit(solution)/shard_map/while/body/eval_jaxpr/ppermute | solution.py:138
  389.1 9.3 %collective-permute-start.22 = (f32[4,4,2,2,32,256]{5,4,3,2,0,1:T(8,128)}, f32[4,4,2,2,32,256]{5,4,3,2,0,1:T(8,128)}, u32[]{:S(2)}, u32[]{:S(2)}) collective-permute-start(f32[4,4,2,2,32,256]{5,4,3,2,0,1:T(8,128)} %bitcast.133), channel_id=1, source_target_pairs={{0,2},{2,0},{4,6},{6,4},{8,10},{10,8},{12,14},{14,12},{16,18},{18,... | collective-permute-start | bytes 6291464 | tf_op jit(solution)/shard_map/ppermute | solution.py:36
  403.4 9.5 %collective-permute-start.23 = (f32[4,2,2,32,128]{4,3,2,1,0:T(8,128)S(1)}, f32[4,2,2,32,128]{4,3,2,1,0:T(8,128)S(1)}, u32[]{:S(2)}, u32[]{:S(2)}) collective-permute-start(f32[4,2,2,32,128]{4,3,2,1,0:T(8,128)S(1)} %dynamic-slice_bitcast_fusion.2), channel_id=1, source_target_pairs={{0,8},{2,10},{4,12},{6,14},{8,16},{10,18},{12,20},{14,22},{16,24},... | collective-permute-start | bytes 786440 | tf_op jit(solution)/shard_map/ppermute | solution.py:36
  (44 other events, 250.8 us)
Sparse Core Ops, SparseCore 0:
  10.4 54.8 all-gather.2
  67.6 54.2 all-gather.4

commit v3 on v2

--- a/solution.py
+++ b/solution.py
@@ -107,7 +107,7 @@
     vocab_size = embed_table.shape[0]
     half_width = prior_weight.shape[2]
     per_device = group_seqs // (segments * replicas)
-    micro_count = 8
+    micro_count = 4
     total_rows = group_seqs * seq_len
     block_rows = total_rows // micro_count
     tick_count = micro_count + 2 * (segments - 1)

time: 471 us -> 522 us (1.11)
  waiting for transfers between devices: 122 us -> 165 us
  local copies, waits for them, and re-layouts: 12.6 us -> 24.4 us
  matrix products: 155 us -> 145 us
  other arithmetic: 49.5 us -> 57.5 us
    ppermute x33 -> x29, waiting for transfers between devices: 111 us -> 151 us  [shifted(): return lax.ppermute(x, axis, [(i, (i + by) % size) for i in range(size)])]
    while x14 -> x10, local copies, waits for them, and re-layouts: 0.57 us -> 12.3 us
    dot_general x14 -> x10, matrix products: 132 us -> 122 us  [apply_segment(): update = jnp.dot(normed, weight_local, preferred_element_type=jnp.float32)]
    while x14 -> x10, other arithmetic: 14.1 us -> 21.3 us
    ppermute x16, starting transfers between devices: 27.5 us -> 22.1 us  [fsdp_moved(): return lax.ppermute(x, 'fsdp', [(f, mapping(f)) for f in range(16)])]
    ppermute x33 -> x29, starting transfers between devices: 33.6 us -> 36.9 us  [shifted(): return lax.ppermute(x, axis, [(i, (i + by) % size) for i in range(size)])]
    ppermute x14 -> x10, starting transfers between devices: 49.6 us -> 51.7 us  [tick_whole(): lax.ppermute(computed, 'segment', [(i, i + 1) for i in range(segments - 1)])]
    reduce_sum x14 -> x10, other arithmetic: 23.3 us -> 23.6 us  [rms_scale(): squares = jnp.mean(values * values, axis=-1, keepdims=True)]
  transfers between devices with their start and end apart: 65 -> 57, of which waited for: 28 -> 26; matrix products, arithmetic and copies ran while one was open for 44% -> 42% of each run, Pallas kernels for 0% -> 0%
where the time goes in v3:
time: 522 us; the launch traced here: 520 us
  waiting for transfers between devices  165 us (32%)
  matrix products  145 us (28%)
  starting transfers between devices  111 us (21%)
  other arithmetic  57.5 us (11%)
  local copies, waits for them, and re-layouts  24.4 us (5%)
  between operations  18 us (3%)
    ppermute x29, waiting for transfers between devices, shifted(): return lax.ppermute(x, axis, [(i, (i + by) % size) for i in range(size)])  151 us
    dot_general x10, matrix products, apply_segment(): update = jnp.dot(normed, weight_local, preferred_element_type=jnp.float32)  122 us
    ppermute x10, starting transfers between devices, tick_whole(): lax.ppermute(computed, 'segment', [(i, i + 1) for i in range(segments - 1)])  51.7 us
    ppermute x29, starting transfers between devices, shifted(): return lax.ppermute(x, axis, [(i, (i + by) % size) for i in range(size)])  36.9 us
    reduce_sum x10, other arithmetic, rms_scale(): squares = jnp.mean(values * values, axis=-1, keepdims=True)  23.6 us
    ppermute x16, starting transfers between devices, fsdp_moved(): return lax.ppermute(x, 'fsdp', [(f, mapping(f)) for f in range(16)])  22.1 us
    while x10, other arithmetic  21.3 us
    while x10, local copies, waits for them, and re-layouts  12.3 us
  transfers between devices with their start and end apart: 57, of which 26 were waited for; matrix products, arithmetic and copies ran while one was open for 42% of the time, Pallas kernels for 0%

profile of v3, /device:TPU:0, one launch (start us, length us, event | category | flops | bytes accessed | tf_op | source)
XLA Modules:
  0.0 520.3 jit_solution(10608181591443100046)
XLA Ops:
  8.7 6.3 %convolution_convert_fusion = bf16[1024,4096]{1,0:T(8,128)(2,1)} fusion(bf16[128,4096]{1,0:T(8,128)(2,1)S(1)} %copy-done, s32[1024]{0:T(1024)} %bitcast.142), kind=kOutput, calls=%fused_computation.18 | convolution fusion | flops 1078067200 | bytes 9441280 | tf_op jit(solution)/shard_map/dot_general | solution.py:22
  17.7 375.7 %while.20 = (s32[]{:T(128)}, bf16[256,2048]{1,0:T(8,128)(2,1)S(1)}, bf16[256,2048]{1,0:T(8,128)(2,1)}, bf16[1024,2048]{1,0:T(8,128)(2,1)}, pred[]{:T(512)}, /*in...) while((s32[]{:T(128)}, bf16[256,2048]{1,0:T(8,128)(2,1)S(1)}, ...), condition=%wide.region_4.5_spmd.clone, body=%wide.region_2.4_spmd.clone.sunk | while | flops 4309647872 | bytes 51401584 | solution.py:158
  25.2 19.1 %collective-permute-done.1 = bf16[256,2048]{1,0:T(8,128)(2,1)S(1)} collective-permute-done((bf16[256,2048]{1,0:T(8,128)(2,1)S(1)}, bf16[256,2048]{1,0:T(8,128)(2,1)S(1)}, u32[]{:S(2)}, u32[]{:S(2)}) %collective-permute-start.1) | collective-permute-done | bytes 1048608 | tf_op jit(solution)/shard_map/while/body/eval_jaxpr/ppermute | solution.py:32
  46.9 12.2 %select_dynamic-update-slice_fusion.2 = (bf16[1024,2048]{1,0:T(8,128)(2,1)}, bf16[256,2048]{1,0:T(8,128)(2,1)}) fusion(bf16[1024,2048]{1,0:T(8,128)(2,1)} %get-tuple-element.476, s32[]{:T(128)S(6)} %select_n.436, pred[]{:T(512)S(6)} %and.148, bf16[4096,2048]{1,0:T(8,128)(2,1)} %get-tuple-element.501, f32[256,4096]{1,0:T(8,128)S(1)} %get-tuple-element.451, ...), kind=kOutput, calls=%fused_computation.8.clone.1 | convolution fusion | flops 4299685888 | bytes 26232324 | tf_op jit(solution)/shard_map/while/body/eval_jaxpr/dot_general | solution.py:129
  68.7 17.3 %collective-permute-done.1 = bf16[256,2048]{1,0:T(8,128)(2,1)S(1)} collective-permute-done((bf16[256,2048]{1,0:T(8,128)(2,1)S(1)}, bf16[256,2048]{1,0:T(8,128)(2,1)S(1)}, u32[]{:S(2)}, u32[]{:S(2)}) %collective-permute-start.1) | collective-permute-done | bytes 1048608 | tf_op jit(solution)/shard_map/while/body/eval_jaxpr/ppermute | solution.py:32
  88.5 12.2 %select_dynamic-update-slice_fusion.2 = (bf16[1024,2048]{1,0:T(8,128)(2,1)}, bf16[256,2048]{1,0:T(8,128)(2,1)}) fusion(bf16[1024,2048]{1,0:T(8,128)(2,1)} %get-tuple-element.476, s32[]{:T(128)S(6)} %select_n.436, pred[]{:T(512)S(6)} %and.148, bf16[4096,2048]{1,0:T(8,128)(2,1)} %get-tuple-element.501, f32[256,4096]{1,0:T(8,128)S(1)} %get-tuple-element.451, ...), kind=kOutput, calls=%fused_computation.8.clone.1 | convolution fusion | flops 4299685888 | bytes 26232324 | tf_op jit(solution)/shard_map/while/body/eval_jaxpr/dot_general | solution.py:129
  110.2 15.3 %collective-permute-done.1 = bf16[256,2048]{1,0:T(8,128)(2,1)S(1)} collective-permute-done((bf16[256,2048]{1,0:T(8,128)(2,1)S(1)}, bf16[256,2048]{1,0:T(8,128)(2,1)S(1)}, u32[]{:S(2)}, u32[]{:S(2)}) %collective-permute-start.1) | collective-permute-done | bytes 1048608 | tf_op jit(solution)/shard_map/while/body/eval_jaxpr/ppermute | solution.py:32
  128.0 12.2 %select_dynamic-update-slice_fusion.2 = (bf16[1024,2048]{1,0:T(8,128)(2,1)}, bf16[256,2048]{1,0:T(8,128)(2,1)}) fusion(bf16[1024,2048]{1,0:T(8,128)(2,1)} %get-tuple-element.476, s32[]{:T(128)S(6)} %select_n.436, pred[]{:T(512)S(6)} %and.148, bf16[4096,2048]{1,0:T(8,128)(2,1)} %get-tuple-element.501, f32[256,4096]{1,0:T(8,128)S(1)} %get-tuple-element.451, ...), kind=kOutput, calls=%fused_computation.8.clone.1 | convolution fusion | flops 4299685888 | bytes 26232324 | tf_op jit(solution)/shard_map/while/body/eval_jaxpr/dot_general | solution.py:129
  145.0 4.5 collective-permute-start
  149.4 14.6 %collective-permute-done.1 = bf16[256,2048]{1,0:T(8,128)(2,1)S(1)} collective-permute-done((bf16[256,2048]{1,0:T(8,128)(2,1)S(1)}, bf16[256,2048]{1,0:T(8,128)(2,1)S(1)}, u32[]{:S(2)}, u32[]{:S(2)}) %collective-permute-start.1) | collective-permute-done | bytes 1048608 | tf_op jit(solution)/shard_map/while/body/eval_jaxpr/ppermute | solution.py:32
  166.5 12.2 %select_dynamic-update-slice_fusion.2 = (bf16[1024,2048]{1,0:T(8,128)(2,1)}, bf16[256,2048]{1,0:T(8,128)(2,1)}) fusion(bf16[1024,2048]{1,0:T(8,128)(2,1)} %get-tuple-element.476, s32[]{:T(128)S(6)} %select_n.436, pred[]{:T(512)S(6)} %and.148, bf16[4096,2048]{1,0:T(8,128)(2,1)} %get-tuple-element.501, f32[256,4096]{1,0:T(8,128)S(1)} %get-tuple-element.451, ...), kind=kOutput, calls=%fused_computation.8.clone.1 | convolution fusion | flops 4299685888 | bytes 26232324 | tf_op jit(solution)/shard_map/while/body/eval_jaxpr/dot_general | solution.py:129
  183.4 4.6 collective-permute-start
  188.0 13.7 %collective-permute-done.1 = bf16[256,2048]{1,0:T(8,128)(2,1)S(1)} collective-permute-done((bf16[256,2048]{1,0:T(8,128)(2,1)S(1)}, bf16[256,2048]{1,0:T(8,128)(2,1)S(1)}, u32[]{:S(2)}, u32[]{:S(2)}) %collective-permute-start.1) | collective-permute-done | bytes 1048608 | tf_op jit(solution)/shard_map/while/body/eval_jaxpr/ppermute | solution.py:32
  204.2 12.2 %select_dynamic-update-slice_fusion.2 = (bf16[1024,2048]{1,0:T(8,128)(2,1)}, bf16[256,2048]{1,0:T(8,128)(2,1)}) fusion(bf16[1024,2048]{1,0:T(8,128)(2,1)} %get-tuple-element.476, s32[]{:T(128)S(6)} %select_n.436, pred[]{:T(512)S(6)} %and.148, bf16[4096,2048]{1,0:T(8,128)(2,1)} %get-tuple-element.501, f32[256,4096]{1,0:T(8,128)S(1)} %get-tuple-element.451, ...), kind=kOutput, calls=%fused_computation.8.clone.1 | convolution fusion | flops 4299685888 | bytes 26232324 | tf_op jit(solution)/shard_map/while/body/eval_jaxpr/dot_general | solution.py:129
  220.9 4.9 collective-permute-start
  225.8 12.7 %collective-permute-done.1 = bf16[256,2048]{1,0:T(8,128)(2,1)S(1)} collective-permute-done((bf16[256,2048]{1,0:T(8,128)(2,1)S(1)}, bf16[256,2048]{1,0:T(8,128)(2,1)S(1)}, u32[]{:S(2)}, u32[]{:S(2)}) %collective-permute-start.1) | collective-permute-done | bytes 1048608 | tf_op jit(solution)/shard_map/while/body/eval_jaxpr/ppermute | solution.py:32
  241.1 12.2 %select_dynamic-update-slice_fusion.2 = (bf16[1024,2048]{1,0:T(8,128)(2,1)}, bf16[256,2048]{1,0:T(8,128)(2,1)}) fusion(bf16[1024,2048]{1,0:T(8,128)(2,1)} %get-tuple-element.476, s32[]{:T(128)S(6)} %select_n.436, pred[]{:T(512)S(6)} %and.148, bf16[4096,2048]{1,0:T(8,128)(2,1)} %get-tuple-element.501, f32[256,4096]{1,0:T(8,128)S(1)} %get-tuple-element.451, ...), kind=kOutput, calls=%fused_computation.8.clone.1 | convolution fusion | flops 4299685888 | bytes 26232324 | tf_op jit(solution)/shard_map/while/body/eval_jaxpr/dot_general | solution.py:129
  257.6 5.3 %collective-permute-start = (bf16[256,2048]{1,0:T(8,128)(2,1)}, bf16[256,2048]{1,0:T(8,128)(2,1)}, u32[]{:S(2)}, u32[]{:S(2)}) collective-permute-start(bf16[256,2048]{1,0:T(8,128)(2,1)} %broadcast_select_fusion.8), channel_id=1, source_target_pairs={{0,32},{32,64},{64,96},{1,33},{33,65},{65,97},{2,34},{34,66},{66,9... | collective-permute-start | bytes 3145736 | tf_op jit(solution)/shard_map/while/body/eval_jaxpr/ppermute | solution.py:138
  262.9 11.7 %collective-permute-done.1 = bf16[256,2048]{1,0:T(8,128)(2,1)S(1)} collective-permute-done((bf16[256,2048]{1,0:T(8,128)(2,1)S(1)}, bf16[256,2048]{1,0:T(8,128)(2,1)S(1)}, u32[]{:S(2)}, u32[]{:S(2)}) %collective-permute-start.1) | collective-permute-done | bytes 1048608 | tf_op jit(solution)/shard_map/while/body/eval_jaxpr/ppermute | solution.py:32
  277.1 12.2 %select_dynamic-update-slice_fusion.2 = (bf16[1024,2048]{1,0:T(8,128)(2,1)}, bf16[256,2048]{1,0:T(8,128)(2,1)}) fusion(bf16[1024,2048]{1,0:T(8,128)(2,1)} %get-tuple-element.476, s32[]{:T(128)S(6)} %select_n.436, pred[]{:T(512)S(6)} %and.148, bf16[4096,2048]{1,0:T(8,128)(2,1)} %get-tuple-element.501, f32[256,4096]{1,0:T(8,128)S(1)} %get-tuple-element.451, ...), kind=kOutput, calls=%fused_computation.8.clone.1 | convolution fusion | flops 4299685888 | bytes 26232324 | tf_op jit(solution)/shard_map/while/body/eval_jaxpr/dot_general | solution.py:129
  293.5 5.8 %collective-permute-start = (bf16[256,2048]{1,0:T(8,128)(2,1)}, bf16[256,2048]{1,0:T(8,128)(2,1)}, u32[]{:S(2)}, u32[]{:S(2)}) collective-permute-start(bf16[256,2048]{1,0:T(8,128)(2,1)} %broadcast_select_fusion.8), channel_id=1, source_target_pairs={{0,32},{32,64},{64,96},{1,33},{33,65},{65,97},{2,34},{34,66},{66,9... | collective-permute-start | bytes 3145736 | tf_op jit(solution)/shard_map/while/body/eval_jaxpr/ppermute | solution.py:138
  299.2 10.5 %collective-permute-done.1 = bf16[256,2048]{1,0:T(8,128)(2,1)S(1)} collective-permute-done((bf16[256,2048]{1,0:T(8,128)(2,1)S(1)}, bf16[256,2048]{1,0:T(8,128)(2,1)S(1)}, u32[]{:S(2)}, u32[]{:S(2)}) %collective-permute-start.1) | collective-permute-done | bytes 1048608 | tf_op jit(solution)/shard_map/while/body/eval_jaxpr/ppermute | solution.py:32
  312.3 12.2 %select_dynamic-update-slice_fusion.2 = (bf16[1024,2048]{1,0:T(8,128)(2,1)}, bf16[256,2048]{1,0:T(8,128)(2,1)}) fusion(bf16[1024,2048]{1,0:T(8,128)(2,1)} %get-tuple-element.476, s32[]{:T(128)S(6)} %select_n.436, pred[]{:T(512)S(6)} %and.148, bf16[4096,2048]{1,0:T(8,128)(2,1)} %get-tuple-element.501, f32[256,4096]{1,0:T(8,128)S(1)} %get-tuple-element.451, ...), kind=kOutput, calls=%fused_computation.8.clone.1 | convolution fusion | flops 4299685888 | bytes 26232324 | tf_op jit(solution)/shard_map/while/body/eval_jaxpr/dot_general | solution.py:129
  328.5 6.4 %collective-permute-start = (bf16[256,2048]{1,0:T(8,128)(2,1)}, bf16[256,2048]{1,0:T(8,128)(2,1)}, u32[]{:S(2)}, u32[]{:S(2)}) collective-permute-start(bf16[256,2048]{1,0:T(8,128)(2,1)} %broadcast_select_fusion.8), channel_id=1, source_target_pairs={{0,32},{32,64},{64,96},{1,33},{33,65},{65,97},{2,34},{34,66},{66,9... | collective-permute-start | bytes 3145736 | tf_op jit(solution)/shard_map/while/body/eval_jaxpr/ppermute | solution.py:138
  334.8 9.2 %collective-permute-done.1 = bf16[256,2048]{1,0:T(8,128)(2,1)S(1)} collective-permute-done((bf16[256,2048]{1,0:T(8,128)(2,1)S(1)}, bf16[256,2048]{1,0:T(8,128)(2,1)S(1)}, u32[]{:S(2)}, u32[]{:S(2)}) %collective-permute-start.1) | collective-permute-done | bytes 1048608 | tf_op jit(solution)/shard_map/while/body/eval_jaxpr/ppermute | solution.py:32
  346.6 12.2 %select_dynamic-update-slice_fusion.2 = (bf16[1024,2048]{1,0:T(8,128)(2,1)}, bf16[256,2048]{1,0:T(8,128)(2,1)}) fusion(bf16[1024,2048]{1,0:T(8,128)(2,1)} %get-tuple-element.476, s32[]{:T(128)S(6)} %select_n.436, pred[]{:T(512)S(6)} %and.148, bf16[4096,2048]{1,0:T(8,128)(2,1)} %get-tuple-element.501, f32[256,4096]{1,0:T(8,128)S(1)} %get-tuple-element.451, ...), kind=kOutput, calls=%fused_computation.8.clone.1 | convolution fusion | flops 4299685888 | bytes 26232324 | tf_op jit(solution)/shard_map/while/body/eval_jaxpr/dot_general | solution.py:129
  362.6 7.1 %collective-permute-start = (bf16[256,2048]{1,0:T(8,128)(2,1)}, bf16[256,2048]{1,0:T(8,128)(2,1)}, u32[]{:S(2)}, u32[]{:S(2)}) collective-permute-start(bf16[256,2048]{1,0:T(8,128)(2,1)} %broadcast_select_fusion.8), channel_id=1, source_target_pairs={{0,32},{32,64},{64,96},{1,33},{33,65},{65,97},{2,34},{34,66},{66,9... | collective-permute-start | bytes 3145736 | tf_op jit(solution)/shard_map/while/body/eval_jaxpr/ppermute | solution.py:138
  369.7 7.8 %collective-permute-done.1 = bf16[256,2048]{1,0:T(8,128)(2,1)S(1)} collective-permute-done((bf16[256,2048]{1,0:T(8,128)(2,1)S(1)}, bf16[256,2048]{1,0:T(8,128)(2,1)S(1)}, u32[]{:S(2)}, u32[]{:S(2)}) %collective-permute-start.1) | collective-permute-done | bytes 1048608 | tf_op jit(solution)/shard_map/while/body/eval_jaxpr/ppermute | solution.py:32
  380.0 12.2 %select_dynamic-update-slice_fusion.2 = (bf16[1024,2048]{1,0:T(8,128)(2,1)}, bf16[256,2048]{1,0:T(8,128)(2,1)}) fusion(bf16[1024,2048]{1,0:T(8,128)(2,1)} %get-tuple-element.476, s32[]{:T(128)S(6)} %select_n.436, pred[]{:T(512)S(6)} %and.148, bf16[4096,2048]{1,0:T(8,128)(2,1)} %get-tuple-element.501, f32[256,4096]{1,0:T(8,128)S(1)} %get-tuple-element.451, ...), kind=kOutput, calls=%fused_computation.8.clone.1 | convolution fusion | flops 4299685888 | bytes 26232324 | tf_op jit(solution)/shard_map/while/body/eval_jaxpr/dot_general | solution.py:129
  405.4 8.1 %collective-permute-done.3 = f32[1024,128]{0,1:T(8,128)S(1)} collective-permute-done((f32[1024,128]{0,1:T(8,128)S(1)}, f32[1024,128]{0,1:T(8,128)S(1)}, u32[]{:S(2)}, u32[]{:S(2)}) %collective-permute-start.3) | collective-permute-done | bytes 524320 | tf_op jit(solution)/shard_map/ppermute | solution.py:32
  413.9 5.4 %collective-permute-start.4 = (f32[8]{0:T(128)S(1)}, f32[8]{0:T(128)S(1)}, u32[]{:S(2)}, u32[]{:S(2)}) collective-permute-start(f32[8]{0:T(128)S(1)} %convert_divide_fusion), channel_id=1, source_target_pairs={{0,96},{32,0},{64,32},{96,64},{1,97},{33,1},{65,33},{97,65},{2,98}... | collective-permute-start | bytes 104 | tf_op jit(solution)/shard_map/ppermute | solution.py:32
  440.2 5.5 %fusion.13 = f32[4096,256]{1,0:T(8,128)} fusion(bf16[128,4096]{1,0:T(8,128)(2,1)} %copy-done.2, bf16[4096,256]{1,0:T(8,128)(2,1)} %all-gather.5.cloned.1.call-done, f32[128,4096]{1,0:T(8,128)S(1)} %get-tuple-element.363, f32[128]{0:T(128)S(1)} %add_rsqrt_fusion.3), kind=kOutput, calls=%fused_computation.39 | convolution fusion | flops 537952256 | bytes 9437696 | tf_op jit(solution)/shard_map/dot_general | solution.py:230
  (254 shorter events, 184.7 us)
Async XLA Ops:
  7.2 419.5 %all-gather.3.cloned.1.call-start = ((), (), s32[]{:S(2)}) async-start(), calls=%async_computation | async-start | bytes 2228224 | tf_op jit(solution)/shard_map/all_gather | solution.py:122
  7.9 420.8 %all-gather.5.cloned.1.call-start = ((), (), s32[]{:S(2)}) async-start(), calls=%async_computation.1 | async-start | bytes 2228224 | tf_op jit(solution)/shard_map/all_gather | solution.py:123
  17.7 26.7 %collective-permute-start.1 = (bf16[256,2048]{1,0:T(8,128)(2,1)S(1)}, bf16[256,2048]{1,0:T(8,128)(2,1)S(1)}, u32[]{:S(2)}, u32[]{:S(2)}) collective-permute-start(bf16[256,2048]{1,0:T(8,128)(2,1)S(1)} %get-tuple-element.474), channel_id=1, source_target_pairs={{0,1},{1,0},{2,3},{3,2},{4,5},{5,4},{6,7},{7,6},{8,9},{9,8},{10,11... | collective-permute-start | bytes 3145736 | tf_op jit(solution)/shard_map/while/body/eval_jaxpr/ppermute | solution.py:32
  20.8 38.2 %collective-permute-start = (bf16[256,2048]{1,0:T(8,128)(2,1)}, bf16[256,2048]{1,0:T(8,128)(2,1)}, u32[]{:S(2)}, u32[]{:S(2)}) collective-permute-start(bf16[256,2048]{1,0:T(8,128)(2,1)} %broadcast_select_fusion.8), channel_id=1, source_target_pairs={{0,32},{32,64},{64,96},{1,33},{33,65},{65,97},{2,34},{34,66},{66,9... | collective-permute-start | bytes 3145736 | tf_op jit(solution)/shard_map/while/body/eval_jaxpr/ppermute | solution.py:138
  60.4 25.7 %collective-permute-start.1 = (bf16[256,2048]{1,0:T(8,128)(2,1)S(1)}, bf16[256,2048]{1,0:T(8,128)(2,1)S(1)}, u32[]{:S(2)}, u32[]{:S(2)}) collective-permute-start(bf16[256,2048]{1,0:T(8,128)(2,1)S(1)} %get-tuple-element.474), channel_id=1, source_target_pairs={{0,1},{1,0},{2,3},{3,2},{4,5},{5,4},{6,7},{7,6},{8,9},{9,8},{10,11... | collective-permute-start | bytes 3145736 | tf_op jit(solution)/shard_map/while/body/eval_jaxpr/ppermute | solution.py:32
  64.3 36.4 %collective-permute-start = (bf16[256,2048]{1,0:T(8,128)(2,1)}, bf16[256,2048]{1,0:T(8,128)(2,1)}, u32[]{:S(2)}, u32[]{:S(2)}) collective-permute-start(bf16[256,2048]{1,0:T(8,128)(2,1)} %broadcast_select_fusion.8), channel_id=1, source_target_pairs={{0,32},{32,64},{64,96},{1,33},{33,65},{65,97},{2,34},{34,66},{66,9... | collective-permute-start | bytes 3145736 | tf_op jit(solution)/shard_map/while/body/eval_jaxpr/ppermute | solution.py:138
  101.9 23.5 %collective-permute-start.1 = (bf16[256,2048]{1,0:T(8,128)(2,1)S(1)}, bf16[256,2048]{1,0:T(8,128)(2,1)S(1)}, u32[]{:S(2)}, u32[]{:S(2)}) collective-permute-start(bf16[256,2048]{1,0:T(8,128)(2,1)S(1)} %get-tuple-element.474), channel_id=1, source_target_pairs={{0,1},{1,0},{2,3},{3,2},{4,5},{5,4},{6,7},{7,6},{8,9},{9,8},{10,11... | collective-permute-start | bytes 3145736 | tf_op jit(solution)/shard_map/while/body/eval_jaxpr/ppermute | solution.py:32
  105.7 34.4 %collective-permute-start = (bf16[256,2048]{1,0:T(8,128)(2,1)}, bf16[256,2048]{1,0:T(8,128)(2,1)}, u32[]{:S(2)}, u32[]{:S(2)}) collective-permute-start(bf16[256,2048]{1,0:T(8,128)(2,1)} %broadcast_select_fusion.8), channel_id=1, source_target_pairs={{0,32},{32,64},{64,96},{1,33},{33,65},{65,97},{2,34},{34,66},{66,9... | collective-permute-start | bytes 3145736 | tf_op jit(solution)/shard_map/while/body/eval_jaxpr/ppermute | solution.py:138
  141.3 22.7 %collective-permute-start.1 = (bf16[256,2048]{1,0:T(8,128)(2,1)S(1)}, bf16[256,2048]{1,0:T(8,128)(2,1)S(1)}, u32[]{:S(2)}, u32[]{:S(2)}) collective-permute-start(bf16[256,2048]{1,0:T(8,128)(2,1)S(1)} %get-tuple-element.474), channel_id=1, source_target_pairs={{0,1},{1,0},{2,3},{3,2},{4,5},{5,4},{6,7},{7,6},{8,9},{9,8},{10,11... | collective-permute-start | bytes 3145736 | tf_op jit(solution)/shard_map/while/body/eval_jaxpr/ppermute | solution.py:32
  145.0 33.7 %collective-permute-start = (bf16[256,2048]{1,0:T(8,128)(2,1)}, bf16[256,2048]{1,0:T(8,128)(2,1)}, u32[]{:S(2)}, u32[]{:S(2)}) collective-permute-start(bf16[256,2048]{1,0:T(8,128)(2,1)} %broadcast_select_fusion.8), channel_id=1, source_target_pairs={{0,32},{32,64},{64,96},{1,33},{33,65},{65,97},{2,34},{34,66},{66,9... | collective-permute-start | bytes 3145736 | tf_op jit(solution)/shard_map/while/body/eval_jaxpr/ppermute | solution.py:138
  179.9 21.8 %collective-permute-start.1 = (bf16[256,2048]{1,0:T(8,128)(2,1)S(1)}, bf16[256,2048]{1,0:T(8,128)(2,1)S(1)}, u32[]{:S(2)}, u32[]{:S(2)}) collective-permute-start(bf16[256,2048]{1,0:T(8,128)(2,1)S(1)} %get-tuple-element.474), channel_id=1, source_target_pairs={{0,1},{1,0},{2,3},{3,2},{4,5},{5,4},{6,7},{7,6},{8,9},{9,8},{10,11... | collective-permute-start | bytes 3145736 | tf_op jit(solution)/shard_map/while/body/eval_jaxpr/ppermute | solution.py:32
  183.4 33.0 %collective-permute-start = (bf16[256,2048]{1,0:T(8,128)(2,1)}, bf16[256,2048]{1,0:T(8,128)(2,1)}, u32[]{:S(2)}, u32[]{:S(2)}) collective-permute-start(bf16[256,2048]{1,0:T(8,128)(2,1)} %broadcast_select_fusion.8), channel_id=1, source_target_pairs={{0,32},{32,64},{64,96},{1,33},{33,65},{65,97},{2,34},{34,66},{66,9... | collective-permute-start | bytes 3145736 | tf_op jit(solution)/shard_map/while/body/eval_jaxpr/ppermute | solution.py:138
  217.6 20.9 %collective-permute-start.1 = (bf16[256,2048]{1,0:T(8,128)(2,1)S(1)}, bf16[256,2048]{1,0:T(8,128)(2,1)S(1)}, u32[]{:S(2)}, u32[]{:S(2)}) collective-permute-start(bf16[256,2048]{1,0:T(8,128)(2,1)S(1)} %get-tuple-element.474), channel_id=1, source_target_pairs={{0,1},{1,0},{2,3},{3,2},{4,5},{5,4},{6,7},{7,6},{8,9},{9,8},{10,11... | collective-permute-start | bytes 3145736 | tf_op jit(solution)/shard_map/while/body/eval_jaxpr/ppermute | solution.py:32
  220.9 32.4 %collective-permute-start = (bf16[256,2048]{1,0:T(8,128)(2,1)}, bf16[256,2048]{1,0:T(8,128)(2,1)}, u32[]{:S(2)}, u32[]{:S(2)}) collective-permute-start(bf16[256,2048]{1,0:T(8,128)(2,1)} %broadcast_select_fusion.8), channel_id=1, source_target_pairs={{0,32},{32,64},{64,96},{1,33},{33,65},{65,97},{2,34},{34,66},{66,9... | collective-permute-start | bytes 3145736 | tf_op jit(solution)/shard_map/while/body/eval_jaxpr/ppermute | solution.py:138
  254.5 20.1 %collective-permute-start.1 = (bf16[256,2048]{1,0:T(8,128)(2,1)S(1)}, bf16[256,2048]{1,0:T(8,128)(2,1)S(1)}, u32[]{:S(2)}, u32[]{:S(2)}) collective-permute-start(bf16[256,2048]{1,0:T(8,128)(2,1)S(1)} %get-tuple-element.474), channel_id=1, source_target_pairs={{0,1},{1,0},{2,3},{3,2},{4,5},{5,4},{6,7},{7,6},{8,9},{9,8},{10,11... | collective-permute-start | bytes 3145736 | tf_op jit(solution)/shard_map/while/body/eval_jaxpr/ppermute | solution.py:32
  257.6 31.7 %collective-permute-start = (bf16[256,2048]{1,0:T(8,128)(2,1)}, bf16[256,2048]{1,0:T(8,128)(2,1)}, u32[]{:S(2)}, u32[]{:S(2)}) collective-permute-start(bf16[256,2048]{1,0:T(8,128)(2,1)} %broadcast_select_fusion.8), channel_id=1, source_target_pairs={{0,32},{32,64},{64,96},{1,33},{33,65},{65,97},{2,34},{34,66},{66,9... | collective-permute-start | bytes 3145736 | tf_op jit(solution)/shard_map/while/body/eval_jaxpr/ppermute | solution.py:138
  290.5 19.2 %collective-permute-start.1 = (bf16[256,2048]{1,0:T(8,128)(2,1)S(1)}, bf16[256,2048]{1,0:T(8,128)(2,1)S(1)}, u32[]{:S(2)}, u32[]{:S(2)}) collective-permute-start(bf16[256,2048]{1,0:T(8,128)(2,1)S(1)} %get-tuple-element.474), channel_id=1, source_target_pairs={{0,1},{1,0},{2,3},{3,2},{4,5},{5,4},{6,7},{7,6},{8,9},{9,8},{10,11... | collective-permute-start | bytes 3145736 | tf_op jit(solution)/shard_map/while/body/eval_jaxpr/ppermute | solution.py:32
  293.5 31.0 %collective-permute-start = (bf16[256,2048]{1,0:T(8,128)(2,1)}, bf16[256,2048]{1,0:T(8,128)(2,1)}, u32[]{:S(2)}, u32[]{:S(2)}) collective-permute-start(bf16[256,2048]{1,0:T(8,128)(2,1)} %broadcast_select_fusion.8), channel_id=1, source_target_pairs={{0,32},{32,64},{64,96},{1,33},{33,65},{65,97},{2,34},{34,66},{66,9... | collective-permute-start | bytes 3145736 | tf_op jit(solution)/shard_map/while/body/eval_jaxpr/ppermute | solution.py:138
  325.7 18.4 %collective-permute-start.1 = (bf16[256,2048]{1,0:T(8,128)(2,1)S(1)}, bf16[256,2048]{1,0:T(8,128)(2,1)S(1)}, u32[]{:S(2)}, u32[]{:S(2)}) collective-permute-start(bf16[256,2048]{1,0:T(8,128)(2,1)S(1)} %get-tuple-element.474), channel_id=1, source_target_pairs={{0,1},{1,0},{2,3},{3,2},{4,5},{5,4},{6,7},{7,6},{8,9},{9,8},{10,11... | collective-permute-start | bytes 3145736 | tf_op jit(solution)/shard_map/while/body/eval_jaxpr/ppermute | solution.py:32
  328.5 30.3 %collective-permute-start = (bf16[256,2048]{1,0:T(8,128)(2,1)}, bf16[256,2048]{1,0:T(8,128)(2,1)}, u32[]{:S(2)}, u32[]{:S(2)}) collective-permute-start(bf16[256,2048]{1,0:T(8,128)(2,1)} %broadcast_select_fusion.8), channel_id=1, source_target_pairs={{0,32},{32,64},{64,96},{1,33},{33,65},{65,97},{2,34},{34,66},{66,9... | collective-permute-start | bytes 3145736 | tf_op jit(solution)/shard_map/while/body/eval_jaxpr/ppermute | solution.py:138
  360.0 17.5 %collective-permute-start.1 = (bf16[256,2048]{1,0:T(8,128)(2,1)S(1)}, bf16[256,2048]{1,0:T(8,128)(2,1)S(1)}, u32[]{:S(2)}, u32[]{:S(2)}) collective-permute-start(bf16[256,2048]{1,0:T(8,128)(2,1)S(1)} %get-tuple-element.474), channel_id=1, source_target_pairs={{0,1},{1,0},{2,3},{3,2},{4,5},{5,4},{6,7},{7,6},{8,9},{9,8},{10,11... | collective-permute-start | bytes 3145736 | tf_op jit(solution)/shard_map/while/body/eval_jaxpr/ppermute | solution.py:32
  362.6 29.6 %collective-permute-start = (bf16[256,2048]{1,0:T(8,128)(2,1)}, bf16[256,2048]{1,0:T(8,128)(2,1)}, u32[]{:S(2)}, u32[]{:S(2)}) collective-permute-start(bf16[256,2048]{1,0:T(8,128)(2,1)} %broadcast_select_fusion.8), channel_id=1, source_target_pairs={{0,32},{32,64},{64,96},{1,33},{33,65},{65,97},{2,34},{34,66},{66,9... | collective-permute-start | bytes 3145736 | tf_op jit(solution)/shard_map/while/body/eval_jaxpr/ppermute | solution.py:138
  404.2 9.3 %collective-permute-start.3 = (f32[1024,128]{0,1:T(8,128)S(1)}, f32[1024,128]{0,1:T(8,128)S(1)}, u32[]{:S(2)}, u32[]{:S(2)}) collective-permute-start(f32[1024,128]{0,1:T(8,128)S(1)} %fusion.8), channel_id=1, source_target_pairs={{0,1},{1,0},{2,3},{3,2},{4,5},{5,4},{6,7},{7,6},{8,9},{9,8},{10,11... | collective-permute-start | bytes 1572872 | tf_op jit(solution)/shard_map/ppermute | solution.py:32
  440.2 9.3 %collective-permute-start.22 = (f32[4,4,2,2,32,256]{5,4,3,2,0,1:T(8,128)}, f32[4,4,2,2,32,256]{5,4,3,2,0,1:T(8,128)}, u32[]{:S(2)}, u32[]{:S(2)}) collective-permute-start(f32[4,4,2,2,32,256]{5,4,3,2,0,1:T(8,128)} %bitcast.133), channel_id=1, source_target_pairs={{0,2},{2,0},{4,6},{6,4},{8,10},{10,8},{12,14},{14,12},{16,18},{18,... | collective-permute-start | bytes 6291464 | tf_op jit(solution)/shard_map/ppermute | solution.py:36
  451.9 9.0 %collective-permute-start.29 = (f32[4,2,2,32,128]{4,3,2,1,0:T(8,128)S(1)}, f32[4,2,2,32,128]{4,3,2,1,0:T(8,128)S(1)}, u32[]{:S(2)}, u32[]{:S(2)}) collective-permute-start(f32[4,2,2,32,128]{4,3,2,1,0:T(8,128)S(1)} %dynamic-slice_bitcast_fusion.1), channel_id=1, source_target_pairs={{0,24},{2,26},{4,28},{6,30},{8,0},{10,2},{12,4},{14,6},{16,8},{18,... | collective-permute-start | bytes 786440 | tf_op jit(solution)/shard_map/ppermute | solution.py:36
  455.2 9.5 %collective-permute-start.23 = (f32[4,2,2,32,128]{4,3,2,1,0:T(8,128)S(1)}, f32[4,2,2,32,128]{4,3,2,1,0:T(8,128)S(1)}, u32[]{:S(2)}, u32[]{:S(2)}) collective-permute-start(f32[4,2,2,32,128]{4,3,2,1,0:T(8,128)S(1)} %dynamic-slice_bitcast_fusion.2), channel_id=1, source_target_pairs={{0,8},{2,10},{4,12},{6,14},{8,16},{10,18},{12,20},{14,22},{16,24},... | collective-permute-start | bytes 786440 | tf_op jit(solution)/shard_map/ppermute | solution.py:36
  457.8 9.4 %collective-permute-start.8 = (f32[4,2,2,32,128]{4,3,2,1,0:T(8,128)S(1)}, f32[4,2,2,32,128]{4,3,2,1,0:T(8,128)S(1)}, u32[]{:S(2)}, u32[]{:S(2)}) collective-permute-start(f32[4,2,2,32,128]{4,3,2,1,0:T(8,128)S(1)} %dynamic-slice_bitcast_fusion.4), channel_id=1, source_target_pairs={{0,32},{32,64},{64,96},{96,0},{1,33},{33,65},{65,97},{97,1},{2,34}... | collective-permute-start | bytes 786440 | tf_op jit(solution)/shard_map/ppermute | solution.py:32
  460.9 8.7 %collective-permute-start.30 = (f32[4,2,2,32,128]{4,3,2,1,0:T(8,128)S(1)}, f32[4,2,2,32,128]{4,3,2,1,0:T(8,128)S(1)}, u32[]{:S(2)}, u32[]{:S(2)}) collective-permute-start(f32[4,2,2,32,128]{4,3,2,1,0:T(8,128)S(1)} %bitcast_add_fusion.4), channel_id=1, source_target_pairs={{0,24},{2,26},{4,28},{6,30},{8,0},{10,2},{12,4},{14,6},{16,8},{18,... | collective-permute-start | bytes 786440 | tf_op jit(solution)/shard_map/ppermute | solution.py:36
  464.7 8.7 %collective-permute-start.24 = (f32[4,2,2,32,128]{4,3,2,1,0:T(8,128)S(1)}, f32[4,2,2,32,128]{4,3,2,1,0:T(8,128)S(1)}, u32[]{:S(2)}, u32[]{:S(2)}) collective-permute-start(f32[4,2,2,32,128]{4,3,2,1,0:T(8,128)S(1)} %bitcast_add_fusion.7), channel_id=1, source_target_pairs={{0,8},{2,10},{4,12},{6,14},{8,16},{10,18},{12,20},{14,22},{16,24},... | collective-permute-start | bytes 786440 | tf_op jit(solution)/shard_map/ppermute | solution.py:36
  467.3 8.6 %collective-permute-start.9 = (f32[4,2,2,32,128]{4,3,2,1,0:T(8,128)S(1)}, f32[4,2,2,32,128]{4,3,2,1,0:T(8,128)S(1)}, u32[]{:S(2)}, u32[]{:S(2)}) collective-permute-start(f32[4,2,2,32,128]{4,3,2,1,0:T(8,128)S(1)} %bitcast_add_fusion.13), channel_id=1, source_target_pairs={{0,32},{32,64},{64,96},{96,0},{1,33},{33,65},{65,97},{97,1},{2,34}... | collective-permute-start | bytes 786440 | tf_op jit(solution)/shard_map/ppermute | solution.py:32
  475.9 8.6 %collective-permute-start.10 = (f32[4,2,2,32,128]{4,3,2,1,0:T(8,128)S(1)}, f32[4,2,2,32,128]{4,3,2,1,0:T(8,128)S(1)}, u32[]{:S(2)}, u32[]{:S(2)}) collective-permute-start(f32[4,2,2,32,128]{4,3,2,1,0:T(8,128)S(1)} %bitcast_add_fusion.12), channel_id=1, source_target_pairs={{0,32},{32,64},{64,96},{96,0},{1,33},{33,65},{65,97},{97,1},{2,34}... | collective-permute-start | bytes 786440 | tf_op jit(solution)/shard_map/ppermute | solution.py:32
  477.5 8.5 %collective-permute-start.32 = (f32[2,2,32,128]{3,2,1,0:T(8,128)S(1)}, f32[2,2,32,128]{3,2,1,0:T(8,128)S(1)}, u32[]{:S(2)}, u32[]{:S(2)}) collective-permute-start(f32[2,2,32,128]{3,2,1,0:T(8,128)S(1)} %dynamic-slice_bitcast_fusion.5), channel_id=1, source_target_pairs={{0,96},{32,0},{64,32},{96,64},{1,97},{33,1},{65,33},{97,65},{2,98}... | collective-permute-start | bytes 196616 | tf_op jit(solution)/shard_map/ppermute | solution.py:32
  (36 other events, 183.6 us)
Sparse Core Ops, SparseCore 0:
  10.4 52.1 all-gather.2
  65.0 47.6 all-gather.4

commit v4 on v2

--- a/solution.py
+++ b/solution.py
@@ -69,10 +69,11 @@
     along_core = lambda v: fsdp_moved(v, lambda g: g ^ 1)
     along_zh = lambda v: fsdp_moved(v, lambda g: g ^ 2)
     along_zl = lambda v: shifted(v, "rep", 2, 1)
+    both = jnp.stack([first, second]).reshape(2, 4, 4, 2, 2, 2, rows // 128, cols)
+    both = pair_scatter(both, 4, core_pos, along_core)
     outs = []
-    for grad, order in ((first, 0), (second, 1)):
-        blocks = grad.reshape(4, 4, 2, 2, 2, rows // 128, cols)
-        blocks = pair_scatter(blocks, 3, core_pos, along_core)
+    for order in (0, 1):
+        blocks = both[order]
         if order == 0:
             blocks = ring_scatter(blocks, seg, 4, along_x)
             blocks = ring_scatter(blocks, y_pos, 4, along_y)
@@ -81,8 +82,10 @@
             blocks = ring_scatter(blocks, y_pos, 4, along_y)
             blocks = ring_scatter(blocks, seg, 4, along_x)
         outs.append(blocks)
-    outs = [pair_scatter(b, 1, rep, along_zl) for b in outs]
-    outs = [pair_scatter(b, 0, zh_pos, along_zh) for b in outs]
+    both = jnp.stack(outs)
+    both = pair_scatter(both, 2, rep, along_zl)
+    both = pair_scatter(both, 1, zh_pos, along_zh)
+    outs = [both[0], both[1]]
     return outs
 
 
@@ -123,28 +126,32 @@
         lax.all_gather(agent_up, "fsdp", axis=0, tiled=True),
     )
 
-    def apply_segment(current):
-        wide_rows = current.astype(jnp.float32)
-        normed = (wide_rows * rms_scale(wide_rows) * gain_local).astype(jnp.bfloat16)
-        update = jnp.dot(normed, weight_local, preferred_element_type=jnp.float32)
-        own_half = lax.dynamic_slice_in_dim(wide_rows, rep_pos * half_width, half_width, 1)
-        return (own_half + update).astype(jnp.bfloat16)
-
+    gain_own = lax.dynamic_slice_in_dim(gain_local, rep_pos * half_width, half_width, 0)
+    gain_other = lax.dynamic_slice_in_dim(gain_local, (1 - rep_pos) * half_width, half_width, 0)
+    weight_own = lax.dynamic_slice_in_dim(weight_local, rep_pos * half_width, half_width, 0)
+    weight_other = lax.dynamic_slice_in_dim(weight_local, (1 - rep_pos) * half_width, half_width, 0)
     embedded_all = lookup_rows(flat_ids, embed_table)
+    embedded_own = lax.dynamic_slice_in_dim(embedded_all, rep_pos * half_width, half_width, 1)
 
     def tick_whole(tick_pos, state):
         arrived, computed, stored = state
-        partner = shifted(arrived, "rep", replicas, 1)
-        passed = lax.ppermute(computed, "segment", [(i, i + 1) for i in range(segments - 1)])
         micro_pos = tick_pos - 2 * segment_pos
         active = (micro_pos >= 0) & (micro_pos < micro_count)
         slot_pos = jnp.clip(micro_pos, 0, micro_count - 1)
-        embedded = lax.dynamic_slice_in_dim(embedded_all, slot_pos * block_rows, block_rows, 0)
-        low = jnp.where(own_first, arrived, partner)
-        high = jnp.where(own_first, partner, arrived)
-        joined = jnp.concatenate([low, high], axis=1)
-        current = jnp.where(is_first, embedded, joined)
-        result = apply_segment(current)
+        embedded = lax.dynamic_slice_in_dim(embedded_own, slot_pos * block_rows, block_rows, 0)
+        own_rows = jnp.where(is_first, embedded, arrived)
+        partner = shifted(own_rows, "rep", replicas, 1)
+        passed = lax.ppermute(computed, "segment", [(i, i + 1) for i in range(segments - 1)])
+        own_wide = own_rows.astype(jnp.float32)
+        own_squares = jnp.sum(own_wide * own_wide, axis=-1, keepdims=True)
+        squares = own_squares + shifted(own_squares, "rep", replicas, 1)
+        scale = lax.rsqrt(squares / model_width + epsilon)
+        normed_own = (own_wide * scale * gain_own).astype(jnp.bfloat16)
+        normed_other = (partner.astype(jnp.float32) * scale * gain_other).astype(jnp.bfloat16)
+        update = jnp.dot(normed_own, weight_own, preferred_element_type=jnp.float32) + jnp.dot(
+            normed_other, weight_other, preferred_element_type=jnp.float32
+        )
+        result = (own_wide + update).astype(jnp.bfloat16)
         previous = lax.dynamic_slice_in_dim(stored, slot_pos * block_rows, block_rows, 0)
         chosen = jnp.where(active & is_last, result, previous)
         stored = lax.dynamic_update_slice_in_dim(stored, chosen, slot_pos * block_rows, 0)

time: 471 us -> 486 us (1.032)
  waiting for transfers between devices: 122 us -> 87.5 us
  starting transfers between devices: 111 us -> 142 us
  matrix products: 155 us -> 168 us
  local copies, waits for them, and re-layouts: 12.6 us -> 21.5 us
    ppermute x33 -> x46, waiting for transfers between devices: 111 us -> 16.4 us  [shifted(): return lax.ppermute(x, axis, [(i, (i + by) % size) for i in range(size)])]
    ppermute x14, waiting for transfers between devices: 0.04 us -> 51.8 us  [tick_whole(): lax.ppermute(computed, 'segment', [(i, i + 1) for i in range(segments - 1)])]
    ppermute x33 -> x46, starting transfers between devices: 33.6 us -> 59.6 us  [shifted(): return lax.ppermute(x, axis, [(i, (i + by) % size) for i in range(size)])]
    dot_general x14 -> x28, matrix products: 132 us -> 147 us  [the longest x14 81.5 us: tick_whole(): jnp.dot(normed_other, weight_other, preferred_element_type=jnp.float32)]
    ppermute x14, starting transfers between devices: 49.6 us -> 59.2 us  [tick_whole(): lax.ppermute(computed, 'segment', [(i, i + 1) for i in range(segments - 1)])]
    dynamic_slice x2, local copies, waits for them, and re-layouts: 3.33 us -> 11.9 us  [the longest x1 11.9 us: on_device(): lax.dynamic_slice_in_dim(weight_local, (1 - rep_pos) * half_width, half_w...]
    ppermute x16 -> x14, waiting for transfers between devices: 9.86 us -> 17.9 us  [fsdp_moved(): return lax.ppermute(x, 'fsdp', [(f, mapping(f)) for f in range(16)])]
    reduce_sum x14, other arithmetic: 23.3 us -> 18.4 us  [tick_whole(): own_squares = jnp.sum(own_wide * own_wide, axis=-1, keepdims=True)]
  transfers between devices with their start and end apart: 65 -> 76, of which waited for: 28 -> 25; matrix products, arithmetic and copies ran while one was open for 44% -> 43% of each run, Pallas kernels for 0% -> 0%
where the time goes in v4:
time: 486 us; the launch traced here: 484 us
  matrix products  168 us (35%)
  starting transfers between devices  142 us (29%)
  waiting for transfers between devices  87.5 us (18%)
  other arithmetic  46 us (9%)
  local copies, waits for them, and re-layouts  21.5 us (4%)
  between operations  18 us (4%)
    dot_general x14, matrix products, tick_whole(): jnp.dot(normed_other, weight_other, preferred_element_type=jnp.float32)  81.5 us
    dot_general x14, matrix products, tick_whole(): jnp.dot(normed_own, weight_own, preferred_element_type=jnp.float32)  65.6 us
    ppermute x46, starting transfers between devices, shifted(): return lax.ppermute(x, axis, [(i, (i + by) % size) for i in range(size)])  59.6 us
    ppermute x14, starting transfers between devices, tick_whole(): lax.ppermute(computed, 'segment', [(i, i + 1) for i in range(segments - 1)])  59.2 us
    ppermute x14, waiting for transfers between devices, tick_whole(): lax.ppermute(computed, 'segment', [(i, i + 1) for i in range(segments - 1)])  51.8 us
    ppermute x14, starting transfers between devices, fsdp_moved(): return lax.ppermute(x, 'fsdp', [(f, mapping(f)) for f in range(16)])  23.2 us
    reduce_sum x14, other arithmetic, tick_whole(): own_squares = jnp.sum(own_wide * own_wide, axis=-1, keepdims=True)  18.4 us
    ppermute x14, waiting for transfers between devices, fsdp_moved(): return lax.ppermute(x, 'fsdp', [(f, mapping(f)) for f in range(16)])  17.9 us
  transfers between devices with their start and end apart: 76, of which 25 were waited for; matrix products, arithmetic and copies ran while one was open for 43% of the time, Pallas kernels for 0%

profile of v4, /device:TPU:0, one launch (start us, length us, event | category | flops | bytes accessed | tf_op | source)
XLA Modules:
  0.0 483.6 jit_solution(16042484993744440340)
XLA Ops:
  8.7 11.9 %dynamic-slice_bitcast_fusion = (bf16[2048,2048]{1,0:T(8,128)(2,1)}, bf16[2048,2048]{1,0:T(8,128)(2,1)}) fusion(bf16[1,4096,2048]{2,1,0:T(8,128)(2,1)} %param.16, s32[]{:T(128)S(6)} %select_n.307, s32[]{:T(128)} %select_n.306), kind=kLoop, calls=%fused_computation.28 | loop fusion | bytes 33554440 | tf_op jit(solution)/shard_map/dynamic_slice | solution.py:132
  27.8 319.6 %while.20 = (s32[]{:T(128)}, bf16[128,2048]{1,0:T(8,128)(2,1)S(1)}, bf16[128,2048]{1,0:T(8,128)(2,1)S(1)}, bf16[1024,2048]{1,0:T(8,128)(2,1)}, pred[]{:T(512)}, ...) while((s32[]{:T(128)}, bf16[128,2048]{1,0:T(8,128)(2,1)S(1)}, ...), condition=%wide.region_4.5_spmd.clone, body=%wide.region_2.4_spmd.clone.sunk | while | flops 2152202496 | bytes 28857752 | solution.py:165
  40.4 6.4 %collective-permute-done = bf16[128,2048]{1,0:T(8,128)(2,1)S(1)} collective-permute-done((bf16[128,2048]{1,0:T(8,128)(2,1)}, bf16[128,2048]{1,0:T(8,128)(2,1)S(1)}, u32[]{:S(2)}, u32[]{:S(2)}) %collective-permute-start) | collective-permute-done | bytes 524320 | tf_op jit(solution)/shard_map/while/body/eval_jaxpr/ppermute | solution.py:144
  46.9 5.8 %select_dynamic-update-slice_fusion.2 = (bf16[1024,2048]{1,0:T(8,128)(2,1)}, bf16[128,2048]{1,0:T(8,128)(2,1)S(1)}) fusion(bf16[1024,2048]{1,0:T(8,128)(2,1)} %get-tuple-element.471, s32[]{:T(128)S(6)} %select_n.388, pred[]{:T(512)S(6)} %and.148, f32[128,2048]{1,0:T(8,128)S(1)} %fusion.76, bf16[2048,2048]{1,0:T(8,128)(2,1)} %get-tuple-element.496, ...), kind=kOutput, calls=%fused_computation.10.clone.1 | convolution fusion | flops 1076101120 | bytes 12067333 | tf_op jit(solution)/shard_map/while/body/eval_jaxpr/dot_general | solution.py:151
  61.4 4.7 fusion.76
  66.0 5.1 %collective-permute-done = bf16[128,2048]{1,0:T(8,128)(2,1)S(1)} collective-permute-done((bf16[128,2048]{1,0:T(8,128)(2,1)}, bf16[128,2048]{1,0:T(8,128)(2,1)S(1)}, u32[]{:S(2)}, u32[]{:S(2)}) %collective-permute-start) | collective-permute-done | bytes 524320 | tf_op jit(solution)/shard_map/while/body/eval_jaxpr/ppermute | solution.py:144
  71.1 5.9 %select_dynamic-update-slice_fusion.2 = (bf16[1024,2048]{1,0:T(8,128)(2,1)}, bf16[128,2048]{1,0:T(8,128)(2,1)S(1)}) fusion(bf16[1024,2048]{1,0:T(8,128)(2,1)} %get-tuple-element.471, s32[]{:T(128)S(6)} %select_n.388, pred[]{:T(512)S(6)} %and.148, f32[128,2048]{1,0:T(8,128)S(1)} %fusion.76, bf16[2048,2048]{1,0:T(8,128)(2,1)} %get-tuple-element.496, ...), kind=kOutput, calls=%fused_computation.10.clone.1 | convolution fusion | flops 1076101120 | bytes 12067333 | tf_op jit(solution)/shard_map/while/body/eval_jaxpr/dot_general | solution.py:151
  85.6 4.7 fusion.76
  93.9 5.8 %select_dynamic-update-slice_fusion.2 = (bf16[1024,2048]{1,0:T(8,128)(2,1)}, bf16[128,2048]{1,0:T(8,128)(2,1)S(1)}) fusion(bf16[1024,2048]{1,0:T(8,128)(2,1)} %get-tuple-element.471, s32[]{:T(128)S(6)} %select_n.388, pred[]{:T(512)S(6)} %and.148, f32[128,2048]{1,0:T(8,128)S(1)} %fusion.76, bf16[2048,2048]{1,0:T(8,128)(2,1)} %get-tuple-element.496, ...), kind=kOutput, calls=%fused_computation.10.clone.1 | convolution fusion | flops 1076101120 | bytes 12067333 | tf_op jit(solution)/shard_map/while/body/eval_jaxpr/dot_general | solution.py:151
  108.3 4.7 fusion.76
  115.5 5.8 %select_dynamic-update-slice_fusion.2 = (bf16[1024,2048]{1,0:T(8,128)(2,1)}, bf16[128,2048]{1,0:T(8,128)(2,1)S(1)}) fusion(bf16[1024,2048]{1,0:T(8,128)(2,1)} %get-tuple-element.471, s32[]{:T(128)S(6)} %select_n.388, pred[]{:T(512)S(6)} %and.148, f32[128,2048]{1,0:T(8,128)S(1)} %fusion.76, bf16[2048,2048]{1,0:T(8,128)(2,1)} %get-tuple-element.496, ...), kind=kOutput, calls=%fused_computation.10.clone.1 | convolution fusion | flops 1076101120 | bytes 12067333 | tf_op jit(solution)/shard_map/while/body/eval_jaxpr/dot_general | solution.py:151
  136.8 5.8 %select_dynamic-update-slice_fusion.2 = (bf16[1024,2048]{1,0:T(8,128)(2,1)}, bf16[128,2048]{1,0:T(8,128)(2,1)S(1)}) fusion(bf16[1024,2048]{1,0:T(8,128)(2,1)} %get-tuple-element.471, s32[]{:T(128)S(6)} %select_n.388, pred[]{:T(512)S(6)} %and.148, f32[128,2048]{1,0:T(8,128)S(1)} %fusion.76, bf16[2048,2048]{1,0:T(8,128)(2,1)} %get-tuple-element.496, ...), kind=kOutput, calls=%fused_computation.10.clone.1 | convolution fusion | flops 1076101120 | bytes 12067333 | tf_op jit(solution)/shard_map/while/body/eval_jaxpr/dot_general | solution.py:151
  151.2 4.7 fusion.76
  158.2 5.8 %select_dynamic-update-slice_fusion.2 = (bf16[1024,2048]{1,0:T(8,128)(2,1)}, bf16[128,2048]{1,0:T(8,128)(2,1)S(1)}) fusion(bf16[1024,2048]{1,0:T(8,128)(2,1)} %get-tuple-element.471, s32[]{:T(128)S(6)} %select_n.388, pred[]{:T(512)S(6)} %and.148, f32[128,2048]{1,0:T(8,128)S(1)} %fusion.76, bf16[2048,2048]{1,0:T(8,128)(2,1)} %get-tuple-element.496, ...), kind=kOutput, calls=%fused_computation.10.clone.1 | convolution fusion | flops 1076101120 | bytes 12067333 | tf_op jit(solution)/shard_map/while/body/eval_jaxpr/dot_general | solution.py:151
  172.6 4.7 fusion.76
  179.5 5.8 %select_dynamic-update-slice_fusion.2 = (bf16[1024,2048]{1,0:T(8,128)(2,1)}, bf16[128,2048]{1,0:T(8,128)(2,1)S(1)}) fusion(bf16[1024,2048]{1,0:T(8,128)(2,1)} %get-tuple-element.471, s32[]{:T(128)S(6)} %select_n.388, pred[]{:T(512)S(6)} %and.148, f32[128,2048]{1,0:T(8,128)S(1)} %fusion.76, bf16[2048,2048]{1,0:T(8,128)(2,1)} %get-tuple-element.496, ...), kind=kOutput, calls=%fused_computation.10.clone.1 | convolution fusion | flops 1076101120 | bytes 12067333 | tf_op jit(solution)/shard_map/while/body/eval_jaxpr/dot_general | solution.py:151
  194.0 4.7 fusion.76
  200.9 5.8 %select_dynamic-update-slice_fusion.2 = (bf16[1024,2048]{1,0:T(8,128)(2,1)}, bf16[128,2048]{1,0:T(8,128)(2,1)S(1)}) fusion(bf16[1024,2048]{1,0:T(8,128)(2,1)} %get-tuple-element.471, s32[]{:T(128)S(6)} %select_n.388, pred[]{:T(512)S(6)} %and.148, f32[128,2048]{1,0:T(8,128)S(1)} %fusion.76, bf16[2048,2048]{1,0:T(8,128)(2,1)} %get-tuple-element.496, ...), kind=kOutput, calls=%fused_computation.10.clone.1 | convolution fusion | flops 1076101120 | bytes 12067333 | tf_op jit(solution)/shard_map/while/body/eval_jaxpr/dot_general | solution.py:151
  222.2 5.8 %select_dynamic-update-slice_fusion.2 = (bf16[1024,2048]{1,0:T(8,128)(2,1)}, bf16[128,2048]{1,0:T(8,128)(2,1)S(1)}) fusion(bf16[1024,2048]{1,0:T(8,128)(2,1)} %get-tuple-element.471, s32[]{:T(128)S(6)} %select_n.388, pred[]{:T(512)S(6)} %and.148, f32[128,2048]{1,0:T(8,128)S(1)} %fusion.76, bf16[2048,2048]{1,0:T(8,128)(2,1)} %get-tuple-element.496, ...), kind=kOutput, calls=%fused_computation.10.clone.1 | convolution fusion | flops 1076101120 | bytes 12067333 | tf_op jit(solution)/shard_map/while/body/eval_jaxpr/dot_general | solution.py:151
  244.0 5.8 %select_dynamic-update-slice_fusion.2 = (bf16[1024,2048]{1,0:T(8,128)(2,1)}, bf16[128,2048]{1,0:T(8,128)(2,1)S(1)}) fusion(bf16[1024,2048]{1,0:T(8,128)(2,1)} %get-tuple-element.471, s32[]{:T(128)S(6)} %select_n.388, pred[]{:T(512)S(6)} %and.148, f32[128,2048]{1,0:T(8,128)S(1)} %fusion.76, bf16[2048,2048]{1,0:T(8,128)(2,1)} %get-tuple-element.496, ...), kind=kOutput, calls=%fused_computation.10.clone.1 | convolution fusion | flops 1076101120 | bytes 12067333 | tf_op jit(solution)/shard_map/while/body/eval_jaxpr/dot_general | solution.py:151
  267.5 5.8 %select_dynamic-update-slice_fusion.2 = (bf16[1024,2048]{1,0:T(8,128)(2,1)}, bf16[128,2048]{1,0:T(8,128)(2,1)S(1)}) fusion(bf16[1024,2048]{1,0:T(8,128)(2,1)} %get-tuple-element.471, s32[]{:T(128)S(6)} %select_n.388, pred[]{:T(512)S(6)} %and.148, f32[128,2048]{1,0:T(8,128)S(1)} %fusion.76, bf16[2048,2048]{1,0:T(8,128)(2,1)} %get-tuple-element.496, ...), kind=kOutput, calls=%fused_computation.10.clone.1 | convolution fusion | flops 1076101120 | bytes 12067333 | tf_op jit(solution)/shard_map/while/body/eval_jaxpr/dot_general | solution.py:151
  286.8 6.1 %collective-permute-done = bf16[128,2048]{1,0:T(8,128)(2,1)S(1)} collective-permute-done((bf16[128,2048]{1,0:T(8,128)(2,1)}, bf16[128,2048]{1,0:T(8,128)(2,1)S(1)}, u32[]{:S(2)}, u32[]{:S(2)}) %collective-permute-start) | collective-permute-done | bytes 524320 | tf_op jit(solution)/shard_map/while/body/eval_jaxpr/ppermute | solution.py:144
  292.9 5.8 %select_dynamic-update-slice_fusion.2 = (bf16[1024,2048]{1,0:T(8,128)(2,1)}, bf16[128,2048]{1,0:T(8,128)(2,1)S(1)}) fusion(bf16[1024,2048]{1,0:T(8,128)(2,1)} %get-tuple-element.471, s32[]{:T(128)S(6)} %select_n.388, pred[]{:T(512)S(6)} %and.148, f32[128,2048]{1,0:T(8,128)S(1)} %fusion.76, bf16[2048,2048]{1,0:T(8,128)(2,1)} %get-tuple-element.496, ...), kind=kOutput, calls=%fused_computation.10.clone.1 | convolution fusion | flops 1076101120 | bytes 12067333 | tf_op jit(solution)/shard_map/while/body/eval_jaxpr/dot_general | solution.py:151
  307.8 4.7 fusion.76
  312.5 7.7 %collective-permute-done = bf16[128,2048]{1,0:T(8,128)(2,1)S(1)} collective-permute-done((bf16[128,2048]{1,0:T(8,128)(2,1)}, bf16[128,2048]{1,0:T(8,128)(2,1)S(1)}, u32[]{:S(2)}, u32[]{:S(2)}) %collective-permute-start) | collective-permute-done | bytes 524320 | tf_op jit(solution)/shard_map/while/body/eval_jaxpr/ppermute | solution.py:144
  320.2 5.8 %select_dynamic-update-slice_fusion.2 = (bf16[1024,2048]{1,0:T(8,128)(2,1)}, bf16[128,2048]{1,0:T(8,128)(2,1)S(1)}) fusion(bf16[1024,2048]{1,0:T(8,128)(2,1)} %get-tuple-element.471, s32[]{:T(128)S(6)} %select_n.388, pred[]{:T(512)S(6)} %and.148, f32[128,2048]{1,0:T(8,128)S(1)} %fusion.76, bf16[2048,2048]{1,0:T(8,128)(2,1)} %get-tuple-element.496, ...), kind=kOutput, calls=%fused_computation.10.clone.1 | convolution fusion | flops 1076101120 | bytes 12067333 | tf_op jit(solution)/shard_map/while/body/eval_jaxpr/dot_general | solution.py:151
  334.7 4.7 fusion.76
  341.6 5.8 %select_dynamic-update-slice_fusion.2 = (bf16[1024,2048]{1,0:T(8,128)(2,1)}, bf16[128,2048]{1,0:T(8,128)(2,1)S(1)}) fusion(bf16[1024,2048]{1,0:T(8,128)(2,1)} %get-tuple-element.471, s32[]{:T(128)S(6)} %select_n.388, pred[]{:T(512)S(6)} %and.148, f32[128,2048]{1,0:T(8,128)S(1)} %fusion.76, bf16[2048,2048]{1,0:T(8,128)(2,1)} %get-tuple-element.496, ...), kind=kOutput, calls=%fused_computation.10.clone.1 | convolution fusion | flops 1076101120 | bytes 12067333 | tf_op jit(solution)/shard_map/while/body/eval_jaxpr/dot_general | solution.py:151
  360.0 8.1 %collective-permute-done.4 = f32[1024,128]{0,1:T(8,128)S(1)} collective-permute-done((f32[1024,128]{0,1:T(8,128)S(1)}, f32[1024,128]{0,1:T(8,128)S(1)}, u32[]{:S(2)}, u32[]{:S(2)}) %collective-permute-start.4) | collective-permute-done | bytes 524320 | tf_op jit(solution)/shard_map/ppermute | solution.py:32
  392.3 5.5 %fusion.24 = f32[4096,256]{1,0:T(8,128)} fusion(bf16[128,4096]{1,0:T(8,128)(2,1)} %copy-done.1, bf16[4096,256]{1,0:T(8,128)(2,1)} %all-gather.5.cloned.1.call-done, f32[128,4096]{1,0:T(8,128)S(1)} %get-tuple-element.362, f32[128]{0:T(128)S(1)} %add_rsqrt_fusion.2), kind=kOutput, calls=%fused_computation.52 | convolution fusion | flops 537952256 | bytes 9437696 | tf_op jit(solution)/shard_map/dot_general | solution.py:237
  397.8 4.8 fusion.18
  402.6 7.5 %collective-permute-done.8 = f32[2,4,4,2,2,32,256]{6,5,4,3,2,1,0:T(8,128)} collective-permute-done((f32[2,4,4,2,2,32,256]{6,5,4,3,2,1,0:T(8,128)}, f32[2,4,4,2,2,32,256]{6,5,4,3,2,1,0:T(8,128)}, u32[]{:S(2)}, u32[]{:S(2)}) %collective-permute-start.8) | collective-permute-done | bytes 4194336 | tf_op jit(solution)/shard_map/ppermute | solution.py:36
  (298 shorter events, 282.8 us)
Async XLA Ops:
  7.2 372.0 %all-gather.3.cloned.1.call-start = ((), (), s32[]{:S(2)}) async-start(), calls=%async_computation | async-start | bytes 2228224 | tf_op jit(solution)/shard_map/all_gather | solution.py:125
  7.9 373.4 %all-gather.5.cloned.1.call-start = ((), (), s32[]{:S(2)}) async-start(), calls=%async_computation.1 | async-start | bytes 2228224 | tf_op jit(solution)/shard_map/all_gather | solution.py:126
  31.3 15.6 %collective-permute-start.2 = (bf16[128,2048]{1,0:T(8,128)(2,1)S(1)}, bf16[128,2048]{1,0:T(8,128)(2,1)S(1)}, u32[]{:S(2)}, u32[]{:S(2)}) collective-permute-start(bf16[128,2048]{1,0:T(8,128)(2,1)S(1)} %get-tuple-element.446), channel_id=1, source_target_pairs={{0,1},{1,0},{2,3},{3,2},{4,5},{5,4},{6,7},{7,6},{8,9},{9,8},{10,11... | collective-permute-start | bytes 1572872 | tf_op jit(solution)/shard_map/while/body/eval_jaxpr/ppermute | solution.py:32
  32.3 14.6 %collective-permute-start = (bf16[128,2048]{1,0:T(8,128)(2,1)}, bf16[128,2048]{1,0:T(8,128)(2,1)S(1)}, u32[]{:S(2)}, u32[]{:S(2)}) collective-permute-start(bf16[128,2048]{1,0:T(8,128)(2,1)} %broadcast_select_fusion.5), channel_id=1, source_target_pairs={{0,32},{32,64},{64,96},{1,33},{33,65},{65,97},{2,34},{34,66},{66,9... | collective-permute-start | bytes 1572872 | tf_op jit(solution)/shard_map/while/body/eval_jaxpr/ppermute | solution.py:144
  55.7 15.4 %collective-permute-start.2 = (bf16[128,2048]{1,0:T(8,128)(2,1)S(1)}, bf16[128,2048]{1,0:T(8,128)(2,1)S(1)}, u32[]{:S(2)}, u32[]{:S(2)}) collective-permute-start(bf16[128,2048]{1,0:T(8,128)(2,1)S(1)} %get-tuple-element.446), channel_id=1, source_target_pairs={{0,1},{1,0},{2,3},{3,2},{4,5},{5,4},{6,7},{7,6},{8,9},{9,8},{10,11... | collective-permute-start | bytes 1572872 | tf_op jit(solution)/shard_map/while/body/eval_jaxpr/ppermute | solution.py:32
  57.0 14.1 %collective-permute-start = (bf16[128,2048]{1,0:T(8,128)(2,1)}, bf16[128,2048]{1,0:T(8,128)(2,1)S(1)}, u32[]{:S(2)}, u32[]{:S(2)}) collective-permute-start(bf16[128,2048]{1,0:T(8,128)(2,1)} %broadcast_select_fusion.5), channel_id=1, source_target_pairs={{0,32},{32,64},{64,96},{1,33},{33,65},{65,97},{2,34},{34,66},{66,9... | collective-permute-start | bytes 1572872 | tf_op jit(solution)/shard_map/while/body/eval_jaxpr/ppermute | solution.py:144
  79.8 14.1 %collective-permute-start.2 = (bf16[128,2048]{1,0:T(8,128)(2,1)S(1)}, bf16[128,2048]{1,0:T(8,128)(2,1)S(1)}, u32[]{:S(2)}, u32[]{:S(2)}) collective-permute-start(bf16[128,2048]{1,0:T(8,128)(2,1)S(1)} %get-tuple-element.446), channel_id=1, source_target_pairs={{0,1},{1,0},{2,3},{3,2},{4,5},{5,4},{6,7},{7,6},{8,9},{9,8},{10,11... | collective-permute-start | bytes 1572872 | tf_op jit(solution)/shard_map/while/body/eval_jaxpr/ppermute | solution.py:32
  81.3 12.6 %collective-permute-start = (bf16[128,2048]{1,0:T(8,128)(2,1)}, bf16[128,2048]{1,0:T(8,128)(2,1)S(1)}, u32[]{:S(2)}, u32[]{:S(2)}) collective-permute-start(bf16[128,2048]{1,0:T(8,128)(2,1)} %broadcast_select_fusion.5), channel_id=1, source_target_pairs={{0,32},{32,64},{64,96},{1,33},{33,65},{65,97},{2,34},{34,66},{66,9... | collective-permute-start | bytes 1572872 | tf_op jit(solution)/shard_map/while/body/eval_jaxpr/ppermute | solution.py:144
  102.2 13.3 %collective-permute-start.2 = (bf16[128,2048]{1,0:T(8,128)(2,1)S(1)}, bf16[128,2048]{1,0:T(8,128)(2,1)S(1)}, u32[]{:S(2)}, u32[]{:S(2)}) collective-permute-start(bf16[128,2048]{1,0:T(8,128)(2,1)S(1)} %get-tuple-element.446), channel_id=1, source_target_pairs={{0,1},{1,0},{2,3},{3,2},{4,5},{5,4},{6,7},{7,6},{8,9},{9,8},{10,11... | collective-permute-start | bytes 1572872 | tf_op jit(solution)/shard_map/while/body/eval_jaxpr/ppermute | solution.py:32
  104.0 11.5 %collective-permute-start = (bf16[128,2048]{1,0:T(8,128)(2,1)}, bf16[128,2048]{1,0:T(8,128)(2,1)S(1)}, u32[]{:S(2)}, u32[]{:S(2)}) collective-permute-start(bf16[128,2048]{1,0:T(8,128)(2,1)} %broadcast_select_fusion.5), channel_id=1, source_target_pairs={{0,32},{32,64},{64,96},{1,33},{33,65},{65,97},{2,34},{34,66},{66,9... | collective-permute-start | bytes 1572872 | tf_op jit(solution)/shard_map/while/body/eval_jaxpr/ppermute | solution.py:144
  123.6 13.3 %collective-permute-start.2 = (bf16[128,2048]{1,0:T(8,128)(2,1)S(1)}, bf16[128,2048]{1,0:T(8,128)(2,1)S(1)}, u32[]{:S(2)}, u32[]{:S(2)}) collective-permute-start(bf16[128,2048]{1,0:T(8,128)(2,1)S(1)} %get-tuple-element.446), channel_id=1, source_target_pairs={{0,1},{1,0},{2,3},{3,2},{4,5},{5,4},{6,7},{7,6},{8,9},{9,8},{10,11... | collective-permute-start | bytes 1572872 | tf_op jit(solution)/shard_map/while/body/eval_jaxpr/ppermute | solution.py:32
  125.6 11.3 %collective-permute-start = (bf16[128,2048]{1,0:T(8,128)(2,1)}, bf16[128,2048]{1,0:T(8,128)(2,1)S(1)}, u32[]{:S(2)}, u32[]{:S(2)}) collective-permute-start(bf16[128,2048]{1,0:T(8,128)(2,1)} %broadcast_select_fusion.5), channel_id=1, source_target_pairs={{0,32},{32,64},{64,96},{1,33},{33,65},{65,97},{2,34},{34,66},{66,9... | collective-permute-start | bytes 1572872 | tf_op jit(solution)/shard_map/while/body/eval_jaxpr/ppermute | solution.py:144
  144.9 13.2 %collective-permute-start.2 = (bf16[128,2048]{1,0:T(8,128)(2,1)S(1)}, bf16[128,2048]{1,0:T(8,128)(2,1)S(1)}, u32[]{:S(2)}, u32[]{:S(2)}) collective-permute-start(bf16[128,2048]{1,0:T(8,128)(2,1)S(1)} %get-tuple-element.446), channel_id=1, source_target_pairs={{0,1},{1,0},{2,3},{3,2},{4,5},{5,4},{6,7},{7,6},{8,9},{9,8},{10,11... | collective-permute-start | bytes 1572872 | tf_op jit(solution)/shard_map/while/body/eval_jaxpr/ppermute | solution.py:32
  146.9 11.3 %collective-permute-start = (bf16[128,2048]{1,0:T(8,128)(2,1)}, bf16[128,2048]{1,0:T(8,128)(2,1)S(1)}, u32[]{:S(2)}, u32[]{:S(2)}) collective-permute-start(bf16[128,2048]{1,0:T(8,128)(2,1)} %broadcast_select_fusion.5), channel_id=1, source_target_pairs={{0,32},{32,64},{64,96},{1,33},{33,65},{65,97},{2,34},{34,66},{66,9... | collective-permute-start | bytes 1572872 | tf_op jit(solution)/shard_map/while/body/eval_jaxpr/ppermute | solution.py:144
  166.2 13.3 %collective-permute-start.2 = (bf16[128,2048]{1,0:T(8,128)(2,1)S(1)}, bf16[128,2048]{1,0:T(8,128)(2,1)S(1)}, u32[]{:S(2)}, u32[]{:S(2)}) collective-permute-start(bf16[128,2048]{1,0:T(8,128)(2,1)S(1)} %get-tuple-element.446), channel_id=1, source_target_pairs={{0,1},{1,0},{2,3},{3,2},{4,5},{5,4},{6,7},{7,6},{8,9},{9,8},{10,11... | collective-permute-start | bytes 1572872 | tf_op jit(solution)/shard_map/while/body/eval_jaxpr/ppermute | solution.py:32
  168.2 11.3 %collective-permute-start = (bf16[128,2048]{1,0:T(8,128)(2,1)}, bf16[128,2048]{1,0:T(8,128)(2,1)S(1)}, u32[]{:S(2)}, u32[]{:S(2)}) collective-permute-start(bf16[128,2048]{1,0:T(8,128)(2,1)} %broadcast_select_fusion.5), channel_id=1, source_target_pairs={{0,32},{32,64},{64,96},{1,33},{33,65},{65,97},{2,34},{34,66},{66,9... | collective-permute-start | bytes 1572872 | tf_op jit(solution)/shard_map/while/body/eval_jaxpr/ppermute | solution.py:144
  187.6 13.3 %collective-permute-start.2 = (bf16[128,2048]{1,0:T(8,128)(2,1)S(1)}, bf16[128,2048]{1,0:T(8,128)(2,1)S(1)}, u32[]{:S(2)}, u32[]{:S(2)}) collective-permute-start(bf16[128,2048]{1,0:T(8,128)(2,1)S(1)} %get-tuple-element.446), channel_id=1, source_target_pairs={{0,1},{1,0},{2,3},{3,2},{4,5},{5,4},{6,7},{7,6},{8,9},{9,8},{10,11... | collective-permute-start | bytes 1572872 | tf_op jit(solution)/shard_map/while/body/eval_jaxpr/ppermute | solution.py:32
  189.6 11.3 %collective-permute-start = (bf16[128,2048]{1,0:T(8,128)(2,1)}, bf16[128,2048]{1,0:T(8,128)(2,1)S(1)}, u32[]{:S(2)}, u32[]{:S(2)}) collective-permute-start(bf16[128,2048]{1,0:T(8,128)(2,1)} %broadcast_select_fusion.5), channel_id=1, source_target_pairs={{0,32},{32,64},{64,96},{1,33},{33,65},{65,97},{2,34},{34,66},{66,9... | collective-permute-start | bytes 1572872 | tf_op jit(solution)/shard_map/while/body/eval_jaxpr/ppermute | solution.py:144
  209.0 13.2 %collective-permute-start.2 = (bf16[128,2048]{1,0:T(8,128)(2,1)S(1)}, bf16[128,2048]{1,0:T(8,128)(2,1)S(1)}, u32[]{:S(2)}, u32[]{:S(2)}) collective-permute-start(bf16[128,2048]{1,0:T(8,128)(2,1)S(1)} %get-tuple-element.446), channel_id=1, source_target_pairs={{0,1},{1,0},{2,3},{3,2},{4,5},{5,4},{6,7},{7,6},{8,9},{9,8},{10,11... | collective-permute-start | bytes 1572872 | tf_op jit(solution)/shard_map/while/body/eval_jaxpr/ppermute | solution.py:32
  211.0 11.2 %collective-permute-start = (bf16[128,2048]{1,0:T(8,128)(2,1)}, bf16[128,2048]{1,0:T(8,128)(2,1)S(1)}, u32[]{:S(2)}, u32[]{:S(2)}) collective-permute-start(bf16[128,2048]{1,0:T(8,128)(2,1)} %broadcast_select_fusion.5), channel_id=1, source_target_pairs={{0,32},{32,64},{64,96},{1,33},{33,65},{65,97},{2,34},{34,66},{66,9... | collective-permute-start | bytes 1572872 | tf_op jit(solution)/shard_map/while/body/eval_jaxpr/ppermute | solution.py:144
  230.4 13.6 %collective-permute-start.2 = (bf16[128,2048]{1,0:T(8,128)(2,1)S(1)}, bf16[128,2048]{1,0:T(8,128)(2,1)S(1)}, u32[]{:S(2)}, u32[]{:S(2)}) collective-permute-start(bf16[128,2048]{1,0:T(8,128)(2,1)S(1)} %get-tuple-element.446), channel_id=1, source_target_pairs={{0,1},{1,0},{2,3},{3,2},{4,5},{5,4},{6,7},{7,6},{8,9},{9,8},{10,11... | collective-permute-start | bytes 1572872 | tf_op jit(solution)/shard_map/while/body/eval_jaxpr/ppermute | solution.py:32
  232.4 11.6 %collective-permute-start = (bf16[128,2048]{1,0:T(8,128)(2,1)}, bf16[128,2048]{1,0:T(8,128)(2,1)S(1)}, u32[]{:S(2)}, u32[]{:S(2)}) collective-permute-start(bf16[128,2048]{1,0:T(8,128)(2,1)} %broadcast_select_fusion.5), channel_id=1, source_target_pairs={{0,32},{32,64},{64,96},{1,33},{33,65},{65,97},{2,34},{34,66},{66,9... | collective-permute-start | bytes 1572872 | tf_op jit(solution)/shard_map/while/body/eval_jaxpr/ppermute | solution.py:144
  252.7 14.8 %collective-permute-start.2 = (bf16[128,2048]{1,0:T(8,128)(2,1)S(1)}, bf16[128,2048]{1,0:T(8,128)(2,1)S(1)}, u32[]{:S(2)}, u32[]{:S(2)}) collective-permute-start(bf16[128,2048]{1,0:T(8,128)(2,1)S(1)} %get-tuple-element.446), channel_id=1, source_target_pairs={{0,1},{1,0},{2,3},{3,2},{4,5},{5,4},{6,7},{7,6},{8,9},{9,8},{10,11... | collective-permute-start | bytes 1572872 | tf_op jit(solution)/shard_map/while/body/eval_jaxpr/ppermute | solution.py:32
  254.1 13.4 %collective-permute-start = (bf16[128,2048]{1,0:T(8,128)(2,1)}, bf16[128,2048]{1,0:T(8,128)(2,1)S(1)}, u32[]{:S(2)}, u32[]{:S(2)}) collective-permute-start(bf16[128,2048]{1,0:T(8,128)(2,1)} %broadcast_select_fusion.5), channel_id=1, source_target_pairs={{0,32},{32,64},{64,96},{1,33},{33,65},{65,97},{2,34},{34,66},{66,9... | collective-permute-start | bytes 1572872 | tf_op jit(solution)/shard_map/while/body/eval_jaxpr/ppermute | solution.py:144
  276.7 16.2 %collective-permute-start.2 = (bf16[128,2048]{1,0:T(8,128)(2,1)S(1)}, bf16[128,2048]{1,0:T(8,128)(2,1)S(1)}, u32[]{:S(2)}, u32[]{:S(2)}) collective-permute-start(bf16[128,2048]{1,0:T(8,128)(2,1)S(1)} %get-tuple-element.446), channel_id=1, source_target_pairs={{0,1},{1,0},{2,3},{3,2},{4,5},{5,4},{6,7},{7,6},{8,9},{9,8},{10,11... | collective-permute-start | bytes 1572872 | tf_op jit(solution)/shard_map/while/body/eval_jaxpr/ppermute | solution.py:32
  277.7 15.2 %collective-permute-start = (bf16[128,2048]{1,0:T(8,128)(2,1)}, bf16[128,2048]{1,0:T(8,128)(2,1)S(1)}, u32[]{:S(2)}, u32[]{:S(2)}) collective-permute-start(bf16[128,2048]{1,0:T(8,128)(2,1)} %broadcast_select_fusion.5), channel_id=1, source_target_pairs={{0,32},{32,64},{64,96},{1,33},{33,65},{65,97},{2,34},{34,66},{66,9... | collective-permute-start | bytes 1572872 | tf_op jit(solution)/shard_map/while/body/eval_jaxpr/ppermute | solution.py:144
  302.5 17.7 %collective-permute-start.2 = (bf16[128,2048]{1,0:T(8,128)(2,1)S(1)}, bf16[128,2048]{1,0:T(8,128)(2,1)S(1)}, u32[]{:S(2)}, u32[]{:S(2)}) collective-permute-start(bf16[128,2048]{1,0:T(8,128)(2,1)S(1)} %get-tuple-element.446), channel_id=1, source_target_pairs={{0,1},{1,0},{2,3},{3,2},{4,5},{5,4},{6,7},{7,6},{8,9},{9,8},{10,11... | collective-permute-start | bytes 1572872 | tf_op jit(solution)/shard_map/while/body/eval_jaxpr/ppermute | solution.py:32
  303.5 16.7 %collective-permute-start = (bf16[128,2048]{1,0:T(8,128)(2,1)}, bf16[128,2048]{1,0:T(8,128)(2,1)S(1)}, u32[]{:S(2)}, u32[]{:S(2)}) collective-permute-start(bf16[128,2048]{1,0:T(8,128)(2,1)} %broadcast_select_fusion.5), channel_id=1, source_target_pairs={{0,32},{32,64},{64,96},{1,33},{33,65},{65,97},{2,34},{34,66},{66,9... | collective-permute-start | bytes 1572872 | tf_op jit(solution)/shard_map/while/body/eval_jaxpr/ppermute | solution.py:144
  329.1 12.5 %collective-permute-start.2 = (bf16[128,2048]{1,0:T(8,128)(2,1)S(1)}, bf16[128,2048]{1,0:T(8,128)(2,1)S(1)}, u32[]{:S(2)}, u32[]{:S(2)}) collective-permute-start(bf16[128,2048]{1,0:T(8,128)(2,1)S(1)} %get-tuple-element.446), channel_id=1, source_target_pairs={{0,1},{1,0},{2,3},{3,2},{4,5},{5,4},{6,7},{7,6},{8,9},{9,8},{10,11... | collective-permute-start | bytes 1572872 | tf_op jit(solution)/shard_map/while/body/eval_jaxpr/ppermute | solution.py:32
  330.4 11.3 %collective-permute-start = (bf16[128,2048]{1,0:T(8,128)(2,1)}, bf16[128,2048]{1,0:T(8,128)(2,1)S(1)}, u32[]{:S(2)}, u32[]{:S(2)}) collective-permute-start(bf16[128,2048]{1,0:T(8,128)(2,1)} %broadcast_select_fusion.5), channel_id=1, source_target_pairs={{0,32},{32,64},{64,96},{1,33},{33,65},{65,97},{2,34},{34,66},{66,9... | collective-permute-start | bytes 1572872 | tf_op jit(solution)/shard_map/while/body/eval_jaxpr/ppermute | solution.py:144
  415.3 9.7 %collective-permute-start.21 = (f32[4,2,2,32,128]{4,3,2,1,0:T(8,128)S(1)}, f32[4,2,2,32,128]{4,3,2,1,0:T(8,128)S(1)}, u32[]{:S(2)}, u32[]{:S(2)}) collective-permute-start(f32[4,2,2,32,128]{4,3,2,1,0:T(8,128)S(1)} %dynamic-slice_bitcast_fusion.3), channel_id=1, source_target_pairs={{0,8},{2,10},{4,12},{6,14},{8,16},{10,18},{12,20},{14,22},{16,24},... | collective-permute-start | bytes 786440 | tf_op jit(solution)/shard_map/ppermute | solution.py:36
  419.1 9.5 %collective-permute-start.15 = (f32[4,2,2,32,128]{4,3,2,1,0:T(8,128)S(1)}, f32[4,2,2,32,128]{4,3,2,1,0:T(8,128)S(1)}, u32[]{:S(2)}, u32[]{:S(2)}) collective-permute-start(f32[4,2,2,32,128]{4,3,2,1,0:T(8,128)S(1)} %dynamic-slice_bitcast_fusion.4), channel_id=1, source_target_pairs={{0,96},{32,0},{64,32},{96,64},{1,97},{33,1},{65,33},{97,65},{2,98}... | collective-permute-start | bytes 786440 | tf_op jit(solution)/shard_map/ppermute | solution.py:32
  (53 other events, 377.0 us)
Sparse Core Ops, SparseCore 0:
  10.4 51.1 all-gather.2
  64.0 47.0 all-gather.4

commit v5 on v2

--- a/solution.py
+++ b/solution.py
@@ -69,20 +69,31 @@
     along_core = lambda v: fsdp_moved(v, lambda g: g ^ 1)
     along_zh = lambda v: fsdp_moved(v, lambda g: g ^ 2)
     along_zl = lambda v: shifted(v, "rep", 2, 1)
+    x_near = lambda v: lax.ppermute(v, "segment", [(i, i ^ 1) for i in range(4)])
+    x_far = lambda v: lax.ppermute(v, "segment", [(i, i ^ 2) for i in range(4)])
+    y_near = lambda v: fsdp_moved(v, lambda g: g ^ 4)
+    y_far = lambda v: fsdp_moved(v, lambda g: g ^ 8)
+    both = jnp.stack([first, second]).reshape(2, 4, 4, 2, 2, 2, rows // 128, cols)
+    both = pair_scatter(both, 4, core_pos, along_core)
     outs = []
-    for grad, order in ((first, 0), (second, 1)):
-        blocks = grad.reshape(4, 4, 2, 2, 2, rows // 128, cols)
-        blocks = pair_scatter(blocks, 3, core_pos, along_core)
+    for order in (0, 1):
+        blocks = both[order]
         if order == 0:
             blocks = ring_scatter(blocks, seg, 4, along_x)
-            blocks = ring_scatter(blocks, y_pos, 4, along_y)
+            blocks = blocks.reshape((2, 2) + blocks.shape[1:])
+            blocks = pair_scatter(blocks, 1, y_pos % 2, y_near)
+            blocks = pair_scatter(blocks, 0, y_pos // 2, y_far)
         else:
             blocks = jnp.swapaxes(blocks, 0, 1)
             blocks = ring_scatter(blocks, y_pos, 4, along_y)
-            blocks = ring_scatter(blocks, seg, 4, along_x)
+            blocks = blocks.reshape((2, 2) + blocks.shape[1:])
+            blocks = pair_scatter(blocks, 1, seg % 2, x_near)
+            blocks = pair_scatter(blocks, 0, seg // 2, x_far)
         outs.append(blocks)
-    outs = [pair_scatter(b, 1, rep, along_zl) for b in outs]
-    outs = [pair_scatter(b, 0, zh_pos, along_zh) for b in outs]
+    both = jnp.stack(outs)
+    both = pair_scatter(both, 2, rep, along_zl)
+    both = pair_scatter(both, 1, zh_pos, along_zh)
+    outs = [both[0], both[1]]
     return outs
 
 

time: 471 us -> 477 us (1.013)
  waiting for transfers between devices: 122 us -> 147 us
  starting transfers between devices: 111 us -> 91.7 us
    ppermute x16 -> x10, starting transfers between devices: 27.5 us -> 13.5 us  [fsdp_moved(): return lax.ppermute(x, 'fsdp', [(f, mapping(f)) for f in range(16)])]
    ppermute x16 -> x10, waiting for transfers between devices: 9.86 us -> 20.3 us  [fsdp_moved(): return lax.ppermute(x, 'fsdp', [(f, mapping(f)) for f in range(16)])]
    ppermute x33 -> x26, waiting for transfers between devices: 111 us -> 119 us  [shifted(): return lax.ppermute(x, axis, [(i, (i + by) % size) for i in range(size)])]
    ppermute x0 -> x2, waiting for transfers between devices: none -> 6.2 us  [the longest x1 3.7 us: gradient_scatter(): lax.ppermute(v, 'segment', [(i, i ^ 1) for i in range(4)])]
    ppermute x33 -> x26, starting transfers between devices: 33.6 us -> 27.8 us  [shifted(): return lax.ppermute(x, axis, [(i, (i + by) % size) for i in range(size)])]
  transfers between devices with their start and end apart: 65 -> 54, of which waited for: 28 -> 30; matrix products, arithmetic and copies ran while one was open for 44% -> 41% of each run, Pallas kernels for 0% -> 0%
where the time goes in v5:
time: 477 us; the launch traced here: 475 us
  matrix products  156 us (33%)
  waiting for transfers between devices  147 us (31%)
  starting transfers between devices  91.7 us (19%)
  other arithmetic  53.5 us (11%)
  between operations  17.9 us (4%)
  local copies, waits for them, and re-layouts  7.92 us (2%)
    dot_general x14, matrix products, apply_segment(): update = jnp.dot(normed, weight_local, preferred_element_type=jnp.float32)  132 us
    ppermute x26, waiting for transfers between devices, shifted(): return lax.ppermute(x, axis, [(i, (i + by) % size) for i in range(size)])  119 us
    ppermute x14, starting transfers between devices, tick_whole(): lax.ppermute(computed, 'segment', [(i, i + 1) for i in range(segments - 1)])  47.4 us
    ppermute x26, starting transfers between devices, shifted(): return lax.ppermute(x, axis, [(i, (i + by) % size) for i in range(size)])  27.8 us
    reduce_sum x14, other arithmetic, rms_scale(): squares = jnp.mean(values * values, axis=-1, keepdims=True)  23.3 us
    ppermute x10, waiting for transfers between devices, fsdp_moved(): return lax.ppermute(x, 'fsdp', [(f, mapping(f)) for f in range(16)])  20.3 us
    while x14, other arithmetic  14.1 us
    ppermute x10, starting transfers between devices, fsdp_moved(): return lax.ppermute(x, 'fsdp', [(f, mapping(f)) for f in range(16)])  13.5 us
  transfers between devices with their start and end apart: 54, of which 30 were waited for; matrix products, arithmetic and copies ran while one was open for 41% of the time, Pallas kernels for 0%

profile of v5, /device:TPU:0, one launch (start us, length us, event | category | flops | bytes accessed | tf_op | source)
XLA Modules:
  0.0 475.1 jit_solution(8743954772559637617)
XLA Ops:
  8.7 6.3 %convolution_convert_fusion = bf16[1024,4096]{1,0:T(8,128)(2,1)} fusion(bf16[128,4096]{1,0:T(8,128)(2,1)S(1)} %copy-done, s32[1024]{0:T(1024)} %bitcast.136), kind=kOutput, calls=%fused_computation.22 | convolution fusion | flops 1078067200 | bytes 9441280 | tf_op jit(solution)/shard_map/dot_general | solution.py:22
  17.6 328.1 %while.20 = (s32[]{:T(128)}, bf16[128,2048]{1,0:T(8,128)(2,1)S(1)}, bf16[128,2048]{1,0:T(8,128)(2,1)}, bf16[1024,2048]{1,0:T(8,128)(2,1)}, pred[]{:T(512)}, /*in...) while((s32[]{:T(128)}, bf16[128,2048]{1,0:T(8,128)(2,1)S(1)}, ...), condition=%wide.region_4.5_spmd.clone, body=%wide.region_2.4_spmd.clone.sunk | while | flops 2154823936 | bytes 34098032 | solution.py:169
  23.2 9.8 %collective-permute-done.1 = bf16[128,2048]{1,0:T(8,128)(2,1)S(1)} collective-permute-done((bf16[128,2048]{1,0:T(8,128)(2,1)S(1)}, bf16[128,2048]{1,0:T(8,128)(2,1)S(1)}, u32[]{:S(2)}, u32[]{:S(2)}) %collective-permute-start.1) | collective-permute-done | bytes 524320 | tf_op jit(solution)/shard_map/while/body/eval_jaxpr/ppermute | solution.py:32
  34.8 9.4 %select_dynamic-update-slice_fusion.2 = (bf16[1024,2048]{1,0:T(8,128)(2,1)}, bf16[128,2048]{1,0:T(8,128)(2,1)}) fusion(bf16[1024,2048]{1,0:T(8,128)(2,1)} %get-tuple-element.478, s32[]{:T(128)S(6)} %select_n.433, pred[]{:T(512)S(6)} %and.152, bf16[4096,2048]{1,0:T(8,128)(2,1)} %get-tuple-element.503, f32[128,4096]{1,0:T(8,128)S(1)} %get-tuple-element.453, ...), kind=kOutput, calls=%fused_computation.8.clone.1 | convolution fusion | flops 2149842944 | bytes 21513220 | tf_op jit(solution)/shard_map/while/body/eval_jaxpr/dot_general | solution.py:140
  50.6 12.1 %collective-permute-done.1 = bf16[128,2048]{1,0:T(8,128)(2,1)S(1)} collective-permute-done((bf16[128,2048]{1,0:T(8,128)(2,1)S(1)}, bf16[128,2048]{1,0:T(8,128)(2,1)S(1)}, u32[]{:S(2)}, u32[]{:S(2)}) %collective-permute-start.1) | collective-permute-done | bytes 524320 | tf_op jit(solution)/shard_map/while/body/eval_jaxpr/ppermute | solution.py:32
  64.4 9.4 %select_dynamic-update-slice_fusion.2 = (bf16[1024,2048]{1,0:T(8,128)(2,1)}, bf16[128,2048]{1,0:T(8,128)(2,1)}) fusion(bf16[1024,2048]{1,0:T(8,128)(2,1)} %get-tuple-element.478, s32[]{:T(128)S(6)} %select_n.433, pred[]{:T(512)S(6)} %and.152, bf16[4096,2048]{1,0:T(8,128)(2,1)} %get-tuple-element.503, f32[128,4096]{1,0:T(8,128)S(1)} %get-tuple-element.453, ...), kind=kOutput, calls=%fused_computation.8.clone.1 | convolution fusion | flops 2149842944 | bytes 21513220 | tf_op jit(solution)/shard_map/while/body/eval_jaxpr/dot_general | solution.py:140
  79.1 9.7 %collective-permute-done.1 = bf16[128,2048]{1,0:T(8,128)(2,1)S(1)} collective-permute-done((bf16[128,2048]{1,0:T(8,128)(2,1)S(1)}, bf16[128,2048]{1,0:T(8,128)(2,1)S(1)}, u32[]{:S(2)}, u32[]{:S(2)}) %collective-permute-start.1) | collective-permute-done | bytes 524320 | tf_op jit(solution)/shard_map/while/body/eval_jaxpr/ppermute | solution.py:32
  90.5 9.4 %select_dynamic-update-slice_fusion.2 = (bf16[1024,2048]{1,0:T(8,128)(2,1)}, bf16[128,2048]{1,0:T(8,128)(2,1)}) fusion(bf16[1024,2048]{1,0:T(8,128)(2,1)} %get-tuple-element.478, s32[]{:T(128)S(6)} %select_n.433, pred[]{:T(512)S(6)} %and.152, bf16[4096,2048]{1,0:T(8,128)(2,1)} %get-tuple-element.503, f32[128,4096]{1,0:T(8,128)S(1)} %get-tuple-element.453, ...), kind=kOutput, calls=%fused_computation.8.clone.1 | convolution fusion | flops 2149842944 | bytes 21513220 | tf_op jit(solution)/shard_map/while/body/eval_jaxpr/dot_general | solution.py:140
  105.2 12.7 %collective-permute-done.1 = bf16[128,2048]{1,0:T(8,128)(2,1)S(1)} collective-permute-done((bf16[128,2048]{1,0:T(8,128)(2,1)S(1)}, bf16[128,2048]{1,0:T(8,128)(2,1)S(1)}, u32[]{:S(2)}, u32[]{:S(2)}) %collective-permute-start.1) | collective-permute-done | bytes 524320 | tf_op jit(solution)/shard_map/while/body/eval_jaxpr/ppermute | solution.py:32
  119.6 9.4 %select_dynamic-update-slice_fusion.2 = (bf16[1024,2048]{1,0:T(8,128)(2,1)}, bf16[128,2048]{1,0:T(8,128)(2,1)}) fusion(bf16[1024,2048]{1,0:T(8,128)(2,1)} %get-tuple-element.478, s32[]{:T(128)S(6)} %select_n.433, pred[]{:T(512)S(6)} %and.152, bf16[4096,2048]{1,0:T(8,128)(2,1)} %get-tuple-element.503, f32[128,4096]{1,0:T(8,128)S(1)} %get-tuple-element.453, ...), kind=kOutput, calls=%fused_computation.8.clone.1 | convolution fusion | flops 2149842944 | bytes 21513220 | tf_op jit(solution)/shard_map/while/body/eval_jaxpr/dot_general | solution.py:140
  134.2 8.2 %collective-permute-done.1 = bf16[128,2048]{1,0:T(8,128)(2,1)S(1)} collective-permute-done((bf16[128,2048]{1,0:T(8,128)(2,1)S(1)}, bf16[128,2048]{1,0:T(8,128)(2,1)S(1)}, u32[]{:S(2)}, u32[]{:S(2)}) %collective-permute-start.1) | collective-permute-done | bytes 524320 | tf_op jit(solution)/shard_map/while/body/eval_jaxpr/ppermute | solution.py:32
  144.1 9.4 %select_dynamic-update-slice_fusion.2 = (bf16[1024,2048]{1,0:T(8,128)(2,1)}, bf16[128,2048]{1,0:T(8,128)(2,1)}) fusion(bf16[1024,2048]{1,0:T(8,128)(2,1)} %get-tuple-element.478, s32[]{:T(128)S(6)} %select_n.433, pred[]{:T(512)S(6)} %and.152, bf16[4096,2048]{1,0:T(8,128)(2,1)} %get-tuple-element.503, f32[128,4096]{1,0:T(8,128)S(1)} %get-tuple-element.453, ...), kind=kOutput, calls=%fused_computation.8.clone.1 | convolution fusion | flops 2149842944 | bytes 21513220 | tf_op jit(solution)/shard_map/while/body/eval_jaxpr/dot_general | solution.py:140
  158.7 7.4 %collective-permute-done.1 = bf16[128,2048]{1,0:T(8,128)(2,1)S(1)} collective-permute-done((bf16[128,2048]{1,0:T(8,128)(2,1)S(1)}, bf16[128,2048]{1,0:T(8,128)(2,1)S(1)}, u32[]{:S(2)}, u32[]{:S(2)}) %collective-permute-start.1) | collective-permute-done | bytes 524320 | tf_op jit(solution)/shard_map/while/body/eval_jaxpr/ppermute | solution.py:32
  167.9 9.4 %select_dynamic-update-slice_fusion.2 = (bf16[1024,2048]{1,0:T(8,128)(2,1)}, bf16[128,2048]{1,0:T(8,128)(2,1)}) fusion(bf16[1024,2048]{1,0:T(8,128)(2,1)} %get-tuple-element.478, s32[]{:T(128)S(6)} %select_n.433, pred[]{:T(512)S(6)} %and.152, bf16[4096,2048]{1,0:T(8,128)(2,1)} %get-tuple-element.503, f32[128,4096]{1,0:T(8,128)S(1)} %get-tuple-element.453, ...), kind=kOutput, calls=%fused_computation.8.clone.1 | convolution fusion | flops 2149842944 | bytes 21513220 | tf_op jit(solution)/shard_map/while/body/eval_jaxpr/dot_general | solution.py:140
  182.4 6.6 %collective-permute-done.1 = bf16[128,2048]{1,0:T(8,128)(2,1)S(1)} collective-permute-done((bf16[128,2048]{1,0:T(8,128)(2,1)S(1)}, bf16[128,2048]{1,0:T(8,128)(2,1)S(1)}, u32[]{:S(2)}, u32[]{:S(2)}) %collective-permute-start.1) | collective-permute-done | bytes 524320 | tf_op jit(solution)/shard_map/while/body/eval_jaxpr/ppermute | solution.py:32
  190.7 9.4 %select_dynamic-update-slice_fusion.2 = (bf16[1024,2048]{1,0:T(8,128)(2,1)}, bf16[128,2048]{1,0:T(8,128)(2,1)}) fusion(bf16[1024,2048]{1,0:T(8,128)(2,1)} %get-tuple-element.478, s32[]{:T(128)S(6)} %select_n.433, pred[]{:T(512)S(6)} %and.152, bf16[4096,2048]{1,0:T(8,128)(2,1)} %get-tuple-element.503, f32[128,4096]{1,0:T(8,128)S(1)} %get-tuple-element.453, ...), kind=kOutput, calls=%fused_computation.8.clone.1 | convolution fusion | flops 2149842944 | bytes 21513220 | tf_op jit(solution)/shard_map/while/body/eval_jaxpr/dot_general | solution.py:140
  205.2 5.7 %collective-permute-done.1 = bf16[128,2048]{1,0:T(8,128)(2,1)S(1)} collective-permute-done((bf16[128,2048]{1,0:T(8,128)(2,1)S(1)}, bf16[128,2048]{1,0:T(8,128)(2,1)S(1)}, u32[]{:S(2)}, u32[]{:S(2)}) %collective-permute-start.1) | collective-permute-done | bytes 524320 | tf_op jit(solution)/shard_map/while/body/eval_jaxpr/ppermute | solution.py:32
  212.7 9.4 %select_dynamic-update-slice_fusion.2 = (bf16[1024,2048]{1,0:T(8,128)(2,1)}, bf16[128,2048]{1,0:T(8,128)(2,1)}) fusion(bf16[1024,2048]{1,0:T(8,128)(2,1)} %get-tuple-element.478, s32[]{:T(128)S(6)} %select_n.433, pred[]{:T(512)S(6)} %and.152, bf16[4096,2048]{1,0:T(8,128)(2,1)} %get-tuple-element.503, f32[128,4096]{1,0:T(8,128)S(1)} %get-tuple-element.453, ...), kind=kOutput, calls=%fused_computation.8.clone.1 | convolution fusion | flops 2149842944 | bytes 21513220 | tf_op jit(solution)/shard_map/while/body/eval_jaxpr/dot_general | solution.py:140
  227.2 4.9 %collective-permute-done.1 = bf16[128,2048]{1,0:T(8,128)(2,1)S(1)} collective-permute-done((bf16[128,2048]{1,0:T(8,128)(2,1)S(1)}, bf16[128,2048]{1,0:T(8,128)(2,1)S(1)}, u32[]{:S(2)}, u32[]{:S(2)}) %collective-permute-start.1) | collective-permute-done | bytes 524320 | tf_op jit(solution)/shard_map/while/body/eval_jaxpr/ppermute | solution.py:32
  233.8 9.4 %select_dynamic-update-slice_fusion.2 = (bf16[1024,2048]{1,0:T(8,128)(2,1)}, bf16[128,2048]{1,0:T(8,128)(2,1)}) fusion(bf16[1024,2048]{1,0:T(8,128)(2,1)} %get-tuple-element.478, s32[]{:T(128)S(6)} %select_n.433, pred[]{:T(512)S(6)} %and.152, bf16[4096,2048]{1,0:T(8,128)(2,1)} %get-tuple-element.503, f32[128,4096]{1,0:T(8,128)S(1)} %get-tuple-element.453, ...), kind=kOutput, calls=%fused_computation.8.clone.1 | convolution fusion | flops 2149842944 | bytes 21513220 | tf_op jit(solution)/shard_map/while/body/eval_jaxpr/dot_general | solution.py:140
  254.3 9.4 %select_dynamic-update-slice_fusion.2 = (bf16[1024,2048]{1,0:T(8,128)(2,1)}, bf16[128,2048]{1,0:T(8,128)(2,1)}) fusion(bf16[1024,2048]{1,0:T(8,128)(2,1)} %get-tuple-element.478, s32[]{:T(128)S(6)} %select_n.433, pred[]{:T(512)S(6)} %and.152, bf16[4096,2048]{1,0:T(8,128)(2,1)} %get-tuple-element.503, f32[128,4096]{1,0:T(8,128)S(1)} %get-tuple-element.453, ...), kind=kOutput, calls=%fused_computation.8.clone.1 | convolution fusion | flops 2149842944 | bytes 21513220 | tf_op jit(solution)/shard_map/while/body/eval_jaxpr/dot_general | solution.py:140
  274.8 9.4 %select_dynamic-update-slice_fusion.2 = (bf16[1024,2048]{1,0:T(8,128)(2,1)}, bf16[128,2048]{1,0:T(8,128)(2,1)}) fusion(bf16[1024,2048]{1,0:T(8,128)(2,1)} %get-tuple-element.478, s32[]{:T(128)S(6)} %select_n.433, pred[]{:T(512)S(6)} %and.152, bf16[4096,2048]{1,0:T(8,128)(2,1)} %get-tuple-element.503, f32[128,4096]{1,0:T(8,128)S(1)} %get-tuple-element.453, ...), kind=kOutput, calls=%fused_computation.8.clone.1 | convolution fusion | flops 2149842944 | bytes 21513220 | tf_op jit(solution)/shard_map/while/body/eval_jaxpr/dot_general | solution.py:140
  295.3 9.4 %select_dynamic-update-slice_fusion.2 = (bf16[1024,2048]{1,0:T(8,128)(2,1)}, bf16[128,2048]{1,0:T(8,128)(2,1)}) fusion(bf16[1024,2048]{1,0:T(8,128)(2,1)} %get-tuple-element.478, s32[]{:T(128)S(6)} %select_n.433, pred[]{:T(512)S(6)} %and.152, bf16[4096,2048]{1,0:T(8,128)(2,1)} %get-tuple-element.503, f32[128,4096]{1,0:T(8,128)S(1)} %get-tuple-element.453, ...), kind=kOutput, calls=%fused_computation.8.clone.1 | convolution fusion | flops 2149842944 | bytes 21513220 | tf_op jit(solution)/shard_map/while/body/eval_jaxpr/dot_general | solution.py:140
  315.8 9.4 %select_dynamic-update-slice_fusion.2 = (bf16[1024,2048]{1,0:T(8,128)(2,1)}, bf16[128,2048]{1,0:T(8,128)(2,1)}) fusion(bf16[1024,2048]{1,0:T(8,128)(2,1)} %get-tuple-element.478, s32[]{:T(128)S(6)} %select_n.433, pred[]{:T(512)S(6)} %and.152, bf16[4096,2048]{1,0:T(8,128)(2,1)} %get-tuple-element.503, f32[128,4096]{1,0:T(8,128)S(1)} %get-tuple-element.453, ...), kind=kOutput, calls=%fused_computation.8.clone.1 | convolution fusion | flops 2149842944 | bytes 21513220 | tf_op jit(solution)/shard_map/while/body/eval_jaxpr/dot_general | solution.py:140
  330.2 4.2 collective-permute-done.1
  336.2 9.4 %select_dynamic-update-slice_fusion.2 = (bf16[1024,2048]{1,0:T(8,128)(2,1)}, bf16[128,2048]{1,0:T(8,128)(2,1)}) fusion(bf16[1024,2048]{1,0:T(8,128)(2,1)} %get-tuple-element.478, s32[]{:T(128)S(6)} %select_n.433, pred[]{:T(512)S(6)} %and.152, bf16[4096,2048]{1,0:T(8,128)(2,1)} %get-tuple-element.503, f32[128,4096]{1,0:T(8,128)S(1)} %get-tuple-element.453, ...), kind=kOutput, calls=%fused_computation.8.clone.1 | convolution fusion | flops 2149842944 | bytes 21513220 | tf_op jit(solution)/shard_map/while/body/eval_jaxpr/dot_general | solution.py:140
  357.6 8.1 %collective-permute-done.3 = f32[1024,128]{0,1:T(8,128)S(1)} collective-permute-done((f32[1024,128]{0,1:T(8,128)S(1)}, f32[1024,128]{0,1:T(8,128)S(1)}, u32[]{:S(2)}, u32[]{:S(2)}) %collective-permute-start.3) | collective-permute-done | bytes 524320 | tf_op jit(solution)/shard_map/ppermute | solution.py:32
  388.5 5.5 %fusion.17 = f32[4096,256]{1,0:T(8,128)} fusion(bf16[128,4096]{1,0:T(8,128)(2,1)} %copy-done.1, bf16[4096,256]{1,0:T(8,128)(2,1)} %all-gather.5.cloned.1.call-done, f32[128,4096]{1,0:T(8,128)S(1)} %get-tuple-element.365, f32[128]{0:T(128)S(1)} %add_rsqrt_fusion.3), kind=kOutput, calls=%fused_computation.45 | convolution fusion | flops 537952256 | bytes 9437696 | tf_op jit(solution)/shard_map/dot_general | solution.py:241
  394.0 4.7 fusion.11
  398.8 7.5 %collective-permute-done.7 = f32[2,4,4,2,2,32,256]{6,5,4,3,2,1,0:T(8,128)} collective-permute-done((f32[2,4,4,2,2,32,256]{6,5,4,3,2,1,0:T(8,128)}, f32[2,4,4,2,2,32,256]{6,5,4,3,2,1,0:T(8,128)}, u32[]{:S(2)}, u32[]{:S(2)}) %collective-permute-start.7) | collective-permute-done | bytes 4194336 | tf_op jit(solution)/shard_map/ppermute | solution.py:36
  406.3 4.4 fusion.14
  457.1 4.6 collective-permute-done.24
  (257 shorter events, 201.9 us)
Async XLA Ops:
  7.2 368.3 %all-gather.3.cloned.1.call-start = ((), (), s32[]{:S(2)}) async-start(), calls=%async_computation | async-start | bytes 2228224 | tf_op jit(solution)/shard_map/all_gather | solution.py:133
  7.9 369.7 %all-gather.5.cloned.1.call-start = ((), (), s32[]{:S(2)}) async-start(), calls=%async_computation.1 | async-start | bytes 2228224 | tf_op jit(solution)/shard_map/all_gather | solution.py:134
  17.6 15.4 %collective-permute-start.1 = (bf16[128,2048]{1,0:T(8,128)(2,1)S(1)}, bf16[128,2048]{1,0:T(8,128)(2,1)S(1)}, u32[]{:S(2)}, u32[]{:S(2)}) collective-permute-start(bf16[128,2048]{1,0:T(8,128)(2,1)S(1)} %get-tuple-element.476), channel_id=1, source_target_pairs={{0,1},{1,0},{2,3},{3,2},{4,5},{5,4},{6,7},{7,6},{8,9},{9,8},{10,11... | collective-permute-start | bytes 1572872 | tf_op jit(solution)/shard_map/while/body/eval_jaxpr/ppermute | solution.py:32
  19.7 24.5 %collective-permute-start = (bf16[128,2048]{1,0:T(8,128)(2,1)S(1)}, bf16[128,2048]{1,0:T(8,128)(2,1)S(1)}, u32[]{:S(2)}, u32[]{:S(2)}) collective-permute-start(bf16[128,2048]{1,0:T(8,128)(2,1)S(1)} %broadcast_select_fusion.8), channel_id=1, source_target_pairs={{0,32},{32,64},{64,96},{1,33},{33,65},{65,97},{2,34},{34,66},{66,9... | collective-permute-start | bytes 1572872 | tf_op jit(solution)/shard_map/while/body/eval_jaxpr/ppermute | solution.py:149
  44.3 18.4 %collective-permute-start.1 = (bf16[128,2048]{1,0:T(8,128)(2,1)S(1)}, bf16[128,2048]{1,0:T(8,128)(2,1)S(1)}, u32[]{:S(2)}, u32[]{:S(2)}) collective-permute-start(bf16[128,2048]{1,0:T(8,128)(2,1)S(1)} %get-tuple-element.476), channel_id=1, source_target_pairs={{0,1},{1,0},{2,3},{3,2},{4,5},{5,4},{6,7},{7,6},{8,9},{9,8},{10,11... | collective-permute-start | bytes 1572872 | tf_op jit(solution)/shard_map/while/body/eval_jaxpr/ppermute | solution.py:32
  47.2 26.7 %collective-permute-start = (bf16[128,2048]{1,0:T(8,128)(2,1)S(1)}, bf16[128,2048]{1,0:T(8,128)(2,1)S(1)}, u32[]{:S(2)}, u32[]{:S(2)}) collective-permute-start(bf16[128,2048]{1,0:T(8,128)(2,1)S(1)} %broadcast_select_fusion.8), channel_id=1, source_target_pairs={{0,32},{32,64},{64,96},{1,33},{33,65},{65,97},{2,34},{34,66},{66,9... | collective-permute-start | bytes 1572872 | tf_op jit(solution)/shard_map/while/body/eval_jaxpr/ppermute | solution.py:149
  73.9 14.9 %collective-permute-start.1 = (bf16[128,2048]{1,0:T(8,128)(2,1)S(1)}, bf16[128,2048]{1,0:T(8,128)(2,1)S(1)}, u32[]{:S(2)}, u32[]{:S(2)}) collective-permute-start(bf16[128,2048]{1,0:T(8,128)(2,1)S(1)} %get-tuple-element.476), channel_id=1, source_target_pairs={{0,1},{1,0},{2,3},{3,2},{4,5},{5,4},{6,7},{7,6},{8,9},{9,8},{10,11... | collective-permute-start | bytes 1572872 | tf_op jit(solution)/shard_map/while/body/eval_jaxpr/ppermute | solution.py:32
  75.5 24.5 %collective-permute-start = (bf16[128,2048]{1,0:T(8,128)(2,1)S(1)}, bf16[128,2048]{1,0:T(8,128)(2,1)S(1)}, u32[]{:S(2)}, u32[]{:S(2)}) collective-permute-start(bf16[128,2048]{1,0:T(8,128)(2,1)S(1)} %broadcast_select_fusion.8), channel_id=1, source_target_pairs={{0,32},{32,64},{64,96},{1,33},{33,65},{65,97},{2,34},{34,66},{66,9... | collective-permute-start | bytes 1572872 | tf_op jit(solution)/shard_map/while/body/eval_jaxpr/ppermute | solution.py:149
  100.0 17.8 %collective-permute-start.1 = (bf16[128,2048]{1,0:T(8,128)(2,1)S(1)}, bf16[128,2048]{1,0:T(8,128)(2,1)S(1)}, u32[]{:S(2)}, u32[]{:S(2)}) collective-permute-start(bf16[128,2048]{1,0:T(8,128)(2,1)S(1)} %get-tuple-element.476), channel_id=1, source_target_pairs={{0,1},{1,0},{2,3},{3,2},{4,5},{5,4},{6,7},{7,6},{8,9},{9,8},{10,11... | collective-permute-start | bytes 1572872 | tf_op jit(solution)/shard_map/while/body/eval_jaxpr/ppermute | solution.py:32
  101.5 27.5 %collective-permute-start = (bf16[128,2048]{1,0:T(8,128)(2,1)S(1)}, bf16[128,2048]{1,0:T(8,128)(2,1)S(1)}, u32[]{:S(2)}, u32[]{:S(2)}) collective-permute-start(bf16[128,2048]{1,0:T(8,128)(2,1)S(1)} %broadcast_select_fusion.8), channel_id=1, source_target_pairs={{0,32},{32,64},{64,96},{1,33},{33,65},{65,97},{2,34},{34,66},{66,9... | collective-permute-start | bytes 1572872 | tf_op jit(solution)/shard_map/while/body/eval_jaxpr/ppermute | solution.py:149
  129.1 13.3 %collective-permute-start.1 = (bf16[128,2048]{1,0:T(8,128)(2,1)S(1)}, bf16[128,2048]{1,0:T(8,128)(2,1)S(1)}, u32[]{:S(2)}, u32[]{:S(2)}) collective-permute-start(bf16[128,2048]{1,0:T(8,128)(2,1)S(1)} %get-tuple-element.476), channel_id=1, source_target_pairs={{0,1},{1,0},{2,3},{3,2},{4,5},{5,4},{6,7},{7,6},{8,9},{9,8},{10,11... | collective-permute-start | bytes 1572872 | tf_op jit(solution)/shard_map/while/body/eval_jaxpr/ppermute | solution.py:32
  130.5 23.1 %collective-permute-start = (bf16[128,2048]{1,0:T(8,128)(2,1)S(1)}, bf16[128,2048]{1,0:T(8,128)(2,1)S(1)}, u32[]{:S(2)}, u32[]{:S(2)}) collective-permute-start(bf16[128,2048]{1,0:T(8,128)(2,1)S(1)} %broadcast_select_fusion.8), channel_id=1, source_target_pairs={{0,32},{32,64},{64,96},{1,33},{33,65},{65,97},{2,34},{34,66},{66,9... | collective-permute-start | bytes 1572872 | tf_op jit(solution)/shard_map/while/body/eval_jaxpr/ppermute | solution.py:149
  153.6 12.5 %collective-permute-start.1 = (bf16[128,2048]{1,0:T(8,128)(2,1)S(1)}, bf16[128,2048]{1,0:T(8,128)(2,1)S(1)}, u32[]{:S(2)}, u32[]{:S(2)}) collective-permute-start(bf16[128,2048]{1,0:T(8,128)(2,1)S(1)} %get-tuple-element.476), channel_id=1, source_target_pairs={{0,1},{1,0},{2,3},{3,2},{4,5},{5,4},{6,7},{7,6},{8,9},{9,8},{10,11... | collective-permute-start | bytes 1572872 | tf_op jit(solution)/shard_map/while/body/eval_jaxpr/ppermute | solution.py:32
  155.1 22.1 %collective-permute-start = (bf16[128,2048]{1,0:T(8,128)(2,1)S(1)}, bf16[128,2048]{1,0:T(8,128)(2,1)S(1)}, u32[]{:S(2)}, u32[]{:S(2)}) collective-permute-start(bf16[128,2048]{1,0:T(8,128)(2,1)S(1)} %broadcast_select_fusion.8), channel_id=1, source_target_pairs={{0,32},{32,64},{64,96},{1,33},{33,65},{65,97},{2,34},{34,66},{66,9... | collective-permute-start | bytes 1572872 | tf_op jit(solution)/shard_map/while/body/eval_jaxpr/ppermute | solution.py:149
  177.3 11.6 %collective-permute-start.1 = (bf16[128,2048]{1,0:T(8,128)(2,1)S(1)}, bf16[128,2048]{1,0:T(8,128)(2,1)S(1)}, u32[]{:S(2)}, u32[]{:S(2)}) collective-permute-start(bf16[128,2048]{1,0:T(8,128)(2,1)S(1)} %get-tuple-element.476), channel_id=1, source_target_pairs={{0,1},{1,0},{2,3},{3,2},{4,5},{5,4},{6,7},{7,6},{8,9},{9,8},{10,11... | collective-permute-start | bytes 1572872 | tf_op jit(solution)/shard_map/while/body/eval_jaxpr/ppermute | solution.py:32
  178.9 21.2 %collective-permute-start = (bf16[128,2048]{1,0:T(8,128)(2,1)S(1)}, bf16[128,2048]{1,0:T(8,128)(2,1)S(1)}, u32[]{:S(2)}, u32[]{:S(2)}) collective-permute-start(bf16[128,2048]{1,0:T(8,128)(2,1)S(1)} %broadcast_select_fusion.8), channel_id=1, source_target_pairs={{0,32},{32,64},{64,96},{1,33},{33,65},{65,97},{2,34},{34,66},{66,9... | collective-permute-start | bytes 1572872 | tf_op jit(solution)/shard_map/while/body/eval_jaxpr/ppermute | solution.py:149
  200.2 10.8 %collective-permute-start.1 = (bf16[128,2048]{1,0:T(8,128)(2,1)S(1)}, bf16[128,2048]{1,0:T(8,128)(2,1)S(1)}, u32[]{:S(2)}, u32[]{:S(2)}) collective-permute-start(bf16[128,2048]{1,0:T(8,128)(2,1)S(1)} %get-tuple-element.476), channel_id=1, source_target_pairs={{0,1},{1,0},{2,3},{3,2},{4,5},{5,4},{6,7},{7,6},{8,9},{9,8},{10,11... | collective-permute-start | bytes 1572872 | tf_op jit(solution)/shard_map/while/body/eval_jaxpr/ppermute | solution.py:32
  201.8 20.3 %collective-permute-start = (bf16[128,2048]{1,0:T(8,128)(2,1)S(1)}, bf16[128,2048]{1,0:T(8,128)(2,1)S(1)}, u32[]{:S(2)}, u32[]{:S(2)}) collective-permute-start(bf16[128,2048]{1,0:T(8,128)(2,1)S(1)} %broadcast_select_fusion.8), channel_id=1, source_target_pairs={{0,32},{32,64},{64,96},{1,33},{33,65},{65,97},{2,34},{34,66},{66,9... | collective-permute-start | bytes 1572872 | tf_op jit(solution)/shard_map/while/body/eval_jaxpr/ppermute | solution.py:149
  222.1 9.9 %collective-permute-start.1 = (bf16[128,2048]{1,0:T(8,128)(2,1)S(1)}, bf16[128,2048]{1,0:T(8,128)(2,1)S(1)}, u32[]{:S(2)}, u32[]{:S(2)}) collective-permute-start(bf16[128,2048]{1,0:T(8,128)(2,1)S(1)} %get-tuple-element.476), channel_id=1, source_target_pairs={{0,1},{1,0},{2,3},{3,2},{4,5},{5,4},{6,7},{7,6},{8,9},{9,8},{10,11... | collective-permute-start | bytes 1572872 | tf_op jit(solution)/shard_map/while/body/eval_jaxpr/ppermute | solution.py:32
  223.9 19.3 %collective-permute-start = (bf16[128,2048]{1,0:T(8,128)(2,1)S(1)}, bf16[128,2048]{1,0:T(8,128)(2,1)S(1)}, u32[]{:S(2)}, u32[]{:S(2)}) collective-permute-start(bf16[128,2048]{1,0:T(8,128)(2,1)S(1)} %broadcast_select_fusion.8), channel_id=1, source_target_pairs={{0,32},{32,64},{64,96},{1,33},{33,65},{65,97},{2,34},{34,66},{66,9... | collective-permute-start | bytes 1572872 | tf_op jit(solution)/shard_map/while/body/eval_jaxpr/ppermute | solution.py:149
  243.3 9.3 %collective-permute-start.1 = (bf16[128,2048]{1,0:T(8,128)(2,1)S(1)}, bf16[128,2048]{1,0:T(8,128)(2,1)S(1)}, u32[]{:S(2)}, u32[]{:S(2)}) collective-permute-start(bf16[128,2048]{1,0:T(8,128)(2,1)S(1)} %get-tuple-element.476), channel_id=1, source_target_pairs={{0,1},{1,0},{2,3},{3,2},{4,5},{5,4},{6,7},{7,6},{8,9},{9,8},{10,11... | collective-permute-start | bytes 1572872 | tf_op jit(solution)/shard_map/while/body/eval_jaxpr/ppermute | solution.py:32
  245.0 18.6 %collective-permute-start = (bf16[128,2048]{1,0:T(8,128)(2,1)S(1)}, bf16[128,2048]{1,0:T(8,128)(2,1)S(1)}, u32[]{:S(2)}, u32[]{:S(2)}) collective-permute-start(bf16[128,2048]{1,0:T(8,128)(2,1)S(1)} %broadcast_select_fusion.8), channel_id=1, source_target_pairs={{0,32},{32,64},{64,96},{1,33},{33,65},{65,97},{2,34},{34,66},{66,9... | collective-permute-start | bytes 1572872 | tf_op jit(solution)/shard_map/while/body/eval_jaxpr/ppermute | solution.py:149
  263.8 9.3 %collective-permute-start.1 = (bf16[128,2048]{1,0:T(8,128)(2,1)S(1)}, bf16[128,2048]{1,0:T(8,128)(2,1)S(1)}, u32[]{:S(2)}, u32[]{:S(2)}) collective-permute-start(bf16[128,2048]{1,0:T(8,128)(2,1)S(1)} %get-tuple-element.476), channel_id=1, source_target_pairs={{0,1},{1,0},{2,3},{3,2},{4,5},{5,4},{6,7},{7,6},{8,9},{9,8},{10,11... | collective-permute-start | bytes 1572872 | tf_op jit(solution)/shard_map/while/body/eval_jaxpr/ppermute | solution.py:32
  265.5 18.6 %collective-permute-start = (bf16[128,2048]{1,0:T(8,128)(2,1)S(1)}, bf16[128,2048]{1,0:T(8,128)(2,1)S(1)}, u32[]{:S(2)}, u32[]{:S(2)}) collective-permute-start(bf16[128,2048]{1,0:T(8,128)(2,1)S(1)} %broadcast_select_fusion.8), channel_id=1, source_target_pairs={{0,32},{32,64},{64,96},{1,33},{33,65},{65,97},{2,34},{34,66},{66,9... | collective-permute-start | bytes 1572872 | tf_op jit(solution)/shard_map/while/body/eval_jaxpr/ppermute | solution.py:149
  286.0 18.7 %collective-permute-start = (bf16[128,2048]{1,0:T(8,128)(2,1)S(1)}, bf16[128,2048]{1,0:T(8,128)(2,1)S(1)}, u32[]{:S(2)}, u32[]{:S(2)}) collective-permute-start(bf16[128,2048]{1,0:T(8,128)(2,1)S(1)} %broadcast_select_fusion.8), channel_id=1, source_target_pairs={{0,32},{32,64},{64,96},{1,33},{33,65},{65,97},{2,34},{34,66},{66,9... | collective-permute-start | bytes 1572872 | tf_op jit(solution)/shard_map/while/body/eval_jaxpr/ppermute | solution.py:149
  304.7 9.3 %collective-permute-start.1 = (bf16[128,2048]{1,0:T(8,128)(2,1)S(1)}, bf16[128,2048]{1,0:T(8,128)(2,1)S(1)}, u32[]{:S(2)}, u32[]{:S(2)}) collective-permute-start(bf16[128,2048]{1,0:T(8,128)(2,1)S(1)} %get-tuple-element.476), channel_id=1, source_target_pairs={{0,1},{1,0},{2,3},{3,2},{4,5},{5,4},{6,7},{7,6},{8,9},{9,8},{10,11... | collective-permute-start | bytes 1572872 | tf_op jit(solution)/shard_map/while/body/eval_jaxpr/ppermute | solution.py:32
  306.5 18.7 %collective-permute-start = (bf16[128,2048]{1,0:T(8,128)(2,1)S(1)}, bf16[128,2048]{1,0:T(8,128)(2,1)S(1)}, u32[]{:S(2)}, u32[]{:S(2)}) collective-permute-start(bf16[128,2048]{1,0:T(8,128)(2,1)S(1)} %broadcast_select_fusion.8), channel_id=1, source_target_pairs={{0,32},{32,64},{64,96},{1,33},{33,65},{65,97},{2,34},{34,66},{66,9... | collective-permute-start | bytes 1572872 | tf_op jit(solution)/shard_map/while/body/eval_jaxpr/ppermute | solution.py:149
  325.2 9.3 %collective-permute-start.1 = (bf16[128,2048]{1,0:T(8,128)(2,1)S(1)}, bf16[128,2048]{1,0:T(8,128)(2,1)S(1)}, u32[]{:S(2)}, u32[]{:S(2)}) collective-permute-start(bf16[128,2048]{1,0:T(8,128)(2,1)S(1)} %get-tuple-element.476), channel_id=1, source_target_pairs={{0,1},{1,0},{2,3},{3,2},{4,5},{5,4},{6,7},{7,6},{8,9},{9,8},{10,11... | collective-permute-start | bytes 1572872 | tf_op jit(solution)/shard_map/while/body/eval_jaxpr/ppermute | solution.py:32
  327.0 18.7 %collective-permute-start = (bf16[128,2048]{1,0:T(8,128)(2,1)S(1)}, bf16[128,2048]{1,0:T(8,128)(2,1)S(1)}, u32[]{:S(2)}, u32[]{:S(2)}) collective-permute-start(bf16[128,2048]{1,0:T(8,128)(2,1)S(1)} %broadcast_select_fusion.8), channel_id=1, source_target_pairs={{0,32},{32,64},{64,96},{1,33},{33,65},{65,97},{2,34},{34,66},{66,9... | collective-permute-start | bytes 1572872 | tf_op jit(solution)/shard_map/while/body/eval_jaxpr/ppermute | solution.py:149
  411.5 9.6 %collective-permute-start.16 = (f32[4,2,2,32,128]{4,3,2,1,0:T(8,128)S(1)}, f32[4,2,2,32,128]{4,3,2,1,0:T(8,128)S(1)}, u32[]{:S(2)}, u32[]{:S(2)}) collective-permute-start(f32[4,2,2,32,128]{4,3,2,1,0:T(8,128)S(1)} %dynamic-slice_bitcast_fusion.2), channel_id=1, source_target_pairs={{0,8},{2,10},{4,12},{6,14},{8,16},{10,18},{12,20},{14,22},{16,24},... | collective-permute-start | bytes 786440 | tf_op jit(solution)/shard_map/ppermute | solution.py:36
  415.2 9.4 %collective-permute-start.8 = (f32[4,2,2,32,128]{4,3,2,1,0:T(8,128)S(1)}, f32[4,2,2,32,128]{4,3,2,1,0:T(8,128)S(1)}, u32[]{:S(2)}, u32[]{:S(2)}) collective-permute-start(f32[4,2,2,32,128]{4,3,2,1,0:T(8,128)S(1)} %dynamic-slice_bitcast_fusion.5), channel_id=1, source_target_pairs={{0,32},{32,64},{64,96},{96,0},{1,33},{33,65},{65,97},{97,1},{2,34}... | collective-permute-start | bytes 786440 | tf_op jit(solution)/shard_map/ppermute | solution.py:32
  415.3 9.4 %collective-permute-start.11 = (f32[4,2,2,32,128]{4,3,2,1,0:T(8,128)S(1)}, f32[4,2,2,32,128]{4,3,2,1,0:T(8,128)S(1)}, u32[]{:S(2)}, u32[]{:S(2)}) collective-permute-start(f32[4,2,2,32,128]{4,3,2,1,0:T(8,128)S(1)} %dynamic-slice_bitcast_fusion.4), channel_id=1, source_target_pairs={{0,96},{32,0},{64,32},{96,64},{1,97},{33,1},{65,33},{97,65},{2,98}... | collective-permute-start | bytes 786440 | tf_op jit(solution)/shard_map/ppermute | solution.py:32
  (31 other events, 181.7 us)
Sparse Core Ops, SparseCore 0:
  10.4 54.9 all-gather.2
  67.7 54.3 all-gather.4

commit v6 on v2

--- a/solution.py
+++ b/solution.py
@@ -155,7 +155,10 @@
         jnp.zeros((block_rows, half_width), jnp.bfloat16),
         jnp.zeros((total_rows, half_width), jnp.bfloat16),
     )
-    final_half = lax.fori_loop(0, tick_count, tick_whole, initial)[2]
+    state = initial
+    for tick_pos in range(tick_count):
+        state = tick_whole(tick_pos, state)
+    final_half = state[2]
 
     positions = jnp.arange(seq_len, dtype=jnp.int32)
     next_ids = jnp.concatenate([token_ids[:, 1:], token_ids[:, :1]], axis=1)

time: 471 us -> 474 us (level); the launches traced: 469 us -> 465 us
  matrix products: 155 us -> 113 us
  starting transfers between devices: 111 us -> 141 us
  waiting for transfers between devices: 122 us -> 147 us
  other arithmetic: 49.5 us -> 33.1 us
    ppermute x14 -> x13, waiting for transfers between devices: 0.04 us -> 61 us  [tick_whole(): lax.ppermute(computed, 'segment', [(i, i + 1) for i in range(segments - 1)])]
    dot_general x14, matrix products: 132 us -> 93 us  [apply_segment(): update = jnp.dot(normed, weight_local, preferred_element_type=jnp.float32)]
    ppermute x33, waiting for transfers between devices: 111 us -> 77.3 us  [shifted(): return lax.ppermute(x, axis, [(i, (i + by) % size) for i in range(size)])]
    ppermute x33, starting transfers between devices: 33.6 us -> 60.5 us  [shifted(): return lax.ppermute(x, axis, [(i, (i + by) % size) for i in range(size)])]
    while x14 -> x0, other arithmetic: 14.1 us -> none
    reduce_sum x14 -> x7, other arithmetic: 23.3 us -> 18.4 us  [rms_scale(): squares = jnp.mean(values * values, axis=-1, keepdims=True)]
    select_n x14, other arithmetic: 1.02 us -> 5.81 us  [tick_whole(): low = jnp.where(own_first, arrived, partner)]
    ppermute x14 -> x13, starting transfers between devices: 49.6 us -> 53.2 us  [tick_whole(): lax.ppermute(computed, 'segment', [(i, i + 1) for i in range(segments - 1)])]
  transfers between devices with their start and end apart: 65 -> 64, of which waited for: 28 -> 36; matrix products, arithmetic and copies ran while one was open for 44% -> 20% of each run, Pallas kernels for 0% -> 0%
where the time goes in v6:
time: 474 us; the launch traced here: 465 us
  waiting for transfers between devices  147 us (31%)
  starting transfers between devices  141 us (30%)
  matrix products  113 us (24%)
  other arithmetic  33.1 us (7%)
  between operations  19.1 us (4%)
  local copies, waits for them, and re-layouts  12.1 us (3%)
    dot_general x14, matrix products, apply_segment(): update = jnp.dot(normed, weight_local, preferred_element_type=jnp.float32)  93 us
    ppermute x33, waiting for transfers between devices, shifted(): return lax.ppermute(x, axis, [(i, (i + by) % size) for i in range(size)])  77.3 us
    ppermute x13, waiting for transfers between devices, tick_whole(): lax.ppermute(computed, 'segment', [(i, i + 1) for i in range(segments - 1)])  61 us
    ppermute x33, starting transfers between devices, shifted(): return lax.ppermute(x, axis, [(i, (i + by) % size) for i in range(size)])  60.5 us
    ppermute x13, starting transfers between devices, tick_whole(): lax.ppermute(computed, 'segment', [(i, i + 1) for i in range(segments - 1)])  53.2 us
    ppermute x16, starting transfers between devices, fsdp_moved(): return lax.ppermute(x, 'fsdp', [(f, mapping(f)) for f in range(16)])  27.2 us
    reduce_sum x7, other arithmetic, rms_scale(): squares = jnp.mean(values * values, axis=-1, keepdims=True)  18.4 us
  transfers between devices with their start and end apart: 64, of which 36 were waited for; matrix products, arithmetic and copies ran while one was open for 20% of the time, Pallas kernels for 0%

profile of v6, /device:TPU:0, one launch (start us, length us, event | category | flops | bytes accessed | tf_op | source)
XLA Modules:
  0.0 465.5 jit_solution(9021193825077441111)
XLA Ops:
  13.0 9.1 %collective-permute-done.1 = bf16[128,2048]{1,0:T(8,128)(2,1)S(1)} collective-permute-done((bf16[128,2048]{1,0:T(8,128)(2,1)S(1)}, bf16[128,2048]{1,0:T(8,128)(2,1)S(1)}, u32[]{:S(2)}, u32[]{:S(2)}) %collective-permute-start.1) | collective-permute-done | bytes 524320 | tf_op jit(solution)/shard_map/ppermute | solution.py:138
  24.0 6.4 %convolution_convert_fusion = bf16[1024,4096]{1,0:T(8,128)(2,1)} fusion(bf16[128,4096]{1,0:T(8,128)(2,1)S(1)} %copy-done, s32[1024]{0:T(1024)} %bitcast.281), kind=kOutput, calls=%fused_computation.33 | convolution fusion | flops 1078067200 | bytes 9441280 | tf_op jit(solution)/shard_map/dot_general | solution.py:22
  30.5 5.4 %collective-permute-done.2 = bf16[128,2048]{1,0:T(8,128)(2,1)S(1)} collective-permute-done((bf16[128,2048]{1,0:T(8,128)(2,1)S(1)}, bf16[128,2048]{1,0:T(8,128)(2,1)S(1)}, u32[]{:S(2)}, u32[]{:S(2)}) %collective-permute-start.2) | collective-permute-done | bytes 524320 | tf_op jit(solution)/shard_map/ppermute | solution.py:32
  38.8 8.6 %select_dynamic-update-slice_fusion.11 = (bf16[1024,2048]{1,0:T(8,128)(2,1)S(1)}, bf16[128,2048]{1,0:T(8,128)(2,1)S(1)}) fusion(bf16[1024,2048]{1,0:T(8,128)(2,1)S(1)} %broadcast_in_dim.14, s32[]{:T(128)S(6)} %select_n.601, pred[]{:T(512)S(6)} %and.191, bf16[1,4096,2048]{2,1,0:T(8,128)(2,1)} %param.14, f32[128,4096]{1,0:T(8,128)S(1)} %get-tuple-element.45, ...), kind=kOutput, calls=%fused_computation.188 | convolution fusion | flops 2149842944 | bytes 20988424 | tf_op jit(solution)/shard_map/dot_general | solution.py:129
  65.3 6.8 %collective-permute-done.5 = bf16[128,2048]{1,0:T(8,128)(2,1)S(1)} collective-permute-done((bf16[128,2048]{1,0:T(8,128)(2,1)S(1)}, bf16[128,2048]{1,0:T(8,128)(2,1)S(1)}, u32[]{:S(2)}, u32[]{:S(2)}) %collective-permute-start.5) | collective-permute-done | bytes 524320 | tf_op jit(solution)/shard_map/ppermute | solution.py:138
  73.9 10.0 %collective-permute-done.6 = bf16[128,2048]{1,0:T(8,128)(2,1)S(1)} collective-permute-done((bf16[128,2048]{1,0:T(8,128)(2,1)S(1)}, bf16[128,2048]{1,0:T(8,128)(2,1)S(1)}, u32[]{:S(2)}, u32[]{:S(2)}) %collective-permute-start.6) | collective-permute-done | bytes 524320 | tf_op jit(solution)/shard_map/ppermute | solution.py:32
  86.5 9.4 %select_dynamic-update-slice_fusion.9 = (bf16[1024,2048]{1,0:T(8,128)(2,1)}, bf16[128,2048]{1,0:T(8,128)(2,1)S(1)}) fusion(bf16[1024,2048]{1,0:T(8,128)(2,1)} %copy-done.2, s32[]{:T(128)S(6)} %select_n.615, pred[]{:T(512)S(6)} %and.195, bf16[1,4096,2048]{2,1,0:T(8,128)(2,1)} %param.14, f32[128,4096]{1,0:T(8,128)S(1)} %get-tuple-element.43, ...), kind=kOutput, calls=%fused_computation.186 | convolution fusion | flops 2149842944 | bytes 21513220 | tf_op jit(solution)/shard_map/dot_general | solution.py:129
  114.1 5.8 %collective-permute-done.9 = bf16[128,2048]{1,0:T(8,128)(2,1)S(1)} collective-permute-done((bf16[128,2048]{1,0:T(8,128)(2,1)S(1)}, bf16[128,2048]{1,0:T(8,128)(2,1)S(1)}, u32[]{:S(2)}, u32[]{:S(2)}) %collective-permute-start.9) | collective-permute-done | bytes 524320 | tf_op jit(solution)/shard_map/ppermute | solution.py:138
  123.5 9.1 %collective-permute-done.10 = bf16[128,2048]{1,0:T(8,128)(2,1)S(1)} collective-permute-done((bf16[128,2048]{1,0:T(8,128)(2,1)S(1)}, bf16[128,2048]{1,0:T(8,128)(2,1)S(1)}, u32[]{:S(2)}, u32[]{:S(2)}) %collective-permute-start.10) | collective-permute-done | bytes 524320 | tf_op jit(solution)/shard_map/ppermute | solution.py:32
  135.2 9.4 %select_dynamic-update-slice_fusion.7 = (bf16[1024,2048]{1,0:T(8,128)(2,1)}, bf16[128,2048]{1,0:T(8,128)(2,1)S(1)}) fusion(bf16[1024,2048]{1,0:T(8,128)(2,1)} %get-tuple-element.92, s32[]{:T(128)S(6)} %select_n.627, pred[]{:T(512)S(6)} %and.199, bf16[1,4096,2048]{2,1,0:T(8,128)(2,1)} %param.14, f32[128,4096]{1,0:T(8,128)S(1)} %get-tuple-element.41, ...), kind=kOutput, calls=%fused_computation.184 | convolution fusion | flops 2149842944 | bytes 21513220 | tf_op jit(solution)/shard_map/dot_general | solution.py:129
  144.5 4.6 collective-permute-start.11
  149.2 4.5 select_dynamic-update-slice_fusion.6
  163.2 6.3 %collective-permute-done.13 = bf16[128,2048]{1,0:T(8,128)(2,1)S(1)} collective-permute-done((bf16[128,2048]{1,0:T(8,128)(2,1)S(1)}, bf16[128,2048]{1,0:T(8,128)(2,1)S(1)}, u32[]{:S(2)}, u32[]{:S(2)}) %collective-permute-start.13) | collective-permute-done | bytes 524320 | tf_op jit(solution)/shard_map/ppermute | solution.py:138
  171.6 11.4 %collective-permute-done.14 = bf16[128,2048]{1,0:T(8,128)(2,1)S(1)} collective-permute-done((bf16[128,2048]{1,0:T(8,128)(2,1)S(1)}, bf16[128,2048]{1,0:T(8,128)(2,1)S(1)}, u32[]{:S(2)}, u32[]{:S(2)}) %collective-permute-start.14) | collective-permute-done | bytes 524320 | tf_op jit(solution)/shard_map/ppermute | solution.py:32
  185.6 9.4 %select_dynamic-update-slice_fusion.5 = (bf16[1024,2048]{1,0:T(8,128)(2,1)}, bf16[128,2048]{1,0:T(8,128)(2,1)S(1)}) fusion(bf16[1024,2048]{1,0:T(8,128)(2,1)} %get-tuple-element.96, s32[]{:T(128)S(6)} %select_n.639, pred[]{:T(512)S(6)} %and.203, bf16[1,4096,2048]{2,1,0:T(8,128)(2,1)} %param.14, f32[128,4096]{1,0:T(8,128)S(1)} %get-tuple-element.39, ...), kind=kOutput, calls=%fused_computation.182 | convolution fusion | flops 2149842944 | bytes 21513220 | tf_op jit(solution)/shard_map/dot_general | solution.py:129
  199.5 4.5 select_dynamic-update-slice_fusion.4
  213.7 5.4 %collective-permute-done.17 = bf16[128,2048]{1,0:T(8,128)(2,1)S(1)} collective-permute-done((bf16[128,2048]{1,0:T(8,128)(2,1)S(1)}, bf16[128,2048]{1,0:T(8,128)(2,1)S(1)}, u32[]{:S(2)}, u32[]{:S(2)}) %collective-permute-start.17) | collective-permute-done | bytes 524320 | tf_op jit(solution)/shard_map/ppermute | solution.py:138
  222.1 11.2 %collective-permute-done.18 = bf16[128,2048]{1,0:T(8,128)(2,1)S(1)} collective-permute-done((bf16[128,2048]{1,0:T(8,128)(2,1)S(1)}, bf16[128,2048]{1,0:T(8,128)(2,1)S(1)}, u32[]{:S(2)}, u32[]{:S(2)}) %collective-permute-start.18) | collective-permute-done | bytes 524320 | tf_op jit(solution)/shard_map/ppermute | solution.py:32
  236.0 9.4 %select_dynamic-update-slice_fusion.3 = (bf16[1024,2048]{1,0:T(8,128)(2,1)}, bf16[128,2048]{1,0:T(8,128)(2,1)S(1)}) fusion(bf16[1024,2048]{1,0:T(8,128)(2,1)} %get-tuple-element.100, s32[]{:T(128)S(6)} %select_n.651, pred[]{:T(512)S(6)} %and.207, bf16[1,4096,2048]{2,1,0:T(8,128)(2,1)} %param.14, f32[128,4096]{1,0:T(8,128)S(1)} %get-tuple-element.37, ...), kind=kOutput, calls=%fused_computation.180 | convolution fusion | flops 2149842944 | bytes 21513220 | tf_op jit(solution)/shard_map/dot_general | solution.py:129
  245.4 5.2 %collective-permute-start.19 = (bf16[128,2048]{1,0:T(8,128)(2,1)S(1)}, bf16[128,2048]{1,0:T(8,128)(2,1)}, u32[]{:S(2)}, u32[]{:S(2)}) collective-permute-start(bf16[128,2048]{1,0:T(8,128)(2,1)S(1)} %get-tuple-element.103), channel_id=1, source_target_pairs={{0,32},{32,64},{64,96},{1,33},{33,65},{65,97},{2,34},{34,66},{66,9... | collective-permute-start | bytes 1572872 | tf_op jit(solution)/shard_map/ppermute | solution.py:138
  250.6 4.5 select_dynamic-update-slice_fusion.2
  264.4 4.8 %collective-permute-done.21 = bf16[128,2048]{1,0:T(8,128)(2,1)} collective-permute-done((bf16[128,2048]{1,0:T(8,128)(2,1)S(1)}, bf16[128,2048]{1,0:T(8,128)(2,1)}, u32[]{:S(2)}, u32[]{:S(2)}) %collective-permute-start.21) | collective-permute-done | bytes 524320 | tf_op jit(solution)/shard_map/ppermute | solution.py:138
  274.9 7.6 %collective-permute-done.22 = bf16[128,2048]{1,0:T(8,128)(2,1)} collective-permute-done((bf16[128,2048]{1,0:T(8,128)(2,1)}, bf16[128,2048]{1,0:T(8,128)(2,1)}, u32[]{:S(2)}, u32[]{:S(2)}) %collective-permute-start.22) | collective-permute-done | bytes 524320 | tf_op jit(solution)/shard_map/ppermute | solution.py:32
  286.4 9.4 %select_dynamic-update-slice_fusion.1 = (bf16[1024,2048]{1,0:T(8,128)(2,1)}, bf16[128,2048]{1,0:T(8,128)(2,1)S(1)}) fusion(bf16[1024,2048]{1,0:T(8,128)(2,1)} %get-tuple-element.104, s32[]{:T(128)S(6)} %select_n.663, pred[]{:T(512)S(6)} %and.211, bf16[1,4096,2048]{2,1,0:T(8,128)(2,1)} %param.14, f32[128,4096]{1,0:T(8,128)S(1)} %get-tuple-element.35, ...), kind=kOutput, calls=%fused_computation.178 | convolution fusion | flops 2149842944 | bytes 21513220 | tf_op jit(solution)/shard_map/dot_general | solution.py:129
  295.7 4.7 %collective-permute-start.23 = (bf16[128,2048]{1,0:T(8,128)(2,1)S(1)}, bf16[128,2048]{1,0:T(8,128)(2,1)S(1)}, u32[]{:S(2)}, u32[]{:S(2)}) collective-permute-start(bf16[128,2048]{1,0:T(8,128)(2,1)S(1)} %get-tuple-element.107), channel_id=1, source_target_pairs={{0,32},{32,64},{64,96},{1,33},{33,65},{65,97},{2,34},{34,66},{66,9... | collective-permute-start | bytes 1572872 | tf_op jit(solution)/shard_map/ppermute | solution.py:138
  300.5 4.7 %select_dynamic-update-slice_fusion = (bf16[1024,2048]{1,0:T(8,128)(2,1)}, bf16[128,2048]{1,0:T(8,128)(2,1)}) fusion(bf16[1024,2048]{1,0:T(8,128)(2,1)} %get-tuple-element.106, s32[]{:T(128)S(6)} %select_n.669, pred[]{:T(512)S(6)} %and.213, bf16[1,4096,2048]{2,1,0:T(8,128)(2,1)S(1)} %bitcast.261, f32[128,4096]{1,0:T(8,128)S(1)} %get-tuple-element.9, ...), kind=kOutput, calls=%fused_computation.177 | convolution fusion | flops 2149842944 | bytes 21513220 | tf_op jit(solution)/shard_map/dot_general | solution.py:129
  316.2 4.5 collective-permute-done.25
  326.4 6.2 %collective-permute-done.26 = bf16[128,2048]{1,0:T(8,128)(2,1)} collective-permute-done((bf16[128,2048]{1,0:T(8,128)(2,1)}, bf16[128,2048]{1,0:T(8,128)(2,1)}, u32[]{:S(2)}, u32[]{:S(2)}) %collective-permute-start.26) | collective-permute-done | bytes 524320 | tf_op jit(solution)/shard_map/ppermute | solution.py:32
  337.7 9.3 %fusion.123 = bf16[1024,2048]{1,0:T(8,128)(2,1)S(1)} fusion(bf16[1024,2048]{1,0:T(8,128)(2,1)S(1)} %copy-done.3, s32[]{:T(128)S(6)} %select_n.675, bf16[1,4096,2048]{2,1,0:T(8,128)(2,1)} %param.14, f32[128,4096]{1,0:T(8,128)} %get-tuple-element.33, f32[128]{0:T(128)S(1)} %get-tuple-element.115, s32[]{:T(128)} %select_n.606, f32[4096]{0:T(1024)S(1)} %bitcast.279, ...), kind=kOutput, calls=%fused_computation.70 | convolution fusion | flops 2149842944 | bytes 20988932 | tf_op jit(solution)/shard_map/dot_general | solution.py:129
  361.0 5.2 %collective-permute-done.28 = f32[1024,128]{0,1:T(8,128)S(1)} collective-permute-done((f32[1024,128]{0,1:T(8,128)S(1)}, f32[1024,128]{0,1:T(8,128)S(1)}, u32[]{:S(2)}, u32[]{:S(2)}) %collective-permute-start.28) | collective-permute-done | bytes 524320 | tf_op jit(solution)/shard_map/ppermute | solution.py:32
  366.7 5.2 %collective-permute-start.29 = (f32[8]{0:T(128)S(1)}, f32[8]{0:T(128)S(1)}, u32[]{:S(2)}, u32[]{:S(2)}) collective-permute-start(f32[8]{0:T(128)S(1)} %convert_divide_fusion), channel_id=1, source_target_pairs={{0,96},{32,0},{64,32},{96,64},{1,97},{33,1},{65,33},{97,65},{2,98}... | collective-permute-start | bytes 104 | tf_op jit(solution)/shard_map/ppermute | solution.py:32
  384.2 5.2 %fusion.133 = f32[4096,256]{1,0:T(8,128)} fusion(bf16[128,4096]{1,0:T(8,128)(2,1)S(1)} %subtract_convert_fusion, bf16[4096,256]{1,0:T(8,128)(2,1)} %all-gather.5.cloned.1.call-done, f32[128,4096]{1,0:T(8,128)S(1)} %get-tuple-element.83, f32[128]{0:T(128)S(1)} %add_rsqrt_fusion.16), kind=kOutput, calls=%fused_computation.114 | convolution fusion | flops 537952256 | bytes 9437696 | tf_op jit(solution)/shard_map/dot_general | solution.py:233
  (325 shorter events, 223.2 us)
Async XLA Ops:
  7.2 306.9 %all-gather.3.cloned.1.call-start = ((), (), s32[]{:S(2)}) async-start(), calls=%async_computation | async-start | bytes 2228224 | tf_op jit(solution)/shard_map/all_gather | solution.py:122
  7.3 14.8 %collective-permute-start.1 = (bf16[128,2048]{1,0:T(8,128)(2,1)S(1)}, bf16[128,2048]{1,0:T(8,128)(2,1)S(1)}, u32[]{:S(2)}, u32[]{:S(2)}) collective-permute-start(bf16[128,2048]{1,0:T(8,128)(2,1)S(1)} %broadcast.232), channel_id=1, source_target_pairs={{0,32},{32,64},{64,96},{1,33},{33,65},{65,97},{2,34},{34,66},{66,9... | collective-permute-start | bytes 1572872 | tf_op jit(solution)/shard_map/ppermute | solution.py:138
  11.0 19.4 %collective-permute-start = (bf16[128,2048]{1,0:T(8,128)(2,1)S(1)}, bf16[128,2048]{1,0:T(8,128)(2,1)S(1)}, u32[]{:S(2)}, u32[]{:S(2)}) collective-permute-start(bf16[128,2048]{1,0:T(8,128)(2,1)S(1)} %broadcast.232), channel_id=1, source_target_pairs={{0,1},{1,0},{2,3},{3,2},{4,5},{5,4},{6,7},{7,6},{8,9},{9,8},{10,11... | collective-permute-start | bytes 1572872 | tf_op jit(solution)/shard_map/ppermute | solution.py:32
  22.1 13.7 %collective-permute-start.2 = (bf16[128,2048]{1,0:T(8,128)(2,1)S(1)}, bf16[128,2048]{1,0:T(8,128)(2,1)S(1)}, u32[]{:S(2)}, u32[]{:S(2)}) collective-permute-start(bf16[128,2048]{1,0:T(8,128)(2,1)S(1)} %collective-permute-done.1), channel_id=1, source_target_pairs={{0,1},{1,0},{2,3},{3,2},{4,5},{5,4},{6,7},{7,6},{8,9},{9,8},{10,11... | collective-permute-start | bytes 1572872 | tf_op jit(solution)/shard_map/ppermute | solution.py:32
  47.4 16.1 %collective-permute-start.3 = (bf16[128,2048]{1,0:T(8,128)(2,1)S(1)}, bf16[128,2048]{1,0:T(8,128)(2,1)S(1)}, u32[]{:S(2)}, u32[]{:S(2)}) collective-permute-start(bf16[128,2048]{1,0:T(8,128)(2,1)S(1)} %get-tuple-element.87), channel_id=1, source_target_pairs={{0,32},{32,64},{64,96},{1,33},{33,65},{65,97},{2,34},{34,66},{66,9... | collective-permute-start | bytes 1572872 | tf_op jit(solution)/shard_map/ppermute | solution.py:138
  56.1 16.0 %collective-permute-start.5 = (bf16[128,2048]{1,0:T(8,128)(2,1)S(1)}, bf16[128,2048]{1,0:T(8,128)(2,1)S(1)}, u32[]{:S(2)}, u32[]{:S(2)}) collective-permute-start(bf16[128,2048]{1,0:T(8,128)(2,1)S(1)} %get-tuple-element.89), channel_id=1, source_target_pairs={{0,32},{32,64},{64,96},{1,33},{33,65},{65,97},{2,34},{34,66},{66,9... | collective-permute-start | bytes 1572872 | tf_op jit(solution)/shard_map/ppermute | solution.py:138
  63.5 10.3 %collective-permute-start.4 = (bf16[128,2048]{1,0:T(8,128)(2,1)S(1)}, bf16[128,2048]{1,0:T(8,128)(2,1)S(1)}, u32[]{:S(2)}, u32[]{:S(2)}) collective-permute-start(bf16[128,2048]{1,0:T(8,128)(2,1)S(1)} %collective-permute-done.3), channel_id=1, source_target_pairs={{0,1},{1,0},{2,3},{3,2},{4,5},{5,4},{6,7},{7,6},{8,9},{9,8},{10,11... | collective-permute-start | bytes 1572872 | tf_op jit(solution)/shard_map/ppermute | solution.py:32
  72.1 11.8 %collective-permute-start.6 = (bf16[128,2048]{1,0:T(8,128)(2,1)S(1)}, bf16[128,2048]{1,0:T(8,128)(2,1)S(1)}, u32[]{:S(2)}, u32[]{:S(2)}) collective-permute-start(bf16[128,2048]{1,0:T(8,128)(2,1)S(1)} %collective-permute-done.5), channel_id=1, source_target_pairs={{0,1},{1,0},{2,3},{3,2},{4,5},{5,4},{6,7},{7,6},{8,9},{9,8},{10,11... | collective-permute-start | bytes 1572872 | tf_op jit(solution)/shard_map/ppermute | solution.py:32
  95.9 16.2 %collective-permute-start.7 = (bf16[128,2048]{1,0:T(8,128)(2,1)S(1)}, bf16[128,2048]{1,0:T(8,128)(2,1)S(1)}, u32[]{:S(2)}, u32[]{:S(2)}) collective-permute-start(bf16[128,2048]{1,0:T(8,128)(2,1)S(1)} %get-tuple-element.91), channel_id=1, source_target_pairs={{0,32},{32,64},{64,96},{1,33},{33,65},{65,97},{2,34},{34,66},{66,9... | collective-permute-start | bytes 1572872 | tf_op jit(solution)/shard_map/ppermute | solution.py:138
  104.9 15.0 %collective-permute-start.9 = (bf16[128,2048]{1,0:T(8,128)(2,1)S(1)}, bf16[128,2048]{1,0:T(8,128)(2,1)S(1)}, u32[]{:S(2)}, u32[]{:S(2)}) collective-permute-start(bf16[128,2048]{1,0:T(8,128)(2,1)S(1)} %get-tuple-element.93), channel_id=1, source_target_pairs={{0,32},{32,64},{64,96},{1,33},{33,65},{65,97},{2,34},{34,66},{66,9... | collective-permute-start | bytes 1572872 | tf_op jit(solution)/shard_map/ppermute | solution.py:138
  112.1 11.3 %collective-permute-start.8 = (bf16[128,2048]{1,0:T(8,128)(2,1)S(1)}, bf16[128,2048]{1,0:T(8,128)(2,1)S(1)}, u32[]{:S(2)}, u32[]{:S(2)}) collective-permute-start(bf16[128,2048]{1,0:T(8,128)(2,1)S(1)} %collective-permute-done.7), channel_id=1, source_target_pairs={{0,1},{1,0},{2,3},{3,2},{4,5},{5,4},{6,7},{7,6},{8,9},{9,8},{10,11... | collective-permute-start | bytes 1572872 | tf_op jit(solution)/shard_map/ppermute | solution.py:32
  119.9 12.7 %collective-permute-start.10 = (bf16[128,2048]{1,0:T(8,128)(2,1)S(1)}, bf16[128,2048]{1,0:T(8,128)(2,1)S(1)}, u32[]{:S(2)}, u32[]{:S(2)}) collective-permute-start(bf16[128,2048]{1,0:T(8,128)(2,1)S(1)} %collective-permute-done.9), channel_id=1, source_target_pairs={{0,1},{1,0},{2,3},{3,2},{4,5},{5,4},{6,7},{7,6},{8,9},{9,8},{10,11... | collective-permute-start | bytes 1572872 | tf_op jit(solution)/shard_map/ppermute | solution.py:32
  144.5 16.7 %collective-permute-start.11 = (bf16[128,2048]{1,0:T(8,128)(2,1)S(1)}, bf16[128,2048]{1,0:T(8,128)(2,1)S(1)}, u32[]{:S(2)}, u32[]{:S(2)}) collective-permute-start(bf16[128,2048]{1,0:T(8,128)(2,1)S(1)} %get-tuple-element.95), channel_id=1, source_target_pairs={{0,32},{32,64},{64,96},{1,33},{33,65},{65,97},{2,34},{34,66},{66,9... | collective-permute-start | bytes 1572872 | tf_op jit(solution)/shard_map/ppermute | solution.py:138
  153.7 15.7 %collective-permute-start.13 = (bf16[128,2048]{1,0:T(8,128)(2,1)S(1)}, bf16[128,2048]{1,0:T(8,128)(2,1)S(1)}, u32[]{:S(2)}, u32[]{:S(2)}) collective-permute-start(bf16[128,2048]{1,0:T(8,128)(2,1)S(1)} %get-tuple-element.97), channel_id=1, source_target_pairs={{0,32},{32,64},{64,96},{1,33},{33,65},{65,97},{2,34},{34,66},{66,9... | collective-permute-start | bytes 1572872 | tf_op jit(solution)/shard_map/ppermute | solution.py:138
  161.2 10.3 %collective-permute-start.12 = (bf16[128,2048]{1,0:T(8,128)(2,1)S(1)}, bf16[128,2048]{1,0:T(8,128)(2,1)S(1)}, u32[]{:S(2)}, u32[]{:S(2)}) collective-permute-start(bf16[128,2048]{1,0:T(8,128)(2,1)S(1)} %collective-permute-done.11), channel_id=1, source_target_pairs={{0,1},{1,0},{2,3},{3,2},{4,5},{5,4},{6,7},{7,6},{8,9},{9,8},{10,11... | collective-permute-start | bytes 1572872 | tf_op jit(solution)/shard_map/ppermute | solution.py:32
  163.1 159.6 %all-gather.5.cloned.1.call-start = ((), (), s32[]{:S(2)}) async-start(), calls=%async_computation.1 | async-start | bytes 2228224 | tf_op jit(solution)/shard_map/all_gather | solution.py:123
  169.5 13.5 %collective-permute-start.14 = (bf16[128,2048]{1,0:T(8,128)(2,1)S(1)}, bf16[128,2048]{1,0:T(8,128)(2,1)S(1)}, u32[]{:S(2)}, u32[]{:S(2)}) collective-permute-start(bf16[128,2048]{1,0:T(8,128)(2,1)S(1)} %collective-permute-done.13), channel_id=1, source_target_pairs={{0,1},{1,0},{2,3},{3,2},{4,5},{5,4},{6,7},{7,6},{8,9},{9,8},{10,11... | collective-permute-start | bytes 1572872 | tf_op jit(solution)/shard_map/ppermute | solution.py:32
  195.0 15.2 %collective-permute-start.15 = (bf16[128,2048]{1,0:T(8,128)(2,1)S(1)}, bf16[128,2048]{1,0:T(8,128)(2,1)S(1)}, u32[]{:S(2)}, u32[]{:S(2)}) collective-permute-start(bf16[128,2048]{1,0:T(8,128)(2,1)S(1)} %get-tuple-element.99), channel_id=1, source_target_pairs={{0,32},{32,64},{64,96},{1,33},{33,65},{65,97},{2,34},{34,66},{66,9... | collective-permute-start | bytes 1572872 | tf_op jit(solution)/shard_map/ppermute | solution.py:138
  204.0 15.0 %collective-permute-start.17 = (bf16[128,2048]{1,0:T(8,128)(2,1)S(1)}, bf16[128,2048]{1,0:T(8,128)(2,1)S(1)}, u32[]{:S(2)}, u32[]{:S(2)}) collective-permute-start(bf16[128,2048]{1,0:T(8,128)(2,1)S(1)} %get-tuple-element.101), channel_id=1, source_target_pairs={{0,32},{32,64},{64,96},{1,33},{33,65},{65,97},{2,34},{34,66},{66,9... | collective-permute-start | bytes 1572872 | tf_op jit(solution)/shard_map/ppermute | solution.py:138
  210.2 11.8 %collective-permute-start.16 = (bf16[128,2048]{1,0:T(8,128)(2,1)S(1)}, bf16[128,2048]{1,0:T(8,128)(2,1)S(1)}, u32[]{:S(2)}, u32[]{:S(2)}) collective-permute-start(bf16[128,2048]{1,0:T(8,128)(2,1)S(1)} %collective-permute-done.15), channel_id=1, source_target_pairs={{0,1},{1,0},{2,3},{3,2},{4,5},{5,4},{6,7},{7,6},{8,9},{9,8},{10,11... | collective-permute-start | bytes 1572872 | tf_op jit(solution)/shard_map/ppermute | solution.py:32
  219.0 14.3 %collective-permute-start.18 = (bf16[128,2048]{1,0:T(8,128)(2,1)S(1)}, bf16[128,2048]{1,0:T(8,128)(2,1)S(1)}, u32[]{:S(2)}, u32[]{:S(2)}) collective-permute-start(bf16[128,2048]{1,0:T(8,128)(2,1)S(1)} %collective-permute-done.17), channel_id=1, source_target_pairs={{0,1},{1,0},{2,3},{3,2},{4,5},{5,4},{6,7},{7,6},{8,9},{9,8},{10,11... | collective-permute-start | bytes 1572872 | tf_op jit(solution)/shard_map/ppermute | solution.py:32
  245.4 15.6 %collective-permute-start.19 = (bf16[128,2048]{1,0:T(8,128)(2,1)S(1)}, bf16[128,2048]{1,0:T(8,128)(2,1)}, u32[]{:S(2)}, u32[]{:S(2)}) collective-permute-start(bf16[128,2048]{1,0:T(8,128)(2,1)S(1)} %get-tuple-element.103), channel_id=1, source_target_pairs={{0,32},{32,64},{64,96},{1,33},{33,65},{65,97},{2,34},{34,66},{66,9... | collective-permute-start | bytes 1572872 | tf_op jit(solution)/shard_map/ppermute | solution.py:138
  255.1 14.1 %collective-permute-start.21 = (bf16[128,2048]{1,0:T(8,128)(2,1)S(1)}, bf16[128,2048]{1,0:T(8,128)(2,1)}, u32[]{:S(2)}, u32[]{:S(2)}) collective-permute-start(bf16[128,2048]{1,0:T(8,128)(2,1)S(1)} %get-tuple-element.105), channel_id=1, source_target_pairs={{0,32},{32,64},{64,96},{1,33},{33,65},{65,97},{2,34},{34,66},{66,9... | collective-permute-start | bytes 1572872 | tf_op jit(solution)/shard_map/ppermute | solution.py:138
  261.0 12.7 %collective-permute-start.20 = (bf16[128,2048]{1,0:T(8,128)(2,1)}, bf16[128,2048]{1,0:T(8,128)(2,1)}, u32[]{:S(2)}, u32[]{:S(2)}) collective-permute-start(bf16[128,2048]{1,0:T(8,128)(2,1)} %collective-permute-done.19), channel_id=1, source_target_pairs={{0,1},{1,0},{2,3},{3,2},{4,5},{5,4},{6,7},{7,6},{8,9},{9,8},{10,11... | collective-permute-start | bytes 1572872 | tf_op jit(solution)/shard_map/ppermute | solution.py:32
  269.2 13.3 %collective-permute-start.22 = (bf16[128,2048]{1,0:T(8,128)(2,1)}, bf16[128,2048]{1,0:T(8,128)(2,1)}, u32[]{:S(2)}, u32[]{:S(2)}) collective-permute-start(bf16[128,2048]{1,0:T(8,128)(2,1)} %collective-permute-done.21), channel_id=1, source_target_pairs={{0,1},{1,0},{2,3},{3,2},{4,5},{5,4},{6,7},{7,6},{8,9},{9,8},{10,11... | collective-permute-start | bytes 1572872 | tf_op jit(solution)/shard_map/ppermute | solution.py:32
  295.7 16.3 %collective-permute-start.23 = (bf16[128,2048]{1,0:T(8,128)(2,1)S(1)}, bf16[128,2048]{1,0:T(8,128)(2,1)S(1)}, u32[]{:S(2)}, u32[]{:S(2)}) collective-permute-start(bf16[128,2048]{1,0:T(8,128)(2,1)S(1)} %get-tuple-element.107), channel_id=1, source_target_pairs={{0,32},{32,64},{64,96},{1,33},{33,65},{65,97},{2,34},{34,66},{66,9... | collective-permute-start | bytes 1572872 | tf_op jit(solution)/shard_map/ppermute | solution.py:138
  305.2 15.4 %collective-permute-start.25 = (bf16[128,2048]{1,0:T(8,128)(2,1)}, bf16[128,2048]{1,0:T(8,128)(2,1)}, u32[]{:S(2)}, u32[]{:S(2)}) collective-permute-start(bf16[128,2048]{1,0:T(8,128)(2,1)} %get-tuple-element.109), channel_id=1, source_target_pairs={{0,32},{32,64},{64,96},{1,33},{33,65},{65,97},{2,34},{34,66},{66,9... | collective-permute-start | bytes 1572872 | tf_op jit(solution)/shard_map/ppermute | solution.py:138
  312.0 13.2 %collective-permute-start.24 = (bf16[128,2048]{1,0:T(8,128)(2,1)S(1)}, bf16[128,2048]{1,0:T(8,128)(2,1)}, u32[]{:S(2)}, u32[]{:S(2)}) collective-permute-start(bf16[128,2048]{1,0:T(8,128)(2,1)S(1)} %collective-permute-done.23), channel_id=1, source_target_pairs={{0,1},{1,0},{2,3},{3,2},{4,5},{5,4},{6,7},{7,6},{8,9},{9,8},{10,11... | collective-permute-start | bytes 1572872 | tf_op jit(solution)/shard_map/ppermute | solution.py:32
  320.7 11.9 %collective-permute-start.26 = (bf16[128,2048]{1,0:T(8,128)(2,1)}, bf16[128,2048]{1,0:T(8,128)(2,1)}, u32[]{:S(2)}, u32[]{:S(2)}) collective-permute-start(bf16[128,2048]{1,0:T(8,128)(2,1)} %collective-permute-done.25), channel_id=1, source_target_pairs={{0,1},{1,0},{2,3},{3,2},{4,5},{5,4},{6,7},{7,6},{8,9},{9,8},{10,11... | collective-permute-start | bytes 1572872 | tf_op jit(solution)/shard_map/ppermute | solution.py:32
  356.3 9.9 %collective-permute-start.28 = (f32[1024,128]{0,1:T(8,128)S(1)}, f32[1024,128]{0,1:T(8,128)S(1)}, u32[]{:S(2)}, u32[]{:S(2)}) collective-permute-start(f32[1024,128]{0,1:T(8,128)S(1)} %fusion.32), channel_id=1, source_target_pairs={{0,1},{1,0},{2,3},{3,2},{4,5},{5,4},{6,7},{7,6},{8,9},{9,8},{10,11... | collective-permute-start | bytes 1572872 | tf_op jit(solution)/shard_map/ppermute | solution.py:32
  398.5 9.5 %collective-permute-start.48 = (f32[4,2,2,32,128]{4,3,2,1,0:T(8,128)S(1)}, f32[4,2,2,32,128]{4,3,2,1,0:T(8,128)S(1)}, u32[]{:S(2)}, u32[]{:S(2)}) collective-permute-start(f32[4,2,2,32,128]{4,3,2,1,0:T(8,128)S(1)} %dynamic-slice_bitcast_fusion.2), channel_id=1, source_target_pairs={{0,8},{2,10},{4,12},{6,14},{8,16},{10,18},{12,20},{14,22},{16,24},... | collective-permute-start | bytes 786440 | tf_op jit(solution)/shard_map/ppermute | solution.py:36
  401.9 9.5 %collective-permute-start.33 = (f32[4,2,2,32,128]{4,3,2,1,0:T(8,128)S(1)}, f32[4,2,2,32,128]{4,3,2,1,0:T(8,128)S(1)}, u32[]{:S(2)}, u32[]{:S(2)}) collective-permute-start(f32[4,2,2,32,128]{4,3,2,1,0:T(8,128)S(1)} %dynamic-slice_bitcast_fusion.4), channel_id=1, source_target_pairs={{0,32},{32,64},{64,96},{96,0},{1,33},{33,65},{65,97},{97,1},{2,34}... | collective-permute-start | bytes 786440 | tf_op jit(solution)/shard_map/ppermute | solution.py:32
  (75 other events, 733.4 us)
Sparse Core Ops, SparseCore 0:
  163.3 52.3 all-gather.2
  218.1 47.9 all-gather.4

commit v7 on v2

--- a/solution.py
+++ b/solution.py
@@ -2,6 +2,8 @@
 import jax.numpy as jnp
 from jax import lax
 from jax.sharding import PartitionSpec as P
+from jax.experimental import pallas as pl
+from jax.experimental.pallas import tpu as pltpu
 
 LEVELS = 64
 
@@ -26,6 +28,29 @@
     vocab_size = logprob.shape[-1]
     column = jnp.arange(vocab_size, dtype=jnp.int32)
     return jnp.sum(jnp.where(column[None, :] == targets[:, None], logprob, 0.0), axis=-1)
+
+
+def stage_kernel(normed_ref, weight_ref, own_ref, out_ref):
+    update = jnp.dot(normed_ref[...], weight_ref[...], preferred_element_type=jnp.float32)
+    out_ref[...] = (own_ref[...].astype(jnp.float32) + update).astype(out_ref.dtype)
+
+
+def stage_product(normed, weight, own):
+    rows, depth = normed.shape
+    width = weight.shape[1]
+    tile = min(width, 256)
+    return pl.pallas_call(
+        stage_kernel,
+        grid=(width // tile,),
+        in_specs=[
+            pl.BlockSpec((rows, depth), lambda j: (0, 0)),
+            pl.BlockSpec((depth, tile), lambda j: (0, j)),
+            pl.BlockSpec((rows, tile), lambda j: (0, j)),
+        ],
+        out_specs=pl.BlockSpec((rows, tile), lambda j: (0, j)),
+        out_shape=jax.ShapeDtypeStruct((rows, width), jnp.bfloat16),
+        compiler_params=pltpu.CompilerParams(vmem_limit_bytes=32 * 1024 * 1024),
+    )(normed, weight, own)
 
 
 def shifted(x, axis, size, by):
@@ -126,9 +151,8 @@
     def apply_segment(current):
         wide_rows = current.astype(jnp.float32)
         normed = (wide_rows * rms_scale(wide_rows) * gain_local).astype(jnp.bfloat16)
-        update = jnp.dot(normed, weight_local, preferred_element_type=jnp.float32)
-        own_half = lax.dynamic_slice_in_dim(wide_rows, rep_pos * half_width, half_width, 1)
-        return (own_half + update).astype(jnp.bfloat16)
+        own_half = lax.dynamic_slice_in_dim(current, rep_pos * half_width, half_width, 1)
+        return stage_product(normed, weight_local, own_half)
 
     embedded_all = lookup_rows(flat_ids, embed_table)
 

time: 471 us -> 504 us (1.070)
  matrix products: 155 us -> 22.8 us
  Pallas kernels: 0 us -> 131 us
  waiting for transfers between devices: 122 us -> 101 us
  starting transfers between devices: 111 us -> 130 us
  other arithmetic: 49.5 us -> 68.3 us
  local copies, waits for them, and re-layouts: 12.6 us -> 27.9 us
    dot_general x14 -> x0, matrix products: 132 us -> none  [apply_segment(): update = jnp.dot(normed, weight_local, preferred_element_type=jnp.float32)]
    pallas_call x0 -> x14, Pallas kernels: none -> 131 us  [stage_product(): pl.pallas_call(stage_kernel, grid=(width // tile,), in_specs=[pl.BlockSpe...]
    dynamic_update_slice x0 -> x14, other arithmetic: none -> 27.8 us  [tick_whole(): lax.dynamic_update_slice_in_dim(stored, chosen, slot_pos * block_rows, 0)]
    ppermute x14, starting transfers between devices: 49.6 us -> 74 us  [tick_whole(): lax.ppermute(computed, 'segment', [(i, i + 1) for i in range(segments - 1)])]
    ppermute x33, waiting for transfers between devices: 111 us -> 87.9 us  [shifted(): return lax.ppermute(x, axis, [(i, (i + by) % size) for i in range(size)])]
    while x14 -> x0, other arithmetic: 14.1 us -> none
    while x14, local copies, waits for them, and re-layouts: 0.57 us -> 14.6 us
  transfers between devices with their start and end apart: 65 -> 65, of which waited for: 28 -> 30; matrix products, arithmetic and copies ran while one was open for 44% -> 22% of each run, Pallas kernels for 0% -> 26%
where the time goes in v7:
time: 504 us; the launch traced here: 500 us
  Pallas kernels  131 us (26%)
  starting transfers between devices  130 us (26%)
  waiting for transfers between devices  101 us (20%)
  other arithmetic  68.3 us (14%)
  local copies, waits for them, and re-layouts  27.9 us (6%)
  matrix products  22.8 us (5%)
  between operations  18 us (4%)
    pallas_call x14, Pallas kernels, stage_product(): pl.pallas_call(stage_kernel, grid=(width // tile,), in_specs=[pl.BlockSpe...  131 us
    ppermute x33, waiting for transfers between devices, shifted(): return lax.ppermute(x, axis, [(i, (i + by) % size) for i in range(size)])  87.9 us
    ppermute x14, starting transfers between devices, tick_whole(): lax.ppermute(computed, 'segment', [(i, i + 1) for i in range(segments - 1)])  74 us
    ppermute x33, starting transfers between devices, shifted(): return lax.ppermute(x, axis, [(i, (i + by) % size) for i in range(size)])  33.1 us
    dynamic_update_slice x14, other arithmetic, tick_whole(): lax.dynamic_update_slice_in_dim(stored, chosen, slot_pos * block_rows, 0)  27.8 us
    reduce_sum x14, other arithmetic, rms_scale(): squares = jnp.mean(values * values, axis=-1, keepdims=True)  23.7 us
    ppermute x16, starting transfers between devices, fsdp_moved(): return lax.ppermute(x, 'fsdp', [(f, mapping(f)) for f in range(16)])  22.7 us
    while x14, local copies, waits for them, and re-layouts  14.6 us
  transfers between devices with their start and end apart: 65, of which 30 were waited for; matrix products, arithmetic and copies ran while one was open for 22% of the time, Pallas kernels for 26%

profile of v7, /device:TPU:0, one launch (start us, length us, event | category | flops | bytes accessed | tf_op | source)
XLA Modules:
  0.0 499.7 jit_solution(14635390797845625232)
XLA Ops:
  8.7 6.3 %convolution_convert_fusion = bf16[1024,4096]{1,0:T(8,128)(2,1)} fusion(bf16[128,4096]{1,0:T(8,128)(2,1)S(1)} %copy-done, s32[1024]{0:T(1024)} %bitcast.141), kind=kOutput, calls=%fused_computation.16 | convolution fusion | flops 1078067200 | bytes 9441280 | tf_op jit(solution)/shard_map/dot_general | solution.py:24
  17.7 357.1 %while.19 = (s32[]{:T(128)}, bf16[128,2048]{1,0:T(8,128)(2,1)S(1)}, bf16[128,2048]{1,0:T(8,128)(2,1)S(1)}, bf16[1024,2048]{1,0:T(8,128)(2,1)}, pred[]{:T(512)}, ...) while((s32[]{:T(128)}, bf16[128,2048]{1,0:T(8,128)(2,1)S(1)}, ...), condition=%wide.region_4.5_spmd, body=%wide.region_2.4_spmd.sunk | while | flops 7078029 | bytes 16271726 | solution.py:182
  24.0 9.1 %collective-permute-done.1 = bf16[128,2048]{1,0:T(8,128)(2,1)S(1)} collective-permute-done((bf16[128,2048]{1,0:T(8,128)(2,1)S(1)}, bf16[128,2048]{1,0:T(8,128)(2,1)S(1)}, u32[]{:S(2)}, u32[]{:S(2)}) %collective-permute-start.1) | collective-permute-done | bytes 524320 | tf_op jit(solution)/shard_map/while/body/eval_jaxpr/ppermute | solution.py:57
  35.3 9.3 %eval_jaxpr.7 = bf16[128,2048]{1,0:T(8,128)(2,1)S(1)} custom-call(bf16[128,4096]{1,0:T(8,128)(2,1)S(1)} %fusion.60.normed_ref, bf16[4096,2048]{1,0:T(8,128)(2,1)} %get-tuple-element.454.weight_ref, bf16[128,2048]{1,0:T(8,128)(2,1)S(1)} %constant_dynamic-slice_fusion.7.own_ref), custom_call_target="tpu_custom_call" | custom-call | tf_op jit(solution)/shard_map/while/body/eval_jaxpr/pallas_call | solution.py:42
  53.7 9.0 %collective-permute-done.1 = bf16[128,2048]{1,0:T(8,128)(2,1)S(1)} collective-permute-done((bf16[128,2048]{1,0:T(8,128)(2,1)S(1)}, bf16[128,2048]{1,0:T(8,128)(2,1)S(1)}, u32[]{:S(2)}, u32[]{:S(2)}) %collective-permute-start.1) | collective-permute-done | bytes 524320 | tf_op jit(solution)/shard_map/while/body/eval_jaxpr/ppermute | solution.py:57
  64.9 9.3 %eval_jaxpr.7 = bf16[128,2048]{1,0:T(8,128)(2,1)S(1)} custom-call(bf16[128,4096]{1,0:T(8,128)(2,1)S(1)} %fusion.60.normed_ref, bf16[4096,2048]{1,0:T(8,128)(2,1)} %get-tuple-element.454.weight_ref, bf16[128,2048]{1,0:T(8,128)(2,1)S(1)} %constant_dynamic-slice_fusion.7.own_ref), custom_call_target="tpu_custom_call" | custom-call | tf_op jit(solution)/shard_map/while/body/eval_jaxpr/pallas_call | solution.py:42
  82.0 8.7 %collective-permute-done.1 = bf16[128,2048]{1,0:T(8,128)(2,1)S(1)} collective-permute-done((bf16[128,2048]{1,0:T(8,128)(2,1)S(1)}, bf16[128,2048]{1,0:T(8,128)(2,1)S(1)}, u32[]{:S(2)}, u32[]{:S(2)}) %collective-permute-start.1) | collective-permute-done | bytes 524320 | tf_op jit(solution)/shard_map/while/body/eval_jaxpr/ppermute | solution.py:57
  92.9 9.6 %eval_jaxpr.7 = bf16[128,2048]{1,0:T(8,128)(2,1)S(1)} custom-call(bf16[128,4096]{1,0:T(8,128)(2,1)S(1)} %fusion.60.normed_ref, bf16[4096,2048]{1,0:T(8,128)(2,1)} %get-tuple-element.454.weight_ref, bf16[128,2048]{1,0:T(8,128)(2,1)S(1)} %constant_dynamic-slice_fusion.7.own_ref), custom_call_target="tpu_custom_call" | custom-call | tf_op jit(solution)/shard_map/while/body/eval_jaxpr/pallas_call | solution.py:42
  110.1 7.9 %collective-permute-done.1 = bf16[128,2048]{1,0:T(8,128)(2,1)S(1)} collective-permute-done((bf16[128,2048]{1,0:T(8,128)(2,1)S(1)}, bf16[128,2048]{1,0:T(8,128)(2,1)S(1)}, u32[]{:S(2)}, u32[]{:S(2)}) %collective-permute-start.1) | collective-permute-done | bytes 524320 | tf_op jit(solution)/shard_map/while/body/eval_jaxpr/ppermute | solution.py:57
  120.2 9.3 %eval_jaxpr.7 = bf16[128,2048]{1,0:T(8,128)(2,1)S(1)} custom-call(bf16[128,4096]{1,0:T(8,128)(2,1)S(1)} %fusion.60.normed_ref, bf16[4096,2048]{1,0:T(8,128)(2,1)} %get-tuple-element.454.weight_ref, bf16[128,2048]{1,0:T(8,128)(2,1)S(1)} %constant_dynamic-slice_fusion.7.own_ref), custom_call_target="tpu_custom_call" | custom-call | tf_op jit(solution)/shard_map/while/body/eval_jaxpr/pallas_call | solution.py:42
  137.4 6.8 %collective-permute-done.1 = bf16[128,2048]{1,0:T(8,128)(2,1)S(1)} collective-permute-done((bf16[128,2048]{1,0:T(8,128)(2,1)S(1)}, bf16[128,2048]{1,0:T(8,128)(2,1)S(1)}, u32[]{:S(2)}, u32[]{:S(2)}) %collective-permute-start.1) | collective-permute-done | bytes 524320 | tf_op jit(solution)/shard_map/while/body/eval_jaxpr/ppermute | solution.py:57
  146.4 9.3 %eval_jaxpr.7 = bf16[128,2048]{1,0:T(8,128)(2,1)S(1)} custom-call(bf16[128,4096]{1,0:T(8,128)(2,1)S(1)} %fusion.60.normed_ref, bf16[4096,2048]{1,0:T(8,128)(2,1)} %get-tuple-element.454.weight_ref, bf16[128,2048]{1,0:T(8,128)(2,1)S(1)} %constant_dynamic-slice_fusion.7.own_ref), custom_call_target="tpu_custom_call" | custom-call | tf_op jit(solution)/shard_map/while/body/eval_jaxpr/pallas_call | solution.py:42
  163.9 5.6 %collective-permute-done.1 = bf16[128,2048]{1,0:T(8,128)(2,1)S(1)} collective-permute-done((bf16[128,2048]{1,0:T(8,128)(2,1)S(1)}, bf16[128,2048]{1,0:T(8,128)(2,1)S(1)}, u32[]{:S(2)}, u32[]{:S(2)}) %collective-permute-start.1) | collective-permute-done | bytes 524320 | tf_op jit(solution)/shard_map/while/body/eval_jaxpr/ppermute | solution.py:57
  171.8 9.3 %eval_jaxpr.7 = bf16[128,2048]{1,0:T(8,128)(2,1)S(1)} custom-call(bf16[128,4096]{1,0:T(8,128)(2,1)S(1)} %fusion.60.normed_ref, bf16[4096,2048]{1,0:T(8,128)(2,1)} %get-tuple-element.454.weight_ref, bf16[128,2048]{1,0:T(8,128)(2,1)S(1)} %constant_dynamic-slice_fusion.7.own_ref), custom_call_target="tpu_custom_call" | custom-call | tf_op jit(solution)/shard_map/while/body/eval_jaxpr/pallas_call | solution.py:42
  184.5 5.2 %collective-permute-start = (bf16[128,2048]{1,0:T(8,128)(2,1)S(1)}, bf16[128,2048]{1,0:T(8,128)(2,1)}, u32[]{:S(2)}, u32[]{:S(2)}) collective-permute-start(bf16[128,2048]{1,0:T(8,128)(2,1)S(1)} %copy.28), channel_id=1, source_target_pairs={{0,32},{32,64},{64,96},{1,33},{33,65},{65,97},{2,34},{34,66},{66,9... | collective-permute-start | bytes 1572872 | tf_op jit(solution)/shard_map/while/body/eval_jaxpr/ppermute | solution.py:162
  196.2 9.3 %eval_jaxpr.7 = bf16[128,2048]{1,0:T(8,128)(2,1)S(1)} custom-call(bf16[128,4096]{1,0:T(8,128)(2,1)S(1)} %fusion.60.normed_ref, bf16[4096,2048]{1,0:T(8,128)(2,1)} %get-tuple-element.454.weight_ref, bf16[128,2048]{1,0:T(8,128)(2,1)S(1)} %constant_dynamic-slice_fusion.7.own_ref), custom_call_target="tpu_custom_call" | custom-call | tf_op jit(solution)/shard_map/while/body/eval_jaxpr/pallas_call | solution.py:42
  209.1 5.7 %collective-permute-start = (bf16[128,2048]{1,0:T(8,128)(2,1)S(1)}, bf16[128,2048]{1,0:T(8,128)(2,1)}, u32[]{:S(2)}, u32[]{:S(2)}) collective-permute-start(bf16[128,2048]{1,0:T(8,128)(2,1)S(1)} %copy.28), channel_id=1, source_target_pairs={{0,32},{32,64},{64,96},{1,33},{33,65},{65,97},{2,34},{34,66},{66,9... | collective-permute-start | bytes 1572872 | tf_op jit(solution)/shard_map/while/body/eval_jaxpr/ppermute | solution.py:162
  220.0 9.3 %eval_jaxpr.7 = bf16[128,2048]{1,0:T(8,128)(2,1)S(1)} custom-call(bf16[128,4096]{1,0:T(8,128)(2,1)S(1)} %fusion.60.normed_ref, bf16[4096,2048]{1,0:T(8,128)(2,1)} %get-tuple-element.454.weight_ref, bf16[128,2048]{1,0:T(8,128)(2,1)S(1)} %constant_dynamic-slice_fusion.7.own_ref), custom_call_target="tpu_custom_call" | custom-call | tf_op jit(solution)/shard_map/while/body/eval_jaxpr/pallas_call | solution.py:42
  232.8 6.1 %collective-permute-start = (bf16[128,2048]{1,0:T(8,128)(2,1)S(1)}, bf16[128,2048]{1,0:T(8,128)(2,1)}, u32[]{:S(2)}, u32[]{:S(2)}) collective-permute-start(bf16[128,2048]{1,0:T(8,128)(2,1)S(1)} %copy.28), channel_id=1, source_target_pairs={{0,32},{32,64},{64,96},{1,33},{33,65},{65,97},{2,34},{34,66},{66,9... | collective-permute-start | bytes 1572872 | tf_op jit(solution)/shard_map/while/body/eval_jaxpr/ppermute | solution.py:162
  243.7 9.3 %eval_jaxpr.7 = bf16[128,2048]{1,0:T(8,128)(2,1)S(1)} custom-call(bf16[128,4096]{1,0:T(8,128)(2,1)S(1)} %fusion.60.normed_ref, bf16[4096,2048]{1,0:T(8,128)(2,1)} %get-tuple-element.454.weight_ref, bf16[128,2048]{1,0:T(8,128)(2,1)S(1)} %constant_dynamic-slice_fusion.7.own_ref), custom_call_target="tpu_custom_call" | custom-call | tf_op jit(solution)/shard_map/while/body/eval_jaxpr/pallas_call | solution.py:42
  256.6 6.1 %collective-permute-start = (bf16[128,2048]{1,0:T(8,128)(2,1)S(1)}, bf16[128,2048]{1,0:T(8,128)(2,1)}, u32[]{:S(2)}, u32[]{:S(2)}) collective-permute-start(bf16[128,2048]{1,0:T(8,128)(2,1)S(1)} %copy.28), channel_id=1, source_target_pairs={{0,32},{32,64},{64,96},{1,33},{33,65},{65,97},{2,34},{34,66},{66,9... | collective-permute-start | bytes 1572872 | tf_op jit(solution)/shard_map/while/body/eval_jaxpr/ppermute | solution.py:162
  267.4 9.3 %eval_jaxpr.7 = bf16[128,2048]{1,0:T(8,128)(2,1)S(1)} custom-call(bf16[128,4096]{1,0:T(8,128)(2,1)S(1)} %fusion.60.normed_ref, bf16[4096,2048]{1,0:T(8,128)(2,1)} %get-tuple-element.454.weight_ref, bf16[128,2048]{1,0:T(8,128)(2,1)S(1)} %constant_dynamic-slice_fusion.7.own_ref), custom_call_target="tpu_custom_call" | custom-call | tf_op jit(solution)/shard_map/while/body/eval_jaxpr/pallas_call | solution.py:42
  280.3 6.1 %collective-permute-start = (bf16[128,2048]{1,0:T(8,128)(2,1)S(1)}, bf16[128,2048]{1,0:T(8,128)(2,1)}, u32[]{:S(2)}, u32[]{:S(2)}) collective-permute-start(bf16[128,2048]{1,0:T(8,128)(2,1)S(1)} %copy.28), channel_id=1, source_target_pairs={{0,32},{32,64},{64,96},{1,33},{33,65},{65,97},{2,34},{34,66},{66,9... | collective-permute-start | bytes 1572872 | tf_op jit(solution)/shard_map/while/body/eval_jaxpr/ppermute | solution.py:162
  291.2 9.3 %eval_jaxpr.7 = bf16[128,2048]{1,0:T(8,128)(2,1)S(1)} custom-call(bf16[128,4096]{1,0:T(8,128)(2,1)S(1)} %fusion.60.normed_ref, bf16[4096,2048]{1,0:T(8,128)(2,1)} %get-tuple-element.454.weight_ref, bf16[128,2048]{1,0:T(8,128)(2,1)S(1)} %constant_dynamic-slice_fusion.7.own_ref), custom_call_target="tpu_custom_call" | custom-call | tf_op jit(solution)/shard_map/while/body/eval_jaxpr/pallas_call | solution.py:42
  304.0 6.1 %collective-permute-start = (bf16[128,2048]{1,0:T(8,128)(2,1)S(1)}, bf16[128,2048]{1,0:T(8,128)(2,1)}, u32[]{:S(2)}, u32[]{:S(2)}) collective-permute-start(bf16[128,2048]{1,0:T(8,128)(2,1)S(1)} %copy.28), channel_id=1, source_target_pairs={{0,32},{32,64},{64,96},{1,33},{33,65},{65,97},{2,34},{34,66},{66,9... | collective-permute-start | bytes 1572872 | tf_op jit(solution)/shard_map/while/body/eval_jaxpr/ppermute | solution.py:162
  314.9 9.3 %eval_jaxpr.7 = bf16[128,2048]{1,0:T(8,128)(2,1)S(1)} custom-call(bf16[128,4096]{1,0:T(8,128)(2,1)S(1)} %fusion.60.normed_ref, bf16[4096,2048]{1,0:T(8,128)(2,1)} %get-tuple-element.454.weight_ref, bf16[128,2048]{1,0:T(8,128)(2,1)S(1)} %constant_dynamic-slice_fusion.7.own_ref), custom_call_target="tpu_custom_call" | custom-call | tf_op jit(solution)/shard_map/while/body/eval_jaxpr/pallas_call | solution.py:42
  327.8 6.1 %collective-permute-start = (bf16[128,2048]{1,0:T(8,128)(2,1)S(1)}, bf16[128,2048]{1,0:T(8,128)(2,1)}, u32[]{:S(2)}, u32[]{:S(2)}) collective-permute-start(bf16[128,2048]{1,0:T(8,128)(2,1)S(1)} %copy.28), channel_id=1, source_target_pairs={{0,32},{32,64},{64,96},{1,33},{33,65},{65,97},{2,34},{34,66},{66,9... | collective-permute-start | bytes 1572872 | tf_op jit(solution)/shard_map/while/body/eval_jaxpr/ppermute | solution.py:162
  338.6 9.3 %eval_jaxpr.7 = bf16[128,2048]{1,0:T(8,128)(2,1)S(1)} custom-call(bf16[128,4096]{1,0:T(8,128)(2,1)S(1)} %fusion.60.normed_ref, bf16[4096,2048]{1,0:T(8,128)(2,1)} %get-tuple-element.454.weight_ref, bf16[128,2048]{1,0:T(8,128)(2,1)S(1)} %constant_dynamic-slice_fusion.7.own_ref), custom_call_target="tpu_custom_call" | custom-call | tf_op jit(solution)/shard_map/while/body/eval_jaxpr/pallas_call | solution.py:42
  351.5 6.1 %collective-permute-start = (bf16[128,2048]{1,0:T(8,128)(2,1)S(1)}, bf16[128,2048]{1,0:T(8,128)(2,1)}, u32[]{:S(2)}, u32[]{:S(2)}) collective-permute-start(bf16[128,2048]{1,0:T(8,128)(2,1)S(1)} %copy.28), channel_id=1, source_target_pairs={{0,32},{32,64},{64,96},{1,33},{33,65},{65,97},{2,34},{34,66},{66,9... | collective-permute-start | bytes 1572872 | tf_op jit(solution)/shard_map/while/body/eval_jaxpr/ppermute | solution.py:162
  362.4 9.3 %eval_jaxpr.7 = bf16[128,2048]{1,0:T(8,128)(2,1)S(1)} custom-call(bf16[128,4096]{1,0:T(8,128)(2,1)S(1)} %fusion.60.normed_ref, bf16[4096,2048]{1,0:T(8,128)(2,1)} %get-tuple-element.454.weight_ref, bf16[128,2048]{1,0:T(8,128)(2,1)S(1)} %constant_dynamic-slice_fusion.7.own_ref), custom_call_target="tpu_custom_call" | custom-call | tf_op jit(solution)/shard_map/while/body/eval_jaxpr/pallas_call | solution.py:42
  386.7 8.0 %collective-permute-done.3 = f32[1024,128]{0,1:T(8,128)S(1)} collective-permute-done((f32[1024,128]{0,1:T(8,128)S(1)}, f32[1024,128]{0,1:T(8,128)S(1)}, u32[]{:S(2)}, u32[]{:S(2)}) %collective-permute-start.3) | collective-permute-done | bytes 524320 | tf_op jit(solution)/shard_map/ppermute | solution.py:57
  420.1 5.5 %fusion.12 = f32[4096,256]{1,0:T(8,128)} fusion(bf16[128,4096]{1,0:T(8,128)(2,1)} %copy-done.2, bf16[4096,256]{1,0:T(8,128)(2,1)} %all-gather.5.cloned.1.call-done, f32[128,4096]{1,0:T(8,128)S(1)} %get-tuple-element.320, f32[128]{0:T(128)S(1)} %add_rsqrt_fusion.3), kind=kOutput, calls=%fused_computation.37 | convolution fusion | flops 537952256 | bytes 9437696 | tf_op jit(solution)/shard_map/dot_general | solution.py:254
  (336 shorter events, 235.6 us)
Async XLA Ops:
  7.2 399.4 %all-gather.3.cloned.1.call-start = ((), (), s32[]{:S(2)}) async-start(), calls=%async_computation | async-start | bytes 2228224 | tf_op jit(solution)/shard_map/all_gather | solution.py:147
  7.9 400.8 %all-gather.5.cloned.1.call-start = ((), (), s32[]{:S(2)}) async-start(), calls=%async_computation.1 | async-start | bytes 2228224 | tf_op jit(solution)/shard_map/all_gather | solution.py:148
  17.7 15.4 %collective-permute-start.1 = (bf16[128,2048]{1,0:T(8,128)(2,1)S(1)}, bf16[128,2048]{1,0:T(8,128)(2,1)S(1)}, u32[]{:S(2)}, u32[]{:S(2)}) collective-permute-start(bf16[128,2048]{1,0:T(8,128)(2,1)S(1)} %get-tuple-element.427), channel_id=1, source_target_pairs={{0,1},{1,0},{2,3},{3,2},{4,5},{5,4},{6,7},{7,6},{8,9},{9,8},{10,11... | collective-permute-start | bytes 1572872 | tf_op jit(solution)/shard_map/while/body/eval_jaxpr/ppermute | solution.py:57
  19.8 26.8 %collective-permute-start = (bf16[128,2048]{1,0:T(8,128)(2,1)S(1)}, bf16[128,2048]{1,0:T(8,128)(2,1)}, u32[]{:S(2)}, u32[]{:S(2)}) collective-permute-start(bf16[128,2048]{1,0:T(8,128)(2,1)S(1)} %copy.28), channel_id=1, source_target_pairs={{0,32},{32,64},{64,96},{1,33},{33,65},{65,97},{2,34},{34,66},{66,9... | collective-permute-start | bytes 1572872 | tf_op jit(solution)/shard_map/while/body/eval_jaxpr/ppermute | solution.py:162
  47.7 15.0 %collective-permute-start.1 = (bf16[128,2048]{1,0:T(8,128)(2,1)S(1)}, bf16[128,2048]{1,0:T(8,128)(2,1)S(1)}, u32[]{:S(2)}, u32[]{:S(2)}) collective-permute-start(bf16[128,2048]{1,0:T(8,128)(2,1)S(1)} %get-tuple-element.427), channel_id=1, source_target_pairs={{0,1},{1,0},{2,3},{3,2},{4,5},{5,4},{6,7},{7,6},{8,9},{9,8},{10,11... | collective-permute-start | bytes 1572872 | tf_op jit(solution)/shard_map/while/body/eval_jaxpr/ppermute | solution.py:57
  49.5 26.7 %collective-permute-start = (bf16[128,2048]{1,0:T(8,128)(2,1)S(1)}, bf16[128,2048]{1,0:T(8,128)(2,1)}, u32[]{:S(2)}, u32[]{:S(2)}) collective-permute-start(bf16[128,2048]{1,0:T(8,128)(2,1)S(1)} %copy.28), channel_id=1, source_target_pairs={{0,32},{32,64},{64,96},{1,33},{33,65},{65,97},{2,34},{34,66},{66,9... | collective-permute-start | bytes 1572872 | tf_op jit(solution)/shard_map/while/body/eval_jaxpr/ppermute | solution.py:162
  77.2 13.4 %collective-permute-start.1 = (bf16[128,2048]{1,0:T(8,128)(2,1)S(1)}, bf16[128,2048]{1,0:T(8,128)(2,1)S(1)}, u32[]{:S(2)}, u32[]{:S(2)}) collective-permute-start(bf16[128,2048]{1,0:T(8,128)(2,1)S(1)} %get-tuple-element.427), channel_id=1, source_target_pairs={{0,1},{1,0},{2,3},{3,2},{4,5},{5,4},{6,7},{7,6},{8,9},{9,8},{10,11... | collective-permute-start | bytes 1572872 | tf_op jit(solution)/shard_map/while/body/eval_jaxpr/ppermute | solution.py:57
  77.5 26.9 %collective-permute-start = (bf16[128,2048]{1,0:T(8,128)(2,1)S(1)}, bf16[128,2048]{1,0:T(8,128)(2,1)}, u32[]{:S(2)}, u32[]{:S(2)}) collective-permute-start(bf16[128,2048]{1,0:T(8,128)(2,1)S(1)} %copy.28), channel_id=1, source_target_pairs={{0,32},{32,64},{64,96},{1,33},{33,65},{65,97},{2,34},{34,66},{66,9... | collective-permute-start | bytes 1572872 | tf_op jit(solution)/shard_map/while/body/eval_jaxpr/ppermute | solution.py:162
  105.5 12.5 %collective-permute-start.1 = (bf16[128,2048]{1,0:T(8,128)(2,1)S(1)}, bf16[128,2048]{1,0:T(8,128)(2,1)S(1)}, u32[]{:S(2)}, u32[]{:S(2)}) collective-permute-start(bf16[128,2048]{1,0:T(8,128)(2,1)S(1)} %get-tuple-element.427), channel_id=1, source_target_pairs={{0,1},{1,0},{2,3},{3,2},{4,5},{5,4},{6,7},{7,6},{8,9},{9,8},{10,11... | collective-permute-start | bytes 1572872 | tf_op jit(solution)/shard_map/while/body/eval_jaxpr/ppermute | solution.py:57
  105.8 25.8 %collective-permute-start = (bf16[128,2048]{1,0:T(8,128)(2,1)S(1)}, bf16[128,2048]{1,0:T(8,128)(2,1)}, u32[]{:S(2)}, u32[]{:S(2)}) collective-permute-start(bf16[128,2048]{1,0:T(8,128)(2,1)S(1)} %copy.28), channel_id=1, source_target_pairs={{0,32},{32,64},{64,96},{1,33},{33,65},{65,97},{2,34},{34,66},{66,9... | collective-permute-start | bytes 1572872 | tf_op jit(solution)/shard_map/while/body/eval_jaxpr/ppermute | solution.py:162
  132.6 11.7 %collective-permute-start.1 = (bf16[128,2048]{1,0:T(8,128)(2,1)S(1)}, bf16[128,2048]{1,0:T(8,128)(2,1)S(1)}, u32[]{:S(2)}, u32[]{:S(2)}) collective-permute-start(bf16[128,2048]{1,0:T(8,128)(2,1)S(1)} %get-tuple-element.427), channel_id=1, source_target_pairs={{0,1},{1,0},{2,3},{3,2},{4,5},{5,4},{6,7},{7,6},{8,9},{9,8},{10,11... | collective-permute-start | bytes 1572872 | tf_op jit(solution)/shard_map/while/body/eval_jaxpr/ppermute | solution.py:57
  132.9 24.8 %collective-permute-start = (bf16[128,2048]{1,0:T(8,128)(2,1)S(1)}, bf16[128,2048]{1,0:T(8,128)(2,1)}, u32[]{:S(2)}, u32[]{:S(2)}) collective-permute-start(bf16[128,2048]{1,0:T(8,128)(2,1)S(1)} %copy.28), channel_id=1, source_target_pairs={{0,32},{32,64},{64,96},{1,33},{33,65},{65,97},{2,34},{34,66},{66,9... | collective-permute-start | bytes 1572872 | tf_op jit(solution)/shard_map/while/body/eval_jaxpr/ppermute | solution.py:162
  158.8 10.8 %collective-permute-start.1 = (bf16[128,2048]{1,0:T(8,128)(2,1)S(1)}, bf16[128,2048]{1,0:T(8,128)(2,1)S(1)}, u32[]{:S(2)}, u32[]{:S(2)}) collective-permute-start(bf16[128,2048]{1,0:T(8,128)(2,1)S(1)} %get-tuple-element.427), channel_id=1, source_target_pairs={{0,1},{1,0},{2,3},{3,2},{4,5},{5,4},{6,7},{7,6},{8,9},{9,8},{10,11... | collective-permute-start | bytes 1572872 | tf_op jit(solution)/shard_map/while/body/eval_jaxpr/ppermute | solution.py:57
  159.2 23.9 %collective-permute-start = (bf16[128,2048]{1,0:T(8,128)(2,1)S(1)}, bf16[128,2048]{1,0:T(8,128)(2,1)}, u32[]{:S(2)}, u32[]{:S(2)}) collective-permute-start(bf16[128,2048]{1,0:T(8,128)(2,1)S(1)} %copy.28), channel_id=1, source_target_pairs={{0,32},{32,64},{64,96},{1,33},{33,65},{65,97},{2,34},{34,66},{66,9... | collective-permute-start | bytes 1572872 | tf_op jit(solution)/shard_map/while/body/eval_jaxpr/ppermute | solution.py:162
  184.1 10.0 %collective-permute-start.1 = (bf16[128,2048]{1,0:T(8,128)(2,1)S(1)}, bf16[128,2048]{1,0:T(8,128)(2,1)S(1)}, u32[]{:S(2)}, u32[]{:S(2)}) collective-permute-start(bf16[128,2048]{1,0:T(8,128)(2,1)S(1)} %get-tuple-element.427), channel_id=1, source_target_pairs={{0,1},{1,0},{2,3},{3,2},{4,5},{5,4},{6,7},{7,6},{8,9},{9,8},{10,11... | collective-permute-start | bytes 1572872 | tf_op jit(solution)/shard_map/while/body/eval_jaxpr/ppermute | solution.py:57
  184.5 23.0 %collective-permute-start = (bf16[128,2048]{1,0:T(8,128)(2,1)S(1)}, bf16[128,2048]{1,0:T(8,128)(2,1)}, u32[]{:S(2)}, u32[]{:S(2)}) collective-permute-start(bf16[128,2048]{1,0:T(8,128)(2,1)S(1)} %copy.28), channel_id=1, source_target_pairs={{0,32},{32,64},{64,96},{1,33},{33,65},{65,97},{2,34},{34,66},{66,9... | collective-permute-start | bytes 1572872 | tf_op jit(solution)/shard_map/while/body/eval_jaxpr/ppermute | solution.py:162
  208.6 9.2 %collective-permute-start.1 = (bf16[128,2048]{1,0:T(8,128)(2,1)S(1)}, bf16[128,2048]{1,0:T(8,128)(2,1)S(1)}, u32[]{:S(2)}, u32[]{:S(2)}) collective-permute-start(bf16[128,2048]{1,0:T(8,128)(2,1)S(1)} %get-tuple-element.427), channel_id=1, source_target_pairs={{0,1},{1,0},{2,3},{3,2},{4,5},{5,4},{6,7},{7,6},{8,9},{9,8},{10,11... | collective-permute-start | bytes 1572872 | tf_op jit(solution)/shard_map/while/body/eval_jaxpr/ppermute | solution.py:57
  209.1 22.2 %collective-permute-start = (bf16[128,2048]{1,0:T(8,128)(2,1)S(1)}, bf16[128,2048]{1,0:T(8,128)(2,1)}, u32[]{:S(2)}, u32[]{:S(2)}) collective-permute-start(bf16[128,2048]{1,0:T(8,128)(2,1)S(1)} %copy.28), channel_id=1, source_target_pairs={{0,32},{32,64},{64,96},{1,33},{33,65},{65,97},{2,34},{34,66},{66,9... | collective-permute-start | bytes 1572872 | tf_op jit(solution)/shard_map/while/body/eval_jaxpr/ppermute | solution.py:162
  232.3 9.2 %collective-permute-start.1 = (bf16[128,2048]{1,0:T(8,128)(2,1)S(1)}, bf16[128,2048]{1,0:T(8,128)(2,1)S(1)}, u32[]{:S(2)}, u32[]{:S(2)}) collective-permute-start(bf16[128,2048]{1,0:T(8,128)(2,1)S(1)} %get-tuple-element.427), channel_id=1, source_target_pairs={{0,1},{1,0},{2,3},{3,2},{4,5},{5,4},{6,7},{7,6},{8,9},{9,8},{10,11... | collective-permute-start | bytes 1572872 | tf_op jit(solution)/shard_map/while/body/eval_jaxpr/ppermute | solution.py:57
  232.8 22.2 %collective-permute-start = (bf16[128,2048]{1,0:T(8,128)(2,1)S(1)}, bf16[128,2048]{1,0:T(8,128)(2,1)}, u32[]{:S(2)}, u32[]{:S(2)}) collective-permute-start(bf16[128,2048]{1,0:T(8,128)(2,1)S(1)} %copy.28), channel_id=1, source_target_pairs={{0,32},{32,64},{64,96},{1,33},{33,65},{65,97},{2,34},{34,66},{66,9... | collective-permute-start | bytes 1572872 | tf_op jit(solution)/shard_map/while/body/eval_jaxpr/ppermute | solution.py:162
  256.6 22.2 %collective-permute-start = (bf16[128,2048]{1,0:T(8,128)(2,1)S(1)}, bf16[128,2048]{1,0:T(8,128)(2,1)}, u32[]{:S(2)}, u32[]{:S(2)}) collective-permute-start(bf16[128,2048]{1,0:T(8,128)(2,1)S(1)} %copy.28), channel_id=1, source_target_pairs={{0,32},{32,64},{64,96},{1,33},{33,65},{65,97},{2,34},{34,66},{66,9... | collective-permute-start | bytes 1572872 | tf_op jit(solution)/shard_map/while/body/eval_jaxpr/ppermute | solution.py:162
  279.8 9.2 %collective-permute-start.1 = (bf16[128,2048]{1,0:T(8,128)(2,1)S(1)}, bf16[128,2048]{1,0:T(8,128)(2,1)S(1)}, u32[]{:S(2)}, u32[]{:S(2)}) collective-permute-start(bf16[128,2048]{1,0:T(8,128)(2,1)S(1)} %get-tuple-element.427), channel_id=1, source_target_pairs={{0,1},{1,0},{2,3},{3,2},{4,5},{5,4},{6,7},{7,6},{8,9},{9,8},{10,11... | collective-permute-start | bytes 1572872 | tf_op jit(solution)/shard_map/while/body/eval_jaxpr/ppermute | solution.py:57
  280.3 22.2 %collective-permute-start = (bf16[128,2048]{1,0:T(8,128)(2,1)S(1)}, bf16[128,2048]{1,0:T(8,128)(2,1)}, u32[]{:S(2)}, u32[]{:S(2)}) collective-permute-start(bf16[128,2048]{1,0:T(8,128)(2,1)S(1)} %copy.28), channel_id=1, source_target_pairs={{0,32},{32,64},{64,96},{1,33},{33,65},{65,97},{2,34},{34,66},{66,9... | collective-permute-start | bytes 1572872 | tf_op jit(solution)/shard_map/while/body/eval_jaxpr/ppermute | solution.py:162
  303.6 9.2 %collective-permute-start.1 = (bf16[128,2048]{1,0:T(8,128)(2,1)S(1)}, bf16[128,2048]{1,0:T(8,128)(2,1)S(1)}, u32[]{:S(2)}, u32[]{:S(2)}) collective-permute-start(bf16[128,2048]{1,0:T(8,128)(2,1)S(1)} %get-tuple-element.427), channel_id=1, source_target_pairs={{0,1},{1,0},{2,3},{3,2},{4,5},{5,4},{6,7},{7,6},{8,9},{9,8},{10,11... | collective-permute-start | bytes 1572872 | tf_op jit(solution)/shard_map/while/body/eval_jaxpr/ppermute | solution.py:57
  304.0 22.2 %collective-permute-start = (bf16[128,2048]{1,0:T(8,128)(2,1)S(1)}, bf16[128,2048]{1,0:T(8,128)(2,1)}, u32[]{:S(2)}, u32[]{:S(2)}) collective-permute-start(bf16[128,2048]{1,0:T(8,128)(2,1)S(1)} %copy.28), channel_id=1, source_target_pairs={{0,32},{32,64},{64,96},{1,33},{33,65},{65,97},{2,34},{34,66},{66,9... | collective-permute-start | bytes 1572872 | tf_op jit(solution)/shard_map/while/body/eval_jaxpr/ppermute | solution.py:162
  327.8 22.2 %collective-permute-start = (bf16[128,2048]{1,0:T(8,128)(2,1)S(1)}, bf16[128,2048]{1,0:T(8,128)(2,1)}, u32[]{:S(2)}, u32[]{:S(2)}) collective-permute-start(bf16[128,2048]{1,0:T(8,128)(2,1)S(1)} %copy.28), channel_id=1, source_target_pairs={{0,32},{32,64},{64,96},{1,33},{33,65},{65,97},{2,34},{34,66},{66,9... | collective-permute-start | bytes 1572872 | tf_op jit(solution)/shard_map/while/body/eval_jaxpr/ppermute | solution.py:162
  351.0 9.2 %collective-permute-start.1 = (bf16[128,2048]{1,0:T(8,128)(2,1)S(1)}, bf16[128,2048]{1,0:T(8,128)(2,1)S(1)}, u32[]{:S(2)}, u32[]{:S(2)}) collective-permute-start(bf16[128,2048]{1,0:T(8,128)(2,1)S(1)} %get-tuple-element.427), channel_id=1, source_target_pairs={{0,1},{1,0},{2,3},{3,2},{4,5},{5,4},{6,7},{7,6},{8,9},{9,8},{10,11... | collective-permute-start | bytes 1572872 | tf_op jit(solution)/shard_map/while/body/eval_jaxpr/ppermute | solution.py:57
  351.5 22.2 %collective-permute-start = (bf16[128,2048]{1,0:T(8,128)(2,1)S(1)}, bf16[128,2048]{1,0:T(8,128)(2,1)}, u32[]{:S(2)}, u32[]{:S(2)}) collective-permute-start(bf16[128,2048]{1,0:T(8,128)(2,1)S(1)} %copy.28), channel_id=1, source_target_pairs={{0,32},{32,64},{64,96},{1,33},{33,65},{65,97},{2,34},{34,66},{66,9... | collective-permute-start | bytes 1572872 | tf_op jit(solution)/shard_map/while/body/eval_jaxpr/ppermute | solution.py:162
  385.5 9.3 %collective-permute-start.3 = (f32[1024,128]{0,1:T(8,128)S(1)}, f32[1024,128]{0,1:T(8,128)S(1)}, u32[]{:S(2)}, u32[]{:S(2)}) collective-permute-start(f32[1024,128]{0,1:T(8,128)S(1)} %fusion.7), channel_id=1, source_target_pairs={{0,1},{1,0},{2,3},{3,2},{4,5},{5,4},{6,7},{7,6},{8,9},{9,8},{10,11... | collective-permute-start | bytes 1572872 | tf_op jit(solution)/shard_map/ppermute | solution.py:57
  420.1 9.3 %collective-permute-start.22 = (f32[4,4,2,2,32,256]{5,4,3,2,0,1:T(8,128)}, f32[4,4,2,2,32,256]{5,4,3,2,0,1:T(8,128)}, u32[]{:S(2)}, u32[]{:S(2)}) collective-permute-start(f32[4,4,2,2,32,256]{5,4,3,2,0,1:T(8,128)} %bitcast.132), channel_id=1, source_target_pairs={{0,2},{2,0},{4,6},{6,4},{8,10},{10,8},{12,14},{14,12},{16,18},{18,... | collective-permute-start | bytes 6291464 | tf_op jit(solution)/shard_map/ppermute | solution.py:61
  434.6 9.5 %collective-permute-start.23 = (f32[4,2,2,32,128]{4,3,2,1,0:T(8,128)S(1)}, f32[4,2,2,32,128]{4,3,2,1,0:T(8,128)S(1)}, u32[]{:S(2)}, u32[]{:S(2)}) collective-permute-start(f32[4,2,2,32,128]{4,3,2,1,0:T(8,128)S(1)} %dynamic-slice_bitcast_fusion.2), channel_id=1, source_target_pairs={{0,8},{2,10},{4,12},{6,14},{8,16},{10,18},{12,20},{14,22},{16,24},... | collective-permute-start | bytes 786440 | tf_op jit(solution)/shard_map/ppermute | solution.py:61
  437.7 9.2 %collective-permute-start.8 = (f32[4,2,2,32,128]{4,3,2,1,0:T(8,128)S(1)}, f32[4,2,2,32,128]{4,3,2,1,0:T(8,128)S(1)}, u32[]{:S(2)}, u32[]{:S(2)}) collective-permute-start(f32[4,2,2,32,128]{4,3,2,1,0:T(8,128)S(1)} %dynamic-slice_bitcast_fusion.4), channel_id=1, source_target_pairs={{0,32},{32,64},{64,96},{96,0},{1,33},{33,65},{65,97},{97,1},{2,34}... | collective-permute-start | bytes 786440 | tf_op jit(solution)/shard_map/ppermute | solution.py:57
  (44 other events, 251.3 us)
Sparse Core Ops, SparseCore 0:
  10.4 51.9 all-gather.2
  64.8 47.8 all-gather.4

commit v8 on v2

--- a/solution.py
+++ b/solution.py
@@ -110,7 +110,7 @@
     micro_count = 8
     total_rows = group_seqs * seq_len
     block_rows = total_rows // micro_count
-    tick_count = micro_count + 2 * (segments - 1)
+    tick_count = micro_count + 3 * (segments - 1)
     flat_ids = token_ids.reshape(-1)
     weight_local = prior_weight[0]
     gain_local = prior_gain[0]
@@ -133,29 +133,31 @@
     embedded_all = lookup_rows(flat_ids, embed_table)
 
     def tick_whole(tick_pos, state):
-        arrived, computed, stored = state
+        arrived, own_prev, partner_prev, computed, stored = state
         partner = shifted(arrived, "rep", replicas, 1)
         passed = lax.ppermute(computed, "segment", [(i, i + 1) for i in range(segments - 1)])
-        micro_pos = tick_pos - 2 * segment_pos
+        micro_pos = tick_pos - 3 * segment_pos
         active = (micro_pos >= 0) & (micro_pos < micro_count)
         slot_pos = jnp.clip(micro_pos, 0, micro_count - 1)
         embedded = lax.dynamic_slice_in_dim(embedded_all, slot_pos * block_rows, block_rows, 0)
-        low = jnp.where(own_first, arrived, partner)
-        high = jnp.where(own_first, partner, arrived)
+        low = jnp.where(own_first, own_prev, partner_prev)
+        high = jnp.where(own_first, partner_prev, own_prev)
         joined = jnp.concatenate([low, high], axis=1)
         current = jnp.where(is_first, embedded, joined)
         result = apply_segment(current)
         previous = lax.dynamic_slice_in_dim(stored, slot_pos * block_rows, block_rows, 0)
         chosen = jnp.where(active & is_last, result, previous)
         stored = lax.dynamic_update_slice_in_dim(stored, chosen, slot_pos * block_rows, 0)
-        return (passed, result, stored)
+        return (passed, arrived, partner, result, stored)
 
     initial = (
         jnp.zeros((block_rows, half_width), jnp.bfloat16),
         jnp.zeros((block_rows, half_width), jnp.bfloat16),
+        jnp.zeros((block_rows, half_width), jnp.bfloat16),
+        jnp.zeros((block_rows, half_width), jnp.bfloat16),
         jnp.zeros((total_rows, half_width), jnp.bfloat16),
     )
-    final_half = lax.fori_loop(0, tick_count, tick_whole, initial)[2]
+    final_half = lax.fori_loop(0, tick_count, tick_whole, initial)[4]
 
     positions = jnp.arange(seq_len, dtype=jnp.int32)
     next_ids = jnp.concatenate([token_ids[:, 1:], token_ids[:, :1]], axis=1)

time: 471 us -> 482 us (1.023)
  waiting for transfers between devices: 122 us -> 30.2 us
  local copies, waits for them, and re-layouts: 12.6 us -> 80.5 us
  matrix products: 155 us -> 181 us
  other arithmetic: 49.5 us -> 55.3 us
    ppermute x33 -> x36, waiting for transfers between devices: 111 us -> 23.2 us  [shifted(): return lax.ppermute(x, axis, [(i, (i + by) % size) for i in range(size)])]
    while x14 -> x102, local copies, waits for them, and re-layouts: 0.57 us -> 68.3 us
    dot_general x14 -> x17, matrix products: 132 us -> 158 us  [apply_segment(): update = jnp.dot(normed, weight_local, preferred_element_type=jnp.float32)]
    ppermute x33 -> x36, starting transfers between devices: 33.6 us -> 43.6 us  [shifted(): return lax.ppermute(x, axis, [(i, (i + by) % size) for i in range(size)])]
    ppermute x14 -> x17, starting transfers between devices: 49.6 us -> 41.4 us  [tick_whole(): lax.ppermute(computed, 'segment', [(i, i + 1) for i in range(segments - 1)])]
    reduce_sum x14 -> x17, other arithmetic: 23.3 us -> 28.2 us  [rms_scale(): squares = jnp.mean(values * values, axis=-1, keepdims=True)]
    while x14 -> x17, other arithmetic: 14.1 us -> 14.7 us
  transfers between devices with their start and end apart: 65 -> 71, of which waited for: 28 -> 17; matrix products, arithmetic and copies ran while one was open for 44% -> 64% of each run, Pallas kernels for 0% -> 0%
where the time goes in v8:
time: 482 us; the launch traced here: 479 us
  matrix products  181 us (38%)
  starting transfers between devices  113 us (23%)
  local copies, waits for them, and re-layouts  80.5 us (17%)
  other arithmetic  55.3 us (11%)
  waiting for transfers between devices  30.2 us (6%)
  between operations  18.1 us (4%)
    dot_general x17, matrix products, apply_segment(): update = jnp.dot(normed, weight_local, preferred_element_type=jnp.float32)  158 us
    while x102, local copies, waits for them, and re-layouts  68.3 us
    ppermute x36, starting transfers between devices, shifted(): return lax.ppermute(x, axis, [(i, (i + by) % size) for i in range(size)])  43.6 us
    ppermute x17, starting transfers between devices, tick_whole(): lax.ppermute(computed, 'segment', [(i, i + 1) for i in range(segments - 1)])  41.4 us
    reduce_sum x17, other arithmetic, rms_scale(): squares = jnp.mean(values * values, axis=-1, keepdims=True)  28.2 us
    ppermute x16, starting transfers between devices, fsdp_moved(): return lax.ppermute(x, 'fsdp', [(f, mapping(f)) for f in range(16)])  28.1 us
    ppermute x36, waiting for transfers between devices, shifted(): return lax.ppermute(x, axis, [(i, (i + by) % size) for i in range(size)])  23.2 us
    while x17, other arithmetic  14.7 us
  transfers between devices with their start and end apart: 71, of which 17 were waited for; matrix products, arithmetic and copies ran while one was open for 64% of the time, Pallas kernels for 0%

profile of v8, /device:TPU:0, one launch (start us, length us, event | category | flops | bytes accessed | tf_op | source)
XLA Modules:
  0.0 478.7 jit_solution(1270964468189478781)
XLA Ops:
  8.7 6.3 %convolution_convert_fusion = bf16[1024,4096]{1,0:T(8,128)(2,1)} fusion(bf16[128,4096]{1,0:T(8,128)(2,1)S(1)} %copy-done, s32[1024]{0:T(1024)} %bitcast.144), kind=kOutput, calls=%fused_computation.18 | convolution fusion | flops 1078067200 | bytes 9441280 | tf_op jit(solution)/shard_map/dot_general | solution.py:22
  17.7 336.6 %while.24 = (s32[]{:T(128)}, bf16[128,2048]{1,0:T(8,128)(2,1)S(1)}, bf16[128,2048]{1,0:T(8,128)(2,1)S(1)}, bf16[128,2048]{1,0:T(8,128)(2,1)S(1)}, bf16[128,2048]...) while((s32[]{:T(128)}, bf16[128,2048]{1,0:T(8,128)(2,1)S(1)}, ...), condition=%wide.region_4.5_spmd.clone, body=%wide.region_2.4_spmd.clone.sunk | while | flops 2154823936 | bytes 39340956 | solution.py:160
  18.6 4.3 collective-permute-start
  27.4 9.4 %select_dynamic-update-slice_fusion.2 = (bf16[1024,2048]{1,0:T(8,128)(2,1)}, bf16[128,2048]{1,0:T(8,128)(2,1)}) fusion(bf16[1024,2048]{1,0:T(8,128)(2,1)} %get-tuple-element.544, s32[]{:T(128)S(6)} %select_n.436, pred[]{:T(512)S(6)} %and.148, bf16[4096,2048]{1,0:T(8,128)(2,1)} %get-tuple-element.571, f32[128,4096]{1,0:T(8,128)S(1)} %get-tuple-element.515, ...), kind=kOutput, calls=%fused_computation.8.clone.1 | convolution fusion | flops 2149842944 | bytes 21513220 | tf_op jit(solution)/shard_map/while/body/eval_jaxpr/dot_general | solution.py:129
  40.9 3.5 collective-permute-start
  47.5 9.3 %select_dynamic-update-slice_fusion.2 = (bf16[1024,2048]{1,0:T(8,128)(2,1)}, bf16[128,2048]{1,0:T(8,128)(2,1)}) fusion(bf16[1024,2048]{1,0:T(8,128)(2,1)} %get-tuple-element.544, s32[]{:T(128)S(6)} %select_n.436, pred[]{:T(512)S(6)} %and.148, bf16[4096,2048]{1,0:T(8,128)(2,1)} %get-tuple-element.571, f32[128,4096]{1,0:T(8,128)S(1)} %get-tuple-element.515, ...), kind=kOutput, calls=%fused_computation.8.clone.1 | convolution fusion | flops 2149842944 | bytes 21513220 | tf_op jit(solution)/shard_map/while/body/eval_jaxpr/dot_general | solution.py:129
  59.0 3.7 collective-permute-done.1
  64.5 4.2 collective-permute-start
  71.8 9.3 %select_dynamic-update-slice_fusion.2 = (bf16[1024,2048]{1,0:T(8,128)(2,1)}, bf16[128,2048]{1,0:T(8,128)(2,1)}) fusion(bf16[1024,2048]{1,0:T(8,128)(2,1)} %get-tuple-element.544, s32[]{:T(128)S(6)} %select_n.436, pred[]{:T(512)S(6)} %and.148, bf16[4096,2048]{1,0:T(8,128)(2,1)} %get-tuple-element.571, f32[128,4096]{1,0:T(8,128)S(1)} %get-tuple-element.515, ...), kind=kOutput, calls=%fused_computation.8.clone.1 | convolution fusion | flops 2149842944 | bytes 21513220 | tf_op jit(solution)/shard_map/while/body/eval_jaxpr/dot_general | solution.py:129
  92.0 9.3 %select_dynamic-update-slice_fusion.2 = (bf16[1024,2048]{1,0:T(8,128)(2,1)}, bf16[128,2048]{1,0:T(8,128)(2,1)}) fusion(bf16[1024,2048]{1,0:T(8,128)(2,1)} %get-tuple-element.544, s32[]{:T(128)S(6)} %select_n.436, pred[]{:T(512)S(6)} %and.148, bf16[4096,2048]{1,0:T(8,128)(2,1)} %get-tuple-element.571, f32[128,4096]{1,0:T(8,128)S(1)} %get-tuple-element.515, ...), kind=kOutput, calls=%fused_computation.8.clone.1 | convolution fusion | flops 2149842944 | bytes 21513220 | tf_op jit(solution)/shard_map/while/body/eval_jaxpr/dot_general | solution.py:129
  113.3 9.4 %select_dynamic-update-slice_fusion.2 = (bf16[1024,2048]{1,0:T(8,128)(2,1)}, bf16[128,2048]{1,0:T(8,128)(2,1)}) fusion(bf16[1024,2048]{1,0:T(8,128)(2,1)} %get-tuple-element.544, s32[]{:T(128)S(6)} %select_n.436, pred[]{:T(512)S(6)} %and.148, bf16[4096,2048]{1,0:T(8,128)(2,1)} %get-tuple-element.571, f32[128,4096]{1,0:T(8,128)S(1)} %get-tuple-element.515, ...), kind=kOutput, calls=%fused_computation.8.clone.1 | convolution fusion | flops 2149842944 | bytes 21513220 | tf_op jit(solution)/shard_map/while/body/eval_jaxpr/dot_general | solution.py:129
  131.4 9.2 %select_dynamic-update-slice_fusion.2 = (bf16[1024,2048]{1,0:T(8,128)(2,1)}, bf16[128,2048]{1,0:T(8,128)(2,1)}) fusion(bf16[1024,2048]{1,0:T(8,128)(2,1)} %get-tuple-element.544, s32[]{:T(128)S(6)} %select_n.436, pred[]{:T(512)S(6)} %and.148, bf16[4096,2048]{1,0:T(8,128)(2,1)} %get-tuple-element.571, f32[128,4096]{1,0:T(8,128)S(1)} %get-tuple-element.515, ...), kind=kOutput, calls=%fused_computation.8.clone.1 | convolution fusion | flops 2149842944 | bytes 21513220 | tf_op jit(solution)/shard_map/while/body/eval_jaxpr/dot_general | solution.py:129
  151.4 9.3 %select_dynamic-update-slice_fusion.2 = (bf16[1024,2048]{1,0:T(8,128)(2,1)}, bf16[128,2048]{1,0:T(8,128)(2,1)}) fusion(bf16[1024,2048]{1,0:T(8,128)(2,1)} %get-tuple-element.544, s32[]{:T(128)S(6)} %select_n.436, pred[]{:T(512)S(6)} %and.148, bf16[4096,2048]{1,0:T(8,128)(2,1)} %get-tuple-element.571, f32[128,4096]{1,0:T(8,128)S(1)} %get-tuple-element.515, ...), kind=kOutput, calls=%fused_computation.8.clone.1 | convolution fusion | flops 2149842944 | bytes 21513220 | tf_op jit(solution)/shard_map/while/body/eval_jaxpr/dot_general | solution.py:129
  169.5 9.3 %select_dynamic-update-slice_fusion.2 = (bf16[1024,2048]{1,0:T(8,128)(2,1)}, bf16[128,2048]{1,0:T(8,128)(2,1)}) fusion(bf16[1024,2048]{1,0:T(8,128)(2,1)} %get-tuple-element.544, s32[]{:T(128)S(6)} %select_n.436, pred[]{:T(512)S(6)} %and.148, bf16[4096,2048]{1,0:T(8,128)(2,1)} %get-tuple-element.571, f32[128,4096]{1,0:T(8,128)S(1)} %get-tuple-element.515, ...), kind=kOutput, calls=%fused_computation.8.clone.1 | convolution fusion | flops 2149842944 | bytes 21513220 | tf_op jit(solution)/shard_map/while/body/eval_jaxpr/dot_general | solution.py:129
  189.6 9.3 %select_dynamic-update-slice_fusion.2 = (bf16[1024,2048]{1,0:T(8,128)(2,1)}, bf16[128,2048]{1,0:T(8,128)(2,1)}) fusion(bf16[1024,2048]{1,0:T(8,128)(2,1)} %get-tuple-element.544, s32[]{:T(128)S(6)} %select_n.436, pred[]{:T(512)S(6)} %and.148, bf16[4096,2048]{1,0:T(8,128)(2,1)} %get-tuple-element.571, f32[128,4096]{1,0:T(8,128)S(1)} %get-tuple-element.515, ...), kind=kOutput, calls=%fused_computation.8.clone.1 | convolution fusion | flops 2149842944 | bytes 21513220 | tf_op jit(solution)/shard_map/while/body/eval_jaxpr/dot_general | solution.py:129
  207.6 9.3 %select_dynamic-update-slice_fusion.2 = (bf16[1024,2048]{1,0:T(8,128)(2,1)}, bf16[128,2048]{1,0:T(8,128)(2,1)}) fusion(bf16[1024,2048]{1,0:T(8,128)(2,1)} %get-tuple-element.544, s32[]{:T(128)S(6)} %select_n.436, pred[]{:T(512)S(6)} %and.148, bf16[4096,2048]{1,0:T(8,128)(2,1)} %get-tuple-element.571, f32[128,4096]{1,0:T(8,128)S(1)} %get-tuple-element.515, ...), kind=kOutput, calls=%fused_computation.8.clone.1 | convolution fusion | flops 2149842944 | bytes 21513220 | tf_op jit(solution)/shard_map/while/body/eval_jaxpr/dot_general | solution.py:129
  227.7 9.3 %select_dynamic-update-slice_fusion.2 = (bf16[1024,2048]{1,0:T(8,128)(2,1)}, bf16[128,2048]{1,0:T(8,128)(2,1)}) fusion(bf16[1024,2048]{1,0:T(8,128)(2,1)} %get-tuple-element.544, s32[]{:T(128)S(6)} %select_n.436, pred[]{:T(512)S(6)} %and.148, bf16[4096,2048]{1,0:T(8,128)(2,1)} %get-tuple-element.571, f32[128,4096]{1,0:T(8,128)S(1)} %get-tuple-element.515, ...), kind=kOutput, calls=%fused_computation.8.clone.1 | convolution fusion | flops 2149842944 | bytes 21513220 | tf_op jit(solution)/shard_map/while/body/eval_jaxpr/dot_general | solution.py:129
  245.7 9.3 %select_dynamic-update-slice_fusion.2 = (bf16[1024,2048]{1,0:T(8,128)(2,1)}, bf16[128,2048]{1,0:T(8,128)(2,1)}) fusion(bf16[1024,2048]{1,0:T(8,128)(2,1)} %get-tuple-element.544, s32[]{:T(128)S(6)} %select_n.436, pred[]{:T(512)S(6)} %and.148, bf16[4096,2048]{1,0:T(8,128)(2,1)} %get-tuple-element.571, f32[128,4096]{1,0:T(8,128)S(1)} %get-tuple-element.515, ...), kind=kOutput, calls=%fused_computation.8.clone.1 | convolution fusion | flops 2149842944 | bytes 21513220 | tf_op jit(solution)/shard_map/while/body/eval_jaxpr/dot_general | solution.py:129
  265.7 9.3 %select_dynamic-update-slice_fusion.2 = (bf16[1024,2048]{1,0:T(8,128)(2,1)}, bf16[128,2048]{1,0:T(8,128)(2,1)}) fusion(bf16[1024,2048]{1,0:T(8,128)(2,1)} %get-tuple-element.544, s32[]{:T(128)S(6)} %select_n.436, pred[]{:T(512)S(6)} %and.148, bf16[4096,2048]{1,0:T(8,128)(2,1)} %get-tuple-element.571, f32[128,4096]{1,0:T(8,128)S(1)} %get-tuple-element.515, ...), kind=kOutput, calls=%fused_computation.8.clone.1 | convolution fusion | flops 2149842944 | bytes 21513220 | tf_op jit(solution)/shard_map/while/body/eval_jaxpr/dot_general | solution.py:129
  283.8 9.3 %select_dynamic-update-slice_fusion.2 = (bf16[1024,2048]{1,0:T(8,128)(2,1)}, bf16[128,2048]{1,0:T(8,128)(2,1)}) fusion(bf16[1024,2048]{1,0:T(8,128)(2,1)} %get-tuple-element.544, s32[]{:T(128)S(6)} %select_n.436, pred[]{:T(512)S(6)} %and.148, bf16[4096,2048]{1,0:T(8,128)(2,1)} %get-tuple-element.571, f32[128,4096]{1,0:T(8,128)S(1)} %get-tuple-element.515, ...), kind=kOutput, calls=%fused_computation.8.clone.1 | convolution fusion | flops 2149842944 | bytes 21513220 | tf_op jit(solution)/shard_map/while/body/eval_jaxpr/dot_general | solution.py:129
  303.8 9.3 %select_dynamic-update-slice_fusion.2 = (bf16[1024,2048]{1,0:T(8,128)(2,1)}, bf16[128,2048]{1,0:T(8,128)(2,1)}) fusion(bf16[1024,2048]{1,0:T(8,128)(2,1)} %get-tuple-element.544, s32[]{:T(128)S(6)} %select_n.436, pred[]{:T(512)S(6)} %and.148, bf16[4096,2048]{1,0:T(8,128)(2,1)} %get-tuple-element.571, f32[128,4096]{1,0:T(8,128)S(1)} %get-tuple-element.515, ...), kind=kOutput, calls=%fused_computation.8.clone.1 | convolution fusion | flops 2149842944 | bytes 21513220 | tf_op jit(solution)/shard_map/while/body/eval_jaxpr/dot_general | solution.py:129
  321.8 9.3 %select_dynamic-update-slice_fusion.2 = (bf16[1024,2048]{1,0:T(8,128)(2,1)}, bf16[128,2048]{1,0:T(8,128)(2,1)}) fusion(bf16[1024,2048]{1,0:T(8,128)(2,1)} %get-tuple-element.544, s32[]{:T(128)S(6)} %select_n.436, pred[]{:T(512)S(6)} %and.148, bf16[4096,2048]{1,0:T(8,128)(2,1)} %get-tuple-element.571, f32[128,4096]{1,0:T(8,128)S(1)} %get-tuple-element.515, ...), kind=kOutput, calls=%fused_computation.8.clone.1 | convolution fusion | flops 2149842944 | bytes 21513220 | tf_op jit(solution)/shard_map/while/body/eval_jaxpr/dot_general | solution.py:129
  341.9 9.3 %select_dynamic-update-slice_fusion.2 = (bf16[1024,2048]{1,0:T(8,128)(2,1)}, bf16[128,2048]{1,0:T(8,128)(2,1)}) fusion(bf16[1024,2048]{1,0:T(8,128)(2,1)} %get-tuple-element.544, s32[]{:T(128)S(6)} %select_n.436, pred[]{:T(512)S(6)} %and.148, bf16[4096,2048]{1,0:T(8,128)(2,1)} %get-tuple-element.571, f32[128,4096]{1,0:T(8,128)S(1)} %get-tuple-element.515, ...), kind=kOutput, calls=%fused_computation.8.clone.1 | convolution fusion | flops 2149842944 | bytes 21513220 | tf_op jit(solution)/shard_map/while/body/eval_jaxpr/dot_general | solution.py:129
  361.3 3.8 fusion.8
  366.3 8.1 %collective-permute-done.3 = f32[1024,128]{0,1:T(8,128)S(1)} collective-permute-done((f32[1024,128]{0,1:T(8,128)S(1)}, f32[1024,128]{0,1:T(8,128)S(1)}, u32[]{:S(2)}, u32[]{:S(2)}) %collective-permute-start.3) | collective-permute-done | bytes 524320 | tf_op jit(solution)/shard_map/ppermute | solution.py:32
  396.0 5.5 %fusion.13 = f32[4096,256]{1,0:T(8,128)} fusion(bf16[128,4096]{1,0:T(8,128)(2,1)} %copy-done.2, bf16[4096,256]{1,0:T(8,128)(2,1)} %all-gather.5.cloned.1.call-done, f32[128,4096]{1,0:T(8,128)S(1)} %get-tuple-element.415, f32[128]{0:T(128)S(1)} %add_rsqrt_fusion.3), kind=kOutput, calls=%fused_computation.39 | convolution fusion | flops 537952256 | bytes 9437696 | tf_op jit(solution)/shard_map/dot_general | solution.py:232
  401.6 3.3 dynamic-slice_bitcast_fusion
  407.7 4.3 collective-permute-start.29
  417.8 3.8 collective-permute-start.30
  422.6 3.3 collective-permute-start.15
  426.5 3.8 collective-permute-start.31
  430.5 3.8 collective-permute-start.16
  (411 shorter events, 240.4 us)
Async XLA Ops:
  7.2 375.3 %all-gather.3.cloned.1.call-start = ((), (), s32[]{:S(2)}) async-start(), calls=%async_computation | async-start | bytes 2228224 | tf_op jit(solution)/shard_map/all_gather | solution.py:122
  7.9 376.6 %all-gather.5.cloned.1.call-start = ((), (), s32[]{:S(2)}) async-start(), calls=%async_computation.1 | async-start | bytes 2228224 | tf_op jit(solution)/shard_map/all_gather | solution.py:123
  18.6 19.3 %collective-permute-start = (bf16[128,2048]{1,0:T(8,128)(2,1)}, bf16[128,2048]{1,0:T(8,128)(2,1)}, u32[]{:S(2)}, u32[]{:S(2)}) collective-permute-start(bf16[128,2048]{1,0:T(8,128)(2,1)} %broadcast_select_fusion.8), channel_id=1, source_target_pairs={{0,32},{32,64},{64,96},{1,33},{33,65},{65,97},{2,34},{34,66},{66,9... | collective-permute-start | bytes 1572872 | tf_op jit(solution)/shard_map/while/body/eval_jaxpr/ppermute | solution.py:138
  23.8 15.2 %collective-permute-start.1 = (bf16[128,2048]{1,0:T(8,128)(2,1)}, bf16[128,2048]{1,0:T(8,128)(2,1)}, u32[]{:S(2)}, u32[]{:S(2)}) collective-permute-start(bf16[128,2048]{1,0:T(8,128)(2,1)} %copy.29), channel_id=1, source_target_pairs={{0,1},{1,0},{2,3},{3,2},{4,5},{5,4},{6,7},{7,6},{8,9},{9,8},{10,11... | collective-permute-start | bytes 1572872 | tf_op jit(solution)/shard_map/while/body/eval_jaxpr/ppermute | solution.py:32
  40.9 17.0 %collective-permute-start = (bf16[128,2048]{1,0:T(8,128)(2,1)}, bf16[128,2048]{1,0:T(8,128)(2,1)}, u32[]{:S(2)}, u32[]{:S(2)}) collective-permute-start(bf16[128,2048]{1,0:T(8,128)(2,1)} %broadcast_select_fusion.8), channel_id=1, source_target_pairs={{0,32},{32,64},{64,96},{1,33},{33,65},{65,97},{2,34},{34,66},{66,9... | collective-permute-start | bytes 1572872 | tf_op jit(solution)/shard_map/while/body/eval_jaxpr/ppermute | solution.py:138
  45.2 17.4 %collective-permute-start.1 = (bf16[128,2048]{1,0:T(8,128)(2,1)}, bf16[128,2048]{1,0:T(8,128)(2,1)}, u32[]{:S(2)}, u32[]{:S(2)}) collective-permute-start(bf16[128,2048]{1,0:T(8,128)(2,1)} %copy.29), channel_id=1, source_target_pairs={{0,1},{1,0},{2,3},{3,2},{4,5},{5,4},{6,7},{7,6},{8,9},{9,8},{10,11... | collective-permute-start | bytes 1572872 | tf_op jit(solution)/shard_map/while/body/eval_jaxpr/ppermute | solution.py:32
  64.5 17.7 %collective-permute-start = (bf16[128,2048]{1,0:T(8,128)(2,1)}, bf16[128,2048]{1,0:T(8,128)(2,1)}, u32[]{:S(2)}, u32[]{:S(2)}) collective-permute-start(bf16[128,2048]{1,0:T(8,128)(2,1)} %broadcast_select_fusion.8), channel_id=1, source_target_pairs={{0,32},{32,64},{64,96},{1,33},{33,65},{65,97},{2,34},{34,66},{66,9... | collective-permute-start | bytes 1572872 | tf_op jit(solution)/shard_map/while/body/eval_jaxpr/ppermute | solution.py:138
  69.6 14.7 %collective-permute-start.1 = (bf16[128,2048]{1,0:T(8,128)(2,1)}, bf16[128,2048]{1,0:T(8,128)(2,1)}, u32[]{:S(2)}, u32[]{:S(2)}) collective-permute-start(bf16[128,2048]{1,0:T(8,128)(2,1)} %copy.29), channel_id=1, source_target_pairs={{0,1},{1,0},{2,3},{3,2},{4,5},{5,4},{6,7},{7,6},{8,9},{9,8},{10,11... | collective-permute-start | bytes 1572872 | tf_op jit(solution)/shard_map/while/body/eval_jaxpr/ppermute | solution.py:32
  86.2 16.2 %collective-permute-start = (bf16[128,2048]{1,0:T(8,128)(2,1)}, bf16[128,2048]{1,0:T(8,128)(2,1)}, u32[]{:S(2)}, u32[]{:S(2)}) collective-permute-start(bf16[128,2048]{1,0:T(8,128)(2,1)} %broadcast_select_fusion.8), channel_id=1, source_target_pairs={{0,32},{32,64},{64,96},{1,33},{33,65},{65,97},{2,34},{34,66},{66,9... | collective-permute-start | bytes 1572872 | tf_op jit(solution)/shard_map/while/body/eval_jaxpr/ppermute | solution.py:138
  89.2 15.2 %collective-permute-start.1 = (bf16[128,2048]{1,0:T(8,128)(2,1)}, bf16[128,2048]{1,0:T(8,128)(2,1)}, u32[]{:S(2)}, u32[]{:S(2)}) collective-permute-start(bf16[128,2048]{1,0:T(8,128)(2,1)} %copy.29), channel_id=1, source_target_pairs={{0,1},{1,0},{2,3},{3,2},{4,5},{5,4},{6,7},{7,6},{8,9},{9,8},{10,11... | collective-permute-start | bytes 1572872 | tf_op jit(solution)/shard_map/while/body/eval_jaxpr/ppermute | solution.py:32
  106.4 17.4 %collective-permute-start = (bf16[128,2048]{1,0:T(8,128)(2,1)}, bf16[128,2048]{1,0:T(8,128)(2,1)}, u32[]{:S(2)}, u32[]{:S(2)}) collective-permute-start(bf16[128,2048]{1,0:T(8,128)(2,1)} %broadcast_select_fusion.8), channel_id=1, source_target_pairs={{0,32},{32,64},{64,96},{1,33},{33,65},{65,97},{2,34},{34,66},{66,9... | collective-permute-start | bytes 1572872 | tf_op jit(solution)/shard_map/while/body/eval_jaxpr/ppermute | solution.py:138
  109.3 15.5 %collective-permute-start.1 = (bf16[128,2048]{1,0:T(8,128)(2,1)}, bf16[128,2048]{1,0:T(8,128)(2,1)}, u32[]{:S(2)}, u32[]{:S(2)}) collective-permute-start(bf16[128,2048]{1,0:T(8,128)(2,1)} %copy.29), channel_id=1, source_target_pairs={{0,1},{1,0},{2,3},{3,2},{4,5},{5,4},{6,7},{7,6},{8,9},{9,8},{10,11... | collective-permute-start | bytes 1572872 | tf_op jit(solution)/shard_map/while/body/eval_jaxpr/ppermute | solution.py:32
  126.7 15.0 %collective-permute-start = (bf16[128,2048]{1,0:T(8,128)(2,1)}, bf16[128,2048]{1,0:T(8,128)(2,1)}, u32[]{:S(2)}, u32[]{:S(2)}) collective-permute-start(bf16[128,2048]{1,0:T(8,128)(2,1)} %broadcast_select_fusion.8), channel_id=1, source_target_pairs={{0,32},{32,64},{64,96},{1,33},{33,65},{65,97},{2,34},{34,66},{66,9... | collective-permute-start | bytes 1572872 | tf_op jit(solution)/shard_map/while/body/eval_jaxpr/ppermute | solution.py:138
  144.7 17.1 %collective-permute-start = (bf16[128,2048]{1,0:T(8,128)(2,1)}, bf16[128,2048]{1,0:T(8,128)(2,1)}, u32[]{:S(2)}, u32[]{:S(2)}) collective-permute-start(bf16[128,2048]{1,0:T(8,128)(2,1)} %broadcast_select_fusion.8), channel_id=1, source_target_pairs={{0,32},{32,64},{64,96},{1,33},{33,65},{65,97},{2,34},{34,66},{66,9... | collective-permute-start | bytes 1572872 | tf_op jit(solution)/shard_map/while/body/eval_jaxpr/ppermute | solution.py:138
  147.7 15.3 %collective-permute-start.1 = (bf16[128,2048]{1,0:T(8,128)(2,1)}, bf16[128,2048]{1,0:T(8,128)(2,1)}, u32[]{:S(2)}, u32[]{:S(2)}) collective-permute-start(bf16[128,2048]{1,0:T(8,128)(2,1)} %copy.29), channel_id=1, source_target_pairs={{0,1},{1,0},{2,3},{3,2},{4,5},{5,4},{6,7},{7,6},{8,9},{9,8},{10,11... | collective-permute-start | bytes 1572872 | tf_op jit(solution)/shard_map/while/body/eval_jaxpr/ppermute | solution.py:32
  164.8 15.1 %collective-permute-start = (bf16[128,2048]{1,0:T(8,128)(2,1)}, bf16[128,2048]{1,0:T(8,128)(2,1)}, u32[]{:S(2)}, u32[]{:S(2)}) collective-permute-start(bf16[128,2048]{1,0:T(8,128)(2,1)} %broadcast_select_fusion.8), channel_id=1, source_target_pairs={{0,32},{32,64},{64,96},{1,33},{33,65},{65,97},{2,34},{34,66},{66,9... | collective-permute-start | bytes 1572872 | tf_op jit(solution)/shard_map/while/body/eval_jaxpr/ppermute | solution.py:138
  167.7 13.2 %collective-permute-start.1 = (bf16[128,2048]{1,0:T(8,128)(2,1)}, bf16[128,2048]{1,0:T(8,128)(2,1)}, u32[]{:S(2)}, u32[]{:S(2)}) collective-permute-start(bf16[128,2048]{1,0:T(8,128)(2,1)} %copy.29), channel_id=1, source_target_pairs={{0,1},{1,0},{2,3},{3,2},{4,5},{5,4},{6,7},{7,6},{8,9},{9,8},{10,11... | collective-permute-start | bytes 1572872 | tf_op jit(solution)/shard_map/while/body/eval_jaxpr/ppermute | solution.py:32
  182.9 17.1 %collective-permute-start = (bf16[128,2048]{1,0:T(8,128)(2,1)}, bf16[128,2048]{1,0:T(8,128)(2,1)}, u32[]{:S(2)}, u32[]{:S(2)}) collective-permute-start(bf16[128,2048]{1,0:T(8,128)(2,1)} %broadcast_select_fusion.8), channel_id=1, source_target_pairs={{0,32},{32,64},{64,96},{1,33},{33,65},{65,97},{2,34},{34,66},{66,9... | collective-permute-start | bytes 1572872 | tf_op jit(solution)/shard_map/while/body/eval_jaxpr/ppermute | solution.py:138
  185.8 15.2 %collective-permute-start.1 = (bf16[128,2048]{1,0:T(8,128)(2,1)}, bf16[128,2048]{1,0:T(8,128)(2,1)}, u32[]{:S(2)}, u32[]{:S(2)}) collective-permute-start(bf16[128,2048]{1,0:T(8,128)(2,1)} %copy.29), channel_id=1, source_target_pairs={{0,1},{1,0},{2,3},{3,2},{4,5},{5,4},{6,7},{7,6},{8,9},{9,8},{10,11... | collective-permute-start | bytes 1572872 | tf_op jit(solution)/shard_map/while/body/eval_jaxpr/ppermute | solution.py:32
  202.9 15.1 %collective-permute-start = (bf16[128,2048]{1,0:T(8,128)(2,1)}, bf16[128,2048]{1,0:T(8,128)(2,1)}, u32[]{:S(2)}, u32[]{:S(2)}) collective-permute-start(bf16[128,2048]{1,0:T(8,128)(2,1)} %broadcast_select_fusion.8), channel_id=1, source_target_pairs={{0,32},{32,64},{64,96},{1,33},{33,65},{65,97},{2,34},{34,66},{66,9... | collective-permute-start | bytes 1572872 | tf_op jit(solution)/shard_map/while/body/eval_jaxpr/ppermute | solution.py:138
  220.9 17.1 %collective-permute-start = (bf16[128,2048]{1,0:T(8,128)(2,1)}, bf16[128,2048]{1,0:T(8,128)(2,1)}, u32[]{:S(2)}, u32[]{:S(2)}) collective-permute-start(bf16[128,2048]{1,0:T(8,128)(2,1)} %broadcast_select_fusion.8), channel_id=1, source_target_pairs={{0,32},{32,64},{64,96},{1,33},{33,65},{65,97},{2,34},{34,66},{66,9... | collective-permute-start | bytes 1572872 | tf_op jit(solution)/shard_map/while/body/eval_jaxpr/ppermute | solution.py:138
  223.9 15.2 %collective-permute-start.1 = (bf16[128,2048]{1,0:T(8,128)(2,1)}, bf16[128,2048]{1,0:T(8,128)(2,1)}, u32[]{:S(2)}, u32[]{:S(2)}) collective-permute-start(bf16[128,2048]{1,0:T(8,128)(2,1)} %copy.29), channel_id=1, source_target_pairs={{0,1},{1,0},{2,3},{3,2},{4,5},{5,4},{6,7},{7,6},{8,9},{9,8},{10,11... | collective-permute-start | bytes 1572872 | tf_op jit(solution)/shard_map/while/body/eval_jaxpr/ppermute | solution.py:32
  241.0 15.1 %collective-permute-start = (bf16[128,2048]{1,0:T(8,128)(2,1)}, bf16[128,2048]{1,0:T(8,128)(2,1)}, u32[]{:S(2)}, u32[]{:S(2)}) collective-permute-start(bf16[128,2048]{1,0:T(8,128)(2,1)} %broadcast_select_fusion.8), channel_id=1, source_target_pairs={{0,32},{32,64},{64,96},{1,33},{33,65},{65,97},{2,34},{34,66},{66,9... | collective-permute-start | bytes 1572872 | tf_op jit(solution)/shard_map/while/body/eval_jaxpr/ppermute | solution.py:138
  259.0 17.1 %collective-permute-start = (bf16[128,2048]{1,0:T(8,128)(2,1)}, bf16[128,2048]{1,0:T(8,128)(2,1)}, u32[]{:S(2)}, u32[]{:S(2)}) collective-permute-start(bf16[128,2048]{1,0:T(8,128)(2,1)} %broadcast_select_fusion.8), channel_id=1, source_target_pairs={{0,32},{32,64},{64,96},{1,33},{33,65},{65,97},{2,34},{34,66},{66,9... | collective-permute-start | bytes 1572872 | tf_op jit(solution)/shard_map/while/body/eval_jaxpr/ppermute | solution.py:138
  261.9 15.2 %collective-permute-start.1 = (bf16[128,2048]{1,0:T(8,128)(2,1)}, bf16[128,2048]{1,0:T(8,128)(2,1)}, u32[]{:S(2)}, u32[]{:S(2)}) collective-permute-start(bf16[128,2048]{1,0:T(8,128)(2,1)} %copy.29), channel_id=1, source_target_pairs={{0,1},{1,0},{2,3},{3,2},{4,5},{5,4},{6,7},{7,6},{8,9},{9,8},{10,11... | collective-permute-start | bytes 1572872 | tf_op jit(solution)/shard_map/while/body/eval_jaxpr/ppermute | solution.py:32
  279.1 15.1 %collective-permute-start = (bf16[128,2048]{1,0:T(8,128)(2,1)}, bf16[128,2048]{1,0:T(8,128)(2,1)}, u32[]{:S(2)}, u32[]{:S(2)}) collective-permute-start(bf16[128,2048]{1,0:T(8,128)(2,1)} %broadcast_select_fusion.8), channel_id=1, source_target_pairs={{0,32},{32,64},{64,96},{1,33},{33,65},{65,97},{2,34},{34,66},{66,9... | collective-permute-start | bytes 1572872 | tf_op jit(solution)/shard_map/while/body/eval_jaxpr/ppermute | solution.py:138
  297.1 17.1 %collective-permute-start = (bf16[128,2048]{1,0:T(8,128)(2,1)}, bf16[128,2048]{1,0:T(8,128)(2,1)}, u32[]{:S(2)}, u32[]{:S(2)}) collective-permute-start(bf16[128,2048]{1,0:T(8,128)(2,1)} %broadcast_select_fusion.8), channel_id=1, source_target_pairs={{0,32},{32,64},{64,96},{1,33},{33,65},{65,97},{2,34},{34,66},{66,9... | collective-permute-start | bytes 1572872 | tf_op jit(solution)/shard_map/while/body/eval_jaxpr/ppermute | solution.py:138
  300.0 15.2 %collective-permute-start.1 = (bf16[128,2048]{1,0:T(8,128)(2,1)}, bf16[128,2048]{1,0:T(8,128)(2,1)}, u32[]{:S(2)}, u32[]{:S(2)}) collective-permute-start(bf16[128,2048]{1,0:T(8,128)(2,1)} %copy.29), channel_id=1, source_target_pairs={{0,1},{1,0},{2,3},{3,2},{4,5},{5,4},{6,7},{7,6},{8,9},{9,8},{10,11... | collective-permute-start | bytes 1572872 | tf_op jit(solution)/shard_map/while/body/eval_jaxpr/ppermute | solution.py:32
  317.2 15.1 %collective-permute-start = (bf16[128,2048]{1,0:T(8,128)(2,1)}, bf16[128,2048]{1,0:T(8,128)(2,1)}, u32[]{:S(2)}, u32[]{:S(2)}) collective-permute-start(bf16[128,2048]{1,0:T(8,128)(2,1)} %broadcast_select_fusion.8), channel_id=1, source_target_pairs={{0,32},{32,64},{64,96},{1,33},{33,65},{65,97},{2,34},{34,66},{66,9... | collective-permute-start | bytes 1572872 | tf_op jit(solution)/shard_map/while/body/eval_jaxpr/ppermute | solution.py:138
  320.1 13.2 %collective-permute-start.1 = (bf16[128,2048]{1,0:T(8,128)(2,1)}, bf16[128,2048]{1,0:T(8,128)(2,1)}, u32[]{:S(2)}, u32[]{:S(2)}) collective-permute-start(bf16[128,2048]{1,0:T(8,128)(2,1)} %copy.29), channel_id=1, source_target_pairs={{0,1},{1,0},{2,3},{3,2},{4,5},{5,4},{6,7},{7,6},{8,9},{9,8},{10,11... | collective-permute-start | bytes 1572872 | tf_op jit(solution)/shard_map/while/body/eval_jaxpr/ppermute | solution.py:32
  335.2 17.1 %collective-permute-start = (bf16[128,2048]{1,0:T(8,128)(2,1)}, bf16[128,2048]{1,0:T(8,128)(2,1)}, u32[]{:S(2)}, u32[]{:S(2)}) collective-permute-start(bf16[128,2048]{1,0:T(8,128)(2,1)} %broadcast_select_fusion.8), channel_id=1, source_target_pairs={{0,32},{32,64},{64,96},{1,33},{33,65},{65,97},{2,34},{34,66},{66,9... | collective-permute-start | bytes 1572872 | tf_op jit(solution)/shard_map/while/body/eval_jaxpr/ppermute | solution.py:138
  338.1 15.2 %collective-permute-start.1 = (bf16[128,2048]{1,0:T(8,128)(2,1)}, bf16[128,2048]{1,0:T(8,128)(2,1)}, u32[]{:S(2)}, u32[]{:S(2)}) collective-permute-start(bf16[128,2048]{1,0:T(8,128)(2,1)} %copy.29), channel_id=1, source_target_pairs={{0,1},{1,0},{2,3},{3,2},{4,5},{5,4},{6,7},{7,6},{8,9},{9,8},{10,11... | collective-permute-start | bytes 1572872 | tf_op jit(solution)/shard_map/while/body/eval_jaxpr/ppermute | solution.py:32
  (67 other events, 390.9 us)
Sparse Core Ops, SparseCore 0:
  10.4 54.9 all-gather.2
  67.8 51.2 all-gather.4

commit v9 on v2

--- a/solution.py
+++ b/solution.py
@@ -71,8 +71,7 @@
     along_zl = lambda v: shifted(v, "rep", 2, 1)
     outs = []
     for grad, order in ((first, 0), (second, 1)):
-        blocks = grad.reshape(4, 4, 2, 2, 2, rows // 128, cols)
-        blocks = pair_scatter(blocks, 3, core_pos, along_core)
+        blocks = grad.reshape(4, 4, 2, 2, rows // 64, cols)
         if order == 0:
             blocks = ring_scatter(blocks, seg, 4, along_x)
             blocks = ring_scatter(blocks, y_pos, 4, along_y)
@@ -221,14 +220,31 @@
         * inverse
         * jnp.mean(hidden * scaled_grad, axis=-1, keepdims=True)
     ).astype(jnp.bfloat16)
-    up_grad = lax.dot_general(
-        hidden_grad, latent, (((0,), (0,)), ((), ())), preferred_element_type=jnp.float32
-    )
+    core_pos = lax.axis_index("fsdp") % 2
+    along_core = lambda v: fsdp_moved(v, lambda g: g ^ 1)
+
+    def core_columns(values, pick):
+        blocks = values.reshape(values.shape[0], 4, 4, 2, 2, 2, model_width // 128)
+        return lax.dynamic_index_in_dim(blocks, pick, 4, keepdims=False).reshape(values.shape[0], -1)
+
+    rank = latent.shape[1]
+    forward_sent = along_core(jnp.concatenate([core_columns(unit_rows, 1 - core_pos), latent], axis=1))
     latent_grad = jnp.dot(hidden_grad, up_full, preferred_element_type=jnp.float32).astype(
         jnp.bfloat16
     )
+    backward_sent = along_core(
+        jnp.concatenate([core_columns(hidden_grad, 1 - core_pos), latent_grad], axis=1)
+    )
+    half_rows = model_width // 2
+    unit_both = jnp.concatenate([core_columns(unit_rows, core_pos), forward_sent[:, :half_rows]], axis=0)
+    latent_both = jnp.concatenate([latent, forward_sent[:, half_rows:]], axis=0)
+    hidden_both = jnp.concatenate([core_columns(hidden_grad, core_pos), backward_sent[:, :half_rows]], axis=0)
+    latent_grad_both = jnp.concatenate([latent_grad, backward_sent[:, half_rows:]], axis=0)
+    up_grad = lax.dot_general(
+        hidden_both, latent_both, (((0,), (0,)), ((), ())), preferred_element_type=jnp.float32
+    )
     down_grad = lax.dot_general(
-        unit_rows, latent_grad, (((0,), (0,)), ((), ())), preferred_element_type=jnp.float32
+        unit_both, latent_grad_both, (((0,), (0,)), ((), ())), preferred_element_type=jnp.float32
     )
     down_share, up_share = gradient_scatter(down_grad, up_grad)
     return (down_share, up_share)

time: 471 us -> 481 us (1.021)
  local copies, waits for them, and re-layouts: 12.6 us -> 18.4 us
  waiting for transfers between devices: 122 us -> 127 us
    all_gather x1, waiting for transfers between devices: 0.02 us -> 17.7 us  [on_device(): lax.all_gather(agent_up, 'fsdp', axis=0, tiled=True)]
    ppermute x33, waiting for transfers between devices: 111 us -> 101 us  [shifted(): return lax.ppermute(x, axis, [(i, (i + by) % size) for i in range(size)])]
    ppermute x33, starting transfers between devices: 33.6 us -> 39.5 us  [shifted(): return lax.ppermute(x, axis, [(i, (i + by) % size) for i in range(size)])]
    ppermute x16, starting transfers between devices: 27.5 us -> 22.4 us  [fsdp_moved(): return lax.ppermute(x, 'fsdp', [(f, mapping(f)) for f in range(16)])]
  transfers between devices with their start and end apart: 65 -> 65, of which waited for: 28 -> 31; matrix products, arithmetic and copies ran while one was open for 44% -> 42% of each run, Pallas kernels for 0% -> 0%
where the time goes in v9:
time: 481 us; the launch traced here: 479 us
  matrix products  152 us (32%)
  waiting for transfers between devices  127 us (26%)
  starting transfers between devices  113 us (23%)
  other arithmetic  48.4 us (10%)
  local copies, waits for them, and re-layouts  18.4 us (4%)
  between operations  18.1 us (4%)
    dot_general x14, matrix products, apply_segment(): update = jnp.dot(normed, weight_local, preferred_element_type=jnp.float32)  132 us
    ppermute x33, waiting for transfers between devices, shifted(): return lax.ppermute(x, axis, [(i, (i + by) % size) for i in range(size)])  101 us
    ppermute x14, starting transfers between devices, tick_whole(): lax.ppermute(computed, 'segment', [(i, i + 1) for i in range(segments - 1)])  51.5 us
    ppermute x33, starting transfers between devices, shifted(): return lax.ppermute(x, axis, [(i, (i + by) % size) for i in range(size)])  39.5 us
    reduce_sum x14, other arithmetic, rms_scale(): squares = jnp.mean(values * values, axis=-1, keepdims=True)  23.3 us
    ppermute x16, starting transfers between devices, fsdp_moved(): return lax.ppermute(x, 'fsdp', [(f, mapping(f)) for f in range(16)])  22.4 us
    all_gather x1, waiting for transfers between devices, on_device(): lax.all_gather(agent_up, 'fsdp', axis=0, tiled=True)  17.7 us
    while x14, other arithmetic  14.1 us
  transfers between devices with their start and end apart: 65, of which 31 were waited for; matrix products, arithmetic and copies ran while one was open for 42% of the time, Pallas kernels for 0%

profile of v9, /device:TPU:0, one launch (start us, length us, event | category | flops | bytes accessed | tf_op | source)
XLA Modules:
  0.0 478.6 jit_solution(5504150839606027539)
XLA Ops:
  8.4 6.3 %convolution_convert_fusion = bf16[1024,4096]{1,0:T(8,128)(2,1)} fusion(bf16[128,4096]{1,0:T(8,128)(2,1)S(1)} %copy-done, s32[1024]{0:T(1024)} %bitcast.143), kind=kOutput, calls=%fused_computation.18 | convolution fusion | flops 1078067200 | bytes 9441280 | tf_op jit(solution)/shard_map/dot_general | solution.py:22
  17.3 314.6 %while.20 = (s32[]{:T(128)}, bf16[128,2048]{1,0:T(8,128)(2,1)S(1)}, bf16[128,2048]{1,0:T(8,128)(2,1)}, bf16[1024,2048]{1,0:T(8,128)(2,1)}, pred[]{:T(512)}, /*in...) while((s32[]{:T(128)}, bf16[128,2048]{1,0:T(8,128)(2,1)S(1)}, ...), condition=%wide.region_4.5_spmd.clone, body=%wide.region_2.4_spmd.clone.sunk | while | flops 2154823936 | bytes 34098032 | solution.py:157
  22.9 9.8 %collective-permute-done.1 = bf16[128,2048]{1,0:T(8,128)(2,1)S(1)} collective-permute-done((bf16[128,2048]{1,0:T(8,128)(2,1)S(1)}, bf16[128,2048]{1,0:T(8,128)(2,1)S(1)}, u32[]{:S(2)}, u32[]{:S(2)}) %collective-permute-start.1) | collective-permute-done | bytes 524320 | tf_op jit(solution)/shard_map/while/body/eval_jaxpr/ppermute | solution.py:32
  34.5 9.5 %select_dynamic-update-slice_fusion.2 = (bf16[1024,2048]{1,0:T(8,128)(2,1)}, bf16[128,2048]{1,0:T(8,128)(2,1)}) fusion(bf16[1024,2048]{1,0:T(8,128)(2,1)} %get-tuple-element.480, s32[]{:T(128)S(6)} %select_n.436, pred[]{:T(512)S(6)} %and.148, bf16[4096,2048]{1,0:T(8,128)(2,1)} %get-tuple-element.505, f32[128,4096]{1,0:T(8,128)S(1)} %get-tuple-element.455, ...), kind=kOutput, calls=%fused_computation.8.clone.1 | convolution fusion | flops 2149842944 | bytes 21513220 | tf_op jit(solution)/shard_map/while/body/eval_jaxpr/dot_general | solution.py:128
  50.4 12.2 %collective-permute-done.1 = bf16[128,2048]{1,0:T(8,128)(2,1)S(1)} collective-permute-done((bf16[128,2048]{1,0:T(8,128)(2,1)S(1)}, bf16[128,2048]{1,0:T(8,128)(2,1)S(1)}, u32[]{:S(2)}, u32[]{:S(2)}) %collective-permute-start.1) | collective-permute-done | bytes 524320 | tf_op jit(solution)/shard_map/while/body/eval_jaxpr/ppermute | solution.py:32
  64.4 9.4 %select_dynamic-update-slice_fusion.2 = (bf16[1024,2048]{1,0:T(8,128)(2,1)}, bf16[128,2048]{1,0:T(8,128)(2,1)}) fusion(bf16[1024,2048]{1,0:T(8,128)(2,1)} %get-tuple-element.480, s32[]{:T(128)S(6)} %select_n.436, pred[]{:T(512)S(6)} %and.148, bf16[4096,2048]{1,0:T(8,128)(2,1)} %get-tuple-element.505, f32[128,4096]{1,0:T(8,128)S(1)} %get-tuple-element.455, ...), kind=kOutput, calls=%fused_computation.8.clone.1 | convolution fusion | flops 2149842944 | bytes 21513220 | tf_op jit(solution)/shard_map/while/body/eval_jaxpr/dot_general | solution.py:128
  79.2 8.1 %collective-permute-done.1 = bf16[128,2048]{1,0:T(8,128)(2,1)S(1)} collective-permute-done((bf16[128,2048]{1,0:T(8,128)(2,1)S(1)}, bf16[128,2048]{1,0:T(8,128)(2,1)S(1)}, u32[]{:S(2)}, u32[]{:S(2)}) %collective-permute-start.1) | collective-permute-done | bytes 524320 | tf_op jit(solution)/shard_map/while/body/eval_jaxpr/ppermute | solution.py:32
  89.1 9.4 %select_dynamic-update-slice_fusion.2 = (bf16[1024,2048]{1,0:T(8,128)(2,1)}, bf16[128,2048]{1,0:T(8,128)(2,1)}) fusion(bf16[1024,2048]{1,0:T(8,128)(2,1)} %get-tuple-element.480, s32[]{:T(128)S(6)} %select_n.436, pred[]{:T(512)S(6)} %and.148, bf16[4096,2048]{1,0:T(8,128)(2,1)} %get-tuple-element.505, f32[128,4096]{1,0:T(8,128)S(1)} %get-tuple-element.455, ...), kind=kOutput, calls=%fused_computation.8.clone.1 | convolution fusion | flops 2149842944 | bytes 21513220 | tf_op jit(solution)/shard_map/while/body/eval_jaxpr/dot_general | solution.py:128
  103.9 7.2 %collective-permute-done.1 = bf16[128,2048]{1,0:T(8,128)(2,1)S(1)} collective-permute-done((bf16[128,2048]{1,0:T(8,128)(2,1)S(1)}, bf16[128,2048]{1,0:T(8,128)(2,1)S(1)}, u32[]{:S(2)}, u32[]{:S(2)}) %collective-permute-start.1) | collective-permute-done | bytes 524320 | tf_op jit(solution)/shard_map/while/body/eval_jaxpr/ppermute | solution.py:32
  112.9 9.4 %select_dynamic-update-slice_fusion.2 = (bf16[1024,2048]{1,0:T(8,128)(2,1)}, bf16[128,2048]{1,0:T(8,128)(2,1)}) fusion(bf16[1024,2048]{1,0:T(8,128)(2,1)} %get-tuple-element.480, s32[]{:T(128)S(6)} %select_n.436, pred[]{:T(512)S(6)} %and.148, bf16[4096,2048]{1,0:T(8,128)(2,1)} %get-tuple-element.505, f32[128,4096]{1,0:T(8,128)S(1)} %get-tuple-element.455, ...), kind=kOutput, calls=%fused_computation.8.clone.1 | convolution fusion | flops 2149842944 | bytes 21513220 | tf_op jit(solution)/shard_map/while/body/eval_jaxpr/dot_general | solution.py:128
  127.7 6.4 %collective-permute-done.1 = bf16[128,2048]{1,0:T(8,128)(2,1)S(1)} collective-permute-done((bf16[128,2048]{1,0:T(8,128)(2,1)S(1)}, bf16[128,2048]{1,0:T(8,128)(2,1)S(1)}, u32[]{:S(2)}, u32[]{:S(2)}) %collective-permute-start.1) | collective-permute-done | bytes 524320 | tf_op jit(solution)/shard_map/while/body/eval_jaxpr/ppermute | solution.py:32
  135.8 9.4 %select_dynamic-update-slice_fusion.2 = (bf16[1024,2048]{1,0:T(8,128)(2,1)}, bf16[128,2048]{1,0:T(8,128)(2,1)}) fusion(bf16[1024,2048]{1,0:T(8,128)(2,1)} %get-tuple-element.480, s32[]{:T(128)S(6)} %select_n.436, pred[]{:T(512)S(6)} %and.148, bf16[4096,2048]{1,0:T(8,128)(2,1)} %get-tuple-element.505, f32[128,4096]{1,0:T(8,128)S(1)} %get-tuple-element.455, ...), kind=kOutput, calls=%fused_computation.8.clone.1 | convolution fusion | flops 2149842944 | bytes 21513220 | tf_op jit(solution)/shard_map/while/body/eval_jaxpr/dot_general | solution.py:128
  150.6 5.5 %collective-permute-done.1 = bf16[128,2048]{1,0:T(8,128)(2,1)S(1)} collective-permute-done((bf16[128,2048]{1,0:T(8,128)(2,1)S(1)}, bf16[128,2048]{1,0:T(8,128)(2,1)S(1)}, u32[]{:S(2)}, u32[]{:S(2)}) %collective-permute-start.1) | collective-permute-done | bytes 524320 | tf_op jit(solution)/shard_map/while/body/eval_jaxpr/ppermute | solution.py:32
  157.8 9.4 %select_dynamic-update-slice_fusion.2 = (bf16[1024,2048]{1,0:T(8,128)(2,1)}, bf16[128,2048]{1,0:T(8,128)(2,1)}) fusion(bf16[1024,2048]{1,0:T(8,128)(2,1)} %get-tuple-element.480, s32[]{:T(128)S(6)} %select_n.436, pred[]{:T(512)S(6)} %and.148, bf16[4096,2048]{1,0:T(8,128)(2,1)} %get-tuple-element.505, f32[128,4096]{1,0:T(8,128)S(1)} %get-tuple-element.455, ...), kind=kOutput, calls=%fused_computation.8.clone.1 | convolution fusion | flops 2149842944 | bytes 21513220 | tf_op jit(solution)/shard_map/while/body/eval_jaxpr/dot_general | solution.py:128
  172.7 4.5 collective-permute-done.1
  179.0 9.4 %select_dynamic-update-slice_fusion.2 = (bf16[1024,2048]{1,0:T(8,128)(2,1)}, bf16[128,2048]{1,0:T(8,128)(2,1)}) fusion(bf16[1024,2048]{1,0:T(8,128)(2,1)} %get-tuple-element.480, s32[]{:T(128)S(6)} %select_n.436, pred[]{:T(512)S(6)} %and.148, bf16[4096,2048]{1,0:T(8,128)(2,1)} %get-tuple-element.505, f32[128,4096]{1,0:T(8,128)S(1)} %get-tuple-element.455, ...), kind=kOutput, calls=%fused_computation.8.clone.1 | convolution fusion | flops 2149842944 | bytes 21513220 | tf_op jit(solution)/shard_map/while/body/eval_jaxpr/dot_general | solution.py:128
  193.9 3.9 collective-permute-done.1
  199.5 9.4 %select_dynamic-update-slice_fusion.2 = (bf16[1024,2048]{1,0:T(8,128)(2,1)}, bf16[128,2048]{1,0:T(8,128)(2,1)}) fusion(bf16[1024,2048]{1,0:T(8,128)(2,1)} %get-tuple-element.480, s32[]{:T(128)S(6)} %select_n.436, pred[]{:T(512)S(6)} %and.148, bf16[4096,2048]{1,0:T(8,128)(2,1)} %get-tuple-element.505, f32[128,4096]{1,0:T(8,128)S(1)} %get-tuple-element.455, ...), kind=kOutput, calls=%fused_computation.8.clone.1 | convolution fusion | flops 2149842944 | bytes 21513220 | tf_op jit(solution)/shard_map/while/body/eval_jaxpr/dot_general | solution.py:128
  214.4 3.9 collective-permute-done.1
  220.0 9.4 %select_dynamic-update-slice_fusion.2 = (bf16[1024,2048]{1,0:T(8,128)(2,1)}, bf16[128,2048]{1,0:T(8,128)(2,1)}) fusion(bf16[1024,2048]{1,0:T(8,128)(2,1)} %get-tuple-element.480, s32[]{:T(128)S(6)} %select_n.436, pred[]{:T(512)S(6)} %and.148, bf16[4096,2048]{1,0:T(8,128)(2,1)} %get-tuple-element.505, f32[128,4096]{1,0:T(8,128)S(1)} %get-tuple-element.455, ...), kind=kOutput, calls=%fused_computation.8.clone.1 | convolution fusion | flops 2149842944 | bytes 21513220 | tf_op jit(solution)/shard_map/while/body/eval_jaxpr/dot_general | solution.py:128
  234.9 3.9 collective-permute-done.1
  240.5 9.4 %select_dynamic-update-slice_fusion.2 = (bf16[1024,2048]{1,0:T(8,128)(2,1)}, bf16[128,2048]{1,0:T(8,128)(2,1)}) fusion(bf16[1024,2048]{1,0:T(8,128)(2,1)} %get-tuple-element.480, s32[]{:T(128)S(6)} %select_n.436, pred[]{:T(512)S(6)} %and.148, bf16[4096,2048]{1,0:T(8,128)(2,1)} %get-tuple-element.505, f32[128,4096]{1,0:T(8,128)S(1)} %get-tuple-element.455, ...), kind=kOutput, calls=%fused_computation.8.clone.1 | convolution fusion | flops 2149842944 | bytes 21513220 | tf_op jit(solution)/shard_map/while/body/eval_jaxpr/dot_general | solution.py:128
  255.4 3.9 collective-permute-done.1
  261.0 9.4 %select_dynamic-update-slice_fusion.2 = (bf16[1024,2048]{1,0:T(8,128)(2,1)}, bf16[128,2048]{1,0:T(8,128)(2,1)}) fusion(bf16[1024,2048]{1,0:T(8,128)(2,1)} %get-tuple-element.480, s32[]{:T(128)S(6)} %select_n.436, pred[]{:T(512)S(6)} %and.148, bf16[4096,2048]{1,0:T(8,128)(2,1)} %get-tuple-element.505, f32[128,4096]{1,0:T(8,128)S(1)} %get-tuple-element.455, ...), kind=kOutput, calls=%fused_computation.8.clone.1 | convolution fusion | flops 2149842944 | bytes 21513220 | tf_op jit(solution)/shard_map/while/body/eval_jaxpr/dot_general | solution.py:128
  275.9 3.9 collective-permute-done.1
  281.5 9.4 %select_dynamic-update-slice_fusion.2 = (bf16[1024,2048]{1,0:T(8,128)(2,1)}, bf16[128,2048]{1,0:T(8,128)(2,1)}) fusion(bf16[1024,2048]{1,0:T(8,128)(2,1)} %get-tuple-element.480, s32[]{:T(128)S(6)} %select_n.436, pred[]{:T(512)S(6)} %and.148, bf16[4096,2048]{1,0:T(8,128)(2,1)} %get-tuple-element.505, f32[128,4096]{1,0:T(8,128)S(1)} %get-tuple-element.455, ...), kind=kOutput, calls=%fused_computation.8.clone.1 | convolution fusion | flops 2149842944 | bytes 21513220 | tf_op jit(solution)/shard_map/while/body/eval_jaxpr/dot_general | solution.py:128
  296.3 3.9 collective-permute-done.1
  302.0 9.4 %select_dynamic-update-slice_fusion.2 = (bf16[1024,2048]{1,0:T(8,128)(2,1)}, bf16[128,2048]{1,0:T(8,128)(2,1)}) fusion(bf16[1024,2048]{1,0:T(8,128)(2,1)} %get-tuple-element.480, s32[]{:T(128)S(6)} %select_n.436, pred[]{:T(512)S(6)} %and.148, bf16[4096,2048]{1,0:T(8,128)(2,1)} %get-tuple-element.505, f32[128,4096]{1,0:T(8,128)S(1)} %get-tuple-element.455, ...), kind=kOutput, calls=%fused_computation.8.clone.1 | convolution fusion | flops 2149842944 | bytes 21513220 | tf_op jit(solution)/shard_map/while/body/eval_jaxpr/dot_general | solution.py:128
  316.8 3.9 collective-permute-done.1
  322.5 9.4 %select_dynamic-update-slice_fusion.2 = (bf16[1024,2048]{1,0:T(8,128)(2,1)}, bf16[128,2048]{1,0:T(8,128)(2,1)}) fusion(bf16[1024,2048]{1,0:T(8,128)(2,1)} %get-tuple-element.480, s32[]{:T(128)S(6)} %select_n.436, pred[]{:T(512)S(6)} %and.148, bf16[4096,2048]{1,0:T(8,128)(2,1)} %get-tuple-element.505, f32[128,4096]{1,0:T(8,128)S(1)} %get-tuple-element.455, ...), kind=kOutput, calls=%fused_computation.8.clone.1 | convolution fusion | flops 2149842944 | bytes 21513220 | tf_op jit(solution)/shard_map/while/body/eval_jaxpr/dot_general | solution.py:128
  347.4 8.8 %collective-permute-done.4 = f32[1024,128]{0,1:T(8,128)S(1)} collective-permute-done((f32[1024,128]{0,1:T(8,128)S(1)}, f32[1024,128]{0,1:T(8,128)S(1)}, u32[]{:S(2)}, u32[]{:S(2)}) %collective-permute-start.4) | collective-permute-done | bytes 524320 | tf_op jit(solution)/shard_map/ppermute | solution.py:32
  369.0 17.7 %all-gather.5.cloned.1.call-done = bf16[4096,256]{1,0:T(8,128)(2,1)} async-done(((bf16[256,256]{1,0:T(8,128)(2,1)}), bf16[4096,256]{1,0:T(8,128)(2,1)}) %all-gather.5.cloned.1.call-update) | async-done | bytes 2097168 | tf_op jit(solution)/shard_map/all_gather | solution.py:122
  (306 shorter events, 213.8 us)
Async XLA Ops:
  7.2 359.5 %all-gather.3.cloned.1.call-start = ((), (), s32[]{:S(2)}) async-start(), calls=%async_computation | async-start | bytes 2228224 | tf_op jit(solution)/shard_map/all_gather | solution.py:121
  7.9 378.8 %all-gather.5.cloned.1.call-start = ((), (), s32[]{:S(2)}) async-start(), calls=%async_computation.1 | async-start | bytes 2228224 | tf_op jit(solution)/shard_map/all_gather | solution.py:122
  17.3 15.4 %collective-permute-start.1 = (bf16[128,2048]{1,0:T(8,128)(2,1)S(1)}, bf16[128,2048]{1,0:T(8,128)(2,1)S(1)}, u32[]{:S(2)}, u32[]{:S(2)}) collective-permute-start(bf16[128,2048]{1,0:T(8,128)(2,1)S(1)} %get-tuple-element.478), channel_id=1, source_target_pairs={{0,1},{1,0},{2,3},{3,2},{4,5},{5,4},{6,7},{7,6},{8,9},{9,8},{10,11... | collective-permute-start | bytes 1572872 | tf_op jit(solution)/shard_map/while/body/eval_jaxpr/ppermute | solution.py:32
  19.5 24.5 %collective-permute-start = (bf16[128,2048]{1,0:T(8,128)(2,1)S(1)}, bf16[128,2048]{1,0:T(8,128)(2,1)S(1)}, u32[]{:S(2)}, u32[]{:S(2)}) collective-permute-start(bf16[128,2048]{1,0:T(8,128)(2,1)S(1)} %broadcast_select_fusion.8), channel_id=1, source_target_pairs={{0,32},{32,64},{64,96},{1,33},{33,65},{65,97},{2,34},{34,66},{66,9... | collective-permute-start | bytes 1572872 | tf_op jit(solution)/shard_map/while/body/eval_jaxpr/ppermute | solution.py:137
  44.1 18.6 %collective-permute-start.1 = (bf16[128,2048]{1,0:T(8,128)(2,1)S(1)}, bf16[128,2048]{1,0:T(8,128)(2,1)S(1)}, u32[]{:S(2)}, u32[]{:S(2)}) collective-permute-start(bf16[128,2048]{1,0:T(8,128)(2,1)S(1)} %get-tuple-element.478), channel_id=1, source_target_pairs={{0,1},{1,0},{2,3},{3,2},{4,5},{5,4},{6,7},{7,6},{8,9},{9,8},{10,11... | collective-permute-start | bytes 1572872 | tf_op jit(solution)/shard_map/while/body/eval_jaxpr/ppermute | solution.py:32
  47.0 26.9 %collective-permute-start = (bf16[128,2048]{1,0:T(8,128)(2,1)S(1)}, bf16[128,2048]{1,0:T(8,128)(2,1)S(1)}, u32[]{:S(2)}, u32[]{:S(2)}) collective-permute-start(bf16[128,2048]{1,0:T(8,128)(2,1)S(1)} %broadcast_select_fusion.8), channel_id=1, source_target_pairs={{0,32},{32,64},{64,96},{1,33},{33,65},{65,97},{2,34},{34,66},{66,9... | collective-permute-start | bytes 1572872 | tf_op jit(solution)/shard_map/while/body/eval_jaxpr/ppermute | solution.py:137
  73.9 13.4 %collective-permute-start.1 = (bf16[128,2048]{1,0:T(8,128)(2,1)S(1)}, bf16[128,2048]{1,0:T(8,128)(2,1)S(1)}, u32[]{:S(2)}, u32[]{:S(2)}) collective-permute-start(bf16[128,2048]{1,0:T(8,128)(2,1)S(1)} %get-tuple-element.478), channel_id=1, source_target_pairs={{0,1},{1,0},{2,3},{3,2},{4,5},{5,4},{6,7},{7,6},{8,9},{9,8},{10,11... | collective-permute-start | bytes 1572872 | tf_op jit(solution)/shard_map/while/body/eval_jaxpr/ppermute | solution.py:32
  75.4 23.1 %collective-permute-start = (bf16[128,2048]{1,0:T(8,128)(2,1)S(1)}, bf16[128,2048]{1,0:T(8,128)(2,1)S(1)}, u32[]{:S(2)}, u32[]{:S(2)}) collective-permute-start(bf16[128,2048]{1,0:T(8,128)(2,1)S(1)} %broadcast_select_fusion.8), channel_id=1, source_target_pairs={{0,32},{32,64},{64,96},{1,33},{33,65},{65,97},{2,34},{34,66},{66,9... | collective-permute-start | bytes 1572872 | tf_op jit(solution)/shard_map/while/body/eval_jaxpr/ppermute | solution.py:137
  98.6 12.5 %collective-permute-start.1 = (bf16[128,2048]{1,0:T(8,128)(2,1)S(1)}, bf16[128,2048]{1,0:T(8,128)(2,1)S(1)}, u32[]{:S(2)}, u32[]{:S(2)}) collective-permute-start(bf16[128,2048]{1,0:T(8,128)(2,1)S(1)} %get-tuple-element.478), channel_id=1, source_target_pairs={{0,1},{1,0},{2,3},{3,2},{4,5},{5,4},{6,7},{7,6},{8,9},{9,8},{10,11... | collective-permute-start | bytes 1572872 | tf_op jit(solution)/shard_map/while/body/eval_jaxpr/ppermute | solution.py:32
  100.1 22.2 %collective-permute-start = (bf16[128,2048]{1,0:T(8,128)(2,1)S(1)}, bf16[128,2048]{1,0:T(8,128)(2,1)S(1)}, u32[]{:S(2)}, u32[]{:S(2)}) collective-permute-start(bf16[128,2048]{1,0:T(8,128)(2,1)S(1)} %broadcast_select_fusion.8), channel_id=1, source_target_pairs={{0,32},{32,64},{64,96},{1,33},{33,65},{65,97},{2,34},{34,66},{66,9... | collective-permute-start | bytes 1572872 | tf_op jit(solution)/shard_map/while/body/eval_jaxpr/ppermute | solution.py:137
  122.4 11.7 %collective-permute-start.1 = (bf16[128,2048]{1,0:T(8,128)(2,1)S(1)}, bf16[128,2048]{1,0:T(8,128)(2,1)S(1)}, u32[]{:S(2)}, u32[]{:S(2)}) collective-permute-start(bf16[128,2048]{1,0:T(8,128)(2,1)S(1)} %get-tuple-element.478), channel_id=1, source_target_pairs={{0,1},{1,0},{2,3},{3,2},{4,5},{5,4},{6,7},{7,6},{8,9},{9,8},{10,11... | collective-permute-start | bytes 1572872 | tf_op jit(solution)/shard_map/while/body/eval_jaxpr/ppermute | solution.py:32
  123.9 21.3 %collective-permute-start = (bf16[128,2048]{1,0:T(8,128)(2,1)S(1)}, bf16[128,2048]{1,0:T(8,128)(2,1)S(1)}, u32[]{:S(2)}, u32[]{:S(2)}) collective-permute-start(bf16[128,2048]{1,0:T(8,128)(2,1)S(1)} %broadcast_select_fusion.8), channel_id=1, source_target_pairs={{0,32},{32,64},{64,96},{1,33},{33,65},{65,97},{2,34},{34,66},{66,9... | collective-permute-start | bytes 1572872 | tf_op jit(solution)/shard_map/while/body/eval_jaxpr/ppermute | solution.py:137
  145.3 10.8 %collective-permute-start.1 = (bf16[128,2048]{1,0:T(8,128)(2,1)S(1)}, bf16[128,2048]{1,0:T(8,128)(2,1)S(1)}, u32[]{:S(2)}, u32[]{:S(2)}) collective-permute-start(bf16[128,2048]{1,0:T(8,128)(2,1)S(1)} %get-tuple-element.478), channel_id=1, source_target_pairs={{0,1},{1,0},{2,3},{3,2},{4,5},{5,4},{6,7},{7,6},{8,9},{9,8},{10,11... | collective-permute-start | bytes 1572872 | tf_op jit(solution)/shard_map/while/body/eval_jaxpr/ppermute | solution.py:32
  146.8 20.4 %collective-permute-start = (bf16[128,2048]{1,0:T(8,128)(2,1)S(1)}, bf16[128,2048]{1,0:T(8,128)(2,1)S(1)}, u32[]{:S(2)}, u32[]{:S(2)}) collective-permute-start(bf16[128,2048]{1,0:T(8,128)(2,1)S(1)} %broadcast_select_fusion.8), channel_id=1, source_target_pairs={{0,32},{32,64},{64,96},{1,33},{33,65},{65,97},{2,34},{34,66},{66,9... | collective-permute-start | bytes 1572872 | tf_op jit(solution)/shard_map/while/body/eval_jaxpr/ppermute | solution.py:137
  167.3 10.0 %collective-permute-start.1 = (bf16[128,2048]{1,0:T(8,128)(2,1)S(1)}, bf16[128,2048]{1,0:T(8,128)(2,1)S(1)}, u32[]{:S(2)}, u32[]{:S(2)}) collective-permute-start(bf16[128,2048]{1,0:T(8,128)(2,1)S(1)} %get-tuple-element.478), channel_id=1, source_target_pairs={{0,1},{1,0},{2,3},{3,2},{4,5},{5,4},{6,7},{7,6},{8,9},{9,8},{10,11... | collective-permute-start | bytes 1572872 | tf_op jit(solution)/shard_map/while/body/eval_jaxpr/ppermute | solution.py:32
  168.9 19.5 %collective-permute-start = (bf16[128,2048]{1,0:T(8,128)(2,1)S(1)}, bf16[128,2048]{1,0:T(8,128)(2,1)S(1)}, u32[]{:S(2)}, u32[]{:S(2)}) collective-permute-start(bf16[128,2048]{1,0:T(8,128)(2,1)S(1)} %broadcast_select_fusion.8), channel_id=1, source_target_pairs={{0,32},{32,64},{64,96},{1,33},{33,65},{65,97},{2,34},{34,66},{66,9... | collective-permute-start | bytes 1572872 | tf_op jit(solution)/shard_map/while/body/eval_jaxpr/ppermute | solution.py:137
  188.5 9.3 %collective-permute-start.1 = (bf16[128,2048]{1,0:T(8,128)(2,1)S(1)}, bf16[128,2048]{1,0:T(8,128)(2,1)S(1)}, u32[]{:S(2)}, u32[]{:S(2)}) collective-permute-start(bf16[128,2048]{1,0:T(8,128)(2,1)S(1)} %get-tuple-element.478), channel_id=1, source_target_pairs={{0,1},{1,0},{2,3},{3,2},{4,5},{5,4},{6,7},{7,6},{8,9},{9,8},{10,11... | collective-permute-start | bytes 1572872 | tf_op jit(solution)/shard_map/while/body/eval_jaxpr/ppermute | solution.py:32
  190.1 18.8 %collective-permute-start = (bf16[128,2048]{1,0:T(8,128)(2,1)S(1)}, bf16[128,2048]{1,0:T(8,128)(2,1)S(1)}, u32[]{:S(2)}, u32[]{:S(2)}) collective-permute-start(bf16[128,2048]{1,0:T(8,128)(2,1)S(1)} %broadcast_select_fusion.8), channel_id=1, source_target_pairs={{0,32},{32,64},{64,96},{1,33},{33,65},{65,97},{2,34},{34,66},{66,9... | collective-permute-start | bytes 1572872 | tf_op jit(solution)/shard_map/while/body/eval_jaxpr/ppermute | solution.py:137
  209.0 9.3 %collective-permute-start.1 = (bf16[128,2048]{1,0:T(8,128)(2,1)S(1)}, bf16[128,2048]{1,0:T(8,128)(2,1)S(1)}, u32[]{:S(2)}, u32[]{:S(2)}) collective-permute-start(bf16[128,2048]{1,0:T(8,128)(2,1)S(1)} %get-tuple-element.478), channel_id=1, source_target_pairs={{0,1},{1,0},{2,3},{3,2},{4,5},{5,4},{6,7},{7,6},{8,9},{9,8},{10,11... | collective-permute-start | bytes 1572872 | tf_op jit(solution)/shard_map/while/body/eval_jaxpr/ppermute | solution.py:32
  210.6 18.8 %collective-permute-start = (bf16[128,2048]{1,0:T(8,128)(2,1)S(1)}, bf16[128,2048]{1,0:T(8,128)(2,1)S(1)}, u32[]{:S(2)}, u32[]{:S(2)}) collective-permute-start(bf16[128,2048]{1,0:T(8,128)(2,1)S(1)} %broadcast_select_fusion.8), channel_id=1, source_target_pairs={{0,32},{32,64},{64,96},{1,33},{33,65},{65,97},{2,34},{34,66},{66,9... | collective-permute-start | bytes 1572872 | tf_op jit(solution)/shard_map/while/body/eval_jaxpr/ppermute | solution.py:137
  229.5 9.3 %collective-permute-start.1 = (bf16[128,2048]{1,0:T(8,128)(2,1)S(1)}, bf16[128,2048]{1,0:T(8,128)(2,1)S(1)}, u32[]{:S(2)}, u32[]{:S(2)}) collective-permute-start(bf16[128,2048]{1,0:T(8,128)(2,1)S(1)} %get-tuple-element.478), channel_id=1, source_target_pairs={{0,1},{1,0},{2,3},{3,2},{4,5},{5,4},{6,7},{7,6},{8,9},{9,8},{10,11... | collective-permute-start | bytes 1572872 | tf_op jit(solution)/shard_map/while/body/eval_jaxpr/ppermute | solution.py:32
  231.1 18.8 %collective-permute-start = (bf16[128,2048]{1,0:T(8,128)(2,1)S(1)}, bf16[128,2048]{1,0:T(8,128)(2,1)S(1)}, u32[]{:S(2)}, u32[]{:S(2)}) collective-permute-start(bf16[128,2048]{1,0:T(8,128)(2,1)S(1)} %broadcast_select_fusion.8), channel_id=1, source_target_pairs={{0,32},{32,64},{64,96},{1,33},{33,65},{65,97},{2,34},{34,66},{66,9... | collective-permute-start | bytes 1572872 | tf_op jit(solution)/shard_map/while/body/eval_jaxpr/ppermute | solution.py:137
  250.0 9.3 %collective-permute-start.1 = (bf16[128,2048]{1,0:T(8,128)(2,1)S(1)}, bf16[128,2048]{1,0:T(8,128)(2,1)S(1)}, u32[]{:S(2)}, u32[]{:S(2)}) collective-permute-start(bf16[128,2048]{1,0:T(8,128)(2,1)S(1)} %get-tuple-element.478), channel_id=1, source_target_pairs={{0,1},{1,0},{2,3},{3,2},{4,5},{5,4},{6,7},{7,6},{8,9},{9,8},{10,11... | collective-permute-start | bytes 1572872 | tf_op jit(solution)/shard_map/while/body/eval_jaxpr/ppermute | solution.py:32
  251.6 18.8 %collective-permute-start = (bf16[128,2048]{1,0:T(8,128)(2,1)S(1)}, bf16[128,2048]{1,0:T(8,128)(2,1)S(1)}, u32[]{:S(2)}, u32[]{:S(2)}) collective-permute-start(bf16[128,2048]{1,0:T(8,128)(2,1)S(1)} %broadcast_select_fusion.8), channel_id=1, source_target_pairs={{0,32},{32,64},{64,96},{1,33},{33,65},{65,97},{2,34},{34,66},{66,9... | collective-permute-start | bytes 1572872 | tf_op jit(solution)/shard_map/while/body/eval_jaxpr/ppermute | solution.py:137
  272.1 18.8 %collective-permute-start = (bf16[128,2048]{1,0:T(8,128)(2,1)S(1)}, bf16[128,2048]{1,0:T(8,128)(2,1)S(1)}, u32[]{:S(2)}, u32[]{:S(2)}) collective-permute-start(bf16[128,2048]{1,0:T(8,128)(2,1)S(1)} %broadcast_select_fusion.8), channel_id=1, source_target_pairs={{0,32},{32,64},{64,96},{1,33},{33,65},{65,97},{2,34},{34,66},{66,9... | collective-permute-start | bytes 1572872 | tf_op jit(solution)/shard_map/while/body/eval_jaxpr/ppermute | solution.py:137
  291.0 9.3 %collective-permute-start.1 = (bf16[128,2048]{1,0:T(8,128)(2,1)S(1)}, bf16[128,2048]{1,0:T(8,128)(2,1)S(1)}, u32[]{:S(2)}, u32[]{:S(2)}) collective-permute-start(bf16[128,2048]{1,0:T(8,128)(2,1)S(1)} %get-tuple-element.478), channel_id=1, source_target_pairs={{0,1},{1,0},{2,3},{3,2},{4,5},{5,4},{6,7},{7,6},{8,9},{9,8},{10,11... | collective-permute-start | bytes 1572872 | tf_op jit(solution)/shard_map/while/body/eval_jaxpr/ppermute | solution.py:32
  292.6 18.8 %collective-permute-start = (bf16[128,2048]{1,0:T(8,128)(2,1)S(1)}, bf16[128,2048]{1,0:T(8,128)(2,1)S(1)}, u32[]{:S(2)}, u32[]{:S(2)}) collective-permute-start(bf16[128,2048]{1,0:T(8,128)(2,1)S(1)} %broadcast_select_fusion.8), channel_id=1, source_target_pairs={{0,32},{32,64},{64,96},{1,33},{33,65},{65,97},{2,34},{34,66},{66,9... | collective-permute-start | bytes 1572872 | tf_op jit(solution)/shard_map/while/body/eval_jaxpr/ppermute | solution.py:137
  311.5 9.3 %collective-permute-start.1 = (bf16[128,2048]{1,0:T(8,128)(2,1)S(1)}, bf16[128,2048]{1,0:T(8,128)(2,1)S(1)}, u32[]{:S(2)}, u32[]{:S(2)}) collective-permute-start(bf16[128,2048]{1,0:T(8,128)(2,1)S(1)} %get-tuple-element.478), channel_id=1, source_target_pairs={{0,1},{1,0},{2,3},{3,2},{4,5},{5,4},{6,7},{7,6},{8,9},{9,8},{10,11... | collective-permute-start | bytes 1572872 | tf_op jit(solution)/shard_map/while/body/eval_jaxpr/ppermute | solution.py:32
  313.1 18.8 %collective-permute-start = (bf16[128,2048]{1,0:T(8,128)(2,1)S(1)}, bf16[128,2048]{1,0:T(8,128)(2,1)S(1)}, u32[]{:S(2)}, u32[]{:S(2)}) collective-permute-start(bf16[128,2048]{1,0:T(8,128)(2,1)S(1)} %broadcast_select_fusion.8), channel_id=1, source_target_pairs={{0,32},{32,64},{64,96},{1,33},{33,65},{65,97},{2,34},{34,66},{66,9... | collective-permute-start | bytes 1572872 | tf_op jit(solution)/shard_map/while/body/eval_jaxpr/ppermute | solution.py:137
  345.5 10.7 %collective-permute-start.4 = (f32[1024,128]{0,1:T(8,128)S(1)}, f32[1024,128]{0,1:T(8,128)S(1)}, u32[]{:S(2)}, u32[]{:S(2)}) collective-permute-start(f32[1024,128]{0,1:T(8,128)S(1)} %fusion.8), channel_id=1, source_target_pairs={{0,1},{1,0},{2,3},{3,2},{4,5},{5,4},{6,7},{7,6},{8,9},{9,8},{10,11... | collective-permute-start | bytes 1572872 | tf_op jit(solution)/shard_map/ppermute | solution.py:32
  410.2 9.8 %collective-permute-start.23 = (f32[4,2,2,32,128]{4,3,2,1,0:T(8,128)S(1)}, f32[4,2,2,32,128]{4,3,2,1,0:T(8,128)S(1)}, u32[]{:S(2)}, u32[]{:S(2)}) collective-permute-start(f32[4,2,2,32,128]{4,3,2,1,0:T(8,128)S(1)} %dynamic-slice_bitcast_fusion.1), channel_id=1, source_target_pairs={{0,8},{2,10},{4,12},{6,14},{8,16},{10,18},{12,20},{14,22},{16,24},... | collective-permute-start | bytes 786440 | tf_op jit(solution)/shard_map/ppermute | solution.py:36
  415.8 9.5 %collective-permute-start.9 = (f32[4,2,2,32,128]{4,3,2,1,0:T(8,128)S(1)}, f32[4,2,2,32,128]{4,3,2,1,0:T(8,128)S(1)}, u32[]{:S(2)}, u32[]{:S(2)}) collective-permute-start(f32[4,2,2,32,128]{4,3,2,1,0:T(8,128)S(1)} %dynamic-slice_bitcast_fusion.3), channel_id=1, source_target_pairs={{0,32},{32,64},{64,96},{96,0},{1,33},{33,65},{65,97},{97,1},{2,34}... | collective-permute-start | bytes 786440 | tf_op jit(solution)/shard_map/ppermute | solution.py:32
  (45 other events, 268.6 us)
Sparse Core Ops, SparseCore 0:
  10.4 55.1 all-gather.2
  335.7 50.9 all-gather.4

commit v10 on v9

--- a/solution.py
+++ b/solution.py
@@ -117,10 +117,8 @@
     is_last = segment_pos == segments - 1
     own_first = rep_pos == 0
 
-    down_full, up_full = (
-        lax.all_gather(agent_down, "fsdp", axis=0, tiled=True),
-        lax.all_gather(agent_up, "fsdp", axis=0, tiled=True),
-    )
+    both_full = lax.all_gather(jnp.stack([agent_down, agent_up]), "fsdp", axis=1, tiled=True)
+    down_full, up_full = both_full[0], both_full[1]
 
     def apply_segment(current):
         wide_rows = current.astype(jnp.float32)

time: 481 us -> 469 us (0.975)
  waiting for transfers between devices: 127 us -> 104 us
  starting transfers between devices: 113 us -> 123 us
    all_gather x2 -> x1, waiting for transfers between devices: 17.7 us -> 0.02 us  [on_device(): lax.all_gather(jnp.stack([agent_down, agent_up]), 'fsdp', axis=1, tiled=T...]
    ppermute x33, starting transfers between devices: 39.5 us -> 48.5 us  [shifted(): return lax.ppermute(x, axis, [(i, (i + by) % size) for i in range(size)])]
    ppermute x33, waiting for transfers between devices: 101 us -> 94.8 us  [shifted(): return lax.ppermute(x, axis, [(i, (i + by) % size) for i in range(size)])]
  transfers between devices with their start and end apart: 65 -> 64, of which waited for: 31 -> 28; matrix products, arithmetic and copies ran while one was open for 42% -> 43% of each run, Pallas kernels for 0% -> 0%
where the time goes in v10:
time: 469 us; the launch traced here: 466 us
  matrix products  152 us (32%)
  starting transfers between devices  123 us (26%)
  waiting for transfers between devices  104 us (22%)
  other arithmetic  51.2 us (11%)
  between operations  18 us (4%)
  local copies, waits for them, and re-layouts  17.1 us (4%)
    dot_general x14, matrix products, apply_segment(): update = jnp.dot(normed, weight_local, preferred_element_type=jnp.float32)  132 us
    ppermute x33, waiting for transfers between devices, shifted(): return lax.ppermute(x, axis, [(i, (i + by) % size) for i in range(size)])  94.8 us
    ppermute x33, starting transfers between devices, shifted(): return lax.ppermute(x, axis, [(i, (i + by) % size) for i in range(size)])  48.5 us
    ppermute x14, starting transfers between devices, tick_whole(): lax.ppermute(computed, 'segment', [(i, i + 1) for i in range(segments - 1)])  47.7 us
    ppermute x16, starting transfers between devices, fsdp_moved(): return lax.ppermute(x, 'fsdp', [(f, mapping(f)) for f in range(16)])  26.4 us
    reduce_sum x14, other arithmetic, rms_scale(): squares = jnp.mean(values * values, axis=-1, keepdims=True)  23.3 us
    while x14, other arithmetic  14.1 us
  transfers between devices with their start and end apart: 64, of which 28 were waited for; matrix products, arithmetic and copies ran while one was open for 43% of the time, Pallas kernels for 0%

profile of v10, /device:TPU:0, one launch (start us, length us, event | category | flops | bytes accessed | tf_op | source)
XLA Modules:
  0.0 466.3 jit_solution(10763484085381684184)
XLA Ops:
  9.1 6.3 %convolution_convert_fusion = bf16[1024,4096]{1,0:T(8,128)(2,1)} fusion(bf16[128,4096]{1,0:T(8,128)(2,1)S(1)} %copy-done, s32[1024]{0:T(1024)} %bitcast.155), kind=kOutput, calls=%fused_computation.18 | convolution fusion | flops 1078067200 | bytes 9441280 | tf_op jit(solution)/shard_map/dot_general | solution.py:22
  17.9 321.7 %while.20 = (s32[]{:T(128)}, bf16[128,2048]{1,0:T(8,128)(2,1)S(1)}, bf16[128,2048]{1,0:T(8,128)(2,1)}, bf16[1024,2048]{1,0:T(8,128)(2,1)}, pred[]{:T(512)}, /*in...) while((s32[]{:T(128)}, bf16[128,2048]{1,0:T(8,128)(2,1)S(1)}, ...), condition=%wide.region_4.5_spmd.clone, body=%wide.region_2.4_spmd.clone.sunk | while | flops 2154823936 | bytes 34098032 | solution.py:155
  23.6 11.2 %collective-permute-done.1 = bf16[128,2048]{1,0:T(8,128)(2,1)S(1)} collective-permute-done((bf16[128,2048]{1,0:T(8,128)(2,1)S(1)}, bf16[128,2048]{1,0:T(8,128)(2,1)S(1)}, u32[]{:S(2)}, u32[]{:S(2)}) %collective-permute-start.1) | collective-permute-done | bytes 524320 | tf_op jit(solution)/shard_map/while/body/eval_jaxpr/ppermute | solution.py:32
  36.5 9.5 %select_dynamic-update-slice_fusion.2 = (bf16[1024,2048]{1,0:T(8,128)(2,1)}, bf16[128,2048]{1,0:T(8,128)(2,1)}) fusion(bf16[1024,2048]{1,0:T(8,128)(2,1)} %get-tuple-element.480, s32[]{:T(128)S(6)} %select_n.436, pred[]{:T(512)S(6)} %and.148, bf16[4096,2048]{1,0:T(8,128)(2,1)} %get-tuple-element.505, f32[128,4096]{1,0:T(8,128)S(1)} %get-tuple-element.455, ...), kind=kOutput, calls=%fused_computation.8.clone.1 | convolution fusion | flops 2149842944 | bytes 21513220 | tf_op jit(solution)/shard_map/while/body/eval_jaxpr/dot_general | solution.py:126
  52.4 18.2 %collective-permute-done.1 = bf16[128,2048]{1,0:T(8,128)(2,1)S(1)} collective-permute-done((bf16[128,2048]{1,0:T(8,128)(2,1)S(1)}, bf16[128,2048]{1,0:T(8,128)(2,1)S(1)}, u32[]{:S(2)}, u32[]{:S(2)}) %collective-permute-start.1) | collective-permute-done | bytes 524320 | tf_op jit(solution)/shard_map/while/body/eval_jaxpr/ppermute | solution.py:32
  72.4 9.7 %select_dynamic-update-slice_fusion.2 = (bf16[1024,2048]{1,0:T(8,128)(2,1)}, bf16[128,2048]{1,0:T(8,128)(2,1)}) fusion(bf16[1024,2048]{1,0:T(8,128)(2,1)} %get-tuple-element.480, s32[]{:T(128)S(6)} %select_n.436, pred[]{:T(512)S(6)} %and.148, bf16[4096,2048]{1,0:T(8,128)(2,1)} %get-tuple-element.505, f32[128,4096]{1,0:T(8,128)S(1)} %get-tuple-element.455, ...), kind=kOutput, calls=%fused_computation.8.clone.1 | convolution fusion | flops 2149842944 | bytes 21513220 | tf_op jit(solution)/shard_map/while/body/eval_jaxpr/dot_general | solution.py:126
  83.7 3.7 collective-permute-start
  87.4 7.8 %collective-permute-done.1 = bf16[128,2048]{1,0:T(8,128)(2,1)S(1)} collective-permute-done((bf16[128,2048]{1,0:T(8,128)(2,1)S(1)}, bf16[128,2048]{1,0:T(8,128)(2,1)S(1)}, u32[]{:S(2)}, u32[]{:S(2)}) %collective-permute-start.1) | collective-permute-done | bytes 524320 | tf_op jit(solution)/shard_map/while/body/eval_jaxpr/ppermute | solution.py:32
  96.9 9.4 %select_dynamic-update-slice_fusion.2 = (bf16[1024,2048]{1,0:T(8,128)(2,1)}, bf16[128,2048]{1,0:T(8,128)(2,1)}) fusion(bf16[1024,2048]{1,0:T(8,128)(2,1)} %get-tuple-element.480, s32[]{:T(128)S(6)} %select_n.436, pred[]{:T(512)S(6)} %and.148, bf16[4096,2048]{1,0:T(8,128)(2,1)} %get-tuple-element.505, f32[128,4096]{1,0:T(8,128)S(1)} %get-tuple-element.455, ...), kind=kOutput, calls=%fused_computation.8.clone.1 | convolution fusion | flops 2149842944 | bytes 21513220 | tf_op jit(solution)/shard_map/while/body/eval_jaxpr/dot_general | solution.py:126
  108.5 3.7 collective-permute-start
  112.2 6.4 %collective-permute-done.1 = bf16[128,2048]{1,0:T(8,128)(2,1)S(1)} collective-permute-done((bf16[128,2048]{1,0:T(8,128)(2,1)S(1)}, bf16[128,2048]{1,0:T(8,128)(2,1)S(1)}, u32[]{:S(2)}, u32[]{:S(2)}) %collective-permute-start.1) | collective-permute-done | bytes 524320 | tf_op jit(solution)/shard_map/while/body/eval_jaxpr/ppermute | solution.py:32
  120.3 9.4 %select_dynamic-update-slice_fusion.2 = (bf16[1024,2048]{1,0:T(8,128)(2,1)}, bf16[128,2048]{1,0:T(8,128)(2,1)}) fusion(bf16[1024,2048]{1,0:T(8,128)(2,1)} %get-tuple-element.480, s32[]{:T(128)S(6)} %select_n.436, pred[]{:T(512)S(6)} %and.148, bf16[4096,2048]{1,0:T(8,128)(2,1)} %get-tuple-element.505, f32[128,4096]{1,0:T(8,128)S(1)} %get-tuple-element.455, ...), kind=kOutput, calls=%fused_computation.8.clone.1 | convolution fusion | flops 2149842944 | bytes 21513220 | tf_op jit(solution)/shard_map/while/body/eval_jaxpr/dot_general | solution.py:126
  132.5 3.6 collective-permute-start
  136.1 5.3 %collective-permute-done.1 = bf16[128,2048]{1,0:T(8,128)(2,1)S(1)} collective-permute-done((bf16[128,2048]{1,0:T(8,128)(2,1)S(1)}, bf16[128,2048]{1,0:T(8,128)(2,1)S(1)}, u32[]{:S(2)}, u32[]{:S(2)}) %collective-permute-start.1) | collective-permute-done | bytes 524320 | tf_op jit(solution)/shard_map/while/body/eval_jaxpr/ppermute | solution.py:32
  143.2 9.4 %select_dynamic-update-slice_fusion.2 = (bf16[1024,2048]{1,0:T(8,128)(2,1)}, bf16[128,2048]{1,0:T(8,128)(2,1)}) fusion(bf16[1024,2048]{1,0:T(8,128)(2,1)} %get-tuple-element.480, s32[]{:T(128)S(6)} %select_n.436, pred[]{:T(512)S(6)} %and.148, bf16[4096,2048]{1,0:T(8,128)(2,1)} %get-tuple-element.505, f32[128,4096]{1,0:T(8,128)S(1)} %get-tuple-element.455, ...), kind=kOutput, calls=%fused_computation.8.clone.1 | convolution fusion | flops 2149842944 | bytes 21513220 | tf_op jit(solution)/shard_map/while/body/eval_jaxpr/dot_general | solution.py:126
  155.5 3.5 collective-permute-start
  159.1 4.6 collective-permute-done.1
  165.4 9.4 %select_dynamic-update-slice_fusion.2 = (bf16[1024,2048]{1,0:T(8,128)(2,1)}, bf16[128,2048]{1,0:T(8,128)(2,1)}) fusion(bf16[1024,2048]{1,0:T(8,128)(2,1)} %get-tuple-element.480, s32[]{:T(128)S(6)} %select_n.436, pred[]{:T(512)S(6)} %and.148, bf16[4096,2048]{1,0:T(8,128)(2,1)} %get-tuple-element.505, f32[128,4096]{1,0:T(8,128)S(1)} %get-tuple-element.455, ...), kind=kOutput, calls=%fused_computation.8.clone.1 | convolution fusion | flops 2149842944 | bytes 21513220 | tf_op jit(solution)/shard_map/while/body/eval_jaxpr/dot_general | solution.py:126
  181.2 3.8 collective-permute-done.1
  186.8 9.4 %select_dynamic-update-slice_fusion.2 = (bf16[1024,2048]{1,0:T(8,128)(2,1)}, bf16[128,2048]{1,0:T(8,128)(2,1)}) fusion(bf16[1024,2048]{1,0:T(8,128)(2,1)} %get-tuple-element.480, s32[]{:T(128)S(6)} %select_n.436, pred[]{:T(512)S(6)} %and.148, bf16[4096,2048]{1,0:T(8,128)(2,1)} %get-tuple-element.505, f32[128,4096]{1,0:T(8,128)S(1)} %get-tuple-element.455, ...), kind=kOutput, calls=%fused_computation.8.clone.1 | convolution fusion | flops 2149842944 | bytes 21513220 | tf_op jit(solution)/shard_map/while/body/eval_jaxpr/dot_general | solution.py:126
  207.3 9.4 %select_dynamic-update-slice_fusion.2 = (bf16[1024,2048]{1,0:T(8,128)(2,1)}, bf16[128,2048]{1,0:T(8,128)(2,1)}) fusion(bf16[1024,2048]{1,0:T(8,128)(2,1)} %get-tuple-element.480, s32[]{:T(128)S(6)} %select_n.436, pred[]{:T(512)S(6)} %and.148, bf16[4096,2048]{1,0:T(8,128)(2,1)} %get-tuple-element.505, f32[128,4096]{1,0:T(8,128)S(1)} %get-tuple-element.455, ...), kind=kOutput, calls=%fused_computation.8.clone.1 | convolution fusion | flops 2149842944 | bytes 21513220 | tf_op jit(solution)/shard_map/while/body/eval_jaxpr/dot_general | solution.py:126
  227.8 9.4 %select_dynamic-update-slice_fusion.2 = (bf16[1024,2048]{1,0:T(8,128)(2,1)}, bf16[128,2048]{1,0:T(8,128)(2,1)}) fusion(bf16[1024,2048]{1,0:T(8,128)(2,1)} %get-tuple-element.480, s32[]{:T(128)S(6)} %select_n.436, pred[]{:T(512)S(6)} %and.148, bf16[4096,2048]{1,0:T(8,128)(2,1)} %get-tuple-element.505, f32[128,4096]{1,0:T(8,128)S(1)} %get-tuple-element.455, ...), kind=kOutput, calls=%fused_computation.8.clone.1 | convolution fusion | flops 2149842944 | bytes 21513220 | tf_op jit(solution)/shard_map/while/body/eval_jaxpr/dot_general | solution.py:126
  248.3 9.4 %select_dynamic-update-slice_fusion.2 = (bf16[1024,2048]{1,0:T(8,128)(2,1)}, bf16[128,2048]{1,0:T(8,128)(2,1)}) fusion(bf16[1024,2048]{1,0:T(8,128)(2,1)} %get-tuple-element.480, s32[]{:T(128)S(6)} %select_n.436, pred[]{:T(512)S(6)} %and.148, bf16[4096,2048]{1,0:T(8,128)(2,1)} %get-tuple-element.505, f32[128,4096]{1,0:T(8,128)S(1)} %get-tuple-element.455, ...), kind=kOutput, calls=%fused_computation.8.clone.1 | convolution fusion | flops 2149842944 | bytes 21513220 | tf_op jit(solution)/shard_map/while/body/eval_jaxpr/dot_general | solution.py:126
  268.7 9.4 %select_dynamic-update-slice_fusion.2 = (bf16[1024,2048]{1,0:T(8,128)(2,1)}, bf16[128,2048]{1,0:T(8,128)(2,1)}) fusion(bf16[1024,2048]{1,0:T(8,128)(2,1)} %get-tuple-element.480, s32[]{:T(128)S(6)} %select_n.436, pred[]{:T(512)S(6)} %and.148, bf16[4096,2048]{1,0:T(8,128)(2,1)} %get-tuple-element.505, f32[128,4096]{1,0:T(8,128)S(1)} %get-tuple-element.455, ...), kind=kOutput, calls=%fused_computation.8.clone.1 | convolution fusion | flops 2149842944 | bytes 21513220 | tf_op jit(solution)/shard_map/while/body/eval_jaxpr/dot_general | solution.py:126
  289.2 9.4 %select_dynamic-update-slice_fusion.2 = (bf16[1024,2048]{1,0:T(8,128)(2,1)}, bf16[128,2048]{1,0:T(8,128)(2,1)}) fusion(bf16[1024,2048]{1,0:T(8,128)(2,1)} %get-tuple-element.480, s32[]{:T(128)S(6)} %select_n.436, pred[]{:T(512)S(6)} %and.148, bf16[4096,2048]{1,0:T(8,128)(2,1)} %get-tuple-element.505, f32[128,4096]{1,0:T(8,128)S(1)} %get-tuple-element.455, ...), kind=kOutput, calls=%fused_computation.8.clone.1 | convolution fusion | flops 2149842944 | bytes 21513220 | tf_op jit(solution)/shard_map/while/body/eval_jaxpr/dot_general | solution.py:126
  309.7 9.4 %select_dynamic-update-slice_fusion.2 = (bf16[1024,2048]{1,0:T(8,128)(2,1)}, bf16[128,2048]{1,0:T(8,128)(2,1)}) fusion(bf16[1024,2048]{1,0:T(8,128)(2,1)} %get-tuple-element.480, s32[]{:T(128)S(6)} %select_n.436, pred[]{:T(512)S(6)} %and.148, bf16[4096,2048]{1,0:T(8,128)(2,1)} %get-tuple-element.505, f32[128,4096]{1,0:T(8,128)S(1)} %get-tuple-element.455, ...), kind=kOutput, calls=%fused_computation.8.clone.1 | convolution fusion | flops 2149842944 | bytes 21513220 | tf_op jit(solution)/shard_map/while/body/eval_jaxpr/dot_general | solution.py:126
  330.2 9.4 %select_dynamic-update-slice_fusion.2 = (bf16[1024,2048]{1,0:T(8,128)(2,1)}, bf16[128,2048]{1,0:T(8,128)(2,1)}) fusion(bf16[1024,2048]{1,0:T(8,128)(2,1)} %get-tuple-element.480, s32[]{:T(128)S(6)} %select_n.436, pred[]{:T(512)S(6)} %and.148, bf16[4096,2048]{1,0:T(8,128)(2,1)} %get-tuple-element.505, f32[128,4096]{1,0:T(8,128)S(1)} %get-tuple-element.455, ...), kind=kOutput, calls=%fused_computation.8.clone.1 | convolution fusion | flops 2149842944 | bytes 21513220 | tf_op jit(solution)/shard_map/while/body/eval_jaxpr/dot_general | solution.py:126
  350.6 3.8 fusion.8
  355.0 8.7 %collective-permute-done.4 = f32[1024,128]{0,1:T(8,128)S(1)} collective-permute-done((f32[1024,128]{0,1:T(8,128)S(1)}, f32[1024,128]{0,1:T(8,128)S(1)}, u32[]{:S(2)}, u32[]{:S(2)}) %collective-permute-start.4) | collective-permute-done | bytes 524320 | tf_op jit(solution)/shard_map/ppermute | solution.py:32
  368.7 3.4 collective-permute-done.6
  406.1 3.8 collective-permute-start.30
  415.1 3.8 collective-permute-start.31
  (304 shorter events, 213.8 us)
Async XLA Ops:
  7.2 366.5 %all-gather.2.cloned.1.call-start = ((), (), s32[]{:S(2)}) async-start(), calls=%async_computation | async-start | bytes 4456448 | tf_op jit(solution)/shard_map/all_gather | solution.py:120
  18.0 16.8 %collective-permute-start.1 = (bf16[128,2048]{1,0:T(8,128)(2,1)S(1)}, bf16[128,2048]{1,0:T(8,128)(2,1)S(1)}, u32[]{:S(2)}, u32[]{:S(2)}) collective-permute-start(bf16[128,2048]{1,0:T(8,128)(2,1)S(1)} %get-tuple-element.478), channel_id=1, source_target_pairs={{0,1},{1,0},{2,3},{3,2},{4,5},{5,4},{6,7},{7,6},{8,9},{9,8},{10,11... | collective-permute-start | bytes 1572872 | tf_op jit(solution)/shard_map/while/body/eval_jaxpr/ppermute | solution.py:32
  20.1 25.9 %collective-permute-start = (bf16[128,2048]{1,0:T(8,128)(2,1)S(1)}, bf16[128,2048]{1,0:T(8,128)(2,1)S(1)}, u32[]{:S(2)}, u32[]{:S(2)}) collective-permute-start(bf16[128,2048]{1,0:T(8,128)(2,1)S(1)} %broadcast_select_fusion.8), channel_id=1, source_target_pairs={{0,32},{32,64},{64,96},{1,33},{33,65},{65,97},{2,34},{34,66},{66,9... | collective-permute-start | bytes 1572872 | tf_op jit(solution)/shard_map/while/body/eval_jaxpr/ppermute | solution.py:135
  46.1 24.5 %collective-permute-start.1 = (bf16[128,2048]{1,0:T(8,128)(2,1)S(1)}, bf16[128,2048]{1,0:T(8,128)(2,1)S(1)}, u32[]{:S(2)}, u32[]{:S(2)}) collective-permute-start(bf16[128,2048]{1,0:T(8,128)(2,1)S(1)} %get-tuple-element.478), channel_id=1, source_target_pairs={{0,1},{1,0},{2,3},{3,2},{4,5},{5,4},{6,7},{7,6},{8,9},{9,8},{10,11... | collective-permute-start | bytes 1572872 | tf_op jit(solution)/shard_map/while/body/eval_jaxpr/ppermute | solution.py:32
  49.0 33.1 %collective-permute-start = (bf16[128,2048]{1,0:T(8,128)(2,1)S(1)}, bf16[128,2048]{1,0:T(8,128)(2,1)S(1)}, u32[]{:S(2)}, u32[]{:S(2)}) collective-permute-start(bf16[128,2048]{1,0:T(8,128)(2,1)S(1)} %broadcast_select_fusion.8), channel_id=1, source_target_pairs={{0,32},{32,64},{64,96},{1,33},{33,65},{65,97},{2,34},{34,66},{66,9... | collective-permute-start | bytes 1572872 | tf_op jit(solution)/shard_map/while/body/eval_jaxpr/ppermute | solution.py:135
  82.2 13.0 %collective-permute-start.1 = (bf16[128,2048]{1,0:T(8,128)(2,1)S(1)}, bf16[128,2048]{1,0:T(8,128)(2,1)S(1)}, u32[]{:S(2)}, u32[]{:S(2)}) collective-permute-start(bf16[128,2048]{1,0:T(8,128)(2,1)S(1)} %get-tuple-element.478), channel_id=1, source_target_pairs={{0,1},{1,0},{2,3},{3,2},{4,5},{5,4},{6,7},{7,6},{8,9},{9,8},{10,11... | collective-permute-start | bytes 1572872 | tf_op jit(solution)/shard_map/while/body/eval_jaxpr/ppermute | solution.py:32
  83.7 22.6 %collective-permute-start = (bf16[128,2048]{1,0:T(8,128)(2,1)S(1)}, bf16[128,2048]{1,0:T(8,128)(2,1)S(1)}, u32[]{:S(2)}, u32[]{:S(2)}) collective-permute-start(bf16[128,2048]{1,0:T(8,128)(2,1)S(1)} %broadcast_select_fusion.8), channel_id=1, source_target_pairs={{0,32},{32,64},{64,96},{1,33},{33,65},{65,97},{2,34},{34,66},{66,9... | collective-permute-start | bytes 1572872 | tf_op jit(solution)/shard_map/while/body/eval_jaxpr/ppermute | solution.py:135
  106.4 12.2 %collective-permute-start.1 = (bf16[128,2048]{1,0:T(8,128)(2,1)S(1)}, bf16[128,2048]{1,0:T(8,128)(2,1)S(1)}, u32[]{:S(2)}, u32[]{:S(2)}) collective-permute-start(bf16[128,2048]{1,0:T(8,128)(2,1)S(1)} %get-tuple-element.478), channel_id=1, source_target_pairs={{0,1},{1,0},{2,3},{3,2},{4,5},{5,4},{6,7},{7,6},{8,9},{9,8},{10,11... | collective-permute-start | bytes 1572872 | tf_op jit(solution)/shard_map/while/body/eval_jaxpr/ppermute | solution.py:32
  108.5 21.2 %collective-permute-start = (bf16[128,2048]{1,0:T(8,128)(2,1)S(1)}, bf16[128,2048]{1,0:T(8,128)(2,1)S(1)}, u32[]{:S(2)}, u32[]{:S(2)}) collective-permute-start(bf16[128,2048]{1,0:T(8,128)(2,1)S(1)} %broadcast_select_fusion.8), channel_id=1, source_target_pairs={{0,32},{32,64},{64,96},{1,33},{33,65},{65,97},{2,34},{34,66},{66,9... | collective-permute-start | bytes 1572872 | tf_op jit(solution)/shard_map/while/body/eval_jaxpr/ppermute | solution.py:135
  129.8 11.6 %collective-permute-start.1 = (bf16[128,2048]{1,0:T(8,128)(2,1)S(1)}, bf16[128,2048]{1,0:T(8,128)(2,1)S(1)}, u32[]{:S(2)}, u32[]{:S(2)}) collective-permute-start(bf16[128,2048]{1,0:T(8,128)(2,1)S(1)} %get-tuple-element.478), channel_id=1, source_target_pairs={{0,1},{1,0},{2,3},{3,2},{4,5},{5,4},{6,7},{7,6},{8,9},{9,8},{10,11... | collective-permute-start | bytes 1572872 | tf_op jit(solution)/shard_map/while/body/eval_jaxpr/ppermute | solution.py:32
  132.5 20.1 %collective-permute-start = (bf16[128,2048]{1,0:T(8,128)(2,1)S(1)}, bf16[128,2048]{1,0:T(8,128)(2,1)S(1)}, u32[]{:S(2)}, u32[]{:S(2)}) collective-permute-start(bf16[128,2048]{1,0:T(8,128)(2,1)S(1)} %broadcast_select_fusion.8), channel_id=1, source_target_pairs={{0,32},{32,64},{64,96},{1,33},{33,65},{65,97},{2,34},{34,66},{66,9... | collective-permute-start | bytes 1572872 | tf_op jit(solution)/shard_map/while/body/eval_jaxpr/ppermute | solution.py:135
  152.6 11.0 %collective-permute-start.1 = (bf16[128,2048]{1,0:T(8,128)(2,1)S(1)}, bf16[128,2048]{1,0:T(8,128)(2,1)S(1)}, u32[]{:S(2)}, u32[]{:S(2)}) collective-permute-start(bf16[128,2048]{1,0:T(8,128)(2,1)S(1)} %get-tuple-element.478), channel_id=1, source_target_pairs={{0,1},{1,0},{2,3},{3,2},{4,5},{5,4},{6,7},{7,6},{8,9},{9,8},{10,11... | collective-permute-start | bytes 1572872 | tf_op jit(solution)/shard_map/while/body/eval_jaxpr/ppermute | solution.py:32
  155.5 19.3 %collective-permute-start = (bf16[128,2048]{1,0:T(8,128)(2,1)S(1)}, bf16[128,2048]{1,0:T(8,128)(2,1)S(1)}, u32[]{:S(2)}, u32[]{:S(2)}) collective-permute-start(bf16[128,2048]{1,0:T(8,128)(2,1)S(1)} %broadcast_select_fusion.8), channel_id=1, source_target_pairs={{0,32},{32,64},{64,96},{1,33},{33,65},{65,97},{2,34},{34,66},{66,9... | collective-permute-start | bytes 1572872 | tf_op jit(solution)/shard_map/while/body/eval_jaxpr/ppermute | solution.py:135
  174.9 10.2 %collective-permute-start.1 = (bf16[128,2048]{1,0:T(8,128)(2,1)S(1)}, bf16[128,2048]{1,0:T(8,128)(2,1)S(1)}, u32[]{:S(2)}, u32[]{:S(2)}) collective-permute-start(bf16[128,2048]{1,0:T(8,128)(2,1)S(1)} %get-tuple-element.478), channel_id=1, source_target_pairs={{0,1},{1,0},{2,3},{3,2},{4,5},{5,4},{6,7},{7,6},{8,9},{9,8},{10,11... | collective-permute-start | bytes 1572872 | tf_op jit(solution)/shard_map/while/body/eval_jaxpr/ppermute | solution.py:32
  177.8 18.4 %collective-permute-start = (bf16[128,2048]{1,0:T(8,128)(2,1)S(1)}, bf16[128,2048]{1,0:T(8,128)(2,1)S(1)}, u32[]{:S(2)}, u32[]{:S(2)}) collective-permute-start(bf16[128,2048]{1,0:T(8,128)(2,1)S(1)} %broadcast_select_fusion.8), channel_id=1, source_target_pairs={{0,32},{32,64},{64,96},{1,33},{33,65},{65,97},{2,34},{34,66},{66,9... | collective-permute-start | bytes 1572872 | tf_op jit(solution)/shard_map/while/body/eval_jaxpr/ppermute | solution.py:135
  196.2 9.3 %collective-permute-start.1 = (bf16[128,2048]{1,0:T(8,128)(2,1)S(1)}, bf16[128,2048]{1,0:T(8,128)(2,1)S(1)}, u32[]{:S(2)}, u32[]{:S(2)}) collective-permute-start(bf16[128,2048]{1,0:T(8,128)(2,1)S(1)} %get-tuple-element.478), channel_id=1, source_target_pairs={{0,1},{1,0},{2,3},{3,2},{4,5},{5,4},{6,7},{7,6},{8,9},{9,8},{10,11... | collective-permute-start | bytes 1572872 | tf_op jit(solution)/shard_map/while/body/eval_jaxpr/ppermute | solution.py:32
  199.1 17.6 %collective-permute-start = (bf16[128,2048]{1,0:T(8,128)(2,1)S(1)}, bf16[128,2048]{1,0:T(8,128)(2,1)S(1)}, u32[]{:S(2)}, u32[]{:S(2)}) collective-permute-start(bf16[128,2048]{1,0:T(8,128)(2,1)S(1)} %broadcast_select_fusion.8), channel_id=1, source_target_pairs={{0,32},{32,64},{64,96},{1,33},{33,65},{65,97},{2,34},{34,66},{66,9... | collective-permute-start | bytes 1572872 | tf_op jit(solution)/shard_map/while/body/eval_jaxpr/ppermute | solution.py:135
  216.8 9.3 %collective-permute-start.1 = (bf16[128,2048]{1,0:T(8,128)(2,1)S(1)}, bf16[128,2048]{1,0:T(8,128)(2,1)S(1)}, u32[]{:S(2)}, u32[]{:S(2)}) collective-permute-start(bf16[128,2048]{1,0:T(8,128)(2,1)S(1)} %get-tuple-element.478), channel_id=1, source_target_pairs={{0,1},{1,0},{2,3},{3,2},{4,5},{5,4},{6,7},{7,6},{8,9},{9,8},{10,11... | collective-permute-start | bytes 1572872 | tf_op jit(solution)/shard_map/while/body/eval_jaxpr/ppermute | solution.py:32
  219.7 17.5 %collective-permute-start = (bf16[128,2048]{1,0:T(8,128)(2,1)S(1)}, bf16[128,2048]{1,0:T(8,128)(2,1)S(1)}, u32[]{:S(2)}, u32[]{:S(2)}) collective-permute-start(bf16[128,2048]{1,0:T(8,128)(2,1)S(1)} %broadcast_select_fusion.8), channel_id=1, source_target_pairs={{0,32},{32,64},{64,96},{1,33},{33,65},{65,97},{2,34},{34,66},{66,9... | collective-permute-start | bytes 1572872 | tf_op jit(solution)/shard_map/while/body/eval_jaxpr/ppermute | solution.py:135
  237.2 9.3 %collective-permute-start.1 = (bf16[128,2048]{1,0:T(8,128)(2,1)S(1)}, bf16[128,2048]{1,0:T(8,128)(2,1)S(1)}, u32[]{:S(2)}, u32[]{:S(2)}) collective-permute-start(bf16[128,2048]{1,0:T(8,128)(2,1)S(1)} %get-tuple-element.478), channel_id=1, source_target_pairs={{0,1},{1,0},{2,3},{3,2},{4,5},{5,4},{6,7},{7,6},{8,9},{9,8},{10,11... | collective-permute-start | bytes 1572872 | tf_op jit(solution)/shard_map/while/body/eval_jaxpr/ppermute | solution.py:32
  240.1 17.5 %collective-permute-start = (bf16[128,2048]{1,0:T(8,128)(2,1)S(1)}, bf16[128,2048]{1,0:T(8,128)(2,1)S(1)}, u32[]{:S(2)}, u32[]{:S(2)}) collective-permute-start(bf16[128,2048]{1,0:T(8,128)(2,1)S(1)} %broadcast_select_fusion.8), channel_id=1, source_target_pairs={{0,32},{32,64},{64,96},{1,33},{33,65},{65,97},{2,34},{34,66},{66,9... | collective-permute-start | bytes 1572872 | tf_op jit(solution)/shard_map/while/body/eval_jaxpr/ppermute | solution.py:135
  257.7 9.3 %collective-permute-start.1 = (bf16[128,2048]{1,0:T(8,128)(2,1)S(1)}, bf16[128,2048]{1,0:T(8,128)(2,1)S(1)}, u32[]{:S(2)}, u32[]{:S(2)}) collective-permute-start(bf16[128,2048]{1,0:T(8,128)(2,1)S(1)} %get-tuple-element.478), channel_id=1, source_target_pairs={{0,1},{1,0},{2,3},{3,2},{4,5},{5,4},{6,7},{7,6},{8,9},{9,8},{10,11... | collective-permute-start | bytes 1572872 | tf_op jit(solution)/shard_map/while/body/eval_jaxpr/ppermute | solution.py:32
  260.6 17.5 %collective-permute-start = (bf16[128,2048]{1,0:T(8,128)(2,1)S(1)}, bf16[128,2048]{1,0:T(8,128)(2,1)S(1)}, u32[]{:S(2)}, u32[]{:S(2)}) collective-permute-start(bf16[128,2048]{1,0:T(8,128)(2,1)S(1)} %broadcast_select_fusion.8), channel_id=1, source_target_pairs={{0,32},{32,64},{64,96},{1,33},{33,65},{65,97},{2,34},{34,66},{66,9... | collective-permute-start | bytes 1572872 | tf_op jit(solution)/shard_map/while/body/eval_jaxpr/ppermute | solution.py:135
  278.2 9.3 %collective-permute-start.1 = (bf16[128,2048]{1,0:T(8,128)(2,1)S(1)}, bf16[128,2048]{1,0:T(8,128)(2,1)S(1)}, u32[]{:S(2)}, u32[]{:S(2)}) collective-permute-start(bf16[128,2048]{1,0:T(8,128)(2,1)S(1)} %get-tuple-element.478), channel_id=1, source_target_pairs={{0,1},{1,0},{2,3},{3,2},{4,5},{5,4},{6,7},{7,6},{8,9},{9,8},{10,11... | collective-permute-start | bytes 1572872 | tf_op jit(solution)/shard_map/while/body/eval_jaxpr/ppermute | solution.py:32
  281.1 17.5 %collective-permute-start = (bf16[128,2048]{1,0:T(8,128)(2,1)S(1)}, bf16[128,2048]{1,0:T(8,128)(2,1)S(1)}, u32[]{:S(2)}, u32[]{:S(2)}) collective-permute-start(bf16[128,2048]{1,0:T(8,128)(2,1)S(1)} %broadcast_select_fusion.8), channel_id=1, source_target_pairs={{0,32},{32,64},{64,96},{1,33},{33,65},{65,97},{2,34},{34,66},{66,9... | collective-permute-start | bytes 1572872 | tf_op jit(solution)/shard_map/while/body/eval_jaxpr/ppermute | solution.py:135
  298.7 9.3 %collective-permute-start.1 = (bf16[128,2048]{1,0:T(8,128)(2,1)S(1)}, bf16[128,2048]{1,0:T(8,128)(2,1)S(1)}, u32[]{:S(2)}, u32[]{:S(2)}) collective-permute-start(bf16[128,2048]{1,0:T(8,128)(2,1)S(1)} %get-tuple-element.478), channel_id=1, source_target_pairs={{0,1},{1,0},{2,3},{3,2},{4,5},{5,4},{6,7},{7,6},{8,9},{9,8},{10,11... | collective-permute-start | bytes 1572872 | tf_op jit(solution)/shard_map/while/body/eval_jaxpr/ppermute | solution.py:32
  301.6 17.5 %collective-permute-start = (bf16[128,2048]{1,0:T(8,128)(2,1)S(1)}, bf16[128,2048]{1,0:T(8,128)(2,1)S(1)}, u32[]{:S(2)}, u32[]{:S(2)}) collective-permute-start(bf16[128,2048]{1,0:T(8,128)(2,1)S(1)} %broadcast_select_fusion.8), channel_id=1, source_target_pairs={{0,32},{32,64},{64,96},{1,33},{33,65},{65,97},{2,34},{34,66},{66,9... | collective-permute-start | bytes 1572872 | tf_op jit(solution)/shard_map/while/body/eval_jaxpr/ppermute | solution.py:135
  319.2 9.3 %collective-permute-start.1 = (bf16[128,2048]{1,0:T(8,128)(2,1)S(1)}, bf16[128,2048]{1,0:T(8,128)(2,1)S(1)}, u32[]{:S(2)}, u32[]{:S(2)}) collective-permute-start(bf16[128,2048]{1,0:T(8,128)(2,1)S(1)} %get-tuple-element.478), channel_id=1, source_target_pairs={{0,1},{1,0},{2,3},{3,2},{4,5},{5,4},{6,7},{7,6},{8,9},{9,8},{10,11... | collective-permute-start | bytes 1572872 | tf_op jit(solution)/shard_map/while/body/eval_jaxpr/ppermute | solution.py:32
  322.1 17.5 %collective-permute-start = (bf16[128,2048]{1,0:T(8,128)(2,1)S(1)}, bf16[128,2048]{1,0:T(8,128)(2,1)S(1)}, u32[]{:S(2)}, u32[]{:S(2)}) collective-permute-start(bf16[128,2048]{1,0:T(8,128)(2,1)S(1)} %broadcast_select_fusion.8), channel_id=1, source_target_pairs={{0,32},{32,64},{64,96},{1,33},{33,65},{65,97},{2,34},{34,66},{66,9... | collective-permute-start | bytes 1572872 | tf_op jit(solution)/shard_map/while/body/eval_jaxpr/ppermute | solution.py:135
  354.4 9.3 %collective-permute-start.4 = (f32[1024,128]{0,1:T(8,128)S(1)}, f32[1024,128]{0,1:T(8,128)S(1)}, u32[]{:S(2)}, u32[]{:S(2)}) collective-permute-start(f32[1024,128]{0,1:T(8,128)S(1)} %fusion.8), channel_id=1, source_target_pairs={{0,1},{1,0},{2,3},{3,2},{4,5},{5,4},{6,7},{7,6},{8,9},{9,8},{10,11... | collective-permute-start | bytes 1572872 | tf_op jit(solution)/shard_map/ppermute | solution.py:32
  400.0 9.9 %collective-permute-start.23 = (f32[4,2,2,32,128]{4,3,2,1,0:T(8,128)S(1)}, f32[4,2,2,32,128]{4,3,2,1,0:T(8,128)S(1)}, u32[]{:S(2)}, u32[]{:S(2)}) collective-permute-start(f32[4,2,2,32,128]{4,3,2,1,0:T(8,128)S(1)} %dynamic-slice_bitcast_fusion.1), channel_id=1, source_target_pairs={{0,8},{2,10},{4,12},{6,14},{8,16},{10,18},{12,20},{14,22},{16,24},... | collective-permute-start | bytes 786440 | tf_op jit(solution)/shard_map/ppermute | solution.py:36
  403.4 9.6 %collective-permute-start.9 = (f32[4,2,2,32,128]{4,3,2,1,0:T(8,128)S(1)}, f32[4,2,2,32,128]{4,3,2,1,0:T(8,128)S(1)}, u32[]{:S(2)}, u32[]{:S(2)}) collective-permute-start(f32[4,2,2,32,128]{4,3,2,1,0:T(8,128)S(1)} %dynamic-slice_bitcast_fusion.3), channel_id=1, source_target_pairs={{0,32},{32,64},{64,96},{96,0},{1,33},{33,65},{65,97},{97,1},{2,34}... | collective-permute-start | bytes 786440 | tf_op jit(solution)/shard_map/ppermute | solution.py:32
  (44 other events, 241.1 us)
Sparse Core Ops, SparseCore 0:
  10.4 69.6 all-gather.1

commit v11 on v10

--- a/solution.py
+++ b/solution.py
@@ -63,10 +63,8 @@
     rep = lax.axis_index("rep")
     y_pos = f // 4
     zh_pos = (f // 2) % 2
-    core_pos = f % 2
     along_x = lambda v, by: shifted(v, "segment", 4, by)
     along_y = lambda v, by: fsdp_moved(v, lambda g: ((g // 4 + by) % 4) * 4 + g % 4)
-    along_core = lambda v: fsdp_moved(v, lambda g: g ^ 1)
     along_zh = lambda v: fsdp_moved(v, lambda g: g ^ 2)
     along_zl = lambda v: shifted(v, "rep", 2, 1)
     outs = []
@@ -167,7 +165,8 @@
     head_half = lax.dynamic_slice_in_dim(head_weight, rep_pos * half_width, half_width, 0)
     prior_half = (wide_half * final_scale * gain_half).astype(jnp.bfloat16)
     own_logits = jnp.dot(prior_half, head_half, preferred_element_type=jnp.float32)
-    prior_logits = own_logits + shifted(own_logits, "rep", replicas, 1)
+    other_logits = shifted(own_logits, "rep", replicas, 1)
+    prior_logits = own_logits + other_logits
     prior_logp = jax.nn.log_softmax(prior_logits, axis=-1)
     token_terms = picked_logprob(prior_logp, next_ids.reshape(-1)).reshape(group_seqs, seq_len)
     prior_group = jnp.sum(token_terms * live_mask, axis=1) / counts
@@ -187,9 +186,7 @@
     start_wide = lookup_rows(mine_ids, embed_table).astype(jnp.float32)
     unit_rows = (start_wide * rms_scale(start_wide)).astype(jnp.bfloat16)
     latent = jnp.dot(unit_rows, down_full, preferred_element_type=jnp.float32).astype(jnp.bfloat16)
-    hidden = start_wide + lax.dot_general(
-        latent, up_full, (((1,), (1,)), ((), ())), preferred_element_type=jnp.float32
-    )
+    hidden = start_wide + lax.dot_general(latent, up_full, (((1,), (1,)), ((), ())), preferred_element_type=jnp.float32)
     inverse = rms_scale(hidden)
     agent_final = (hidden * inverse * final_gain).astype(jnp.bfloat16)
     logprob = jax.nn.log_softmax(
@@ -225,8 +222,8 @@
         blocks = values.reshape(values.shape[0], 4, 4, 2, 2, 2, model_width // 128)
         return lax.dynamic_index_in_dim(blocks, pick, 4, keepdims=False).reshape(values.shape[0], -1)
 
-    rank = latent.shape[1]
-    forward_sent = along_core(jnp.concatenate([core_columns(unit_rows, 1 - core_pos), latent], axis=1))
+    forward_given = jnp.concatenate([core_columns(unit_rows, 1 - core_pos), latent], axis=1)
+    forward_sent = along_core(forward_given)
     latent_grad = jnp.dot(hidden_grad, up_full, preferred_element_type=jnp.float32).astype(
         jnp.bfloat16
     )
@@ -261,6 +258,7 @@
         P("fsdp", None),
         P("fsdp", None),
     )
+
     return jax.shard_map(
         on_device,
         mesh=mesh,

time: 469 us -> 469 us (level)
  no operation moved by 1% of the time
where the time goes in v11:
time: 469 us; the launch traced here: 466 us
  matrix products  152 us (32%)
  starting transfers between devices  123 us (26%)
  waiting for transfers between devices  104 us (22%)
  other arithmetic  51.2 us (11%)
  between operations  18 us (4%)
  local copies, waits for them, and re-layouts  17.1 us (4%)
    dot_general x14, matrix products, apply_segment(): update = jnp.dot(normed, weight_local, preferred_element_type=jnp.float32)  132 us
    ppermute x33, waiting for transfers between devices, shifted(): return lax.ppermute(x, axis, [(i, (i + by) % size) for i in range(size)])  94.8 us
    ppermute x33, starting transfers between devices, shifted(): return lax.ppermute(x, axis, [(i, (i + by) % size) for i in range(size)])  48.5 us
    ppermute x14, starting transfers between devices, tick_whole(): lax.ppermute(computed, 'segment', [(i, i + 1) for i in range(segments - 1)])  47.7 us
    ppermute x16, starting transfers between devices, fsdp_moved(): return lax.ppermute(x, 'fsdp', [(f, mapping(f)) for f in range(16)])  26.4 us
    reduce_sum x14, other arithmetic, rms_scale(): squares = jnp.mean(values * values, axis=-1, keepdims=True)  23.3 us
    while x14, other arithmetic  14.1 us
  transfers between devices with their start and end apart: 64, of which 28 were waited for; matrix products, arithmetic and copies ran while one was open for 43% of the time, Pallas kernels for 0%

profile of v11, /device:TPU:0, one launch (start us, length us, event | category | flops | bytes accessed | tf_op | source)
XLA Modules:
  0.0 466.3 jit_solution(10763484085381684184)
XLA Ops:
  9.1 6.3 %convolution_convert_fusion = bf16[1024,4096]{1,0:T(8,128)(2,1)} fusion(bf16[128,4096]{1,0:T(8,128)(2,1)S(1)} %copy-done, s32[1024]{0:T(1024)} %bitcast.155), kind=kOutput, calls=%fused_computation.18 | convolution fusion | flops 1078067200 | bytes 9441280 | tf_op jit(solution)/shard_map/dot_general | solution.py:22
  17.9 321.7 %while.20 = (s32[]{:T(128)}, bf16[128,2048]{1,0:T(8,128)(2,1)S(1)}, bf16[128,2048]{1,0:T(8,128)(2,1)}, bf16[1024,2048]{1,0:T(8,128)(2,1)}, pred[]{:T(512)}, /*in...) while((s32[]{:T(128)}, bf16[128,2048]{1,0:T(8,128)(2,1)S(1)}, ...), condition=%wide.region_4.5_spmd.clone, body=%wide.region_2.4_spmd.clone.sunk | while | flops 2154823936 | bytes 34098032 | solution.py:153
  23.6 11.2 %collective-permute-done.1 = bf16[128,2048]{1,0:T(8,128)(2,1)S(1)} collective-permute-done((bf16[128,2048]{1,0:T(8,128)(2,1)S(1)}, bf16[128,2048]{1,0:T(8,128)(2,1)S(1)}, u32[]{:S(2)}, u32[]{:S(2)}) %collective-permute-start.1) | collective-permute-done | bytes 524320 | tf_op jit(solution)/shard_map/while/body/eval_jaxpr/ppermute | solution.py:32
  36.5 9.5 %select_dynamic-update-slice_fusion.2 = (bf16[1024,2048]{1,0:T(8,128)(2,1)}, bf16[128,2048]{1,0:T(8,128)(2,1)}) fusion(bf16[1024,2048]{1,0:T(8,128)(2,1)} %get-tuple-element.480, s32[]{:T(128)S(6)} %select_n.436, pred[]{:T(512)S(6)} %and.148, bf16[4096,2048]{1,0:T(8,128)(2,1)} %get-tuple-element.505, f32[128,4096]{1,0:T(8,128)S(1)} %get-tuple-element.455, ...), kind=kOutput, calls=%fused_computation.8.clone.1 | convolution fusion | flops 2149842944 | bytes 21513220 | tf_op jit(solution)/shard_map/while/body/eval_jaxpr/dot_general | solution.py:124
  52.4 18.2 %collective-permute-done.1 = bf16[128,2048]{1,0:T(8,128)(2,1)S(1)} collective-permute-done((bf16[128,2048]{1,0:T(8,128)(2,1)S(1)}, bf16[128,2048]{1,0:T(8,128)(2,1)S(1)}, u32[]{:S(2)}, u32[]{:S(2)}) %collective-permute-start.1) | collective-permute-done | bytes 524320 | tf_op jit(solution)/shard_map/while/body/eval_jaxpr/ppermute | solution.py:32
  72.4 9.7 %select_dynamic-update-slice_fusion.2 = (bf16[1024,2048]{1,0:T(8,128)(2,1)}, bf16[128,2048]{1,0:T(8,128)(2,1)}) fusion(bf16[1024,2048]{1,0:T(8,128)(2,1)} %get-tuple-element.480, s32[]{:T(128)S(6)} %select_n.436, pred[]{:T(512)S(6)} %and.148, bf16[4096,2048]{1,0:T(8,128)(2,1)} %get-tuple-element.505, f32[128,4096]{1,0:T(8,128)S(1)} %get-tuple-element.455, ...), kind=kOutput, calls=%fused_computation.8.clone.1 | convolution fusion | flops 2149842944 | bytes 21513220 | tf_op jit(solution)/shard_map/while/body/eval_jaxpr/dot_general | solution.py:124
  83.7 3.7 collective-permute-start
  87.4 7.8 %collective-permute-done.1 = bf16[128,2048]{1,0:T(8,128)(2,1)S(1)} collective-permute-done((bf16[128,2048]{1,0:T(8,128)(2,1)S(1)}, bf16[128,2048]{1,0:T(8,128)(2,1)S(1)}, u32[]{:S(2)}, u32[]{:S(2)}) %collective-permute-start.1) | collective-permute-done | bytes 524320 | tf_op jit(solution)/shard_map/while/body/eval_jaxpr/ppermute | solution.py:32
  96.9 9.4 %select_dynamic-update-slice_fusion.2 = (bf16[1024,2048]{1,0:T(8,128)(2,1)}, bf16[128,2048]{1,0:T(8,128)(2,1)}) fusion(bf16[1024,2048]{1,0:T(8,128)(2,1)} %get-tuple-element.480, s32[]{:T(128)S(6)} %select_n.436, pred[]{:T(512)S(6)} %and.148, bf16[4096,2048]{1,0:T(8,128)(2,1)} %get-tuple-element.505, f32[128,4096]{1,0:T(8,128)S(1)} %get-tuple-element.455, ...), kind=kOutput, calls=%fused_computation.8.clone.1 | convolution fusion | flops 2149842944 | bytes 21513220 | tf_op jit(solution)/shard_map/while/body/eval_jaxpr/dot_general | solution.py:124
  108.5 3.7 collective-permute-start
  112.2 6.4 %collective-permute-done.1 = bf16[128,2048]{1,0:T(8,128)(2,1)S(1)} collective-permute-done((bf16[128,2048]{1,0:T(8,128)(2,1)S(1)}, bf16[128,2048]{1,0:T(8,128)(2,1)S(1)}, u32[]{:S(2)}, u32[]{:S(2)}) %collective-permute-start.1) | collective-permute-done | bytes 524320 | tf_op jit(solution)/shard_map/while/body/eval_jaxpr/ppermute | solution.py:32
  120.3 9.4 %select_dynamic-update-slice_fusion.2 = (bf16[1024,2048]{1,0:T(8,128)(2,1)}, bf16[128,2048]{1,0:T(8,128)(2,1)}) fusion(bf16[1024,2048]{1,0:T(8,128)(2,1)} %get-tuple-element.480, s32[]{:T(128)S(6)} %select_n.436, pred[]{:T(512)S(6)} %and.148, bf16[4096,2048]{1,0:T(8,128)(2,1)} %get-tuple-element.505, f32[128,4096]{1,0:T(8,128)S(1)} %get-tuple-element.455, ...), kind=kOutput, calls=%fused_computation.8.clone.1 | convolution fusion | flops 2149842944 | bytes 21513220 | tf_op jit(solution)/shard_map/while/body/eval_jaxpr/dot_general | solution.py:124
  132.5 3.6 collective-permute-start
  136.1 5.3 %collective-permute-done.1 = bf16[128,2048]{1,0:T(8,128)(2,1)S(1)} collective-permute-done((bf16[128,2048]{1,0:T(8,128)(2,1)S(1)}, bf16[128,2048]{1,0:T(8,128)(2,1)S(1)}, u32[]{:S(2)}, u32[]{:S(2)}) %collective-permute-start.1) | collective-permute-done | bytes 524320 | tf_op jit(solution)/shard_map/while/body/eval_jaxpr/ppermute | solution.py:32
  143.2 9.4 %select_dynamic-update-slice_fusion.2 = (bf16[1024,2048]{1,0:T(8,128)(2,1)}, bf16[128,2048]{1,0:T(8,128)(2,1)}) fusion(bf16[1024,2048]{1,0:T(8,128)(2,1)} %get-tuple-element.480, s32[]{:T(128)S(6)} %select_n.436, pred[]{:T(512)S(6)} %and.148, bf16[4096,2048]{1,0:T(8,128)(2,1)} %get-tuple-element.505, f32[128,4096]{1,0:T(8,128)S(1)} %get-tuple-element.455, ...), kind=kOutput, calls=%fused_computation.8.clone.1 | convolution fusion | flops 2149842944 | bytes 21513220 | tf_op jit(solution)/shard_map/while/body/eval_jaxpr/dot_general | solution.py:124
  155.5 3.5 collective-permute-start
  159.1 4.6 collective-permute-done.1
  165.4 9.4 %select_dynamic-update-slice_fusion.2 = (bf16[1024,2048]{1,0:T(8,128)(2,1)}, bf16[128,2048]{1,0:T(8,128)(2,1)}) fusion(bf16[1024,2048]{1,0:T(8,128)(2,1)} %get-tuple-element.480, s32[]{:T(128)S(6)} %select_n.436, pred[]{:T(512)S(6)} %and.148, bf16[4096,2048]{1,0:T(8,128)(2,1)} %get-tuple-element.505, f32[128,4096]{1,0:T(8,128)S(1)} %get-tuple-element.455, ...), kind=kOutput, calls=%fused_computation.8.clone.1 | convolution fusion | flops 2149842944 | bytes 21513220 | tf_op jit(solution)/shard_map/while/body/eval_jaxpr/dot_general | solution.py:124
  181.2 3.8 collective-permute-done.1
  186.8 9.4 %select_dynamic-update-slice_fusion.2 = (bf16[1024,2048]{1,0:T(8,128)(2,1)}, bf16[128,2048]{1,0:T(8,128)(2,1)}) fusion(bf16[1024,2048]{1,0:T(8,128)(2,1)} %get-tuple-element.480, s32[]{:T(128)S(6)} %select_n.436, pred[]{:T(512)S(6)} %and.148, bf16[4096,2048]{1,0:T(8,128)(2,1)} %get-tuple-element.505, f32[128,4096]{1,0:T(8,128)S(1)} %get-tuple-element.455, ...), kind=kOutput, calls=%fused_computation.8.clone.1 | convolution fusion | flops 2149842944 | bytes 21513220 | tf_op jit(solution)/shard_map/while/body/eval_jaxpr/dot_general | solution.py:124
  207.3 9.4 %select_dynamic-update-slice_fusion.2 = (bf16[1024,2048]{1,0:T(8,128)(2,1)}, bf16[128,2048]{1,0:T(8,128)(2,1)}) fusion(bf16[1024,2048]{1,0:T(8,128)(2,1)} %get-tuple-element.480, s32[]{:T(128)S(6)} %select_n.436, pred[]{:T(512)S(6)} %and.148, bf16[4096,2048]{1,0:T(8,128)(2,1)} %get-tuple-element.505, f32[128,4096]{1,0:T(8,128)S(1)} %get-tuple-element.455, ...), kind=kOutput, calls=%fused_computation.8.clone.1 | convolution fusion | flops 2149842944 | bytes 21513220 | tf_op jit(solution)/shard_map/while/body/eval_jaxpr/dot_general | solution.py:124
  227.8 9.4 %select_dynamic-update-slice_fusion.2 = (bf16[1024,2048]{1,0:T(8,128)(2,1)}, bf16[128,2048]{1,0:T(8,128)(2,1)}) fusion(bf16[1024,2048]{1,0:T(8,128)(2,1)} %get-tuple-element.480, s32[]{:T(128)S(6)} %select_n.436, pred[]{:T(512)S(6)} %and.148, bf16[4096,2048]{1,0:T(8,128)(2,1)} %get-tuple-element.505, f32[128,4096]{1,0:T(8,128)S(1)} %get-tuple-element.455, ...), kind=kOutput, calls=%fused_computation.8.clone.1 | convolution fusion | flops 2149842944 | bytes 21513220 | tf_op jit(solution)/shard_map/while/body/eval_jaxpr/dot_general | solution.py:124
  248.3 9.4 %select_dynamic-update-slice_fusion.2 = (bf16[1024,2048]{1,0:T(8,128)(2,1)}, bf16[128,2048]{1,0:T(8,128)(2,1)}) fusion(bf16[1024,2048]{1,0:T(8,128)(2,1)} %get-tuple-element.480, s32[]{:T(128)S(6)} %select_n.436, pred[]{:T(512)S(6)} %and.148, bf16[4096,2048]{1,0:T(8,128)(2,1)} %get-tuple-element.505, f32[128,4096]{1,0:T(8,128)S(1)} %get-tuple-element.455, ...), kind=kOutput, calls=%fused_computation.8.clone.1 | convolution fusion | flops 2149842944 | bytes 21513220 | tf_op jit(solution)/shard_map/while/body/eval_jaxpr/dot_general | solution.py:124
  268.7 9.4 %select_dynamic-update-slice_fusion.2 = (bf16[1024,2048]{1,0:T(8,128)(2,1)}, bf16[128,2048]{1,0:T(8,128)(2,1)}) fusion(bf16[1024,2048]{1,0:T(8,128)(2,1)} %get-tuple-element.480, s32[]{:T(128)S(6)} %select_n.436, pred[]{:T(512)S(6)} %and.148, bf16[4096,2048]{1,0:T(8,128)(2,1)} %get-tuple-element.505, f32[128,4096]{1,0:T(8,128)S(1)} %get-tuple-element.455, ...), kind=kOutput, calls=%fused_computation.8.clone.1 | convolution fusion | flops 2149842944 | bytes 21513220 | tf_op jit(solution)/shard_map/while/body/eval_jaxpr/dot_general | solution.py:124
  289.2 9.4 %select_dynamic-update-slice_fusion.2 = (bf16[1024,2048]{1,0:T(8,128)(2,1)}, bf16[128,2048]{1,0:T(8,128)(2,1)}) fusion(bf16[1024,2048]{1,0:T(8,128)(2,1)} %get-tuple-element.480, s32[]{:T(128)S(6)} %select_n.436, pred[]{:T(512)S(6)} %and.148, bf16[4096,2048]{1,0:T(8,128)(2,1)} %get-tuple-element.505, f32[128,4096]{1,0:T(8,128)S(1)} %get-tuple-element.455, ...), kind=kOutput, calls=%fused_computation.8.clone.1 | convolution fusion | flops 2149842944 | bytes 21513220 | tf_op jit(solution)/shard_map/while/body/eval_jaxpr/dot_general | solution.py:124
  309.7 9.4 %select_dynamic-update-slice_fusion.2 = (bf16[1024,2048]{1,0:T(8,128)(2,1)}, bf16[128,2048]{1,0:T(8,128)(2,1)}) fusion(bf16[1024,2048]{1,0:T(8,128)(2,1)} %get-tuple-element.480, s32[]{:T(128)S(6)} %select_n.436, pred[]{:T(512)S(6)} %and.148, bf16[4096,2048]{1,0:T(8,128)(2,1)} %get-tuple-element.505, f32[128,4096]{1,0:T(8,128)S(1)} %get-tuple-element.455, ...), kind=kOutput, calls=%fused_computation.8.clone.1 | convolution fusion | flops 2149842944 | bytes 21513220 | tf_op jit(solution)/shard_map/while/body/eval_jaxpr/dot_general | solution.py:124
  330.2 9.4 %select_dynamic-update-slice_fusion.2 = (bf16[1024,2048]{1,0:T(8,128)(2,1)}, bf16[128,2048]{1,0:T(8,128)(2,1)}) fusion(bf16[1024,2048]{1,0:T(8,128)(2,1)} %get-tuple-element.480, s32[]{:T(128)S(6)} %select_n.436, pred[]{:T(512)S(6)} %and.148, bf16[4096,2048]{1,0:T(8,128)(2,1)} %get-tuple-element.505, f32[128,4096]{1,0:T(8,128)S(1)} %get-tuple-element.455, ...), kind=kOutput, calls=%fused_computation.8.clone.1 | convolution fusion | flops 2149842944 | bytes 21513220 | tf_op jit(solution)/shard_map/while/body/eval_jaxpr/dot_general | solution.py:124
  350.6 3.8 fusion.8
  355.0 8.7 %collective-permute-done.4 = f32[1024,128]{0,1:T(8,128)S(1)} collective-permute-done((f32[1024,128]{0,1:T(8,128)S(1)}, f32[1024,128]{0,1:T(8,128)S(1)}, u32[]{:S(2)}, u32[]{:S(2)}) %collective-permute-start.4) | collective-permute-done | bytes 524320 | tf_op jit(solution)/shard_map/ppermute | solution.py:32
  368.7 3.4 collective-permute-done.6
  406.1 3.8 collective-permute-start.30
  415.1 3.8 collective-permute-start.31
  (304 shorter events, 213.8 us)
Async XLA Ops:
  7.2 366.5 %all-gather.2.cloned.1.call-start = ((), (), s32[]{:S(2)}) async-start(), calls=%async_computation | async-start | bytes 4456448 | tf_op jit(solution)/shard_map/all_gather | solution.py:118
  18.0 16.8 %collective-permute-start.1 = (bf16[128,2048]{1,0:T(8,128)(2,1)S(1)}, bf16[128,2048]{1,0:T(8,128)(2,1)S(1)}, u32[]{:S(2)}, u32[]{:S(2)}) collective-permute-start(bf16[128,2048]{1,0:T(8,128)(2,1)S(1)} %get-tuple-element.478), channel_id=1, source_target_pairs={{0,1},{1,0},{2,3},{3,2},{4,5},{5,4},{6,7},{7,6},{8,9},{9,8},{10,11... | collective-permute-start | bytes 1572872 | tf_op jit(solution)/shard_map/while/body/eval_jaxpr/ppermute | solution.py:32
  20.1 25.9 %collective-permute-start = (bf16[128,2048]{1,0:T(8,128)(2,1)S(1)}, bf16[128,2048]{1,0:T(8,128)(2,1)S(1)}, u32[]{:S(2)}, u32[]{:S(2)}) collective-permute-start(bf16[128,2048]{1,0:T(8,128)(2,1)S(1)} %broadcast_select_fusion.8), channel_id=1, source_target_pairs={{0,32},{32,64},{64,96},{1,33},{33,65},{65,97},{2,34},{34,66},{66,9... | collective-permute-start | bytes 1572872 | tf_op jit(solution)/shard_map/while/body/eval_jaxpr/ppermute | solution.py:133
  46.1 24.5 %collective-permute-start.1 = (bf16[128,2048]{1,0:T(8,128)(2,1)S(1)}, bf16[128,2048]{1,0:T(8,128)(2,1)S(1)}, u32[]{:S(2)}, u32[]{:S(2)}) collective-permute-start(bf16[128,2048]{1,0:T(8,128)(2,1)S(1)} %get-tuple-element.478), channel_id=1, source_target_pairs={{0,1},{1,0},{2,3},{3,2},{4,5},{5,4},{6,7},{7,6},{8,9},{9,8},{10,11... | collective-permute-start | bytes 1572872 | tf_op jit(solution)/shard_map/while/body/eval_jaxpr/ppermute | solution.py:32
  49.0 33.1 %collective-permute-start = (bf16[128,2048]{1,0:T(8,128)(2,1)S(1)}, bf16[128,2048]{1,0:T(8,128)(2,1)S(1)}, u32[]{:S(2)}, u32[]{:S(2)}) collective-permute-start(bf16[128,2048]{1,0:T(8,128)(2,1)S(1)} %broadcast_select_fusion.8), channel_id=1, source_target_pairs={{0,32},{32,64},{64,96},{1,33},{33,65},{65,97},{2,34},{34,66},{66,9... | collective-permute-start | bytes 1572872 | tf_op jit(solution)/shard_map/while/body/eval_jaxpr/ppermute | solution.py:133
  82.2 13.0 %collective-permute-start.1 = (bf16[128,2048]{1,0:T(8,128)(2,1)S(1)}, bf16[128,2048]{1,0:T(8,128)(2,1)S(1)}, u32[]{:S(2)}, u32[]{:S(2)}) collective-permute-start(bf16[128,2048]{1,0:T(8,128)(2,1)S(1)} %get-tuple-element.478), channel_id=1, source_target_pairs={{0,1},{1,0},{2,3},{3,2},{4,5},{5,4},{6,7},{7,6},{8,9},{9,8},{10,11... | collective-permute-start | bytes 1572872 | tf_op jit(solution)/shard_map/while/body/eval_jaxpr/ppermute | solution.py:32
  83.7 22.6 %collective-permute-start = (bf16[128,2048]{1,0:T(8,128)(2,1)S(1)}, bf16[128,2048]{1,0:T(8,128)(2,1)S(1)}, u32[]{:S(2)}, u32[]{:S(2)}) collective-permute-start(bf16[128,2048]{1,0:T(8,128)(2,1)S(1)} %broadcast_select_fusion.8), channel_id=1, source_target_pairs={{0,32},{32,64},{64,96},{1,33},{33,65},{65,97},{2,34},{34,66},{66,9... | collective-permute-start | bytes 1572872 | tf_op jit(solution)/shard_map/while/body/eval_jaxpr/ppermute | solution.py:133
  106.4 12.2 %collective-permute-start.1 = (bf16[128,2048]{1,0:T(8,128)(2,1)S(1)}, bf16[128,2048]{1,0:T(8,128)(2,1)S(1)}, u32[]{:S(2)}, u32[]{:S(2)}) collective-permute-start(bf16[128,2048]{1,0:T(8,128)(2,1)S(1)} %get-tuple-element.478), channel_id=1, source_target_pairs={{0,1},{1,0},{2,3},{3,2},{4,5},{5,4},{6,7},{7,6},{8,9},{9,8},{10,11... | collective-permute-start | bytes 1572872 | tf_op jit(solution)/shard_map/while/body/eval_jaxpr/ppermute | solution.py:32
  108.5 21.2 %collective-permute-start = (bf16[128,2048]{1,0:T(8,128)(2,1)S(1)}, bf16[128,2048]{1,0:T(8,128)(2,1)S(1)}, u32[]{:S(2)}, u32[]{:S(2)}) collective-permute-start(bf16[128,2048]{1,0:T(8,128)(2,1)S(1)} %broadcast_select_fusion.8), channel_id=1, source_target_pairs={{0,32},{32,64},{64,96},{1,33},{33,65},{65,97},{2,34},{34,66},{66,9... | collective-permute-start | bytes 1572872 | tf_op jit(solution)/shard_map/while/body/eval_jaxpr/ppermute | solution.py:133
  129.8 11.6 %collective-permute-start.1 = (bf16[128,2048]{1,0:T(8,128)(2,1)S(1)}, bf16[128,2048]{1,0:T(8,128)(2,1)S(1)}, u32[]{:S(2)}, u32[]{:S(2)}) collective-permute-start(bf16[128,2048]{1,0:T(8,128)(2,1)S(1)} %get-tuple-element.478), channel_id=1, source_target_pairs={{0,1},{1,0},{2,3},{3,2},{4,5},{5,4},{6,7},{7,6},{8,9},{9,8},{10,11... | collective-permute-start | bytes 1572872 | tf_op jit(solution)/shard_map/while/body/eval_jaxpr/ppermute | solution.py:32
  132.5 20.1 %collective-permute-start = (bf16[128,2048]{1,0:T(8,128)(2,1)S(1)}, bf16[128,2048]{1,0:T(8,128)(2,1)S(1)}, u32[]{:S(2)}, u32[]{:S(2)}) collective-permute-start(bf16[128,2048]{1,0:T(8,128)(2,1)S(1)} %broadcast_select_fusion.8), channel_id=1, source_target_pairs={{0,32},{32,64},{64,96},{1,33},{33,65},{65,97},{2,34},{34,66},{66,9... | collective-permute-start | bytes 1572872 | tf_op jit(solution)/shard_map/while/body/eval_jaxpr/ppermute | solution.py:133
  152.6 11.0 %collective-permute-start.1 = (bf16[128,2048]{1,0:T(8,128)(2,1)S(1)}, bf16[128,2048]{1,0:T(8,128)(2,1)S(1)}, u32[]{:S(2)}, u32[]{:S(2)}) collective-permute-start(bf16[128,2048]{1,0:T(8,128)(2,1)S(1)} %get-tuple-element.478), channel_id=1, source_target_pairs={{0,1},{1,0},{2,3},{3,2},{4,5},{5,4},{6,7},{7,6},{8,9},{9,8},{10,11... | collective-permute-start | bytes 1572872 | tf_op jit(solution)/shard_map/while/body/eval_jaxpr/ppermute | solution.py:32
  155.5 19.3 %collective-permute-start = (bf16[128,2048]{1,0:T(8,128)(2,1)S(1)}, bf16[128,2048]{1,0:T(8,128)(2,1)S(1)}, u32[]{:S(2)}, u32[]{:S(2)}) collective-permute-start(bf16[128,2048]{1,0:T(8,128)(2,1)S(1)} %broadcast_select_fusion.8), channel_id=1, source_target_pairs={{0,32},{32,64},{64,96},{1,33},{33,65},{65,97},{2,34},{34,66},{66,9... | collective-permute-start | bytes 1572872 | tf_op jit(solution)/shard_map/while/body/eval_jaxpr/ppermute | solution.py:133
  174.9 10.2 %collective-permute-start.1 = (bf16[128,2048]{1,0:T(8,128)(2,1)S(1)}, bf16[128,2048]{1,0:T(8,128)(2,1)S(1)}, u32[]{:S(2)}, u32[]{:S(2)}) collective-permute-start(bf16[128,2048]{1,0:T(8,128)(2,1)S(1)} %get-tuple-element.478), channel_id=1, source_target_pairs={{0,1},{1,0},{2,3},{3,2},{4,5},{5,4},{6,7},{7,6},{8,9},{9,8},{10,11... | collective-permute-start | bytes 1572872 | tf_op jit(solution)/shard_map/while/body/eval_jaxpr/ppermute | solution.py:32
  177.8 18.4 %collective-permute-start = (bf16[128,2048]{1,0:T(8,128)(2,1)S(1)}, bf16[128,2048]{1,0:T(8,128)(2,1)S(1)}, u32[]{:S(2)}, u32[]{:S(2)}) collective-permute-start(bf16[128,2048]{1,0:T(8,128)(2,1)S(1)} %broadcast_select_fusion.8), channel_id=1, source_target_pairs={{0,32},{32,64},{64,96},{1,33},{33,65},{65,97},{2,34},{34,66},{66,9... | collective-permute-start | bytes 1572872 | tf_op jit(solution)/shard_map/while/body/eval_jaxpr/ppermute | solution.py:133
  196.2 9.3 %collective-permute-start.1 = (bf16[128,2048]{1,0:T(8,128)(2,1)S(1)}, bf16[128,2048]{1,0:T(8,128)(2,1)S(1)}, u32[]{:S(2)}, u32[]{:S(2)}) collective-permute-start(bf16[128,2048]{1,0:T(8,128)(2,1)S(1)} %get-tuple-element.478), channel_id=1, source_target_pairs={{0,1},{1,0},{2,3},{3,2},{4,5},{5,4},{6,7},{7,6},{8,9},{9,8},{10,11... | collective-permute-start | bytes 1572872 | tf_op jit(solution)/shard_map/while/body/eval_jaxpr/ppermute | solution.py:32
  199.1 17.6 %collective-permute-start = (bf16[128,2048]{1,0:T(8,128)(2,1)S(1)}, bf16[128,2048]{1,0:T(8,128)(2,1)S(1)}, u32[]{:S(2)}, u32[]{:S(2)}) collective-permute-start(bf16[128,2048]{1,0:T(8,128)(2,1)S(1)} %broadcast_select_fusion.8), channel_id=1, source_target_pairs={{0,32},{32,64},{64,96},{1,33},{33,65},{65,97},{2,34},{34,66},{66,9... | collective-permute-start | bytes 1572872 | tf_op jit(solution)/shard_map/while/body/eval_jaxpr/ppermute | solution.py:133
  216.8 9.3 %collective-permute-start.1 = (bf16[128,2048]{1,0:T(8,128)(2,1)S(1)}, bf16[128,2048]{1,0:T(8,128)(2,1)S(1)}, u32[]{:S(2)}, u32[]{:S(2)}) collective-permute-start(bf16[128,2048]{1,0:T(8,128)(2,1)S(1)} %get-tuple-element.478), channel_id=1, source_target_pairs={{0,1},{1,0},{2,3},{3,2},{4,5},{5,4},{6,7},{7,6},{8,9},{9,8},{10,11... | collective-permute-start | bytes 1572872 | tf_op jit(solution)/shard_map/while/body/eval_jaxpr/ppermute | solution.py:32
  219.7 17.5 %collective-permute-start = (bf16[128,2048]{1,0:T(8,128)(2,1)S(1)}, bf16[128,2048]{1,0:T(8,128)(2,1)S(1)}, u32[]{:S(2)}, u32[]{:S(2)}) collective-permute-start(bf16[128,2048]{1,0:T(8,128)(2,1)S(1)} %broadcast_select_fusion.8), channel_id=1, source_target_pairs={{0,32},{32,64},{64,96},{1,33},{33,65},{65,97},{2,34},{34,66},{66,9... | collective-permute-start | bytes 1572872 | tf_op jit(solution)/shard_map/while/body/eval_jaxpr/ppermute | solution.py:133
  237.2 9.3 %collective-permute-start.1 = (bf16[128,2048]{1,0:T(8,128)(2,1)S(1)}, bf16[128,2048]{1,0:T(8,128)(2,1)S(1)}, u32[]{:S(2)}, u32[]{:S(2)}) collective-permute-start(bf16[128,2048]{1,0:T(8,128)(2,1)S(1)} %get-tuple-element.478), channel_id=1, source_target_pairs={{0,1},{1,0},{2,3},{3,2},{4,5},{5,4},{6,7},{7,6},{8,9},{9,8},{10,11... | collective-permute-start | bytes 1572872 | tf_op jit(solution)/shard_map/while/body/eval_jaxpr/ppermute | solution.py:32
  240.1 17.5 %collective-permute-start = (bf16[128,2048]{1,0:T(8,128)(2,1)S(1)}, bf16[128,2048]{1,0:T(8,128)(2,1)S(1)}, u32[]{:S(2)}, u32[]{:S(2)}) collective-permute-start(bf16[128,2048]{1,0:T(8,128)(2,1)S(1)} %broadcast_select_fusion.8), channel_id=1, source_target_pairs={{0,32},{32,64},{64,96},{1,33},{33,65},{65,97},{2,34},{34,66},{66,9... | collective-permute-start | bytes 1572872 | tf_op jit(solution)/shard_map/while/body/eval_jaxpr/ppermute | solution.py:133
  257.7 9.3 %collective-permute-start.1 = (bf16[128,2048]{1,0:T(8,128)(2,1)S(1)}, bf16[128,2048]{1,0:T(8,128)(2,1)S(1)}, u32[]{:S(2)}, u32[]{:S(2)}) collective-permute-start(bf16[128,2048]{1,0:T(8,128)(2,1)S(1)} %get-tuple-element.478), channel_id=1, source_target_pairs={{0,1},{1,0},{2,3},{3,2},{4,5},{5,4},{6,7},{7,6},{8,9},{9,8},{10,11... | collective-permute-start | bytes 1572872 | tf_op jit(solution)/shard_map/while/body/eval_jaxpr/ppermute | solution.py:32
  260.6 17.5 %collective-permute-start = (bf16[128,2048]{1,0:T(8,128)(2,1)S(1)}, bf16[128,2048]{1,0:T(8,128)(2,1)S(1)}, u32[]{:S(2)}, u32[]{:S(2)}) collective-permute-start(bf16[128,2048]{1,0:T(8,128)(2,1)S(1)} %broadcast_select_fusion.8), channel_id=1, source_target_pairs={{0,32},{32,64},{64,96},{1,33},{33,65},{65,97},{2,34},{34,66},{66,9... | collective-permute-start | bytes 1572872 | tf_op jit(solution)/shard_map/while/body/eval_jaxpr/ppermute | solution.py:133
  278.2 9.3 %collective-permute-start.1 = (bf16[128,2048]{1,0:T(8,128)(2,1)S(1)}, bf16[128,2048]{1,0:T(8,128)(2,1)S(1)}, u32[]{:S(2)}, u32[]{:S(2)}) collective-permute-start(bf16[128,2048]{1,0:T(8,128)(2,1)S(1)} %get-tuple-element.478), channel_id=1, source_target_pairs={{0,1},{1,0},{2,3},{3,2},{4,5},{5,4},{6,7},{7,6},{8,9},{9,8},{10,11... | collective-permute-start | bytes 1572872 | tf_op jit(solution)/shard_map/while/body/eval_jaxpr/ppermute | solution.py:32
  281.1 17.5 %collective-permute-start = (bf16[128,2048]{1,0:T(8,128)(2,1)S(1)}, bf16[128,2048]{1,0:T(8,128)(2,1)S(1)}, u32[]{:S(2)}, u32[]{:S(2)}) collective-permute-start(bf16[128,2048]{1,0:T(8,128)(2,1)S(1)} %broadcast_select_fusion.8), channel_id=1, source_target_pairs={{0,32},{32,64},{64,96},{1,33},{33,65},{65,97},{2,34},{34,66},{66,9... | collective-permute-start | bytes 1572872 | tf_op jit(solution)/shard_map/while/body/eval_jaxpr/ppermute | solution.py:133
  298.7 9.3 %collective-permute-start.1 = (bf16[128,2048]{1,0:T(8,128)(2,1)S(1)}, bf16[128,2048]{1,0:T(8,128)(2,1)S(1)}, u32[]{:S(2)}, u32[]{:S(2)}) collective-permute-start(bf16[128,2048]{1,0:T(8,128)(2,1)S(1)} %get-tuple-element.478), channel_id=1, source_target_pairs={{0,1},{1,0},{2,3},{3,2},{4,5},{5,4},{6,7},{7,6},{8,9},{9,8},{10,11... | collective-permute-start | bytes 1572872 | tf_op jit(solution)/shard_map/while/body/eval_jaxpr/ppermute | solution.py:32
  301.6 17.5 %collective-permute-start = (bf16[128,2048]{1,0:T(8,128)(2,1)S(1)}, bf16[128,2048]{1,0:T(8,128)(2,1)S(1)}, u32[]{:S(2)}, u32[]{:S(2)}) collective-permute-start(bf16[128,2048]{1,0:T(8,128)(2,1)S(1)} %broadcast_select_fusion.8), channel_id=1, source_target_pairs={{0,32},{32,64},{64,96},{1,33},{33,65},{65,97},{2,34},{34,66},{66,9... | collective-permute-start | bytes 1572872 | tf_op jit(solution)/shard_map/while/body/eval_jaxpr/ppermute | solution.py:133
  319.2 9.3 %collective-permute-start.1 = (bf16[128,2048]{1,0:T(8,128)(2,1)S(1)}, bf16[128,2048]{1,0:T(8,128)(2,1)S(1)}, u32[]{:S(2)}, u32[]{:S(2)}) collective-permute-start(bf16[128,2048]{1,0:T(8,128)(2,1)S(1)} %get-tuple-element.478), channel_id=1, source_target_pairs={{0,1},{1,0},{2,3},{3,2},{4,5},{5,4},{6,7},{7,6},{8,9},{9,8},{10,11... | collective-permute-start | bytes 1572872 | tf_op jit(solution)/shard_map/while/body/eval_jaxpr/ppermute | solution.py:32
  322.1 17.5 %collective-permute-start = (bf16[128,2048]{1,0:T(8,128)(2,1)S(1)}, bf16[128,2048]{1,0:T(8,128)(2,1)S(1)}, u32[]{:S(2)}, u32[]{:S(2)}) collective-permute-start(bf16[128,2048]{1,0:T(8,128)(2,1)S(1)} %broadcast_select_fusion.8), channel_id=1, source_target_pairs={{0,32},{32,64},{64,96},{1,33},{33,65},{65,97},{2,34},{34,66},{66,9... | collective-permute-start | bytes 1572872 | tf_op jit(solution)/shard_map/while/body/eval_jaxpr/ppermute | solution.py:133
  354.4 9.3 %collective-permute-start.4 = (f32[1024,128]{0,1:T(8,128)S(1)}, f32[1024,128]{0,1:T(8,128)S(1)}, u32[]{:S(2)}, u32[]{:S(2)}) collective-permute-start(f32[1024,128]{0,1:T(8,128)S(1)} %fusion.8), channel_id=1, source_target_pairs={{0,1},{1,0},{2,3},{3,2},{4,5},{5,4},{6,7},{7,6},{8,9},{9,8},{10,11... | collective-permute-start | bytes 1572872 | tf_op jit(solution)/shard_map/ppermute | solution.py:32
  400.0 9.9 %collective-permute-start.23 = (f32[4,2,2,32,128]{4,3,2,1,0:T(8,128)S(1)}, f32[4,2,2,32,128]{4,3,2,1,0:T(8,128)S(1)}, u32[]{:S(2)}, u32[]{:S(2)}) collective-permute-start(f32[4,2,2,32,128]{4,3,2,1,0:T(8,128)S(1)} %dynamic-slice_bitcast_fusion.1), channel_id=1, source_target_pairs={{0,8},{2,10},{4,12},{6,14},{8,16},{10,18},{12,20},{14,22},{16,24},... | collective-permute-start | bytes 786440 | tf_op jit(solution)/shard_map/ppermute | solution.py:36
  403.4 9.6 %collective-permute-start.9 = (f32[4,2,2,32,128]{4,3,2,1,0:T(8,128)S(1)}, f32[4,2,2,32,128]{4,3,2,1,0:T(8,128)S(1)}, u32[]{:S(2)}, u32[]{:S(2)}) collective-permute-start(f32[4,2,2,32,128]{4,3,2,1,0:T(8,128)S(1)} %dynamic-slice_bitcast_fusion.3), channel_id=1, source_target_pairs={{0,32},{32,64},{64,96},{96,0},{1,33},{33,65},{65,97},{97,1},{2,34}... | collective-permute-start | bytes 786440 | tf_op jit(solution)/shard_map/ppermute | solution.py:32
  (44 other events, 241.1 us)
Sparse Core Ops, SparseCore 0:
  10.4 69.6 all-gather.1
